TPU v7x, 256 devices: a whole 4x4x8 slice. The times are simulated.
256 devices in a mesh: theta: 16 (over y, x_hi, core), phi: 16 (over x_lo, z).
Axes of the slice: x: 4 (x_hi: 2, x_lo: 2; x = x_hi * 2 + x_lo), y: 4, z: 8, core: 2. Of those that a mesh axis runs over, the one named last changes fastest.
Arguments:
- density: float32 [2, 128, 1536, 128], P(None, 'theta', 'phi'), may hold values from 0.5 to 2
- velocity: float32 [3, 128, 1536, 128], P(None, 'theta', 'phi'), may hold values from -3 to 3
- bfield: float32 [3, 128, 1536, 128], P(None, 'theta', 'phi'), may hold values from -6 to 6
- levels: int32 [2, 4], replicated, may hold values from 0 to 3
Outputs:
- density_new: float32 [2, 128, 1536, 128], P(None, 'theta', 'phi')
- bfield_new: float32 [3, 128, 1536, 128], P(None, 'theta', 'phi')
Inputs may be any that keep to these rules, and one draw needn't show every extreme that they name: `levels`: a row at level l keeps the azimuthal modes below 128 // 2**l.
All inputs are finite; a program needn't handle non-finite values.
Results may differ from a plain program's by a relative error of at most 0.00007.
Values sent between devices are 32-bit elements; how exact they have to be, the bound alone decides.
No kernel may reach another device: no remote copies, remote signals or barrier semaphores. Data moves between devices by JAX's collectives and lax.ppermute only.
A program may use at most 64 MiB of HBM per device.

v0:
```python
import math

import jax
import jax.numpy as jnp
from jax import lax
from jax.sharding import PartitionSpec as P

CAP = 4
KMAX = 128


TIME_STEP = 0.2
PARITY = (1.0, 1.0, 1.0, -1.0, -1.0, 1.0, -1.0, -1.0)


def shifted_2(block, axis, distance):
    devices = range(lax.axis_size(axis))
    route = [((i - distance) % len(devices), i) for i in devices]
    return lax.ppermute(block, axis, route)


def with_halo(cells, sides, width, closed):
    for axis, dim in sides:
        count = lax.axis_size(axis)
        ends = count if closed else count - 1
        head = lax.slice_in_dim(cells, 0, width, axis=dim)
        tail = lax.slice_in_dim(cells, cells.shape[dim] - width, cells.shape[dim], axis=dim)
        cells = jnp.concatenate(
            [
                lax.ppermute(tail, axis, [(i, (i + 1) % count) for i in range(ends)]),
                cells,
                lax.ppermute(head, axis, [((i + 1) % count, i) for i in range(ends)]),
            ],
            axis=dim,
        )
    return cells


def window_of(array, spans):
    return array[spans[0][0] : spans[0][1], spans[1][0] : spans[1][1], spans[2][0] : spans[2][1]]


def moved(spans, direction, start, length):
    return tuple(
        ((start, start + length) if other == direction else spans[other] for other in range(3))
    )


def corner_mean(field, extents, first_axis, second_axis):
    base = [(1, extents[0] + 1), (1, extents[1] + 1), (1, extents[2] + 1)]
    total = jnp.zeros((), jnp.float32)
    for first_start in (0, 1):
        for second_start in (0, 1):
            spans_now = list(base)
            spans_now[first_axis] = (first_start, first_start + extents[first_axis] + 1)
            spans_now[second_axis] = (second_start, second_start + extents[second_axis] + 1)
            total = total + window_of(field, spans_now)
    return 0.25 * total


def advance(extended):
    extents = (extended.shape[1] - 4, extended.shape[2] - 4, extended.shape[3] - 4)
    inner_span = tuple(((2, extent + 2) for extent in extents))
    speed_for = (3, 4, 2)
    densities = []
    for channel in range(2):
        amount = extended[channel]
        tendency = jnp.zeros(extents, jnp.float32)
        for direction in range(3):
            extent_now = extents[direction]
            lower_span = moved(inner_span, direction, 1, extent_now + 1)
            upper_span = moved(inner_span, direction, 2, extent_now + 1)
            speed_field = extended[speed_for[direction]]
            left_amount = window_of(amount, lower_span)
            right_amount = window_of(amount, upper_span)
            left_speed = window_of(speed_field, lower_span)
            right_speed = window_of(speed_field, upper_span)
            fluxes = 0.5 * (
                left_amount * left_speed + right_amount * right_speed
            ) - 0.5 * jnp.maximum(jnp.abs(left_speed), jnp.abs(right_speed)) * (
                right_amount - left_amount
            )
            tendency = (
                tendency
                + lax.slice_in_dim(fluxes, 1, extent_now + 1, axis=direction)
                - lax.slice_in_dim(fluxes, 0, extent_now, axis=direction)
            )
        densities.append(window_of(amount, inner_span) - TIME_STEP * tendency)
    wide_span = tuple(((1, extent + 3) for extent in extents))
    axis_of = (2, 0, 1)
    centred = []
    for component in range(3):
        direction = axis_of[component]
        shifted = moved(wide_span, direction, 2, extents[direction] + 2)
        face_field = extended[5 + component]
        centred.append(0.5 * (window_of(face_field, wide_span) + window_of(face_field, shifted)))
    speeds = [window_of(extended[2 + component], wide_span) for component in range(3)]
    emf_radial = -(speeds[1] * centred[2] - speeds[2] * centred[1])
    emf_theta = -(speeds[2] * centred[0] - speeds[0] * centred[2])
    emf_phi = -(speeds[0] * centred[1] - speeds[1] * centred[0])
    edge_phi = corner_mean(emf_phi, extents, 0, 2)
    edge_theta = corner_mean(emf_theta, extents, 1, 2)
    edge_radial = corner_mean(emf_radial, extents, 0, 1)
    radial_len = extents[2]
    inner_faces = [window_of(extended[5 + component], inner_span) for component in range(3)]
    new_radial = inner_faces[0] - TIME_STEP * (
        edge_phi[1:, :, :radial_len]
        - edge_phi[:-1, :, :radial_len]
        - (edge_theta[:, 1:, :radial_len] - edge_theta[:, :-1, :radial_len])
    )
    new_theta = inner_faces[1] - TIME_STEP * (
        edge_radial[:-1, 1:, :]
        - edge_radial[:-1, :-1, :]
        - (edge_phi[:-1, :, 1:] - edge_phi[:-1, :, :-1])
    )
    new_phi = inner_faces[2] - TIME_STEP * (
        edge_theta[:, :-1, 1:]
        - edge_theta[:, :-1, :-1]
        - (edge_radial[1:, :-1, :] - edge_radial[:-1, :-1, :])
    )
    return (jnp.stack(densities), jnp.stack([new_radial, new_theta, new_phi]))


def fourier_table(cycle_len, orders_kept):
    points = jnp.arange(cycle_len, dtype=jnp.int32)[:, None]
    orders = jnp.arange(orders_kept, dtype=jnp.int32)[None, :]
    phase = points * orders % cycle_len
    angle = phase.astype(jnp.float32) * (2.0 * math.pi / cycle_len)
    return jnp.concatenate([jnp.cos(angle), jnp.sin(angle)], axis=1)


def local(density, velocity, bfield, levels):
    combined = jnp.concatenate([density, velocity, bfield], axis=0)
    channels, theta_len, phi_len, radial_len = combined.shape
    theta_count = lax.axis_size("theta")
    phi_count = lax.axis_size("phi")
    theta_index = lax.axis_index("theta")
    phi_index = lax.axis_index("phi")
    at_north = theta_index == 0
    at_south = theta_index == theta_count - 1
    edge_rows = jnp.where(at_north, combined[:, :CAP], combined[:, theta_len - CAP :])
    slot_rows = edge_rows.reshape(channels * CAP, phi_len, radial_len)
    cycle_rows = lax.all_to_all(slot_rows, "phi", split_axis=0, concat_axis=1, tiled=True)
    per_device = cycle_rows.shape[0]
    cycle_len = cycle_rows.shape[1]
    fourier = fourier_table(cycle_len, KMAX)
    pole_pick = jnp.where(at_north, 0, 1).astype(jnp.int32)
    level_row = lax.dynamic_index_in_dim(levels, pole_pick, 0, keepdims=False)
    slot_ids = phi_index * per_device + jnp.arange(per_device, dtype=jnp.int32)
    row_ids = slot_ids % CAP
    slot_levels = jnp.sum(
        jnp.where(
            row_ids[:, None] == jnp.arange(CAP, dtype=jnp.int32)[None, :], level_row[None, :], 0
        ),
        axis=1,
    )
    limits = jnp.right_shift(jnp.int32(KMAX), slot_levels)
    column_order = jnp.arange(2 * KMAX, dtype=jnp.int32) % KMAX
    column_weight = jnp.where(column_order == 0, 1.0 / cycle_len, 2.0 / cycle_len).astype(
        jnp.float32
    )
    kept_weight = jnp.where(column_order[None, :] < limits[:, None], column_weight[None, :], 0.0)
    coeffs = jnp.einsum("spr,pm->smr", cycle_rows, fourier, precision=lax.Precision.HIGHEST)
    coeffs = coeffs * kept_weight[:, :, None]
    filtered = jnp.einsum("smr,pm->spr", coeffs, fourier, precision=lax.Precision.HIGHEST)
    parity = jnp.array(PARITY, jnp.float32)
    returned = lax.all_to_all(filtered, "phi", split_axis=1, concat_axis=0, tiled=True)
    cap_rows = returned.reshape(channels, CAP, phi_len, radial_len)
    north_version = jnp.concatenate([cap_rows, combined[:, CAP:]], axis=1)
    south_version = jnp.concatenate([combined[:, : theta_len - CAP], cap_rows], axis=1)
    combined = jnp.where(at_north, north_version, jnp.where(at_south, south_version, combined))
    pole_rows = jnp.concatenate([combined[:, :1], combined[:, theta_len - 2 :]], axis=1)
    received = shifted_2(pole_rows, "phi", phi_count // 2)
    column_parity = parity[:, None, None]
    ghost_north = received[:, 0] * column_parity
    ghost_first = received[:, 2] * column_parity
    ghost_second = received[:, 1] * column_parity
    widened = with_halo(combined, (("theta", 1),), 2, False)
    row_place = jnp.arange(theta_len + 4, dtype=jnp.int32)[None, :, None, None]
    widened = jnp.where(at_north & (row_place == 1), ghost_north[:, None], widened)
    widened = jnp.where(at_south & (row_place == theta_len + 2), ghost_first[:, None], widened)
    widened = jnp.where(at_south & (row_place == theta_len + 3), ghost_second[:, None], widened)
    wrapped = with_halo(widened, (("phi", 2),), 2, True)
    padded = jnp.pad(wrapped, ((0, 0), (0, 0), (0, 0), (2, 2)), mode="edge")
    return advance(padded)


def solution(mesh):
    return jax.shard_map(
        local,
        mesh=mesh,
        in_specs=(
            P(None, "theta", "phi", None),
            P(None, "theta", "phi", None),
            P(None, "theta", "phi", None),
            P(),
        ),
        out_specs=(P(None, "theta", "phi", None), P(None, "theta", "phi", None)),
        check_vma=False,
    )
```

profile of v0, /device:TPU:1, one launch (start us, length us, event | category | flops | bytes accessed | tf_op | source)
XLA Modules:
  0.0 206.1 jit_solution(10269946624002756463)
XLA Ops:
  3.6 2.5 %fusion.46 = (f32[8,4,96,128]{3,2,1,0:T(8,128)}, f32[8,4,96,128]{3,2,1,0:T(8,128)}, f32[8,4,96,128]{3,2,1,0:T(8,128)}) fusion(f32[8,8,96,128]{3,2,1,0:T(8,128)S(1)} %constant_dynamic-update-slice_fusion, pred[]{:T(512)S(6)} %eq.59), kind=kLoop, calls=%fused_computation.125 | loop fusion | flops 393216 | bytes 7864321 | tf_op jit(solution)/shard_map/slice | solution.py:141
  6.1 10.1 %all-to-all-start = ((f32[32,96,128]{2,1,0:T(8,128)}), f32[32,96,128]{2,1,0:T(8,128)}, u32[]{:S(2)}, u32[]{:S(2)}) async-start(f32[32,96,128]{2,1,0:T(8,128)} %bitcast.68), calls=%async_computation | async-start | bytes 3145728 | tf_op jit(solution)/shard_map/all_to_all | solution.py:143
  16.5 4.3 %fusion.14 = (f32[1536,128]{0,1:T(8,128)}, f32[1536,128]{0,1:T(8,128)}) fusion(), kind=kLoop, calls=%fused_computation.49 | loop fusion | flops 1769472 | bytes 1572864 | tf_op jit(solution)/shard_map/sin | solution.py:129
  20.8 31.7 %all-to-all-done = f32[32,96,128]{2,1,0:T(8,128)} async-done(((f32[32,96,128]{2,1,0:T(8,128)}), f32[32,96,128]{2,1,0:T(8,128)}, u32[]{:S(2)}, u32[]{:S(2)}) %all-to-all-start) | async-done | bytes 1572896 | tf_op jit(solution)/shard_map/all_to_all | solution.py:143
  52.5 1.6 copy.43
  55.8 2.7 %convolution_bitcast_fusion = f32[2,1536,128]{2,1,0:T(8,128)S(1)} fusion(f32[2,256,128]{2,1,0:T(8,128)S(1)} %fusion.4, f32[1536,128]{0,1:T(8,128)S(1)} %copy-done.3, f32[1536,128]{0,1:T(8,128)S(1)} %copy-done.4), kind=kOutput, calls=%fused_computation.7 | convolution fusion | flops 1208352768 | bytes 3407872 | tf_op jit(solution)/shard_map/smr,pm->spr/dot_general | solution.py:165
  58.5 6.6 %copy.45 = f32[2,1536,128]{2,0,1:T(2,128)} copy(f32[2,1536,128]{2,1,0:T(8,128)S(1)} %convolution_bitcast_fusion) | data formatting | bytes 3145728 | tf_op jit(solution)/shard_map/smr,pm->spr/transpose | solution.py:165
  65.0 6.7 %all-to-all-start.1 = ((f32[2,1536,128]{2,0,1:T(2,128)}), f32[2,1536,128]{2,0,1:T(2,128)}, u32[]{:S(2)}, u32[]{:S(2)}) async-start(f32[2,1536,128]{2,0,1:T(2,128)} %copy.45), calls=%async_computation.1 | async-start | bytes 3145728 | tf_op jit(solution)/shard_map/all_to_all | solution.py:167
  71.7 36.3 %all-to-all-done.1 = f32[2,1536,128]{2,0,1:T(2,128)} async-done(((f32[2,1536,128]{2,0,1:T(2,128)}), f32[2,1536,128]{2,0,1:T(2,128)}, u32[]{:S(2)}, u32[]{:S(2)}) %all-to-all-start.1) | async-done | bytes 1572896 | tf_op jit(solution)/shard_map/all_to_all | solution.py:167
  108.0 1.5 copy.46
  113.0 4.7 %collective-permute-start.2 = (f32[8,2,96,128]{3,2,1,0:T(8,128)S(1)}, f32[8,2,96,128]{3,2,1,0:T(8,128)S(1)}, u32[]{:S(2)}, u32[]{:S(2)}) collective-permute-start(f32[8,2,96,128]{3,2,1,0:T(8,128)S(1)} %get-tuple-element.17), channel_id=1, source_target_pairs={{16,0},{32,16},{48,32},{64,48},{80,64},{96,80},{112,96},{128,112},... | collective-permute-start | bytes 2359304 | tf_op jit(solution)/shard_map/ppermute | solution.py:32
  117.6 4.4 %collective-permute-start.1 = (f32[8,2,96,128]{3,2,1,0:T(8,128)S(1)}, f32[8,2,96,128]{3,2,1,0:T(8,128)S(1)}, u32[]{:S(2)}, u32[]{:S(2)}) collective-permute-start(f32[8,2,96,128]{3,2,1,0:T(8,128)S(1)} %get-tuple-element.16), channel_id=1, source_target_pairs={{0,16},{16,32},{32,48},{48,64},{64,80},{80,96},{96,112},{112,128},... | collective-permute-start | bytes 2359304 | tf_op jit(solution)/shard_map/ppermute | solution.py:30
  122.1 15.3 %collective-permute-done = f32[8,3,96,128]{3,2,1,0:T(8,128)S(1)} collective-permute-done((f32[8,3,96,128]{3,2,1,0:T(8,128)S(1)}, f32[8,3,96,128]{3,2,1,0:T(8,128)S(1)}, u32[]{:S(2)}, u32[]{:S(2)}) %collective-permute-start) | collective-permute-done | bytes 1179680 | tf_op jit(solution)/shard_map/ppermute | solution.py:19
  137.6 20.9 %collective-permute-done.2 = f32[8,2,96,128]{3,2,1,0:T(8,128)S(1)} collective-permute-done((f32[8,2,96,128]{3,2,1,0:T(8,128)S(1)}, f32[8,2,96,128]{3,2,1,0:T(8,128)S(1)}, u32[]{:S(2)}, u32[]{:S(2)}) %collective-permute-start.2) | collective-permute-done | bytes 786464 | tf_op jit(solution)/shard_map/ppermute | solution.py:32
  159.8 1.5 collective-permute-start.3
  161.3 2.1 %collective-permute-start.4 = (f32[8,12,2,128]{3,2,1,0:T(2,128)S(1)}, f32[8,12,2,128]{3,2,1,0:T(2,128)S(1)}, u32[]{:S(2)}, u32[]{:S(2)}) collective-permute-start(f32[8,12,2,128]{3,2,1,0:T(2,128)S(1)} %get-tuple-element.15), channel_id=1, source_target_pairs={{1,0},{2,1},{3,2},{4,3},{5,4},{6,5},{7,6},{8,7},{9,8},{10,9},{11,1... | collective-permute-start | bytes 294920 | tf_op jit(solution)/shard_map/ppermute | solution.py:32
  163.4 2.0 collective-permute-done.3
  166.3 5.6 %fusion.43 = (f32[8,12,100,1]{3,2,1,0:T(8,128)}, f32[8,12,100,1]{3,2,1,0:T(8,128)}) fusion(f32[8,12,100,128]{3,2,1,0:T(8,128)S(1)} %pad_maximum_fusion.1), kind=kLoop, calls=%fused_computation.122 | loop fusion | bytes 153600 | tf_op jit(solution)/shard_map/jit(_pad)/slice | solution.py:184
  171.8 3.8 %copy.54 = f32[8,12,100,1]{2,1,0,3:T(8,128)S(1)} copy(f32[8,12,100,1]{3,2,1,0:T(8,128)} %get-tuple-element.12) | data formatting | bytes 76800 | tf_op jit(solution)/shard_map/jit(_pad)/slice | solution.py:184
  175.7 3.9 %copy.55 = f32[8,12,100,1]{2,1,0,3:T(8,128)S(1)} copy(f32[8,12,100,1]{3,2,1,0:T(8,128)} %get-tuple-element.13) | data formatting | bytes 76800 | tf_op jit(solution)/shard_map/jit(_pad)/slice | solution.py:184
  179.6 1.5 reshape.117
  182.6 8.5 %pad_maximum_fusion = f32[8,12,100,132]{3,2,1,0:T(8,128)} fusion(f32[8,12,100,2]{3,2,1,0:T(8,128)S(1)} %reshape.117, f32[8,12,2,128]{3,2,1,0:T(2,128)S(1)} %collective-permute-done.4, f32[8,12,96,128]{3,2,1,0:T(8,128)S(1)} %bitcast.65, f32[8,12,2,128]{3,2,1,0:T(2,128)S(1)} %collective-permute-done.3, f32[8,12,100,2]{3,2,1,0:T(8,128)S(1)} %reshape.116), kind=kLoop, calls=%fused_computation | loop fusion | flops 5068800 | bytes 10137600 | tf_op jit(solution)/shard_map/jit(_pad)/concatenate | solution.py:184
  191.1 4.6 %slice_bitcast_fusion.2 = (f32[12,100,132]{2,1,0:T(8,128)S(1)}, f32[12,100,132]{2,1,0:T(8,128)S(1)}, f32[12,100,132]{2,1,0:T(8,128)S(1)}, f32[12,100,132]{2,1,0:...) fusion(f32[8,12,100,132]{3,2,1,0:T(8,128)} %pad_maximum_fusion), kind=kLoop, calls=%fused_computation.12 | loop fusion | bytes 10137600 | tf_op jit(solution)/shard_map/squeeze | solution.py:105
  198.4 2.6 %subtract_negate_fusion.2 = (f32[10,98,130]{2,1,0:T(8,128)S(1)}, f32[10,98,130]{2,1,0:T(8,128)S(1)}, f32[10,98,130]{2,1,0:T(8,128)S(1)}) fusion(f32[12,100,132]{2,1,0:T(8,128)S(1)} %get-tuple-element.10, f32[12,100,132]{2,1,0:T(8,128)S(1)} %get-tuple-element.8, f32[12,100,132]{2,1,0:T(8,128)S(1)} %get-tuple-element.6, ...), kind=kLoop, calls=%fused_computation.31 | loop fusion | flops 2293200 | bytes 6115200 | tf_op jit(solution)/shard_map/neg | solution.py:100
  (60 shorter events, 19.8 us)
Async XLA Ops:
  0.6 15.6 %copy-start = (s32[2,4]{1,0:T(2,128)S(1)}, s32[2,4]{1,0:T(2,128)}, u32[]{:S(2)}) copy-start(s32[2,4]{1,0:T(2,128)} %param.8) | copy-start | bytes 100
  1.9 1.6 copy-start.7
  6.1 46.4 %all-to-all-start = ((f32[32,96,128]{2,1,0:T(8,128)}), f32[32,96,128]{2,1,0:T(8,128)}, u32[]{:S(2)}, u32[]{:S(2)}) async-start(f32[32,96,128]{2,1,0:T(8,128)} %bitcast.68), calls=%async_computation | async-start | bytes 3145728 | tf_op jit(solution)/shard_map/all_to_all | solution.py:143
  52.5 1.6 copy-start.3
  52.5 1.8 copy-start.4
  65.0 43.0 %all-to-all-start.1 = ((f32[2,1536,128]{2,0,1:T(2,128)}), f32[2,1536,128]{2,0,1:T(2,128)}, u32[]{:S(2)}, u32[]{:S(2)}) async-start(f32[2,1536,128]{2,0,1:T(2,128)} %copy.45), calls=%async_computation.1 | async-start | bytes 3145728 | tf_op jit(solution)/shard_map/all_to_all | solution.py:167
  109.5 1.4 copy-start.5
  109.5 1.9 copy-start.6
  112.4 24.9 %copy-start.8 = (f32[8]{0:T(128)S(1)}, f32[8]{0:T(128)}, u32[]{:S(2)}) copy-start(f32[8]{0:T(128)} %constant.88.clone) | copy-start | bytes 100
  112.6 24.8 %collective-permute-start = (f32[8,3,96,128]{3,2,1,0:T(8,128)S(1)}, f32[8,3,96,128]{3,2,1,0:T(8,128)S(1)}, u32[]{:S(2)}, u32[]{:S(2)}) collective-permute-start(f32[8,3,96,128]{3,2,1,0:T(8,128)S(1)} %pad_maximum_fusion.2), channel_id=1, source_target_pairs={{8,0},{9,1},{10,2},{11,3},{12,4},{13,5},{14,6},{15,7},{0,8},{1,9},... | collective-permute-start | bytes 3538952 | tf_op jit(solution)/shard_map/ppermute | solution.py:19
  113.0 45.5 %collective-permute-start.2 = (f32[8,2,96,128]{3,2,1,0:T(8,128)S(1)}, f32[8,2,96,128]{3,2,1,0:T(8,128)S(1)}, u32[]{:S(2)}, u32[]{:S(2)}) collective-permute-start(f32[8,2,96,128]{3,2,1,0:T(8,128)S(1)} %get-tuple-element.17), channel_id=1, source_target_pairs={{16,0},{32,16},{48,32},{64,48},{80,64},{96,80},{112,96},{128,112},... | collective-permute-start | bytes 2359304 | tf_op jit(solution)/shard_map/ppermute | solution.py:32
  117.6 40.9 %collective-permute-start.1 = (f32[8,2,96,128]{3,2,1,0:T(8,128)S(1)}, f32[8,2,96,128]{3,2,1,0:T(8,128)S(1)}, u32[]{:S(2)}, u32[]{:S(2)}) collective-permute-start(f32[8,2,96,128]{3,2,1,0:T(8,128)S(1)} %get-tuple-element.16), channel_id=1, source_target_pairs={{0,16},{16,32},{32,48},{48,64},{64,80},{80,96},{96,112},{112,128},... | collective-permute-start | bytes 2359304 | tf_op jit(solution)/shard_map/ppermute | solution.py:30
  159.7 5.7 %copy-start.2 = (f32[8,12,96,128]{3,2,1,0:T(8,128)}, f32[8,12,96,128]{3,2,1,0:T(8,128)S(1)}, u32[]{:S(2)}) copy-start(f32[8,12,96,128]{3,2,1,0:T(8,128)S(1)} %fusion.1) | copy-start | bytes 14155780
  159.8 5.7 %collective-permute-start.3 = (f32[8,12,2,128]{3,2,1,0:T(2,128)S(1)}, f32[8,12,2,128]{3,2,1,0:T(2,128)S(1)}, u32[]{:S(2)}, u32[]{:S(2)}) collective-permute-start(f32[8,12,2,128]{3,2,1,0:T(2,128)S(1)} %get-tuple-element.14), channel_id=1, source_target_pairs={{0,1},{1,2},{2,3},{3,4},{4,5},{5,6},{6,7},{7,8},{8,9},{9,10},{10,1... | collective-permute-start | bytes 294920 | tf_op jit(solution)/shard_map/ppermute | solution.py:30
  161.3 4.1 %collective-permute-start.4 = (f32[8,12,2,128]{3,2,1,0:T(2,128)S(1)}, f32[8,12,2,128]{3,2,1,0:T(2,128)S(1)}, u32[]{:S(2)}, u32[]{:S(2)}) collective-permute-start(f32[8,12,2,128]{3,2,1,0:T(2,128)S(1)} %get-tuple-element.15), channel_id=1, source_target_pairs={{1,0},{2,1},{3,2},{4,3},{5,4},{6,5},{7,6},{8,7},{9,8},{10,9},{11,1... | collective-permute-start | bytes 294920 | tf_op jit(solution)/shard_map/ppermute | solution.py:32
  175.7 6.9 %slice-start = ((s8[4718592]{0:T(1024)(128)(4,1)}), s8[524288]{0:T(1024)(128)(4,1)S(1)}, s32[]{:S(2)}) async-start(s8[4718592]{0:T(1024)(128)(4,1)} %bitcast.64), calls=%async_computation.2 | async-start | bytes 1048576
  179.6 3.0 %slice-start.1 = ((s8[4718592]{0:T(1024)(128)(4,1)}), s8[4194304]{0:T(1024)(128)(4,1)S(1)}, s32[]{:S(2)}) async-start(s8[4718592]{0:T(1024)(128)(4,1)} %bitcast.64), calls=%async_computation.3 | async-start | bytes 8388608
  204.3 1.8 copy-start.1
where the time goes:
time: 207 us; the launch traced here: 206 us
  waiting for transfers between devices  106 us (51%)
  local copies, waits for them, and re-layouts  35.8 us (17%)
  starting transfers between devices  29.9 us (14%)
  other arithmetic  29 us (14%)
  matrix products  4.13 us (2%)
    all_to_all x1, waiting for transfers between devices, local(): lax.all_to_all(filtered, 'phi', split_axis=1, concat_axis=0, tiled=True)  36.3 us
    all_to_all x1, waiting for transfers between devices, local(): lax.all_to_all(slot_rows, 'phi', split_axis=0, concat_axis=1, tiled=True)  31.7 us
    ppermute x2, waiting for transfers between devices, with_halo(): lax.ppermute(head, axis, [((i + 1) % count, i) for i in range(ends)])  20.9 us
    ppermute x1, waiting for transfers between devices, shifted_2(): return lax.ppermute(block, axis, route)  15.3 us
    slice x3, local copies, waits for them, and re-layouts, local(): padded = jnp.pad(wrapped, ((0, 0), (0, 0), (0, 0), (2, 2)), mode='edge')  13.3 us
    all_to_all x1, starting transfers between devices, local(): lax.all_to_all(slot_rows, 'phi', split_axis=0, concat_axis=1, tiled=True)  10.1 us
    concatenate x1, other arithmetic, local(): padded = jnp.pad(wrapped, ((0, 0), (0, 0), (0, 0), (2, 2)), mode='edge')  8.46 us
    ppermute x2, starting transfers between devices, with_halo(): lax.ppermute(head, axis, [((i + 1) % count, i) for i in range(ends)])  6.81 us
  transfers between devices with their start and end apart: 7, of which 5 were waited for; matrix products, arithmetic and copies ran while one was open for 2% of the time, Pallas kernels for 0%

commit v1 on v0

v1 whole, which is shorter than its diff:
```python
import math

import jax
import jax.numpy as jnp
from jax import lax
from jax.sharding import PartitionSpec as P

CAP = 4
KMAX = 128


TIME_STEP = 0.2
PARITY = (1.0, 1.0, 1.0, -1.0, -1.0, 1.0, -1.0, -1.0)


def up_r(a):
    return jnp.concatenate([a[..., 1:], a[..., -1:]], axis=-1)


def down_r(a):
    return jnp.concatenate([a[..., :1], a[..., :-1]], axis=-1)


def face_flux(left_amount, right_amount, left_speed, right_speed):
    return 0.5 * (left_amount * left_speed + right_amount * right_speed) - 0.5 * jnp.maximum(
        jnp.abs(left_speed), jnp.abs(right_speed)
    ) * (right_amount - left_amount)


def corner4(e00, e01, e10, e11):
    return 0.25 * (((e00 + e01) + e10) + e11)


def advance(x):
    ct = x.shape[1] - 3
    npc = x.shape[2] - 3
    densities = []
    for channel in range(2):
        q = x[channel]
        v_t = x[3]
        v_p = x[4]
        v_r = x[2]
        fl_t = face_flux(
            q[0 : ct + 1, 1 : npc + 1], q[1 : ct + 2, 1 : npc + 1],
            v_t[0 : ct + 1, 1 : npc + 1], v_t[1 : ct + 2, 1 : npc + 1],
        )
        fl_p = face_flux(
            q[1 : ct + 1, 0 : npc + 1], q[1 : ct + 1, 1 : npc + 2],
            v_p[1 : ct + 1, 0 : npc + 1], v_p[1 : ct + 1, 1 : npc + 2],
        )
        qi = q[1 : ct + 1, 1 : npc + 1]
        vi = v_r[1 : ct + 1, 1 : npc + 1]
        fl_lo = face_flux(down_r(qi), qi, down_r(vi), vi)
        fl_hi = face_flux(qi, up_r(qi), vi, up_r(vi))
        tendency = (fl_t[1:] - fl_t[:-1]) + (fl_p[:, 1:] - fl_p[:, :-1]) + (fl_hi - fl_lo)
        densities.append(qi - TIME_STEP * tendency)

    wr = slice(0, ct + 2)
    wc = slice(0, npc + 2)
    b_r = x[5][wr, wc]
    b_t = x[6]
    b_p = x[7]
    c_r = 0.5 * (b_r + up_r(b_r))
    c_t = 0.5 * (b_t[0 : ct + 2, wc] + b_t[1 : ct + 3, wc])
    c_p = 0.5 * (b_p[wr, 0 : npc + 2] + b_p[wr, 1 : npc + 3])
    s_r = x[2][wr, wc]
    s_t = x[3][wr, wc]
    s_p = x[4][wr, wc]
    emf_r = -(s_t * c_p - s_p * c_t)
    emf_t = -(s_p * c_r - s_r * c_p)
    emf_p = -(s_r * c_t - s_t * c_r)
    lane = lax.broadcasted_iota(jnp.int32, emf_t.shape, 2)
    last = emf_t.shape[2] - 1
    edge_t = -(s_p * b_r - s_r * c_p)
    edge_p = -(s_r * c_t - s_t * b_r)
    t_lo = jnp.where(lane == 0, edge_t, down_r(emf_t))
    t_hi = jnp.where(lane == last, edge_t, up_r(emf_t))
    p_lo = jnp.where(lane == 0, edge_p, down_r(emf_p))
    p_hi = jnp.where(lane == last, edge_p, up_r(emf_p))

    rows_a = slice(0, ct + 1)
    rows_b = slice(1, ct + 2)
    cols_in = slice(1, npc + 1)
    ep_lo = corner4(p_lo[rows_a, cols_in], emf_p[rows_a, cols_in], p_lo[rows_b, cols_in], emf_p[rows_b, cols_in])
    ep_hi = corner4(emf_p[rows_a, cols_in], p_hi[rows_a, cols_in], emf_p[rows_b, cols_in], p_hi[rows_b, cols_in])
    rows_in = slice(1, ct + 1)
    cols_a = slice(0, npc + 1)
    cols_b = slice(1, npc + 2)
    et_lo = corner4(t_lo[rows_in, cols_a], emf_t[rows_in, cols_a], t_lo[rows_in, cols_b], emf_t[rows_in, cols_b])
    et_hi = corner4(emf_t[rows_in, cols_a], t_hi[rows_in, cols_a], emf_t[rows_in, cols_b], t_hi[rows_in, cols_b])
    er = corner4(emf_r[rows_a, cols_a], emf_r[rows_a, cols_b], emf_r[rows_b, cols_a], emf_r[rows_b, cols_b])

    inner = (slice(1, ct + 1), slice(1, npc + 1))
    new_radial = x[5][inner] - TIME_STEP * (
        (ep_lo[1:] - ep_lo[:-1]) - (et_lo[:, 1:] - et_lo[:, :-1])
    )
    new_theta = x[6][inner] - TIME_STEP * (
        (er[:-1, 1:] - er[:-1, :-1]) - (ep_hi[:-1] - ep_lo[:-1])
    )
    new_phi = x[7][inner] - TIME_STEP * (
        (et_hi[:, :-1] - et_lo[:, :-1]) - (er[1:, :-1] - er[:-1, :-1])
    )
    return jnp.stack(densities), jnp.stack([new_radial, new_theta, new_phi])


def fourier_rows(cols, cycle_len):
    orders = jnp.arange(KMAX, dtype=jnp.int32)
    phase = (cols[..., None] * orders) % cycle_len
    angle = phase.astype(jnp.float32) * (2.0 * math.pi / cycle_len)
    return jnp.concatenate([jnp.cos(angle), jnp.sin(angle)], axis=-1)


def local(density, velocity, bfield, levels):
    combined = jnp.concatenate([density, velocity, bfield], axis=0)
    channels, ct, npc, nr = combined.shape
    theta_count = lax.axis_size("theta")
    phi_count = lax.axis_size("phi")
    t = lax.axis_index("theta")
    p = lax.axis_index("phi")
    at_north = t == 0
    at_south = t == theta_count - 1
    is_pole = at_north | at_south
    cycle_len = npc * phi_count
    parity = jnp.array(PARITY, jnp.float32)
    poles = (0, theta_count - 1)
    both = ("theta", "phi")

    def pole_pairs(shift):
        return [
            (a * phi_count + b, a * phi_count + (b + shift) % phi_count)
            for a in poles
            for b in range(phi_count)
        ]

    low_halo = lax.ppermute(
        combined[:, ct - 1], "theta", [(i, i + 1) for i in range(theta_count - 1)]
    )
    up_send = jnp.concatenate([combined[:, 0], combined[6:7, 1]], axis=0)
    up_halo = lax.ppermute(up_send, "theta", [(i + 1, i) for i in range(theta_count - 1)])
    rows_ext = jnp.concatenate(
        [
            low_halo[:, None],
            combined,
            up_halo[:channels, None],
            jnp.broadcast_to(up_halo[channels:], (channels, npc, nr))[:, None],
        ],
        axis=1,
    )
    left_cols = lax.ppermute(
        rows_ext[:, :, npc - 1 :], "phi", [(i, (i + 1) % phi_count) for i in range(phi_count)]
    )
    right_cols = lax.ppermute(
        rows_ext[:, :, :2], "phi", [((i + 1) % phi_count, i) for i in range(phi_count)]
    )
    early = jnp.concatenate([left_cols, rows_ext, right_cols], axis=2)

    edge_rows = jnp.where(at_north, combined[:, :CAP], combined[:, ct - CAP :])
    slot_rows = edge_rows.reshape(channels * CAP, npc, nr)
    per_device = channels * CAP // phi_count
    pieces = []
    for shift in range(phi_count):
        target = (p + shift) % phi_count
        piece = lax.dynamic_slice_in_dim(slot_rows, target * per_device, per_device, axis=0)
        if shift:
            piece = lax.ppermute(piece, both, pole_pairs(shift))
        pieces.append(piece)
    cycle = jnp.concatenate(pieces, axis=1)
    shifts = jnp.arange(phi_count, dtype=jnp.int32)
    src_cols = (
        ((p - shifts) % phi_count)[:, None] * npc + jnp.arange(npc, dtype=jnp.int32)[None, :]
    ).reshape(-1)
    analysis = fourier_rows(src_cols, cycle_len)
    dst_cols = (
        ((p - shifts) % phi_count)[:, None] * npc
        - 1
        + jnp.arange(npc + 3, dtype=jnp.int32)[None, :]
    ) % cycle_len
    synthesis = fourier_rows(dst_cols, cycle_len)

    pole_pick = jnp.where(at_north, 0, 1).astype(jnp.int32)
    level_row = lax.dynamic_index_in_dim(levels, pole_pick, 0, keepdims=False)
    slot_ids = p * per_device + jnp.arange(per_device, dtype=jnp.int32)
    row_ids = slot_ids % CAP
    slot_levels = jnp.sum(
        jnp.where(
            row_ids[:, None] == jnp.arange(CAP, dtype=jnp.int32)[None, :], level_row[None, :], 0
        ),
        axis=1,
    )
    limits = jnp.right_shift(jnp.int32(KMAX), slot_levels)
    column_order = jnp.arange(2 * KMAX, dtype=jnp.int32) % KMAX
    column_weight = jnp.where(column_order == 0, 1.0 / cycle_len, 2.0 / cycle_len).astype(
        jnp.float32
    )
    kept_weight = jnp.where(column_order[None, :] < limits[:, None], column_weight[None, :], 0.0)
    coeffs = jnp.einsum("smr,mn->snr", cycle, analysis, precision=lax.Precision.HIGHEST)
    coeffs = coeffs * kept_weight[:, :, None]
    out = jnp.einsum("snr,kjn->skjr", coeffs, synthesis, precision=lax.Precision.HIGHEST)

    back = []
    for shift in range(phi_count):
        piece = out[:, shift]
        if shift:
            piece = lax.ppermute(piece, both, pole_pairs(-shift))
        back.append(piece)
    stacked = jnp.stack(back, axis=0)
    ordered = jnp.roll(stacked, p, axis=0)
    cap_rows = ordered.reshape(channels, CAP, npc + 3, nr)

    ghost_send = jnp.where(
        at_north,
        jnp.concatenate([cap_rows[:, 0], cap_rows[6:7, 1]], axis=0),
        jnp.concatenate([cap_rows[:, CAP - 1], cap_rows[6:7, CAP - 2]], axis=0),
    )
    ghost = lax.ppermute(ghost_send, both, pole_pairs(phi_count // 2))
    ghost_main = ghost[:channels] * parity[:, None, None]
    ghost_b = ghost[channels:] * parity[6]
    north_block = jnp.concatenate(
        [ghost_main[:, None], cap_rows, early[:, CAP + 1 : CAP + 2]], axis=1
    )
    south_block = jnp.concatenate(
        [
            cap_rows,
            ghost_main[:, None],
            jnp.broadcast_to(ghost_b, (channels, npc + 3, nr))[:, None],
        ],
        axis=1,
    )
    offset = jnp.where(at_north, 0, ct - CAP + 1)
    kept_block = lax.dynamic_slice_in_dim(early, offset, CAP + 2, axis=1)
    block = jnp.where(
        at_north, north_block, jnp.where(at_south, south_block, kept_block)
    )
    extended = lax.dynamic_update_slice_in_dim(early, block, offset, axis=1)
    del is_pole
    return advance(extended)


def solution(mesh):
    return jax.shard_map(
        local,
        mesh=mesh,
        in_specs=(
            P(None, "theta", "phi", None),
            P(None, "theta", "phi", None),
            P(None, "theta", "phi", None),
            P(),
        ),
        out_specs=(P(None, "theta", "phi", None), P(None, "theta", "phi", None)),
        check_vma=False,
    )
```

time: 207 us -> 205 us (level)
  the two profiles are of different devices: /device:TPU:1 before, /device:TPU:2 now
where the time goes in v1:
time: 205 us; the launch traced here: 203 us
  starting transfers between devices  134 us (65%)
  other arithmetic  28.4 us (14%)
  local copies, waits for them, and re-layouts  25.9 us (13%)
  waiting for transfers between devices  8.83 us (4%)
  matrix products  4.35 us (2%)
    ppermute x15, starting transfers between devices, local(): piece = lax.ppermute(piece, both, pole_pairs(shift))  63.6 us
    ppermute x15, starting transfers between devices, local(): piece = lax.ppermute(piece, both, pole_pairs(-shift))  58.8 us
    unnamed x69, local copies, waits for them, and re-layouts  16.5 us
    cos x2, other arithmetic, fourier_rows(): return jnp.concatenate([jnp.cos(angle), jnp.sin(angle)], axis=-1)  9.69 us
    ppermute x15, waiting for transfers between devices, local(): piece = lax.ppermute(piece, both, pole_pairs(-shift))  6.34 us
    ppermute x1, starting transfers between devices, local(): lax.ppermute(rows_ext[:, :, :2], 'phi', [((i + 1) % phi_count, i) for i i...  4.13 us
  transfers between devices with their start and end apart: 35, of which 4 were waited for; matrix products, arithmetic and copies ran while one was open for 20% of the time, Pallas kernels for 0%

profile of v1, /device:TPU:2, one launch (start us, length us, event | category | flops | bytes accessed | tf_op | source)
XLA Modules:
  0.0 203.1 jit_solution(6970224128607802734)
XLA Ops:
  6.3 3.8 %collective-permute-start.4 = (f32[2,96,128]{2,1,0:T(8,128)}, f32[2,96,128]{2,1,0:T(8,128)}, u32[]{:S(2)}, u32[]{:S(2)}) collective-permute-start(f32[2,96,128]{2,1,0:T(8,128)} %get-tuple-element.51), channel_id=1, source_target_pairs={{0,1},{1,2},{2,3},{3,4},{4,5},{5,6},{6,7},{7,8},{8,9},{9,10},{10,1... | collective-permute-start | bytes 294920 | tf_op jit(solution)/shard_map/ppermute | solution.py:165
  10.1 5.2 %collective-permute-start.5 = (f32[2,96,128]{2,1,0:T(8,128)}, f32[2,96,128]{2,1,0:T(8,128)}, u32[]{:S(2)}, u32[]{:S(2)}) collective-permute-start(f32[2,96,128]{2,1,0:T(8,128)} %get-tuple-element.50), channel_id=1, source_target_pairs={{0,2},{1,3},{2,4},{3,5},{4,6},{5,7},{6,8},{7,9},{8,10},{9,11},{10,... | collective-permute-start | bytes 294920 | tf_op jit(solution)/shard_map/ppermute | solution.py:165
  15.3 5.9 %collective-permute-start.6 = (f32[2,96,128]{2,1,0:T(8,128)}, f32[2,96,128]{2,1,0:T(8,128)}, u32[]{:S(2)}, u32[]{:S(2)}) collective-permute-start(f32[2,96,128]{2,1,0:T(8,128)} %get-tuple-element.49), channel_id=1, source_target_pairs={{0,3},{1,4},{2,5},{3,6},{4,7},{5,8},{6,9},{7,10},{8,11},{9,12},{10... | collective-permute-start | bytes 294920 | tf_op jit(solution)/shard_map/ppermute | solution.py:165
  23.7 6.9 %collective-permute-start.8 = (f32[2,96,128]{2,1,0:T(8,128)}, f32[2,96,128]{2,1,0:T(8,128)}, u32[]{:S(2)}, u32[]{:S(2)}) collective-permute-start(f32[2,96,128]{2,1,0:T(8,128)} %get-tuple-element.47), channel_id=1, source_target_pairs={{0,5},{1,6},{2,7},{3,8},{4,9},{5,10},{6,11},{7,12},{8,13},{9,14},{... | collective-permute-start | bytes 294920 | tf_op jit(solution)/shard_map/ppermute | solution.py:165
  36.1 4.4 %fusion.23 = (f32[1536,128]{0,1:T(8,128)}, f32[1536,128]{0,1:T(8,128)}) fusion(s32[1536]{0:T(1024)S(1)} %add.368), kind=kLoop, calls=%fused_computation.35 | loop fusion | flops 1769472 | bytes 1579008 | tf_op jit(solution)/shard_map/cos | solution.py:110
  41.2 5.3 %fusion.16 = (f32[16,99,128]{2,1,0:T(8,128)}, f32[16,99,128]{2,1,0:T(8,128)}) fusion(s32[16,99]{1,0:T(8,128)S(1)} %add_select_fusion.2), kind=kLoop, calls=%fused_computation.26 | loop fusion | flops 1824768 | bytes 1628352 | tf_op jit(solution)/shard_map/cos | solution.py:110
  48.4 5.5 %collective-permute-start.9 = (f32[2,96,128]{2,1,0:T(8,128)}, f32[2,96,128]{2,1,0:T(8,128)S(1)}, u32[]{:S(2)}, u32[]{:S(2)}) collective-permute-start(f32[2,96,128]{2,1,0:T(8,128)} %get-tuple-element.46), channel_id=1, source_target_pairs={{0,6},{1,7},{2,8},{3,9},{4,10},{5,11},{6,12},{7,13},{8,14},{9,15},... | collective-permute-start | bytes 294920 | tf_op jit(solution)/shard_map/ppermute | solution.py:165
  59.9 3.4 %collective-permute-start.11 = (f32[2,96,128]{2,1,0:T(8,128)}, f32[2,96,128]{2,1,0:T(8,128)S(1)}, u32[]{:S(2)}, u32[]{:S(2)}) collective-permute-start(f32[2,96,128]{2,1,0:T(8,128)} %get-tuple-element.44), channel_id=1, source_target_pairs={{0,8},{1,9},{2,10},{3,11},{4,12},{5,13},{6,14},{7,15},{8,0},{9,1},... | collective-permute-start | bytes 294920 | tf_op jit(solution)/shard_map/ppermute | solution.py:165
  73.9 3.5 %collective-permute-start.14 = (f32[2,96,128]{2,1,0:T(8,128)}, f32[2,96,128]{2,1,0:T(8,128)S(1)}, u32[]{:S(2)}, u32[]{:S(2)}) collective-permute-start(f32[2,96,128]{2,1,0:T(8,128)} %get-tuple-element.41), channel_id=1, source_target_pairs={{0,11},{1,12},{2,13},{3,14},{4,15},{5,0},{6,1},{7,2},{8,3},{9,4},{... | collective-permute-start | bytes 294920 | tf_op jit(solution)/shard_map/ppermute | solution.py:165
  78.1 6.0 %collective-permute-start.15 = (f32[2,96,128]{2,1,0:T(8,128)}, f32[2,96,128]{2,1,0:T(8,128)S(1)}, u32[]{:S(2)}, u32[]{:S(2)}) collective-permute-start(f32[2,96,128]{2,1,0:T(8,128)} %get-tuple-element.40), channel_id=1, source_target_pairs={{0,12},{1,13},{2,14},{3,15},{4,0},{5,1},{6,2},{7,3},{8,4},{9,5},{1... | collective-permute-start | bytes 294920 | tf_op jit(solution)/shard_map/ppermute | solution.py:165
  84.8 4.7 %collective-permute-start.16 = (f32[2,96,128]{2,1,0:T(8,128)}, f32[2,96,128]{2,1,0:T(8,128)S(1)}, u32[]{:S(2)}, u32[]{:S(2)}) collective-permute-start(f32[2,96,128]{2,1,0:T(8,128)} %get-tuple-element.39), channel_id=1, source_target_pairs={{0,13},{1,14},{2,15},{3,0},{4,1},{5,2},{6,3},{7,4},{8,5},{9,6},{10... | collective-permute-start | bytes 294920 | tf_op jit(solution)/shard_map/ppermute | solution.py:165
  90.1 4.1 %collective-permute-start.17 = (f32[2,96,128]{2,1,0:T(8,128)}, f32[2,96,128]{2,1,0:T(8,128)S(1)}, u32[]{:S(2)}, u32[]{:S(2)}) collective-permute-start(f32[2,96,128]{2,1,0:T(8,128)} %get-tuple-element.38), channel_id=1, source_target_pairs={{0,14},{1,15},{2,0},{3,1},{4,2},{5,3},{6,4},{7,5},{8,6},{9,7},{10,... | collective-permute-start | bytes 294920 | tf_op jit(solution)/shard_map/ppermute | solution.py:165
  113.8 5.8 %collective-permute-start.20 = (f32[2,99,128]{2,1,0:T(8,128)S(1)}, f32[2,99,128]{2,1,0:T(8,128)S(1)}, u32[]{:S(2)}, u32[]{:S(2)}) collective-permute-start(f32[2,99,128]{2,1,0:T(8,128)S(1)} %get-tuple-element.35), channel_id=1, source_target_pairs={{0,14},{1,15},{2,0},{3,1},{4,2},{5,3},{6,4},{7,5},{8,6},{9,7},{10,... | collective-permute-start | bytes 304136 | tf_op jit(solution)/shard_map/ppermute | solution.py:204
  121.9 4.7 %collective-permute-start.22 = (f32[2,99,128]{2,1,0:T(8,128)S(1)}, f32[2,99,128]{2,1,0:T(8,128)S(1)}, u32[]{:S(2)}, u32[]{:S(2)}) collective-permute-start(f32[2,99,128]{2,1,0:T(8,128)S(1)} %get-tuple-element.33), channel_id=1, source_target_pairs={{0,12},{1,13},{2,14},{3,15},{4,0},{5,1},{6,2},{7,3},{8,4},{9,5},{1... | collective-permute-start | bytes 304136 | tf_op jit(solution)/shard_map/ppermute | solution.py:204
  126.7 4.3 %collective-permute-start.23 = (f32[2,99,128]{2,1,0:T(8,128)S(1)}, f32[2,99,128]{2,1,0:T(8,128)S(1)}, u32[]{:S(2)}, u32[]{:S(2)}) collective-permute-start(f32[2,99,128]{2,1,0:T(8,128)S(1)} %get-tuple-element.32), channel_id=1, source_target_pairs={{0,11},{1,12},{2,13},{3,14},{4,15},{5,0},{6,1},{7,2},{8,3},{9,4},{... | collective-permute-start | bytes 304136 | tf_op jit(solution)/shard_map/ppermute | solution.py:204
  131.0 5.0 %collective-permute-start.24 = (f32[2,99,128]{2,1,0:T(8,128)S(1)}, f32[2,99,128]{2,1,0:T(8,128)S(1)}, u32[]{:S(2)}, u32[]{:S(2)}) collective-permute-start(f32[2,99,128]{2,1,0:T(8,128)S(1)} %get-tuple-element.31), channel_id=1, source_target_pairs={{0,10},{1,11},{2,12},{3,13},{4,14},{5,15},{6,0},{7,1},{8,2},{9,3},... | collective-permute-start | bytes 304136 | tf_op jit(solution)/shard_map/ppermute | solution.py:204
  136.1 3.9 %collective-permute-start.25 = (f32[2,99,128]{2,1,0:T(8,128)S(1)}, f32[2,99,128]{2,1,0:T(8,128)S(1)}, u32[]{:S(2)}, u32[]{:S(2)}) collective-permute-start(f32[2,99,128]{2,1,0:T(8,128)S(1)} %get-tuple-element.30), channel_id=1, source_target_pairs={{0,9},{1,10},{2,11},{3,12},{4,13},{5,14},{6,15},{7,0},{8,1},{9,2},... | collective-permute-start | bytes 304136 | tf_op jit(solution)/shard_map/ppermute | solution.py:204
  140.0 3.4 %collective-permute-start.26 = (f32[2,99,128]{2,1,0:T(8,128)S(1)}, f32[2,99,128]{2,1,0:T(8,128)S(1)}, u32[]{:S(2)}, u32[]{:S(2)}) collective-permute-start(f32[2,99,128]{2,1,0:T(8,128)S(1)} %get-tuple-element.29), channel_id=1, source_target_pairs={{0,8},{1,9},{2,10},{3,11},{4,12},{5,13},{6,14},{7,15},{8,0},{9,1},... | collective-permute-start | bytes 304136 | tf_op jit(solution)/shard_map/ppermute | solution.py:204
  145.7 4.7 %collective-permute-start.28 = (f32[2,99,128]{2,1,0:T(8,128)S(1)}, f32[2,99,128]{2,1,0:T(8,128)S(1)}, u32[]{:S(2)}, u32[]{:S(2)}) collective-permute-start(f32[2,99,128]{2,1,0:T(8,128)S(1)} %get-tuple-element.27), channel_id=1, source_target_pairs={{0,6},{1,7},{2,8},{3,9},{4,10},{5,11},{6,12},{7,13},{8,14},{9,15},... | collective-permute-start | bytes 304136 | tf_op jit(solution)/shard_map/ppermute | solution.py:204
  150.4 4.1 %collective-permute-start.29 = (f32[2,99,128]{2,1,0:T(8,128)S(1)}, f32[2,99,128]{2,1,0:T(8,128)S(1)}, u32[]{:S(2)}, u32[]{:S(2)}) collective-permute-start(f32[2,99,128]{2,1,0:T(8,128)S(1)} %get-tuple-element.26), channel_id=1, source_target_pairs={{0,5},{1,6},{2,7},{3,8},{4,9},{5,10},{6,11},{7,12},{8,13},{9,14},{... | collective-permute-start | bytes 304136 | tf_op jit(solution)/shard_map/ppermute | solution.py:204
  154.6 5.7 %collective-permute-start.30 = (f32[2,99,128]{2,1,0:T(8,128)S(1)}, f32[2,99,128]{2,1,0:T(8,128)S(1)}, u32[]{:S(2)}, u32[]{:S(2)}) collective-permute-start(f32[2,99,128]{2,1,0:T(8,128)S(1)} %get-tuple-element.25), channel_id=1, source_target_pairs={{0,4},{1,5},{2,6},{3,7},{4,8},{5,9},{6,10},{7,11},{8,12},{9,13},{1... | collective-permute-start | bytes 304136 | tf_op jit(solution)/shard_map/ppermute | solution.py:204
  160.3 3.5 %collective-permute-start.31 = (f32[2,99,128]{2,1,0:T(8,128)S(1)}, f32[2,99,128]{2,1,0:T(8,128)S(1)}, u32[]{:S(2)}, u32[]{:S(2)}) collective-permute-start(f32[2,99,128]{2,1,0:T(8,128)S(1)} %get-tuple-element.24), channel_id=1, source_target_pairs={{0,3},{1,4},{2,5},{3,6},{4,7},{5,8},{6,9},{7,10},{8,11},{9,12},{10... | collective-permute-start | bytes 304136 | tf_op jit(solution)/shard_map/ppermute | solution.py:204
  163.9 4.0 %collective-permute-start.32 = (f32[2,99,128]{2,1,0:T(8,128)S(1)}, f32[2,99,128]{2,1,0:T(8,128)S(1)}, u32[]{:S(2)}, u32[]{:S(2)}) collective-permute-start(f32[2,99,128]{2,1,0:T(8,128)S(1)} %get-tuple-element.23), channel_id=1, source_target_pairs={{0,2},{1,3},{2,4},{3,5},{4,6},{5,7},{6,8},{7,9},{8,10},{9,11},{10,... | collective-permute-start | bytes 304136 | tf_op jit(solution)/shard_map/ppermute | solution.py:204
  182.6 4.1 %collective-permute-start.3 = (f32[8,11,2,128]{3,2,1,0:T(2,128)}, f32[8,11,2,128]{3,2,1,0:T(2,128)}, u32[]{:S(2)}, u32[]{:S(2)}) collective-permute-start(f32[8,11,2,128]{3,2,1,0:T(2,128)} %pad_maximum_fusion.10), channel_id=1, source_target_pairs={{1,0},{2,1},{3,2},{4,3},{5,4},{6,5},{7,6},{8,7},{9,8},{10,9},{11,1... | collective-permute-start | bytes 270344 | tf_op jit(solution)/shard_map/ppermute | solution.py:152
  (186 shorter events, 89.1 us)
Async XLA Ops:
  6.3 42.1 %collective-permute-start.4 = (f32[2,96,128]{2,1,0:T(8,128)}, f32[2,96,128]{2,1,0:T(8,128)}, u32[]{:S(2)}, u32[]{:S(2)}) collective-permute-start(f32[2,96,128]{2,1,0:T(8,128)} %get-tuple-element.51), channel_id=1, source_target_pairs={{0,1},{1,2},{2,3},{3,4},{4,5},{5,6},{6,7},{7,8},{8,9},{9,10},{10,1... | collective-permute-start | bytes 294920 | tf_op jit(solution)/shard_map/ppermute | solution.py:165
  10.1 45.3 %collective-permute-start.5 = (f32[2,96,128]{2,1,0:T(8,128)}, f32[2,96,128]{2,1,0:T(8,128)}, u32[]{:S(2)}, u32[]{:S(2)}) collective-permute-start(f32[2,96,128]{2,1,0:T(8,128)} %get-tuple-element.50), channel_id=1, source_target_pairs={{0,2},{1,3},{2,4},{3,5},{4,6},{5,7},{6,8},{7,9},{8,10},{9,11},{10,... | collective-permute-start | bytes 294920 | tf_op jit(solution)/shard_map/ppermute | solution.py:165
  15.3 44.6 %collective-permute-start.6 = (f32[2,96,128]{2,1,0:T(8,128)}, f32[2,96,128]{2,1,0:T(8,128)}, u32[]{:S(2)}, u32[]{:S(2)}) collective-permute-start(f32[2,96,128]{2,1,0:T(8,128)} %get-tuple-element.49), channel_id=1, source_target_pairs={{0,3},{1,4},{2,5},{3,6},{4,7},{5,8},{6,9},{7,10},{8,11},{9,12},{10... | collective-permute-start | bytes 294920 | tf_op jit(solution)/shard_map/ppermute | solution.py:165
  21.3 43.6 %collective-permute-start.7 = (f32[2,96,128]{2,1,0:T(8,128)}, f32[2,96,128]{2,1,0:T(8,128)}, u32[]{:S(2)}, u32[]{:S(2)}) collective-permute-start(f32[2,96,128]{2,1,0:T(8,128)} %get-tuple-element.48), channel_id=1, source_target_pairs={{0,4},{1,5},{2,6},{3,7},{4,8},{5,9},{6,10},{7,11},{8,12},{9,13},{1... | collective-permute-start | bytes 294920 | tf_op jit(solution)/shard_map/ppermute | solution.py:165
  23.7 45.6 %collective-permute-start.8 = (f32[2,96,128]{2,1,0:T(8,128)}, f32[2,96,128]{2,1,0:T(8,128)}, u32[]{:S(2)}, u32[]{:S(2)}) collective-permute-start(f32[2,96,128]{2,1,0:T(8,128)} %get-tuple-element.47), channel_id=1, source_target_pairs={{0,5},{1,6},{2,7},{3,8},{4,9},{5,10},{6,11},{7,12},{8,13},{9,14},{... | collective-permute-start | bytes 294920 | tf_op jit(solution)/shard_map/ppermute | solution.py:165
  48.4 25.5 %collective-permute-start.9 = (f32[2,96,128]{2,1,0:T(8,128)}, f32[2,96,128]{2,1,0:T(8,128)S(1)}, u32[]{:S(2)}, u32[]{:S(2)}) collective-permute-start(f32[2,96,128]{2,1,0:T(8,128)} %get-tuple-element.46), channel_id=1, source_target_pairs={{0,6},{1,7},{2,8},{3,9},{4,10},{5,11},{6,12},{7,13},{8,14},{9,15},... | collective-permute-start | bytes 294920 | tf_op jit(solution)/shard_map/ppermute | solution.py:165
  55.5 22.7 %collective-permute-start.10 = (f32[2,96,128]{2,1,0:T(8,128)}, f32[2,96,128]{2,1,0:T(8,128)S(1)}, u32[]{:S(2)}, u32[]{:S(2)}) collective-permute-start(f32[2,96,128]{2,1,0:T(8,128)} %get-tuple-element.45), channel_id=1, source_target_pairs={{0,7},{1,8},{2,9},{3,10},{4,11},{5,12},{6,13},{7,14},{8,15},{9,0},... | collective-permute-start | bytes 294920 | tf_op jit(solution)/shard_map/ppermute | solution.py:165
  59.9 24.8 %collective-permute-start.11 = (f32[2,96,128]{2,1,0:T(8,128)}, f32[2,96,128]{2,1,0:T(8,128)S(1)}, u32[]{:S(2)}, u32[]{:S(2)}) collective-permute-start(f32[2,96,128]{2,1,0:T(8,128)} %get-tuple-element.44), channel_id=1, source_target_pairs={{0,8},{1,9},{2,10},{3,11},{4,12},{5,13},{6,14},{7,15},{8,0},{9,1},... | collective-permute-start | bytes 294920 | tf_op jit(solution)/shard_map/ppermute | solution.py:165
  64.8 25.3 %collective-permute-start.12 = (f32[2,96,128]{2,1,0:T(8,128)}, f32[2,96,128]{2,1,0:T(8,128)S(1)}, u32[]{:S(2)}, u32[]{:S(2)}) collective-permute-start(f32[2,96,128]{2,1,0:T(8,128)} %get-tuple-element.43), channel_id=1, source_target_pairs={{0,9},{1,10},{2,11},{3,12},{4,13},{5,14},{6,15},{7,0},{8,1},{9,2},... | collective-permute-start | bytes 294920 | tf_op jit(solution)/shard_map/ppermute | solution.py:165
  69.3 25.6 %collective-permute-start.13 = (f32[2,96,128]{2,1,0:T(8,128)}, f32[2,96,128]{2,1,0:T(8,128)S(1)}, u32[]{:S(2)}, u32[]{:S(2)}) collective-permute-start(f32[2,96,128]{2,1,0:T(8,128)} %get-tuple-element.42), channel_id=1, source_target_pairs={{0,10},{1,11},{2,12},{3,13},{4,14},{5,15},{6,0},{7,1},{8,2},{9,3},... | collective-permute-start | bytes 294920 | tf_op jit(solution)/shard_map/ppermute | solution.py:165
  73.9 25.0 %collective-permute-start.14 = (f32[2,96,128]{2,1,0:T(8,128)}, f32[2,96,128]{2,1,0:T(8,128)S(1)}, u32[]{:S(2)}, u32[]{:S(2)}) collective-permute-start(f32[2,96,128]{2,1,0:T(8,128)} %get-tuple-element.41), channel_id=1, source_target_pairs={{0,11},{1,12},{2,13},{3,14},{4,15},{5,0},{6,1},{7,2},{8,3},{9,4},{... | collective-permute-start | bytes 294920 | tf_op jit(solution)/shard_map/ppermute | solution.py:165
  78.1 22.7 %collective-permute-start.15 = (f32[2,96,128]{2,1,0:T(8,128)}, f32[2,96,128]{2,1,0:T(8,128)S(1)}, u32[]{:S(2)}, u32[]{:S(2)}) collective-permute-start(f32[2,96,128]{2,1,0:T(8,128)} %get-tuple-element.40), channel_id=1, source_target_pairs={{0,12},{1,13},{2,14},{3,15},{4,0},{5,1},{6,2},{7,3},{8,4},{9,5},{1... | collective-permute-start | bytes 294920 | tf_op jit(solution)/shard_map/ppermute | solution.py:165
  84.8 19.8 %collective-permute-start.16 = (f32[2,96,128]{2,1,0:T(8,128)}, f32[2,96,128]{2,1,0:T(8,128)S(1)}, u32[]{:S(2)}, u32[]{:S(2)}) collective-permute-start(f32[2,96,128]{2,1,0:T(8,128)} %get-tuple-element.39), channel_id=1, source_target_pairs={{0,13},{1,14},{2,15},{3,0},{4,1},{5,2},{6,3},{7,4},{8,5},{9,6},{10... | collective-permute-start | bytes 294920 | tf_op jit(solution)/shard_map/ppermute | solution.py:165
  90.1 15.1 %collective-permute-start.17 = (f32[2,96,128]{2,1,0:T(8,128)}, f32[2,96,128]{2,1,0:T(8,128)S(1)}, u32[]{:S(2)}, u32[]{:S(2)}) collective-permute-start(f32[2,96,128]{2,1,0:T(8,128)} %get-tuple-element.38), channel_id=1, source_target_pairs={{0,14},{1,15},{2,0},{3,1},{4,2},{5,3},{6,4},{7,5},{8,6},{9,7},{10,... | collective-permute-start | bytes 294920 | tf_op jit(solution)/shard_map/ppermute | solution.py:165
  98.9 82.0 %collective-permute-start.1 = (f32[9,96,128]{2,1,0:T(8,128)S(1)}, f32[9,96,128]{2,1,0:T(8,128)S(1)}, u32[]{:S(2)}, u32[]{:S(2)}) collective-permute-start(f32[9,96,128]{2,1,0:T(8,128)S(1)} %pad_maximum_fusion.3), channel_id=1, source_target_pairs={{16,0},{32,16},{48,32},{64,48},{80,64},{96,80},{112,96},{128,112},... | collective-permute-start | bytes 1327112 | tf_op jit(solution)/shard_map/ppermute | solution.py:139
  100.9 80.1 %collective-permute-start = (f32[8,96,128]{2,1,0:T(8,128)}, f32[8,96,128]{2,1,0:T(8,128)S(1)}, u32[]{:S(2)}, u32[]{:S(2)}) collective-permute-start(f32[8,96,128]{2,1,0:T(8,128)} %get-tuple-element.14), channel_id=1, source_target_pairs={{0,16},{16,32},{32,48},{48,64},{64,80},{80,96},{96,112},{112,128},... | collective-permute-start | bytes 1179656 | tf_op jit(solution)/shard_map/ppermute | solution.py:135
  113.8 12.9 %collective-permute-start.20 = (f32[2,99,128]{2,1,0:T(8,128)S(1)}, f32[2,99,128]{2,1,0:T(8,128)S(1)}, u32[]{:S(2)}, u32[]{:S(2)}) collective-permute-start(f32[2,99,128]{2,1,0:T(8,128)S(1)} %get-tuple-element.35), channel_id=1, source_target_pairs={{0,14},{1,15},{2,0},{3,1},{4,2},{5,3},{6,4},{7,5},{8,6},{9,7},{10,... | collective-permute-start | bytes 304136 | tf_op jit(solution)/shard_map/ppermute | solution.py:204
  121.9 14.1 %collective-permute-start.22 = (f32[2,99,128]{2,1,0:T(8,128)S(1)}, f32[2,99,128]{2,1,0:T(8,128)S(1)}, u32[]{:S(2)}, u32[]{:S(2)}) collective-permute-start(f32[2,99,128]{2,1,0:T(8,128)S(1)} %get-tuple-element.33), channel_id=1, source_target_pairs={{0,12},{1,13},{2,14},{3,15},{4,0},{5,1},{6,2},{7,3},{8,4},{9,5},{1... | collective-permute-start | bytes 304136 | tf_op jit(solution)/shard_map/ppermute | solution.py:204
  126.7 13.3 %collective-permute-start.23 = (f32[2,99,128]{2,1,0:T(8,128)S(1)}, f32[2,99,128]{2,1,0:T(8,128)S(1)}, u32[]{:S(2)}, u32[]{:S(2)}) collective-permute-start(f32[2,99,128]{2,1,0:T(8,128)S(1)} %get-tuple-element.32), channel_id=1, source_target_pairs={{0,11},{1,12},{2,13},{3,14},{4,15},{5,0},{6,1},{7,2},{8,3},{9,4},{... | collective-permute-start | bytes 304136 | tf_op jit(solution)/shard_map/ppermute | solution.py:204
  131.0 12.4 %collective-permute-start.24 = (f32[2,99,128]{2,1,0:T(8,128)S(1)}, f32[2,99,128]{2,1,0:T(8,128)S(1)}, u32[]{:S(2)}, u32[]{:S(2)}) collective-permute-start(f32[2,99,128]{2,1,0:T(8,128)S(1)} %get-tuple-element.31), channel_id=1, source_target_pairs={{0,10},{1,11},{2,12},{3,13},{4,14},{5,15},{6,0},{7,1},{8,2},{9,3},... | collective-permute-start | bytes 304136 | tf_op jit(solution)/shard_map/ppermute | solution.py:204
  145.7 14.6 %collective-permute-start.28 = (f32[2,99,128]{2,1,0:T(8,128)S(1)}, f32[2,99,128]{2,1,0:T(8,128)S(1)}, u32[]{:S(2)}, u32[]{:S(2)}) collective-permute-start(f32[2,99,128]{2,1,0:T(8,128)S(1)} %get-tuple-element.27), channel_id=1, source_target_pairs={{0,6},{1,7},{2,8},{3,9},{4,10},{5,11},{6,12},{7,13},{8,14},{9,15},... | collective-permute-start | bytes 304136 | tf_op jit(solution)/shard_map/ppermute | solution.py:204
  150.4 13.5 %collective-permute-start.29 = (f32[2,99,128]{2,1,0:T(8,128)S(1)}, f32[2,99,128]{2,1,0:T(8,128)S(1)}, u32[]{:S(2)}, u32[]{:S(2)}) collective-permute-start(f32[2,99,128]{2,1,0:T(8,128)S(1)} %get-tuple-element.26), channel_id=1, source_target_pairs={{0,5},{1,6},{2,7},{3,8},{4,9},{5,10},{6,11},{7,12},{8,13},{9,14},{... | collective-permute-start | bytes 304136 | tf_op jit(solution)/shard_map/ppermute | solution.py:204
  154.6 13.4 %collective-permute-start.30 = (f32[2,99,128]{2,1,0:T(8,128)S(1)}, f32[2,99,128]{2,1,0:T(8,128)S(1)}, u32[]{:S(2)}, u32[]{:S(2)}) collective-permute-start(f32[2,99,128]{2,1,0:T(8,128)S(1)} %get-tuple-element.25), channel_id=1, source_target_pairs={{0,4},{1,5},{2,6},{3,7},{4,8},{5,9},{6,10},{7,11},{8,12},{9,13},{1... | collective-permute-start | bytes 304136 | tf_op jit(solution)/shard_map/ppermute | solution.py:204
  178.2 12.9 %collective-permute-start.34 = (f32[9,99,128]{2,1,0:T(8,128)}, f32[9,99,128]{2,1,0:T(8,128)}, u32[]{:S(2)}, u32[]{:S(2)}) collective-permute-start(f32[9,99,128]{2,1,0:T(8,128)} %maximum_select_fusion.6), channel_id=1, source_target_pairs={{0,8},{1,9},{2,10},{3,11},{4,12},{5,13},{6,14},{7,15},{8,0},{9,1},... | collective-permute-start | bytes 1368584 | tf_op jit(solution)/shard_map/ppermute | solution.py:215
  (22 other events, 401.0 us)

commit v2 on v1

--- a/solution.py
+++ b/solution.py
@@ -119,7 +119,6 @@
     p = lax.axis_index("phi")
     at_north = t == 0
     at_south = t == theta_count - 1
-    is_pole = at_north | at_south
     cycle_len = npc * phi_count
     parity = jnp.array(PARITY, jnp.float32)
     poles = (0, theta_count - 1)
@@ -154,32 +153,31 @@
     )
     early = jnp.concatenate([left_cols, rows_ext, right_cols], axis=2)
 
+    north_side = t <= 1
+    helper = (t == 1) | (t == theta_count - 2)
     edge_rows = jnp.where(at_north, combined[:, :CAP], combined[:, ct - CAP :])
     slot_rows = edge_rows.reshape(channels * CAP, npc, nr)
-    per_device = channels * CAP // phi_count
-    pieces = []
-    for shift in range(phi_count):
-        target = (p + shift) % phi_count
-        piece = lax.dynamic_slice_in_dim(slot_rows, target * per_device, per_device, axis=0)
-        if shift:
-            piece = lax.ppermute(piece, both, pole_pairs(shift))
-        pieces.append(piece)
-    cycle = jnp.concatenate(pieces, axis=1)
-    shifts = jnp.arange(phi_count, dtype=jnp.int32)
-    src_cols = (
-        ((p - shifts) % phi_count)[:, None] * npc + jnp.arange(npc, dtype=jnp.int32)[None, :]
-    ).reshape(-1)
-    analysis = fourier_rows(src_cols, cycle_len)
+    half = channels * CAP // 2
+    pairs_out = [(0, 1), (theta_count - 1, theta_count - 2)]
+    pairs_in = [(1, 0), (theta_count - 2, theta_count - 1)]
+    handed = lax.ppermute(slot_rows[half:], "theta", pairs_out)
+    work = jnp.where(helper, handed, slot_rows[:half])
+    per_device = half // phi_count
+    cycle = lax.all_to_all(
+        work.reshape(phi_count, per_device, npc, nr), "phi", split_axis=0, concat_axis=2, tiled=True
+    )
+    cycle = cycle.reshape(per_device, cycle_len, nr)
+    analysis = fourier_rows(jnp.arange(cycle_len, dtype=jnp.int32), cycle_len)
     dst_cols = (
-        ((p - shifts) % phi_count)[:, None] * npc
+        jnp.arange(phi_count, dtype=jnp.int32)[:, None] * npc
         - 1
         + jnp.arange(npc + 3, dtype=jnp.int32)[None, :]
     ) % cycle_len
     synthesis = fourier_rows(dst_cols, cycle_len)
 
-    pole_pick = jnp.where(at_north, 0, 1).astype(jnp.int32)
+    pole_pick = jnp.where(north_side, 0, 1).astype(jnp.int32)
     level_row = lax.dynamic_index_in_dim(levels, pole_pick, 0, keepdims=False)
-    slot_ids = p * per_device + jnp.arange(per_device, dtype=jnp.int32)
+    slot_ids = jnp.where(helper, half, 0) + p * per_device + jnp.arange(per_device, dtype=jnp.int32)
     row_ids = slot_ids % CAP
     slot_levels = jnp.sum(
         jnp.where(
@@ -195,26 +193,35 @@
     kept_weight = jnp.where(column_order[None, :] < limits[:, None], column_weight[None, :], 0.0)
     coeffs = jnp.einsum("smr,mn->snr", cycle, analysis, precision=lax.Precision.HIGHEST)
     coeffs = coeffs * kept_weight[:, :, None]
-    out = jnp.einsum("snr,kjn->skjr", coeffs, synthesis, precision=lax.Precision.HIGHEST)
-
-    back = []
-    for shift in range(phi_count):
-        piece = out[:, shift]
-        if shift:
-            piece = lax.ppermute(piece, both, pole_pairs(-shift))
-        back.append(piece)
-    stacked = jnp.stack(back, axis=0)
-    ordered = jnp.roll(stacked, p, axis=0)
-    cap_rows = ordered.reshape(channels, CAP, npc + 3, nr)
-
-    ghost_send = jnp.where(
-        at_north,
-        jnp.concatenate([cap_rows[:, 0], cap_rows[6:7, 1]], axis=0),
-        jnp.concatenate([cap_rows[:, CAP - 1], cap_rows[6:7, CAP - 2]], axis=0),
-    )
-    ghost = lax.ppermute(ghost_send, both, pole_pairs(phi_count // 2))
-    ghost_main = ghost[:channels] * parity[:, None, None]
-    ghost_b = ghost[channels:] * parity[6]
+    out = jnp.einsum("snr,kjn->ksjr", coeffs, synthesis, precision=lax.Precision.HIGHEST)
+    mine = lax.all_to_all(out, "phi", split_axis=0, concat_axis=0, tiled=True)
+    mine = mine.reshape(half, npc + 3, nr)
+
+    from_helper = lax.ppermute(mine, "theta", pairs_in)
+    cap_rows = jnp.concatenate([mine, from_helper], axis=0).reshape(channels, CAP, npc + 3, nr)
+    per_half = channels // 2
+    first_rows = mine[0::CAP]
+    last_rows = mine[CAP - 1 :: CAP]
+    spare = mine[(6 - per_half) * CAP + CAP - 2 : (6 - per_half) * CAP + CAP - 1]
+    ghost_send = jnp.concatenate([jnp.where(north_side, first_rows, last_rows), spare], axis=0)
+    turn = phi_count // 2
+    pole_ghost = lax.ppermute(
+        ghost_send,
+        both,
+        [(a * phi_count + b, a * phi_count + (b + turn) % phi_count) for a in poles for b in range(phi_count)],
+    )
+    helper_ghost = lax.ppermute(
+        ghost_send,
+        both,
+        [
+            (h * phi_count + b, a * phi_count + (b + turn) % phi_count)
+            for h, a in ((1, 0), (theta_count - 2, theta_count - 1))
+            for b in range(phi_count)
+        ],
+    )
+    ghost_main = jnp.concatenate([pole_ghost[:per_half], helper_ghost[:per_half]], axis=0)
+    ghost_main = ghost_main * parity[:, None, None]
+    ghost_b = helper_ghost[per_half:] * parity[6]
     north_block = jnp.concatenate(
         [ghost_main[:, None], cap_rows, early[:, CAP + 1 : CAP + 2]], axis=1
     )
@@ -232,7 +239,6 @@
         at_north, north_block, jnp.where(at_south, south_block, kept_block)
     )
     extended = lax.dynamic_update_slice_in_dim(early, block, offset, axis=1)
-    del is_pole
     return advance(extended)
 
 

time: 205 us -> 110 us (0.54)
  the two profiles are of different devices: /device:TPU:2 before, /device:TPU:1 now
where the time goes in v2:
time: 110 us; the launch traced here: 109 us
  starting transfers between devices  30.5 us (28%)
  waiting for transfers between devices  28.4 us (26%)
  other arithmetic  25.9 us (24%)
  local copies, waits for them, and re-layouts  16.4 us (15%)
  matrix products  5.87 us (5%)
  between operations  1.81 us (2%)
    ppermute x1, waiting for transfers between devices, local(): lax.ppermute(up_send, 'theta', [(i + 1, i) for i in range(theta_count - 1)])  12.6 us
    all_to_all x1, waiting for transfers between devices, local(): lax.all_to_all(work.reshape(phi_count, per_device, npc, nr), 'phi', split...  8.97 us
    all_to_all x1, starting transfers between devices, local(): lax.all_to_all(work.reshape(phi_count, per_device, npc, nr), 'phi', split...  7.97 us
    all_to_all x1, starting transfers between devices, local(): mine = lax.all_to_all(out, 'phi', split_axis=0, concat_axis=0, tiled=True)  6.19 us
    ppermute x1, waiting for transfers between devices, local(): handed = lax.ppermute(slot_rows[half:], 'theta', pairs_out)  5.33 us
    cos x1, other arithmetic, fourier_rows(): return jnp.concatenate([jnp.cos(angle), jnp.sin(angle)], axis=-1)  5.31 us
    dot_general x1, matrix products, local(): jnp.einsum('smr,mn->snr', cycle, analysis, precision=lax.Precision.HIGHEST)  4.34 us
    ppermute x1, starting transfers between devices, local(): lax.ppermute(combined[:, ct - 1], 'theta', [(i, i + 1) for i in range(the...  4.34 us
  transfers between devices with their start and end apart: 10, of which 4 were waited for; matrix products, arithmetic and copies ran while one was open for 21% of the time, Pallas kernels for 0%

profile of v2, /device:TPU:1, one launch (start us, length us, event | category | flops | bytes accessed | tf_op | source)
XLA Modules:
  0.0 108.9 jit_solution(17664351503872645881)
XLA Ops:
  1.8 1.4 %constant_dynamic-update-slice_fusion.1 = f32[8,8,96,128]{3,2,1,0:T(8,128)S(1)} fusion(f32[8,8,96,128]{3,2,1,0:T(8,128)S(1)} %constant_dynamic-update-slice_fusion.2, f32[3,8,96,128]{3,2,1,0:T(8,128)} %param.6), kind=kLoop, calls=%fused_computation.151 | loop fusion | bytes 2359296
  3.8 1.3 %fusion.73 = (f32[4,4,96,128]{3,2,1,0:T(8,128)}, f32[4,4,96,128]{3,2,1,0:T(8,128)}) fusion(f32[8,4,96,128]{3,2,1,0:T(8,128)S(1)} %slice_select_fusion), kind=kLoop, calls=%fused_computation.168 | loop fusion | bytes 3145728 | tf_op jit(solution)/shard_map/slice | solution.py:164
  5.1 1.4 %collective-permute-start.4 = (f32[16,96,128]{2,1,0:T(8,128)}, f32[16,96,128]{2,1,0:T(8,128)}, u32[]{:S(2)}, u32[]{:S(2)}) collective-permute-start(f32[16,96,128]{2,1,0:T(8,128)} %bitcast.6), channel_id=1, source_target_pairs={{0,16},{240,224},{1,17},{241,225},{2,18},{242,226},{3,19},{243,227... | collective-permute-start | bytes 2359304 | tf_op jit(solution)/shard_map/ppermute | solution.py:163
  6.5 5.3 %collective-permute-done.4 = f32[16,96,128]{2,1,0:T(8,128)} collective-permute-done((f32[16,96,128]{2,1,0:T(8,128)}, f32[16,96,128]{2,1,0:T(8,128)}, u32[]{:S(2)}, u32[]{:S(2)}) %collective-permute-start.4) | collective-permute-done | bytes 786464 | tf_op jit(solution)/shard_map/ppermute | solution.py:163
  11.8 2.3 %bitcast_select_fusion = f32[16,96,128]{2,1,0:T(8,128)} fusion(f32[16,96,128]{2,1,0:T(8,128)} %collective-permute-done.4, f32[4,4,96,128]{3,2,1,0:T(8,128)} %get-tuple-element.18, pred[]{:T(512)S(6)} %or.3), kind=kLoop, calls=%fused_computation.33 | loop fusion | flops 196608 | bytes 2359297 | tf_op jit(solution)/shard_map/jit(_where)/select_n | solution.py:164
  14.2 8.0 %all-to-all-start = ((f32[16,1,96,128]{3,2,1,0:T(8,128)}), f32[16,1,96,128]{3,2,1,0:T(8,128)}, u32[]{:S(2)}, u32[]{:S(2)}) async-start(f32[16,1,96,128]{3,2,1,0:T(8,128)} %bitcast.78), calls=%async_computation | async-start | bytes 1572864 | tf_op jit(solution)/shard_map/all_to_all | solution.py:166
  23.6 5.3 %fusion.23 = (f32[16,99,128]{2,1,0:T(8,128)}, f32[16,99,128]{2,1,0:T(8,128)}) fusion(s32[16,99]{1,0:T(8,128)S(1)} %add_select_fusion.2), kind=kLoop, calls=%fused_computation.27 | loop fusion | flops 1824768 | bytes 1628352 | tf_op jit(solution)/shard_map/cos | solution.py:110
  28.9 4.3 %fusion.29 = (f32[1536,128]{1,0:T(8,128)}, f32[1536,128]{1,0:T(8,128)}) fusion(), kind=kLoop, calls=%fused_computation.37 | loop fusion | flops 1769472 | bytes 1572864 | tf_op jit(solution)/shard_map/sin | solution.py:110
  33.2 9.0 %all-to-all-done = f32[16,1,96,128]{3,2,1,0:T(8,128)} async-done(((f32[16,1,96,128]{3,2,1,0:T(8,128)}), f32[16,1,96,128]{3,2,1,0:T(8,128)}, u32[]{:S(2)}, u32[]{:S(2)}) %all-to-all-start) | async-done | bytes 786464 | tf_op jit(solution)/shard_map/all_to_all | solution.py:166
  42.1 4.3 %fusion.15 = f32[256,128,1]{1,0,2:T(8,128)S(1)} fusion(f32[1536,128]{1,0:T(8,128)} %bitcast.10, f32[1536,128]{1,0:T(8,128)} %get-tuple-element.62, f32[1536,128]{1,0:T(8,128)} %get-tuple-element.63, f32[256]{0:T(256)S(1)} %compare_select_fusion.1), kind=kOutput, calls=%fused_computation.19 | convolution fusion | flops 604405760 | bytes 2491392 | tf_op jit(solution)/shard_map/smr,mn->snr/dot_general | solution.py:194
  46.5 1.5 %fusion.9 = f32[16,1,99,128]{3,2,0,1:T(8,128)S(1)} fusion(f32[256,128,1]{1,0,2:T(8,128)S(1)} %fusion.15, f32[16,99,128]{2,1,0:T(8,128)S(1)} %copy-done.3, f32[16,99,128]{2,1,0:T(8,128)S(1)} %copy-done.2), kind=kOutput, calls=%fused_computation.14 | convolution fusion | flops 623259648 | bytes 2564096 | tf_op jit(solution)/shard_map/snr,kjn->ksjr/dot_general | solution.py:196
  48.0 1.7 %copy.29 = f32[16,1,99,128]{3,1,2,0:T(1,128)} copy(f32[16,1,99,128]{3,2,0,1:T(8,128)S(1)} %fusion.9) | data formatting | bytes 1622016 | tf_op jit(solution)/shard_map/snr,kjn->ksjr/transpose | solution.py:196
  49.8 6.2 %all-to-all-start.1 = ((f32[16,1,99,128]{3,1,2,0:T(1,128)}), f32[16,1,99,128]{3,1,2,0:T(1,128)}, u32[]{:S(2)}, u32[]{:S(2)}) async-start(f32[16,1,99,128]{3,1,2,0:T(1,128)} %copy.29), calls=%async_computation.1 | async-start | bytes 1622016 | tf_op jit(solution)/shard_map/all_to_all | solution.py:197
  58.4 2.7 %collective-permute-start.1 = (f32[9,96,128]{2,1,0:T(8,128)}, f32[9,96,128]{2,1,0:T(8,128)}, u32[]{:S(2)}, u32[]{:S(2)}) collective-permute-start(f32[9,96,128]{2,1,0:T(8,128)} %pad_maximum_fusion.4), channel_id=1, source_target_pairs={{16,0},{32,16},{48,32},{64,48},{80,64},{96,80},{112,96},{128,112},... | collective-permute-start | bytes 1327112 | tf_op jit(solution)/shard_map/ppermute | solution.py:138
  61.1 4.3 %collective-permute-start = (f32[8,96,128]{2,1,0:T(8,128)}, f32[8,96,128]{2,1,0:T(8,128)}, u32[]{:S(2)}, u32[]{:S(2)}) collective-permute-start(f32[8,96,128]{2,1,0:T(8,128)} %get-tuple-element.14), channel_id=1, source_target_pairs={{0,16},{16,32},{32,48},{48,64},{64,80},{80,96},{96,112},{112,128},... | collective-permute-start | bytes 1179656 | tf_op jit(solution)/shard_map/ppermute | solution.py:134
  65.5 12.6 %collective-permute-done.1 = f32[9,96,128]{2,1,0:T(8,128)} collective-permute-done((f32[9,96,128]{2,1,0:T(8,128)}, f32[9,96,128]{2,1,0:T(8,128)}, u32[]{:S(2)}, u32[]{:S(2)}) %collective-permute-start.1) | collective-permute-done | bytes 442400 | tf_op jit(solution)/shard_map/ppermute | solution.py:138
  80.0 1.4 %pad_maximum_fusion.15 = f32[8,11,1,128]{3,2,1,0:T(1,128)} fusion(f32[8,1,96,128]{3,2,1,0:T(8,128)S(1)} %broadcast_in_dim_broadcast_in_dim.4, f32[8,1,96,128]{3,2,1,0:T(8,128)S(1)} %slice_bitcast_fusion.8, f32[8,8,96,128]{3,2,1,0:T(8,128)S(1)} %constant_dynamic-update-slice_fusion, f32[8,1,96,128]{3,2,1,0:T(8,128)} %bitcast.1), kind=kLoop, calls=%fused_computation.148 | loop fusion | flops 33792 | bytes 4370432 | tf_op jit(solution)/shard_map/slice | solution.py:149
  81.4 1.5 %collective-permute-start.2 = (f32[8,11,1,128]{3,2,1,0:T(1,128)}, f32[8,11,1,128]{3,2,1,0:T(1,128)}, u32[]{:S(2)}, u32[]{:S(2)}) collective-permute-start(f32[8,11,1,128]{3,2,1,0:T(1,128)} %pad_maximum_fusion.15), channel_id=1, source_target_pairs={{0,1},{1,2},{2,3},{3,4},{4,5},{5,6},{6,7},{7,8},{8,9},{9,10},{10,1... | collective-permute-start | bytes 135176 | tf_op jit(solution)/shard_map/ppermute | solution.py:148
  82.9 1.4 %pad_maximum_fusion.12 = f32[8,11,2,128]{3,2,1,0:T(2,128)} fusion(f32[8,1,96,128]{3,2,1,0:T(8,128)S(1)} %broadcast_in_dim_broadcast_in_dim.4, f32[8,1,96,128]{3,2,1,0:T(8,128)S(1)} %slice_bitcast_fusion.8, f32[8,8,96,128]{3,2,1,0:T(8,128)S(1)} %constant_dynamic-update-slice_fusion, f32[8,1,96,128]{3,2,1,0:T(8,128)} %bitcast.1), kind=kLoop, calls=%fused_computation.140 | loop fusion | flops 67584 | bytes 4415488 | tf_op jit(solution)/shard_map/concatenate | solution.py:139
  84.4 2.8 %collective-permute-start.3 = (f32[8,11,2,128]{3,2,1,0:T(2,128)}, f32[8,11,2,128]{3,2,1,0:T(2,128)}, u32[]{:S(2)}, u32[]{:S(2)}) collective-permute-start(f32[8,11,2,128]{3,2,1,0:T(2,128)} %pad_maximum_fusion.12), channel_id=1, source_target_pairs={{1,0},{2,1},{3,2},{4,3},{5,4},{6,5},{7,6},{8,7},{9,8},{10,9},{11,1... | collective-permute-start | bytes 270344 | tf_op jit(solution)/shard_map/ppermute | solution.py:151
  89.3 1.3 %collective-permute-start.6 = (f32[5,99,128]{2,1,0:T(8,128)S(1)}, f32[5,99,128]{2,1,0:T(8,128)S(1)}, u32[]{:S(2)}, u32[]{:S(2)}) collective-permute-start(f32[5,99,128]{2,1,0:T(8,128)S(1)} %pad_maximum_fusion.11), channel_id=1, source_target_pairs={{16,8},{17,9},{18,10},{19,11},{20,12},{21,13},{22,14},{23,15},{24,... | collective-permute-start | bytes 760328 | tf_op jit(solution)/shard_map/ppermute | solution.py:213
  90.7 1.8 %pad_maximum_fusion = f32[8,11,99,128]{3,2,1,0:T(8,128)S(1)} fusion(f32[8,11,2,128]{3,2,1,0:T(2,128)} %collective-permute-done.3, f32[8,1,96,128]{3,2,1,0:T(8,128)S(1)} %copy-done.1, f32[8,1,96,128]{3,2,1,0:T(8,128)S(1)} %slice_bitcast_fusion.8, f32[8,8,96,128]{3,2,1,0:T(8,128)S(1)} %constant_dynamic-update-slice_fusion, f32[8,1,96,128]{3,2,1,0:T(8,128)} %bitcast.1, ...), kind=kLoop, calls=%fused_computation | loop fusion | flops 5575680 | bytes 8921088 | tf_op jit(solution)/shard_map/concatenate | solution.py:154
  94.4 1.5 %collective-permute-start.7 = (f32[16,99,128]{2,0,1:T(8,128)S(1)}, f32[16,99,128]{2,0,1:T(8,128)S(1)}, u32[]{:S(2)}, u32[]{:S(2)}) collective-permute-start(f32[16,99,128]{2,0,1:T(8,128)S(1)} %bitcast.76), channel_id=1, source_target_pairs={{16,0},{224,240},{17,1},{225,241},{18,2},{226,242},{19,3},{227,243... | collective-permute-start | bytes 2433032 | tf_op jit(solution)/shard_map/ppermute | solution.py:200
  96.2 1.5 %collective-permute-done.7 = f32[16,99,128]{2,0,1:T(8,128)S(1)} collective-permute-done((f32[16,99,128]{2,0,1:T(8,128)S(1)}, f32[16,99,128]{2,0,1:T(8,128)S(1)}, u32[]{:S(2)}, u32[]{:S(2)}) %collective-permute-start.7) | collective-permute-done | bytes 811040 | tf_op jit(solution)/shard_map/ppermute | solution.py:200
  (81 shorter events, 21.9 us)
Async XLA Ops:
  1.8 1.6 %copy-start.4 = (f32[3,8,96,128]{3,2,1,0:T(8,128)S(1)}, f32[3,8,96,128]{3,2,1,0:T(8,128)}, u32[]{:S(2)}) copy-start(f32[3,8,96,128]{3,2,1,0:T(8,128)} %param.7) | copy-start | bytes 3538948
  5.1 17.1 %copy-start.6 = (s32[2,4]{1,0:T(2,128)S(1)}, s32[2,4]{1,0:T(2,128)}, u32[]{:S(2)}) copy-start(s32[2,4]{1,0:T(2,128)} %param.8) | copy-start | bytes 100
  5.1 6.8 %collective-permute-start.4 = (f32[16,96,128]{2,1,0:T(8,128)}, f32[16,96,128]{2,1,0:T(8,128)}, u32[]{:S(2)}, u32[]{:S(2)}) collective-permute-start(f32[16,96,128]{2,1,0:T(8,128)} %bitcast.6), channel_id=1, source_target_pairs={{0,16},{240,224},{1,17},{241,225},{2,18},{242,226},{3,19},{243,227... | collective-permute-start | bytes 2359304 | tf_op jit(solution)/shard_map/ppermute | solution.py:163
  14.2 28.0 %all-to-all-start = ((f32[16,1,96,128]{3,2,1,0:T(8,128)}), f32[16,1,96,128]{3,2,1,0:T(8,128)}, u32[]{:S(2)}, u32[]{:S(2)}) async-start(f32[16,1,96,128]{3,2,1,0:T(8,128)} %bitcast.78), calls=%async_computation | async-start | bytes 1572864 | tf_op jit(solution)/shard_map/all_to_all | solution.py:166
  42.1 4.4 %copy-start.2 = (f32[16,99,128]{2,1,0:T(8,128)S(1)}, f32[16,99,128]{2,1,0:T(8,128)}, u32[]{:S(2)}) copy-start(f32[16,99,128]{2,1,0:T(8,128)} %get-tuple-element.58) | copy-start | bytes 2433028
  42.1 4.4 %copy-start.3 = (f32[16,99,128]{2,1,0:T(8,128)S(1)}, f32[16,99,128]{2,1,0:T(8,128)}, u32[]{:S(2)}) copy-start(f32[16,99,128]{2,1,0:T(8,128)} %get-tuple-element.59) | copy-start | bytes 2433028
  49.8 37.4 %all-to-all-start.1 = ((f32[16,1,99,128]{3,1,2,0:T(1,128)}), f32[16,1,99,128]{3,1,2,0:T(1,128)}, u32[]{:S(2)}, u32[]{:S(2)}) async-start(f32[16,1,99,128]{3,1,2,0:T(1,128)} %copy.29), calls=%async_computation.1 | async-start | bytes 1622016 | tf_op jit(solution)/shard_map/all_to_all | solution.py:197
  58.4 19.7 %collective-permute-start.1 = (f32[9,96,128]{2,1,0:T(8,128)}, f32[9,96,128]{2,1,0:T(8,128)}, u32[]{:S(2)}, u32[]{:S(2)}) collective-permute-start(f32[9,96,128]{2,1,0:T(8,128)} %pad_maximum_fusion.4), channel_id=1, source_target_pairs={{16,0},{32,16},{48,32},{64,48},{80,64},{96,80},{112,96},{128,112},... | collective-permute-start | bytes 1327112 | tf_op jit(solution)/shard_map/ppermute | solution.py:138
  61.1 18.8 %collective-permute-start = (f32[8,96,128]{2,1,0:T(8,128)}, f32[8,96,128]{2,1,0:T(8,128)}, u32[]{:S(2)}, u32[]{:S(2)}) collective-permute-start(f32[8,96,128]{2,1,0:T(8,128)} %get-tuple-element.14), channel_id=1, source_target_pairs={{0,16},{16,32},{32,48},{48,64},{64,80},{80,96},{96,112},{112,128},... | collective-permute-start | bytes 1179656 | tf_op jit(solution)/shard_map/ppermute | solution.py:134
  80.0 4.4 %copy-start = (f32[8,1,96,128]{3,2,1,0:T(8,128)}, f32[8,1,96,128]{3,2,1,0:T(8,128)S(1)}, u32[]{:S(2)}) copy-start(f32[8,1,96,128]{3,2,1,0:T(8,128)S(1)} %broadcast_in_dim_broadcast_in_dim.4) | copy-start | bytes 1179652
  81.4 9.2 %collective-permute-start.2 = (f32[8,11,1,128]{3,2,1,0:T(1,128)}, f32[8,11,1,128]{3,2,1,0:T(1,128)}, u32[]{:S(2)}, u32[]{:S(2)}) collective-permute-start(f32[8,11,1,128]{3,2,1,0:T(1,128)} %pad_maximum_fusion.15), channel_id=1, source_target_pairs={{0,1},{1,2},{2,3},{3,4},{4,5},{5,6},{6,7},{7,8},{8,9},{9,10},{10,1... | collective-permute-start | bytes 135176 | tf_op jit(solution)/shard_map/ppermute | solution.py:148
  84.4 6.3 %collective-permute-start.3 = (f32[8,11,2,128]{3,2,1,0:T(2,128)}, f32[8,11,2,128]{3,2,1,0:T(2,128)}, u32[]{:S(2)}, u32[]{:S(2)}) collective-permute-start(f32[8,11,2,128]{3,2,1,0:T(2,128)} %pad_maximum_fusion.12), channel_id=1, source_target_pairs={{1,0},{2,1},{3,2},{4,3},{5,4},{6,5},{7,6},{8,7},{9,8},{10,9},{11,1... | collective-permute-start | bytes 270344 | tf_op jit(solution)/shard_map/ppermute | solution.py:151
  87.2 3.5 %copy-start.1 = (f32[8,1,96,128]{3,2,1,0:T(8,128)S(1)}, f32[8,1,96,128]{3,2,1,0:T(8,128)}, u32[]{:S(2)}) copy-start(f32[8,1,96,128]{3,2,1,0:T(8,128)} %copy-done) | copy-start | bytes 1179652
  89.3 6.6 %collective-permute-start.6 = (f32[5,99,128]{2,1,0:T(8,128)S(1)}, f32[5,99,128]{2,1,0:T(8,128)S(1)}, u32[]{:S(2)}, u32[]{:S(2)}) collective-permute-start(f32[5,99,128]{2,1,0:T(8,128)S(1)} %pad_maximum_fusion.11), channel_id=1, source_target_pairs={{16,8},{17,9},{18,10},{19,11},{20,12},{21,13},{22,14},{23,15},{24,... | collective-permute-start | bytes 760328 | tf_op jit(solution)/shard_map/ppermute | solution.py:213
  92.5 3.6 %copy-start.5 = (f32[8]{0:T(128)S(1)}, f32[8]{0:T(128)}, u32[]{:S(2)}) copy-start(f32[8]{0:T(128)} %constant.115.clone) | copy-start | bytes 100
  92.5 3.5 %collective-permute-start.5 = (f32[5,99,128]{2,1,0:T(8,128)S(1)}, f32[5,99,128]{2,1,0:T(8,128)S(1)}, u32[]{:S(2)}, u32[]{:S(2)}) collective-permute-start(f32[5,99,128]{2,1,0:T(8,128)S(1)} %pad_maximum_fusion.11), channel_id=1, source_target_pairs={{0,8},{1,9},{2,10},{3,11},{4,12},{5,13},{6,14},{7,15},{8,0},{9,1},... | collective-permute-start | bytes 760328 | tf_op jit(solution)/shard_map/ppermute | solution.py:208
  94.4 3.2 %collective-permute-start.7 = (f32[16,99,128]{2,0,1:T(8,128)S(1)}, f32[16,99,128]{2,0,1:T(8,128)S(1)}, u32[]{:S(2)}, u32[]{:S(2)}) collective-permute-start(f32[16,99,128]{2,0,1:T(8,128)S(1)} %bitcast.76), channel_id=1, source_target_pairs={{16,0},{224,240},{17,1},{225,241},{18,2},{226,242},{19,3},{227,243... | collective-permute-start | bytes 2433032 | tf_op jit(solution)/shard_map/ppermute | solution.py:200

commit v3 on v2

--- a/solution.py
+++ b/solution.py
@@ -155,18 +155,20 @@
 
     north_side = t <= 1
     helper = (t == 1) | (t == theta_count - 2)
-    edge_rows = jnp.where(at_north, combined[:, :CAP], combined[:, ct - CAP :])
-    slot_rows = edge_rows.reshape(channels * CAP, npc, nr)
     half = channels * CAP // 2
+    first_half = jnp.concatenate([density, velocity[:2]], axis=0)
+    second_half = jnp.concatenate([velocity[2:], bfield], axis=0)
+
+    def cap_of(fields):
+        rows = jnp.where(at_north, fields[:, :CAP], fields[:, ct - CAP :])
+        return rows.reshape(half, npc, nr)
+
     pairs_out = [(0, 1), (theta_count - 1, theta_count - 2)]
     pairs_in = [(1, 0), (theta_count - 2, theta_count - 1)]
-    handed = lax.ppermute(slot_rows[half:], "theta", pairs_out)
-    work = jnp.where(helper, handed, slot_rows[:half])
+    handed = lax.ppermute(cap_of(second_half), "theta", pairs_out)
+    work = jnp.where(helper, handed, cap_of(first_half))
     per_device = half // phi_count
-    cycle = lax.all_to_all(
-        work.reshape(phi_count, per_device, npc, nr), "phi", split_axis=0, concat_axis=2, tiled=True
-    )
-    cycle = cycle.reshape(per_device, cycle_len, nr)
+    cycle = lax.all_to_all(work, "phi", split_axis=0, concat_axis=1, tiled=True)
     analysis = fourier_rows(jnp.arange(cycle_len, dtype=jnp.int32), cycle_len)
     dst_cols = (
         jnp.arange(phi_count, dtype=jnp.int32)[:, None] * npc
@@ -194,8 +196,8 @@
     coeffs = jnp.einsum("smr,mn->snr", cycle, analysis, precision=lax.Precision.HIGHEST)
     coeffs = coeffs * kept_weight[:, :, None]
     out = jnp.einsum("snr,kjn->ksjr", coeffs, synthesis, precision=lax.Precision.HIGHEST)
+    out = out.reshape(phi_count * per_device, npc + 3, nr)
     mine = lax.all_to_all(out, "phi", split_axis=0, concat_axis=0, tiled=True)
-    mine = mine.reshape(half, npc + 3, nr)
 
     from_helper = lax.ppermute(mine, "theta", pairs_in)
     cap_rows = jnp.concatenate([mine, from_helper], axis=0).reshape(channels, CAP, npc + 3, nr)

time: 110 us -> 114 us (1.036)
  waiting for transfers between devices: 28.4 us -> 23.5 us
  local copies, waits for them, and re-layouts: 16.4 us -> 21.1 us
  other arithmetic: 25.9 us -> 28.1 us
    slice x1 -> x5, local copies, waits for them, and re-layouts: 1.3 us -> 7.44 us  [the longest x1 3.15 us: local(): last_rows = mine[CAP - 1::CAP]]
    all_to_all x1, waiting for transfers between devices: 8.97 us -> 6.61 us  [local(): cycle = lax.all_to_all(work, 'phi', split_axis=0, concat_axis=1, tiled=True)]
    ppermute x1, waiting for transfers between devices: 5.33 us -> 3.55 us  [local(): handed = lax.ppermute(cap_of(second_half), 'theta', pairs_out)]
    transpose x1 -> x0, local copies, waits for them, and re-layouts: 1.72 us -> none  [local(): jnp.einsum('snr,kjn->ksjr', coeffs, synthesis, precision=lax.Precision.HI...]
    concatenate x1, local copies, waits for them, and re-layouts: 0.09 us -> 1.35 us  [local(): combined = jnp.concatenate([density, velocity, bfield], axis=0)]
    reshape x1 -> x0, local copies, waits for them, and re-layouts: 1.25 us -> none  [local(): mine = mine.reshape(half, npc + 3, nr)]
    select_n x2 -> x3, other arithmetic: 2.54 us -> 2.4 us  [the longest x2 1.43 us: cap_of(): rows = jnp.where(at_north, fields[:, :CAP], fields[:, ct - CAP:])]
  transfers between devices with their start and end apart: 10 -> 10, of which waited for: 4 -> 5; matrix products, arithmetic and copies ran while one was open for 21% -> 30% of each run, Pallas kernels for 0% -> 0%
where the time goes in v3:
time: 114 us; the launch traced here: 113 us
  starting transfers between devices  31.4 us (28%)
  other arithmetic  28.1 us (25%)
  waiting for transfers between devices  23.5 us (21%)
  local copies, waits for them, and re-layouts  21.1 us (19%)
  matrix products  6.74 us (6%)
  between operations  1.83 us (2%)
    ppermute x1, waiting for transfers between devices, local(): lax.ppermute(up_send, 'theta', [(i + 1, i) for i in range(theta_count - 1)])  12 us
    all_to_all x1, starting transfers between devices, local(): cycle = lax.all_to_all(work, 'phi', split_axis=0, concat_axis=1, tiled=True)  7.97 us
    all_to_all x1, waiting for transfers between devices, local(): cycle = lax.all_to_all(work, 'phi', split_axis=0, concat_axis=1, tiled=True)  6.61 us
    all_to_all x1, starting transfers between devices, local(): mine = lax.all_to_all(out, 'phi', split_axis=0, concat_axis=0, tiled=True)  6.4 us
    cos x1, other arithmetic, fourier_rows(): return jnp.concatenate([jnp.cos(angle), jnp.sin(angle)], axis=-1)  5.31 us
    sin x1, other arithmetic, fourier_rows(): return jnp.concatenate([jnp.cos(angle), jnp.sin(angle)], axis=-1)  4.34 us
    dot_general x1, matrix products, local(): jnp.einsum('smr,mn->snr', cycle, analysis, precision=lax.Precision.HIGHEST)  4.34 us
    ppermute x1, starting transfers between devices, local(): lax.ppermute(combined[:, ct - 1], 'theta', [(i, i + 1) for i in range(the...  4.3 us
  transfers between devices with their start and end apart: 10, of which 5 were waited for; matrix products, arithmetic and copies ran while one was open for 30% of the time, Pallas kernels for 0%

profile of v3, /device:TPU:1, one launch (start us, length us, event | category | flops | bytes accessed | tf_op | source)
XLA Modules:
  0.0 112.5 jit_solution(388218869511577274)
XLA Ops:
  1.8 1.3 %fusion.27 = f32[4,4,96,128]{3,2,1,0:T(8,128)S(1)} fusion(f32[1,8,96,128]{3,2,1,0:T(8,128)S(1)} %slice.379, f32[3,8,96,128]{3,2,1,0:T(8,128)} %param.7, pred[]{:T(512)S(6)} %eq.63), kind=kLoop, calls=%fused_computation.35 | loop fusion | flops 589824 | bytes 2359297 | tf_op jit(solution)/shard_map/jit(_where)/select_n | solution.py:163
  5.9 3.6 %collective-permute-done.4 = f32[16,96,128]{2,1,0:T(8,128)S(1)} collective-permute-done((f32[16,96,128]{2,1,0:T(8,128)S(1)}, f32[16,96,128]{2,1,0:T(8,128)S(1)}, u32[]{:S(2)}, u32[]{:S(2)}) %collective-permute-start.4) | collective-permute-done | bytes 786464 | tf_op jit(solution)/shard_map/ppermute | solution.py:168
  10.4 8.0 %all-to-all-start = ((f32[16,96,128]{2,1,0:T(8,128)}), f32[16,96,128]{2,1,0:T(8,128)}, u32[]{:S(2)}, u32[]{:S(2)}) async-start(f32[16,96,128]{2,1,0:T(8,128)} %bitcast_select_fusion), calls=%async_computation | async-start | bytes 1572864 | tf_op jit(solution)/shard_map/all_to_all | solution.py:171
  19.6 1.4 %constant_dynamic-update-slice_fusion.1 = f32[8,8,96,128]{3,2,1,0:T(8,128)S(1)} fusion(f32[8,8,96,128]{3,2,1,0:T(8,128)S(1)} %constant_dynamic-update-slice_fusion.2, f32[3,8,96,128]{3,2,1,0:T(8,128)} %param.6), kind=kLoop, calls=%fused_computation.156 | loop fusion | bytes 2359296
  21.9 5.3 %fusion.20 = (f32[16,99,128]{2,1,0:T(8,128)}, f32[16,99,128]{2,1,0:T(8,128)}) fusion(s32[16,99]{1,0:T(8,128)S(1)} %add_select_fusion.2), kind=kLoop, calls=%fused_computation.28 | loop fusion | flops 1824768 | bytes 1628352 | tf_op jit(solution)/shard_map/cos | solution.py:110
  27.2 4.3 %fusion.30 = (f32[1536,128]{1,0:T(8,128)}, f32[1536,128]{1,0:T(8,128)}) fusion(), kind=kLoop, calls=%fused_computation.43 | loop fusion | flops 1769472 | bytes 1572864 | tf_op jit(solution)/shard_map/sin | solution.py:110
  31.5 6.6 %all-to-all-done = f32[16,96,128]{2,1,0:T(8,128)} async-done(((f32[16,96,128]{2,1,0:T(8,128)}), f32[16,96,128]{2,1,0:T(8,128)}, u32[]{:S(2)}, u32[]{:S(2)}) %all-to-all-start) | async-done | bytes 786464 | tf_op jit(solution)/shard_map/all_to_all | solution.py:171
  38.2 4.3 %fusion.12 = f32[256,128,1]{1,0,2:T(8,128)S(1)} fusion(f32[1536,128]{1,0:T(8,128)} %bitcast.9, f32[1536,128]{1,0:T(8,128)} %get-tuple-element.60, f32[1536,128]{1,0:T(8,128)} %get-tuple-element.61, f32[256]{0:T(256)S(1)} %compare_select_fusion.1), kind=kOutput, calls=%fused_computation.21 | convolution fusion | flops 604405760 | bytes 2491392 | tf_op jit(solution)/shard_map/smr,mn->snr/dot_general | solution.py:196
  42.5 2.4 %fusion.1 = f32[16,99,128]{2,1,0:T(8,128)} fusion(f32[256,128,1]{1,0,2:T(8,128)S(1)} %fusion.12, f32[16,99,128]{2,1,0:T(8,128)S(1)} %copy-done.2, f32[16,99,128]{2,1,0:T(8,128)S(1)} %copy-done.1), kind=kOutput, calls=%fused_computation.4 | convolution fusion | flops 623259648 | bytes 2564096 | tf_op jit(solution)/shard_map/snr,kjn->ksjr/dot_general | solution.py:198
  44.9 6.4 %all-to-all-start.1 = ((f32[16,99,128]{2,1,0:T(8,128)}), f32[16,99,128]{2,1,0:T(8,128)}, u32[]{:S(2)}, u32[]{:S(2)}) async-start(f32[16,99,128]{2,1,0:T(8,128)} %fusion.1), calls=%async_computation.1 | async-start | bytes 1703936 | tf_op jit(solution)/shard_map/all_to_all | solution.py:200
  51.3 1.4 %constant_dynamic-update-slice_fusion = f32[8,8,96,128]{3,2,1,0:T(8,128)S(1)} fusion(f32[8,8,96,128]{3,2,1,0:T(8,128)S(1)} %constant_dynamic-update-slice_fusion.1, f32[3,8,96,128]{3,2,1,0:T(8,128)} %param.7), kind=kLoop, calls=%fused_computation.155 | loop fusion | bytes 2359296 | tf_op jit(solution)/shard_map/concatenate | solution.py:114
  54.3 2.8 %collective-permute-start.1 = (f32[9,96,128]{2,1,0:T(8,128)}, f32[9,96,128]{2,1,0:T(8,128)}, u32[]{:S(2)}, u32[]{:S(2)}) collective-permute-start(f32[9,96,128]{2,1,0:T(8,128)} %pad_maximum_fusion.6), channel_id=1, source_target_pairs={{16,0},{32,16},{48,32},{64,48},{80,64},{96,80},{112,96},{128,112},... | collective-permute-start | bytes 1327112 | tf_op jit(solution)/shard_map/ppermute | solution.py:138
  57.0 4.3 %collective-permute-start = (f32[8,96,128]{2,1,0:T(8,128)}, f32[8,96,128]{2,1,0:T(8,128)}, u32[]{:S(2)}, u32[]{:S(2)}) collective-permute-start(f32[8,96,128]{2,1,0:T(8,128)} %get-tuple-element.14), channel_id=1, source_target_pairs={{0,16},{16,32},{32,48},{48,64},{64,80},{80,96},{96,112},{112,128},... | collective-permute-start | bytes 1179656 | tf_op jit(solution)/shard_map/ppermute | solution.py:134
  61.4 12.0 %collective-permute-done.1 = f32[9,96,128]{2,1,0:T(8,128)} collective-permute-done((f32[9,96,128]{2,1,0:T(8,128)}, f32[9,96,128]{2,1,0:T(8,128)}, u32[]{:S(2)}, u32[]{:S(2)}) %collective-permute-start.1) | collective-permute-done | bytes 442400 | tf_op jit(solution)/shard_map/ppermute | solution.py:138
  75.3 1.4 %pad_maximum_fusion.17 = f32[8,11,1,128]{3,2,1,0:T(1,128)} fusion(f32[8,1,96,128]{3,2,1,0:T(8,128)S(1)} %broadcast_in_dim_broadcast_in_dim.4, f32[8,1,96,128]{3,2,1,0:T(8,128)S(1)} %slice_bitcast_fusion.8, f32[8,8,96,128]{3,2,1,0:T(8,128)S(1)} %constant_dynamic-update-slice_fusion, f32[8,1,96,128]{3,2,1,0:T(8,128)} %bitcast.2), kind=kLoop, calls=%fused_computation.153 | loop fusion | flops 33792 | bytes 4370432 | tf_op jit(solution)/shard_map/slice | solution.py:149
  76.7 2.3 %collective-permute-start.2 = (f32[8,11,1,128]{3,2,1,0:T(1,128)}, f32[8,11,1,128]{3,2,1,0:T(1,128)}, u32[]{:S(2)}, u32[]{:S(2)}) collective-permute-start(f32[8,11,1,128]{3,2,1,0:T(1,128)} %pad_maximum_fusion.17), channel_id=1, source_target_pairs={{0,1},{1,2},{2,3},{3,4},{4,5},{5,6},{6,7},{7,8},{8,9},{9,10},{10,1... | collective-permute-start | bytes 135176 | tf_op jit(solution)/shard_map/ppermute | solution.py:148
  79.0 1.4 %pad_maximum_fusion.14 = f32[8,11,2,128]{3,2,1,0:T(2,128)} fusion(f32[8,1,96,128]{3,2,1,0:T(8,128)S(1)} %broadcast_in_dim_broadcast_in_dim.4, f32[8,1,96,128]{3,2,1,0:T(8,128)S(1)} %slice_bitcast_fusion.8, f32[8,8,96,128]{3,2,1,0:T(8,128)S(1)} %constant_dynamic-update-slice_fusion, f32[8,1,96,128]{3,2,1,0:T(8,128)} %bitcast.2), kind=kLoop, calls=%fused_computation.146 | loop fusion | flops 67584 | bytes 4415488 | tf_op jit(solution)/shard_map/concatenate | solution.py:139
  80.4 2.7 %collective-permute-start.3 = (f32[8,11,2,128]{3,2,1,0:T(2,128)}, f32[8,11,2,128]{3,2,1,0:T(2,128)}, u32[]{:S(2)}, u32[]{:S(2)}) collective-permute-start(f32[8,11,2,128]{3,2,1,0:T(2,128)} %pad_maximum_fusion.14), channel_id=1, source_target_pairs={{1,0},{2,1},{3,2},{4,3},{5,4},{6,5},{7,6},{8,7},{9,8},{10,9},{11,1... | collective-permute-start | bytes 270344 | tf_op jit(solution)/shard_map/ppermute | solution.py:151
  83.1 2.2 %copy.38 = f32[16,99,128]{2,0,1:T(8,128)} copy(f32[16,99,128]{2,1,0:T(8,128)} %all-to-all-done.1) | data formatting | bytes 1622016 | tf_op jit(solution)/shard_map/all_to_all | solution.py:200
  85.3 3.1 %slice.385 = f32[4,99,128]{2,0,1:T(4,128)} slice(f32[16,99,128]{2,0,1:T(8,128)} %copy.38), slice={[0:16:4], [0:99:1], [0:128:1]} | slice | bytes 405504 | tf_op jit(solution)/shard_map/slice | solution.py:205
  88.5 3.1 %slice.386 = f32[4,99,128]{2,0,1:T(4,128)} slice(f32[16,99,128]{2,0,1:T(8,128)} %copy.38), slice={[3:16:4], [0:99:1], [0:128:1]} | slice | bytes 405504 | tf_op jit(solution)/shard_map/slice | solution.py:206
  93.6 1.4 %collective-permute-start.6 = (f32[5,99,128]{2,0,1:T(8,128)S(1)}, f32[5,99,128]{2,0,1:T(8,128)S(1)}, u32[]{:S(2)}, u32[]{:S(2)}) collective-permute-start(f32[5,99,128]{2,0,1:T(8,128)S(1)} %pad_maximum_fusion.7), channel_id=1, source_target_pairs={{16,8},{17,9},{18,10},{19,11},{20,12},{21,13},{22,14},{23,15},{24,... | collective-permute-start | bytes 760328 | tf_op jit(solution)/shard_map/ppermute | solution.py:215
  95.8 1.9 %pad_maximum_fusion = f32[8,11,99,128]{3,2,1,0:T(8,128)S(1)} fusion(f32[8,11,2,128]{3,2,1,0:T(2,128)} %collective-permute-done.3, f32[8,1,96,128]{3,2,1,0:T(8,128)} %copy-done, f32[8,1,96,128]{3,2,1,0:T(8,128)S(1)} %slice_bitcast_fusion.8, f32[8,8,96,128]{3,2,1,0:T(8,128)S(1)} %constant_dynamic-update-slice_fusion, f32[8,1,96,128]{3,2,1,0:T(8,128)} %bitcast.2, ...), kind=kLoop, calls=%fused_computation | loop fusion | flops 5575680 | bytes 8921088 | tf_op jit(solution)/shard_map/concatenate | solution.py:154
  97.7 1.5 %collective-permute-start.7 = (f32[16,99,128]{2,0,1:T(8,128)S(1)}, f32[16,99,128]{2,0,1:T(8,128)S(1)}, u32[]{:S(2)}, u32[]{:S(2)}) collective-permute-start(f32[16,99,128]{2,0,1:T(8,128)S(1)} %copy-done.4), channel_id=1, source_target_pairs={{16,0},{224,240},{17,1},{225,241},{18,2},{226,242},{19,3},{227,243... | collective-permute-start | bytes 2433032 | tf_op jit(solution)/shard_map/ppermute | solution.py:202
  (86 shorter events, 25.5 us)
Async XLA Ops:
  0.6 5.2 %slice-start = ((f32[3,8,96,128]{3,2,1,0:T(8,128)}), f32[2,8,96,128]{3,2,1,0:T(8,128)S(1)}, s32[]{:S(2)}) async-start(f32[3,8,96,128]{3,2,1,0:T(8,128)} %param.6), calls=%async_computation.2 | async-start | bytes 1572864 | tf_op jit(solution)/shard_map/slice | solution.py:159
  0.6 3.8 %copy-start.6 = (s32[2,4]{1,0:T(2,128)S(1)}, s32[2,4]{1,0:T(2,128)}, u32[]{:S(2)}) copy-start(s32[2,4]{1,0:T(2,128)} %param.8) | copy-start | bytes 100
  0.7 5.1 %copy-start.3 = (f32[2,8,96,128]{3,2,1,0:T(8,128)S(1)}, f32[2,8,96,128]{3,2,1,0:T(8,128)}, u32[]{:S(2)}) copy-start(f32[2,8,96,128]{3,2,1,0:T(8,128)} %param.5) | copy-start | bytes 2359300
  3.2 6.3 %collective-permute-start.4 = (f32[16,96,128]{2,1,0:T(8,128)S(1)}, f32[16,96,128]{2,1,0:T(8,128)S(1)}, u32[]{:S(2)}, u32[]{:S(2)}) collective-permute-start(f32[16,96,128]{2,1,0:T(8,128)S(1)} %bitcast.62), channel_id=1, source_target_pairs={{0,16},{240,224},{1,17},{241,225},{2,18},{242,226},{3,19},{243,227... | collective-permute-start | bytes 2359304 | tf_op jit(solution)/shard_map/ppermute | solution.py:168
  10.4 27.7 %all-to-all-start = ((f32[16,96,128]{2,1,0:T(8,128)}), f32[16,96,128]{2,1,0:T(8,128)}, u32[]{:S(2)}, u32[]{:S(2)}) async-start(f32[16,96,128]{2,1,0:T(8,128)} %bitcast_select_fusion), calls=%async_computation | async-start | bytes 1572864 | tf_op jit(solution)/shard_map/all_to_all | solution.py:171
  38.1 4.4 %copy-start.1 = (f32[16,99,128]{2,1,0:T(8,128)S(1)}, f32[16,99,128]{2,1,0:T(8,128)}, u32[]{:S(2)}) copy-start(f32[16,99,128]{2,1,0:T(8,128)} %get-tuple-element.56) | copy-start | bytes 2433028
  38.1 4.4 %copy-start.2 = (f32[16,99,128]{2,1,0:T(8,128)S(1)}, f32[16,99,128]{2,1,0:T(8,128)}, u32[]{:S(2)}) copy-start(f32[16,99,128]{2,1,0:T(8,128)} %get-tuple-element.57) | copy-start | bytes 2433028
  44.9 38.2 %all-to-all-start.1 = ((f32[16,99,128]{2,1,0:T(8,128)}), f32[16,99,128]{2,1,0:T(8,128)}, u32[]{:S(2)}, u32[]{:S(2)}) async-start(f32[16,99,128]{2,1,0:T(8,128)} %fusion.1), calls=%async_computation.1 | async-start | bytes 1703936 | tf_op jit(solution)/shard_map/all_to_all | solution.py:200
  54.3 19.1 %collective-permute-start.1 = (f32[9,96,128]{2,1,0:T(8,128)}, f32[9,96,128]{2,1,0:T(8,128)}, u32[]{:S(2)}, u32[]{:S(2)}) collective-permute-start(f32[9,96,128]{2,1,0:T(8,128)} %pad_maximum_fusion.6), channel_id=1, source_target_pairs={{16,0},{32,16},{48,32},{64,48},{80,64},{96,80},{112,96},{128,112},... | collective-permute-start | bytes 1327112 | tf_op jit(solution)/shard_map/ppermute | solution.py:138
  57.0 18.2 %collective-permute-start = (f32[8,96,128]{2,1,0:T(8,128)}, f32[8,96,128]{2,1,0:T(8,128)}, u32[]{:S(2)}, u32[]{:S(2)}) collective-permute-start(f32[8,96,128]{2,1,0:T(8,128)} %get-tuple-element.14), channel_id=1, source_target_pairs={{0,16},{16,32},{32,48},{48,64},{64,80},{80,96},{96,112},{112,128},... | collective-permute-start | bytes 1179656 | tf_op jit(solution)/shard_map/ppermute | solution.py:134
  75.2 5.2 %copy-start = (f32[8,1,96,128]{3,2,1,0:T(8,128)}, f32[8,1,96,128]{3,2,1,0:T(8,128)S(1)}, u32[]{:S(2)}) copy-start(f32[8,1,96,128]{3,2,1,0:T(8,128)S(1)} %broadcast_in_dim_broadcast_in_dim.4) | copy-start | bytes 1179652
  76.7 19.1 %collective-permute-start.2 = (f32[8,11,1,128]{3,2,1,0:T(1,128)}, f32[8,11,1,128]{3,2,1,0:T(1,128)}, u32[]{:S(2)}, u32[]{:S(2)}) collective-permute-start(f32[8,11,1,128]{3,2,1,0:T(1,128)} %pad_maximum_fusion.17), channel_id=1, source_target_pairs={{0,1},{1,2},{2,3},{3,4},{4,5},{5,6},{6,7},{7,8},{8,9},{9,10},{10,1... | collective-permute-start | bytes 135176 | tf_op jit(solution)/shard_map/ppermute | solution.py:148
  80.4 15.4 %collective-permute-start.3 = (f32[8,11,2,128]{3,2,1,0:T(2,128)}, f32[8,11,2,128]{3,2,1,0:T(2,128)}, u32[]{:S(2)}, u32[]{:S(2)}) collective-permute-start(f32[8,11,2,128]{3,2,1,0:T(2,128)} %pad_maximum_fusion.14), channel_id=1, source_target_pairs={{1,0},{2,1},{3,2},{4,3},{5,4},{6,5},{7,6},{8,7},{9,8},{10,9},{11,1... | collective-permute-start | bytes 270344 | tf_op jit(solution)/shard_map/ppermute | solution.py:151
  93.6 4.1 %copy-start.4 = (f32[16,99,128]{2,0,1:T(8,128)S(1)}, f32[16,99,128]{2,0,1:T(8,128)}, u32[]{:S(2)}) copy-start(f32[16,99,128]{2,0,1:T(8,128)} %copy.38) | copy-start | bytes 2433028
  93.6 6.4 %copy-start.5 = (f32[8]{0:T(128)S(1)}, f32[8]{0:T(128)}, u32[]{:S(2)}) copy-start(f32[8]{0:T(128)} %constant.115.clone) | copy-start | bytes 100
  93.6 6.3 %collective-permute-start.6 = (f32[5,99,128]{2,0,1:T(8,128)S(1)}, f32[5,99,128]{2,0,1:T(8,128)S(1)}, u32[]{:S(2)}, u32[]{:S(2)}) collective-permute-start(f32[5,99,128]{2,0,1:T(8,128)S(1)} %pad_maximum_fusion.7), channel_id=1, source_target_pairs={{16,8},{17,9},{18,10},{19,11},{20,12},{21,13},{22,14},{23,15},{24,... | collective-permute-start | bytes 760328 | tf_op jit(solution)/shard_map/ppermute | solution.py:215
  95.1 4.9 %collective-permute-start.5 = (f32[5,99,128]{2,0,1:T(8,128)S(1)}, f32[5,99,128]{2,0,1:T(8,128)S(1)}, u32[]{:S(2)}, u32[]{:S(2)}) collective-permute-start(f32[5,99,128]{2,0,1:T(8,128)S(1)} %pad_maximum_fusion.7), channel_id=1, source_target_pairs={{0,8},{1,9},{2,10},{3,11},{4,12},{5,13},{6,14},{7,15},{8,0},{9,1},... | collective-permute-start | bytes 760328 | tf_op jit(solution)/shard_map/ppermute | solution.py:210
  97.7 3.2 %collective-permute-start.7 = (f32[16,99,128]{2,0,1:T(8,128)S(1)}, f32[16,99,128]{2,0,1:T(8,128)S(1)}, u32[]{:S(2)}, u32[]{:S(2)}) collective-permute-start(f32[16,99,128]{2,0,1:T(8,128)S(1)} %copy-done.4), channel_id=1, source_target_pairs={{16,0},{224,240},{17,1},{225,241},{18,2},{226,242},{19,3},{227,243... | collective-permute-start | bytes 2433032 | tf_op jit(solution)/shard_map/ppermute | solution.py:202

commit v4 on v3

--- a/solution.py
+++ b/solution.py
@@ -161,7 +161,7 @@
 
     def cap_of(fields):
         rows = jnp.where(at_north, fields[:, :CAP], fields[:, ct - CAP :])
-        return rows.reshape(half, npc, nr)
+        return jnp.swapaxes(rows, 0, 1).reshape(half, npc, nr)
 
     pairs_out = [(0, 1), (theta_count - 1, theta_count - 2)]
     pairs_in = [(1, 0), (theta_count - 2, theta_count - 1)]
@@ -179,8 +179,8 @@
 
     pole_pick = jnp.where(north_side, 0, 1).astype(jnp.int32)
     level_row = lax.dynamic_index_in_dim(levels, pole_pick, 0, keepdims=False)
-    slot_ids = jnp.where(helper, half, 0) + p * per_device + jnp.arange(per_device, dtype=jnp.int32)
-    row_ids = slot_ids % CAP
+    slot_ids = p * per_device + jnp.arange(per_device, dtype=jnp.int32)
+    row_ids = slot_ids // (channels // 2)
     slot_levels = jnp.sum(
         jnp.where(
             row_ids[:, None] == jnp.arange(CAP, dtype=jnp.int32)[None, :], level_row[None, :], 0
@@ -200,11 +200,13 @@
     mine = lax.all_to_all(out, "phi", split_axis=0, concat_axis=0, tiled=True)
 
     from_helper = lax.ppermute(mine, "theta", pairs_in)
-    cap_rows = jnp.concatenate([mine, from_helper], axis=0).reshape(channels, CAP, npc + 3, nr)
     per_half = channels // 2
-    first_rows = mine[0::CAP]
-    last_rows = mine[CAP - 1 :: CAP]
-    spare = mine[(6 - per_half) * CAP + CAP - 2 : (6 - per_half) * CAP + CAP - 1]
+    cap_rows = jnp.concatenate([mine, from_helper], axis=0).reshape(2, CAP, per_half, npc + 3, nr)
+    cap_rows = jnp.transpose(cap_rows, (0, 2, 1, 3, 4)).reshape(channels, CAP, npc + 3, nr)
+    first_rows = mine[:per_half]
+    last_rows = mine[(CAP - 1) * per_half :]
+    spare_at = (CAP - 2) * per_half + 6 - per_half
+    spare = mine[spare_at : spare_at + 1]
     ghost_send = jnp.concatenate([jnp.where(north_side, first_rows, last_rows), spare], axis=0)
     turn = phi_count // 2
     pole_ghost = lax.ppermute(

time: 114 us -> 111 us (0.974)
  local copies, waits for them, and re-layouts: 21.1 us -> 17.2 us
  other arithmetic: 28.1 us -> 30.1 us
    slice x5 -> x2, local copies, waits for them, and re-layouts: 8.29 us -> 0.87 us  [local(): spare = mine[spare_at:spare_at + 1]]
    dynamic_update_slice x1, other arithmetic: 0.56 us -> 3.56 us  [local(): extended = lax.dynamic_update_slice_in_dim(early, block, offset, axis=1)]
    squeeze x1, local copies, waits for them, and re-layouts: 0.31 us -> 2.6 us  [advance(): x[5][inner]]
    unnamed x17 -> x20, local copies, waits for them, and re-layouts: 2.58 us -> 3.72 us
  transfers between devices with their start and end apart: 10 -> 10, of which waited for: 5 -> 5; matrix products, arithmetic and copies ran while one was open for 30% -> 24% of each run, Pallas kernels for 0% -> 0%
where the time goes in v4:
time: 111 us; the launch traced here: 110 us
  starting transfers between devices  31.2 us (28%)
  other arithmetic  30.1 us (27%)
  waiting for transfers between devices  23.3 us (21%)
  local copies, waits for them, and re-layouts  17.2 us (15%)
  matrix products  6.74 us (6%)
  between operations  1.85 us (2%)
    ppermute x1, waiting for transfers between devices, local(): lax.ppermute(up_send, 'theta', [(i + 1, i) for i in range(theta_count - 1)])  11.9 us
    all_to_all x1, starting transfers between devices, local(): cycle = lax.all_to_all(work, 'phi', split_axis=0, concat_axis=1, tiled=True)  7.97 us
    all_to_all x1, waiting for transfers between devices, local(): cycle = lax.all_to_all(work, 'phi', split_axis=0, concat_axis=1, tiled=True)  6.65 us
    all_to_all x1, starting transfers between devices, local(): mine = lax.all_to_all(out, 'phi', split_axis=0, concat_axis=0, tiled=True)  6.4 us
    cos x1, other arithmetic, fourier_rows(): return jnp.concatenate([jnp.cos(angle), jnp.sin(angle)], axis=-1)  5.26 us
    sin x1, other arithmetic, fourier_rows(): return jnp.concatenate([jnp.cos(angle), jnp.sin(angle)], axis=-1)  4.36 us
    dot_general x1, matrix products, local(): jnp.einsum('smr,mn->snr', cycle, analysis, precision=lax.Precision.HIGHEST)  4.34 us
    ppermute x1, starting transfers between devices, local(): lax.ppermute(combined[:, ct - 1], 'theta', [(i, i + 1) for i in range(the...  4.3 us
  transfers between devices with their start and end apart: 10, of which 5 were waited for; matrix products, arithmetic and copies ran while one was open for 24% of the time, Pallas kernels for 0%

profile of v4, /device:TPU:1, one launch (start us, length us, event | category | flops | bytes accessed | tf_op | source)
XLA Modules:
  0.0 110.4 jit_solution(5502076893371346412)
XLA Ops:
  1.8 1.3 %fusion.26 = f32[4,4,96,128]{3,2,0,1:T(8,128)S(1)} fusion(f32[1,8,96,128]{3,2,0,1:T(8,128)S(1)} %slice_bitcast_fusion.11, pred[]{:T(512)S(6)} %eq.61, f32[3,8,96,128]{3,2,1,0:T(8,128)} %param.7), kind=kLoop, calls=%fused_computation.34 | loop fusion | flops 589824 | bytes 2359297 | tf_op jit(solution)/shard_map/jit(_where)/select_n | solution.py:163
  6.0 3.4 %collective-permute-done.4 = f32[16,96,128]{2,1,0:T(8,128)S(1)} collective-permute-done((f32[16,96,128]{2,1,0:T(8,128)S(1)}, f32[16,96,128]{2,1,0:T(8,128)S(1)}, u32[]{:S(2)}, u32[]{:S(2)}) %collective-permute-start.4) | collective-permute-done | bytes 786464 | tf_op jit(solution)/shard_map/ppermute | solution.py:168
  10.4 8.0 %all-to-all-start = ((f32[16,96,128]{2,1,0:T(8,128)}), f32[16,96,128]{2,1,0:T(8,128)}, u32[]{:S(2)}, u32[]{:S(2)}) async-start(f32[16,96,128]{2,1,0:T(8,128)} %bitcast_select_fusion), calls=%async_computation | async-start | bytes 1572864 | tf_op jit(solution)/shard_map/all_to_all | solution.py:171
  19.6 1.4 %constant_dynamic-update-slice_fusion.1 = f32[8,8,96,128]{3,2,1,0:T(8,128)S(1)} fusion(f32[8,8,96,128]{3,2,1,0:T(8,128)S(1)} %constant_dynamic-update-slice_fusion.2, f32[3,8,96,128]{3,2,1,0:T(8,128)} %param.6), kind=kLoop, calls=%fused_computation.157 | loop fusion | bytes 2359296
  21.9 5.3 %fusion.20 = (f32[16,99,128]{2,1,0:T(8,128)}, f32[16,99,128]{2,1,0:T(8,128)}) fusion(s32[16,99]{1,0:T(8,128)S(1)} %add_select_fusion.2), kind=kLoop, calls=%fused_computation.28 | loop fusion | flops 1824768 | bytes 1628352 | tf_op jit(solution)/shard_map/cos | solution.py:110
  27.1 4.4 %fusion.29 = (f32[1536,128]{1,0:T(8,128)}, f32[1536,128]{1,0:T(8,128)}) fusion(), kind=kLoop, calls=%fused_computation.43 | loop fusion | flops 1769472 | bytes 1572864 | tf_op jit(solution)/shard_map/sin | solution.py:110
  31.5 6.7 %all-to-all-done = f32[16,96,128]{2,1,0:T(8,128)} async-done(((f32[16,96,128]{2,1,0:T(8,128)}), f32[16,96,128]{2,1,0:T(8,128)}, u32[]{:S(2)}, u32[]{:S(2)}) %all-to-all-start) | async-done | bytes 786464 | tf_op jit(solution)/shard_map/all_to_all | solution.py:171
  38.1 4.3 %fusion.12 = f32[256,128,1]{1,0,2:T(8,128)S(1)} fusion(f32[1536,128]{1,0:T(8,128)} %bitcast.11, f32[1536,128]{1,0:T(8,128)} %get-tuple-element.62, f32[1536,128]{1,0:T(8,128)} %get-tuple-element.63, f32[256]{0:T(256)S(1)} %compare_select_fusion.1), kind=kOutput, calls=%fused_computation.21 | convolution fusion | flops 604405760 | bytes 2491392 | tf_op jit(solution)/shard_map/smr,mn->snr/dot_general | solution.py:196
  42.5 2.4 %fusion.1 = f32[16,99,128]{2,1,0:T(8,128)} fusion(f32[256,128,1]{1,0,2:T(8,128)S(1)} %fusion.12, f32[16,99,128]{2,1,0:T(8,128)S(1)} %copy-done.4, f32[16,99,128]{2,1,0:T(8,128)S(1)} %copy-done.3), kind=kOutput, calls=%fused_computation.4 | convolution fusion | flops 623259648 | bytes 2564096 | tf_op jit(solution)/shard_map/snr,kjn->ksjr/dot_general | solution.py:198
  44.9 6.4 %all-to-all-start.1 = ((f32[16,99,128]{2,1,0:T(8,128)}), f32[16,99,128]{2,1,0:T(8,128)}, u32[]{:S(2)}, u32[]{:S(2)}) async-start(f32[16,99,128]{2,1,0:T(8,128)} %fusion.1), calls=%async_computation.1 | async-start | bytes 1703936 | tf_op jit(solution)/shard_map/all_to_all | solution.py:200
  51.3 1.4 %constant_dynamic-update-slice_fusion = f32[8,8,96,128]{3,2,1,0:T(8,128)S(1)} fusion(f32[8,8,96,128]{3,2,1,0:T(8,128)S(1)} %constant_dynamic-update-slice_fusion.1, f32[3,8,96,128]{3,2,1,0:T(8,128)} %param.7), kind=kLoop, calls=%fused_computation.156 | loop fusion | bytes 2359296 | tf_op jit(solution)/shard_map/concatenate | solution.py:114
  54.3 2.8 %collective-permute-start.1 = (f32[9,96,128]{2,1,0:T(8,128)}, f32[9,96,128]{2,1,0:T(8,128)}, u32[]{:S(2)}, u32[]{:S(2)}) collective-permute-start(f32[9,96,128]{2,1,0:T(8,128)} %pad_maximum_fusion.6), channel_id=1, source_target_pairs={{16,0},{32,16},{48,32},{64,48},{80,64},{96,80},{112,96},{128,112},... | collective-permute-start | bytes 1327112 | tf_op jit(solution)/shard_map/ppermute | solution.py:138
  57.0 4.3 %collective-permute-start = (f32[8,96,128]{2,1,0:T(8,128)}, f32[8,96,128]{2,1,0:T(8,128)}, u32[]{:S(2)}, u32[]{:S(2)}) collective-permute-start(f32[8,96,128]{2,1,0:T(8,128)} %get-tuple-element.14), channel_id=1, source_target_pairs={{0,16},{16,32},{32,48},{48,64},{64,80},{80,96},{96,112},{112,128},... | collective-permute-start | bytes 1179656 | tf_op jit(solution)/shard_map/ppermute | solution.py:134
  61.4 11.9 %collective-permute-done.1 = f32[9,96,128]{2,1,0:T(8,128)} collective-permute-done((f32[9,96,128]{2,1,0:T(8,128)}, f32[9,96,128]{2,1,0:T(8,128)}, u32[]{:S(2)}, u32[]{:S(2)}) %collective-permute-start.1) | collective-permute-done | bytes 442400 | tf_op jit(solution)/shard_map/ppermute | solution.py:138
  75.2 1.4 %pad_maximum_fusion.17 = f32[8,11,1,128]{3,2,1,0:T(1,128)} fusion(f32[8,1,96,128]{3,2,1,0:T(8,128)S(1)} %broadcast_in_dim_broadcast_in_dim.4, f32[8,1,96,128]{3,2,1,0:T(8,128)S(1)} %slice_bitcast_fusion.8, f32[8,8,96,128]{3,2,1,0:T(8,128)S(1)} %constant_dynamic-update-slice_fusion, f32[8,1,96,128]{3,2,1,0:T(8,128)} %bitcast.2), kind=kLoop, calls=%fused_computation.154 | loop fusion | flops 33792 | bytes 4370432 | tf_op jit(solution)/shard_map/slice | solution.py:149
  76.7 2.3 %collective-permute-start.2 = (f32[8,11,1,128]{3,2,1,0:T(1,128)}, f32[8,11,1,128]{3,2,1,0:T(1,128)}, u32[]{:S(2)}, u32[]{:S(2)}) collective-permute-start(f32[8,11,1,128]{3,2,1,0:T(1,128)} %pad_maximum_fusion.17), channel_id=1, source_target_pairs={{0,1},{1,2},{2,3},{3,4},{4,5},{5,6},{6,7},{7,8},{8,9},{9,10},{10,1... | collective-permute-start | bytes 135176 | tf_op jit(solution)/shard_map/ppermute | solution.py:148
  79.0 1.4 %pad_maximum_fusion.14 = f32[8,11,2,128]{3,2,1,0:T(2,128)} fusion(f32[8,1,96,128]{3,2,1,0:T(8,128)S(1)} %broadcast_in_dim_broadcast_in_dim.4, f32[8,1,96,128]{3,2,1,0:T(8,128)S(1)} %slice_bitcast_fusion.8, f32[8,8,96,128]{3,2,1,0:T(8,128)S(1)} %constant_dynamic-update-slice_fusion, f32[8,1,96,128]{3,2,1,0:T(8,128)} %bitcast.2), kind=kLoop, calls=%fused_computation.147 | loop fusion | flops 67584 | bytes 4415488 | tf_op jit(solution)/shard_map/concatenate | solution.py:139
  80.4 2.6 %collective-permute-start.3 = (f32[8,11,2,128]{3,2,1,0:T(2,128)}, f32[8,11,2,128]{3,2,1,0:T(2,128)}, u32[]{:S(2)}, u32[]{:S(2)}) collective-permute-start(f32[8,11,2,128]{3,2,1,0:T(2,128)} %pad_maximum_fusion.14), channel_id=1, source_target_pairs={{1,0},{2,1},{3,2},{4,3},{5,4},{6,5},{7,6},{8,7},{9,8},{10,9},{11,1... | collective-permute-start | bytes 270344 | tf_op jit(solution)/shard_map/ppermute | solution.py:151
  83.0 1.4 %copy.63 = f32[16,99,128]{2,0,1:T(8,128)S(1)} copy(f32[16,99,128]{2,1,0:T(8,128)} %all-to-all-done.1) | data formatting | bytes 1622016 | tf_op jit(solution)/shard_map/all_to_all | solution.py:200
  85.4 1.3 %collective-permute-start.6 = (f32[5,99,128]{2,0,1:T(8,128)S(1)}, f32[5,99,128]{2,0,1:T(8,128)S(1)}, u32[]{:S(2)}, u32[]{:S(2)}) collective-permute-start(f32[5,99,128]{2,0,1:T(8,128)S(1)} %pad_maximum_fusion.7), channel_id=1, source_target_pairs={{16,8},{17,9},{18,10},{19,11},{20,12},{21,13},{22,14},{23,15},{24,... | collective-permute-start | bytes 760328 | tf_op jit(solution)/shard_map/ppermute | solution.py:217
  87.5 1.8 %pad_maximum_fusion = f32[8,11,99,128]{3,2,1,0:T(8,128)S(1)} fusion(f32[8,11,2,128]{3,2,1,0:T(2,128)} %collective-permute-done.3, f32[8,1,96,128]{3,2,1,0:T(8,128)S(1)} %copy-done.2, f32[8,1,96,128]{3,2,1,0:T(8,128)S(1)} %slice_bitcast_fusion.8, f32[8,8,96,128]{3,2,1,0:T(8,128)S(1)} %constant_dynamic-update-slice_fusion, f32[8,1,96,128]{3,2,1,0:T(8,128)} %bitcast.2, ...), kind=kLoop, calls=%fused_computation | loop fusion | flops 5575680 | bytes 8921088 | tf_op jit(solution)/shard_map/concatenate | solution.py:154
  89.3 1.5 %collective-permute-start.7 = (f32[16,99,128]{2,0,1:T(8,128)S(1)}, f32[16,99,128]{2,0,1:T(8,128)S(1)}, u32[]{:S(2)}, u32[]{:S(2)}) collective-permute-start(f32[16,99,128]{2,0,1:T(8,128)S(1)} %copy.63), channel_id=1, source_target_pairs={{16,0},{224,240},{17,1},{225,241},{18,2},{226,242},{19,3},{227,243... | collective-permute-start | bytes 2433032 | tf_op jit(solution)/shard_map/ppermute | solution.py:202
  95.1 3.6 %fusion = f32[8,11,99,128]{3,2,1,0:T(8,128)} fusion(f32[8,11,99,128]{3,2,1,0:T(8,128)} %copy-done, s32[]{:T(128)S(6)} %select_n.154, f32[8,1,99,128]{3,2,1,0:T(8,128)S(1)} %slice-done, f32[8,4,99,128]{3,2,1,0:T(8,128)S(1)} %bitcast.70, f32[8,1,99,128]{3,2,1,0:T(8,128)S(1)} %copy.69, f32[8,1,99,128]{3,2,1,0:T(8,128)S(1)} %broadcast_in_dim_broadcast_in_dim.5, ...), kind=kLoop, calls=%fused_computation.2 | loop fusion | flops 3649536 | bytes 7950342 | tf_op jit(solution)/shard_map/dynamic_update_slice | solution.py:245
  98.7 2.6 %slice_bitcast_fusion.2 = (f32[11,99,128]{2,1,0:T(8,128)S(1)}, f32[11,99,128]{2,1,0:T(8,128)S(1)}, f32[11,99,128]{2,1,0:T(8,128)S(1)}, f32[11,99,128]{2,1,0:T(8,...) fusion(f32[8,11,99,128]{3,2,1,0:T(8,128)} %fusion), kind=kLoop, calls=%fused_computation.48 | loop fusion | bytes 8921088 | tf_op jit(solution)/shard_map/squeeze | solution.py:94
  (89 shorter events, 24.7 us)
Async XLA Ops:
  0.6 5.2 %slice-start.1 = ((f32[3,8,96,128]{3,2,1,0:T(8,128)}), f32[2,8,96,128]{3,2,1,0:T(8,128)S(1)}, s32[]{:S(2)}) async-start(f32[3,8,96,128]{3,2,1,0:T(8,128)} %param.6), calls=%async_computation.3 | async-start | bytes 1572864 | tf_op jit(solution)/shard_map/slice | solution.py:159
  0.6 3.8 %copy-start.7 = (s32[2,4]{1,0:T(2,128)S(1)}, s32[2,4]{1,0:T(2,128)}, u32[]{:S(2)}) copy-start(s32[2,4]{1,0:T(2,128)} %param.8) | copy-start | bytes 100
  0.7 5.1 %copy-start.5 = (f32[2,8,96,128]{3,2,1,0:T(8,128)S(1)}, f32[2,8,96,128]{3,2,1,0:T(8,128)}, u32[]{:S(2)}) copy-start(f32[2,8,96,128]{3,2,1,0:T(8,128)} %param.5) | copy-start | bytes 2359300
  3.2 6.3 %collective-permute-start.4 = (f32[16,96,128]{2,1,0:T(8,128)S(1)}, f32[16,96,128]{2,1,0:T(8,128)S(1)}, u32[]{:S(2)}, u32[]{:S(2)}) collective-permute-start(f32[16,96,128]{2,1,0:T(8,128)S(1)} %bitcast.72), channel_id=1, source_target_pairs={{0,16},{240,224},{1,17},{241,225},{2,18},{242,226},{3,19},{243,227... | collective-permute-start | bytes 2359304 | tf_op jit(solution)/shard_map/ppermute | solution.py:168
  10.4 27.7 %all-to-all-start = ((f32[16,96,128]{2,1,0:T(8,128)}), f32[16,96,128]{2,1,0:T(8,128)}, u32[]{:S(2)}, u32[]{:S(2)}) async-start(f32[16,96,128]{2,1,0:T(8,128)} %bitcast_select_fusion), calls=%async_computation | async-start | bytes 1572864 | tf_op jit(solution)/shard_map/all_to_all | solution.py:171
  38.1 4.4 %copy-start.3 = (f32[16,99,128]{2,1,0:T(8,128)S(1)}, f32[16,99,128]{2,1,0:T(8,128)}, u32[]{:S(2)}) copy-start(f32[16,99,128]{2,1,0:T(8,128)} %get-tuple-element.58) | copy-start | bytes 2433028
  38.1 4.4 %copy-start.4 = (f32[16,99,128]{2,1,0:T(8,128)S(1)}, f32[16,99,128]{2,1,0:T(8,128)}, u32[]{:S(2)}) copy-start(f32[16,99,128]{2,1,0:T(8,128)} %get-tuple-element.59) | copy-start | bytes 2433028
  44.9 38.1 %all-to-all-start.1 = ((f32[16,99,128]{2,1,0:T(8,128)}), f32[16,99,128]{2,1,0:T(8,128)}, u32[]{:S(2)}, u32[]{:S(2)}) async-start(f32[16,99,128]{2,1,0:T(8,128)} %fusion.1), calls=%async_computation.1 | async-start | bytes 1703936 | tf_op jit(solution)/shard_map/all_to_all | solution.py:200
  54.3 19.1 %collective-permute-start.1 = (f32[9,96,128]{2,1,0:T(8,128)}, f32[9,96,128]{2,1,0:T(8,128)}, u32[]{:S(2)}, u32[]{:S(2)}) collective-permute-start(f32[9,96,128]{2,1,0:T(8,128)} %pad_maximum_fusion.6), channel_id=1, source_target_pairs={{16,0},{32,16},{48,32},{64,48},{80,64},{96,80},{112,96},{128,112},... | collective-permute-start | bytes 1327112 | tf_op jit(solution)/shard_map/ppermute | solution.py:138
  57.0 18.1 %collective-permute-start = (f32[8,96,128]{2,1,0:T(8,128)}, f32[8,96,128]{2,1,0:T(8,128)}, u32[]{:S(2)}, u32[]{:S(2)}) collective-permute-start(f32[8,96,128]{2,1,0:T(8,128)} %get-tuple-element.14), channel_id=1, source_target_pairs={{0,16},{16,32},{32,48},{48,64},{64,80},{80,96},{96,112},{112,128},... | collective-permute-start | bytes 1179656 | tf_op jit(solution)/shard_map/ppermute | solution.py:134
  75.2 5.2 %copy-start.1 = (f32[8,1,96,128]{3,2,1,0:T(8,128)}, f32[8,1,96,128]{3,2,1,0:T(8,128)S(1)}, u32[]{:S(2)}) copy-start(f32[8,1,96,128]{3,2,1,0:T(8,128)S(1)} %broadcast_in_dim_broadcast_in_dim.4) | copy-start | bytes 1179652
  76.7 10.8 %collective-permute-start.2 = (f32[8,11,1,128]{3,2,1,0:T(1,128)}, f32[8,11,1,128]{3,2,1,0:T(1,128)}, u32[]{:S(2)}, u32[]{:S(2)}) collective-permute-start(f32[8,11,1,128]{3,2,1,0:T(1,128)} %pad_maximum_fusion.17), channel_id=1, source_target_pairs={{0,1},{1,2},{2,3},{3,4},{4,5},{5,6},{6,7},{7,8},{8,9},{9,10},{10,1... | collective-permute-start | bytes 135176 | tf_op jit(solution)/shard_map/ppermute | solution.py:148
  80.4 7.1 %collective-permute-start.3 = (f32[8,11,2,128]{3,2,1,0:T(2,128)}, f32[8,11,2,128]{3,2,1,0:T(2,128)}, u32[]{:S(2)}, u32[]{:S(2)}) collective-permute-start(f32[8,11,2,128]{3,2,1,0:T(2,128)} %pad_maximum_fusion.14), channel_id=1, source_target_pairs={{1,0},{2,1},{3,2},{4,3},{5,4},{6,5},{7,6},{8,7},{9,8},{10,9},{11,1... | collective-permute-start | bytes 270344 | tf_op jit(solution)/shard_map/ppermute | solution.py:151
  83.0 4.5 %copy-start.2 = (f32[8,1,96,128]{3,2,1,0:T(8,128)S(1)}, f32[8,1,96,128]{3,2,1,0:T(8,128)}, u32[]{:S(2)}) copy-start(f32[8,1,96,128]{3,2,1,0:T(8,128)} %copy-done.1) | copy-start | bytes 1179652
  85.4 6.2 %copy-start.6 = (f32[8]{0:T(128)S(1)}, f32[8]{0:T(128)}, u32[]{:S(2)}) copy-start(f32[8]{0:T(128)} %constant.116.clone) | copy-start | bytes 100
  85.4 6.1 %collective-permute-start.6 = (f32[5,99,128]{2,0,1:T(8,128)S(1)}, f32[5,99,128]{2,0,1:T(8,128)S(1)}, u32[]{:S(2)}, u32[]{:S(2)}) collective-permute-start(f32[5,99,128]{2,0,1:T(8,128)S(1)} %pad_maximum_fusion.7), channel_id=1, source_target_pairs={{16,8},{17,9},{18,10},{19,11},{20,12},{21,13},{22,14},{23,15},{24,... | collective-permute-start | bytes 760328 | tf_op jit(solution)/shard_map/ppermute | solution.py:217
  86.8 4.9 %collective-permute-start.5 = (f32[5,99,128]{2,0,1:T(8,128)S(1)}, f32[5,99,128]{2,0,1:T(8,128)S(1)}, u32[]{:S(2)}, u32[]{:S(2)}) collective-permute-start(f32[5,99,128]{2,0,1:T(8,128)S(1)} %pad_maximum_fusion.7), channel_id=1, source_target_pairs={{0,8},{1,9},{2,10},{3,11},{4,12},{5,13},{6,14},{7,15},{8,0},{9,1},... | collective-permute-start | bytes 760328 | tf_op jit(solution)/shard_map/ppermute | solution.py:212
  89.3 3.5 %copy-start = (f32[8,11,99,128]{3,2,1,0:T(8,128)}, f32[8,11,99,128]{3,2,1,0:T(8,128)S(1)}, u32[]{:S(2)}) copy-start(f32[8,11,99,128]{3,2,1,0:T(8,128)S(1)} %pad_maximum_fusion) | copy-start | bytes 13381636
  89.3 3.2 %collective-permute-start.7 = (f32[16,99,128]{2,0,1:T(8,128)S(1)}, f32[16,99,128]{2,0,1:T(8,128)S(1)}, u32[]{:S(2)}, u32[]{:S(2)}) collective-permute-start(f32[16,99,128]{2,0,1:T(8,128)S(1)} %copy.63), channel_id=1, source_target_pairs={{16,0},{224,240},{17,1},{225,241},{18,2},{226,242},{19,3},{227,243... | collective-permute-start | bytes 2433032 | tf_op jit(solution)/shard_map/ppermute | solution.py:202
  94.1 1.0 slice-start

commit v5 on v4

--- a/solution.py
+++ b/solution.py
@@ -239,11 +239,30 @@
     )
     offset = jnp.where(at_north, 0, ct - CAP + 1)
     kept_block = lax.dynamic_slice_in_dim(early, offset, CAP + 2, axis=1)
-    block = jnp.where(
-        at_north, north_block, jnp.where(at_south, south_block, kept_block)
-    )
+    block = jnp.where(at_north, north_block, jnp.where(at_south, south_block, kept_block))
     extended = lax.dynamic_update_slice_in_dim(early, block, offset, axis=1)
-    return advance(extended)
+
+    cap_start = jnp.where(at_north, 1, ct - CAP + 1)
+    kept_cap = lax.dynamic_slice_in_dim(early, cap_start, CAP, axis=1)
+    cap_block = jnp.where(at_north | at_south, cap_rows, kept_cap)
+    with_caps = lax.dynamic_update_slice_in_dim(early, cap_block, cap_start, axis=1)
+
+    near_rows = 2
+    far_rows = ct - CAP - near_rows
+    mid_rows = CAP
+
+    def rows_from(x, first, count):
+        return advance(lax.dynamic_slice_in_dim(x, first, count + 3, axis=1))
+
+    far = rows_from(early, jnp.where(at_north, ct - far_rows, 0), far_rows)
+    mid = rows_from(with_caps, jnp.where(at_north, near_rows, far_rows), mid_rows)
+    near = rows_from(extended, jnp.where(at_north, 0, ct - near_rows), near_rows)
+    outs = []
+    for a, b, c in zip(far, mid, near):
+        north_order = jnp.concatenate([c, b, a], axis=1)
+        other_order = jnp.concatenate([a, b, c], axis=1)
+        outs.append(jnp.where(at_north, north_order, other_order))
+    return tuple(outs)
 
 
 def solution(mesh):

time: 111 us -> 143 us (1.29)
  waiting for transfers between devices: 23.3 us -> 32.8 us
  local copies, waits for them, and re-layouts: 17.2 us -> 26.6 us
  other arithmetic: 30.1 us -> 36.2 us
  starting transfers between devices: 31.2 us -> 37 us
    all_to_all x1, waiting for transfers between devices: 0.01 us -> 14.5 us  [local(): mine = lax.all_to_all(out, 'phi', split_axis=0, concat_axis=0, tiled=True)]
    ppermute x1, waiting for transfers between devices: 11.9 us -> 0.01 us  [local(): lax.ppermute(up_send, 'theta', [(i + 1, i) for i in range(theta_count - 1)])]
    slice x12 -> x36, local copies, waits for them, and re-layouts: 2.26 us -> 10.9 us  [up_r(): return jnp.concatenate([a[..., 1:], a[..., -1:]], axis=-1)]
    all_to_all x1, waiting for transfers between devices: 6.65 us -> 14.5 us  [local(): cycle = lax.all_to_all(work, 'phi', split_axis=0, concat_axis=1, tiled=True)]
    unnamed x20 -> x93, local copies, waits for them, and re-layouts: 3.72 us -> 10.6 us
    ppermute x1, starting transfers between devices: 1.32 us -> 5.3 us  [local(): lax.ppermute(ghost_send, both, [(h * phi_count + b, a * phi_count + (b +...]
    ppermute x1, waiting for transfers between devices: 3.41 us -> 0.01 us  [local(): handed = lax.ppermute(cap_of(second_half), 'theta', pairs_out)]
    ppermute x1, starting transfers between devices: 2.76 us -> 6.03 us  [local(): lax.ppermute(up_send, 'theta', [(i + 1, i) for i in range(theta_count - 1)])]
  transfers between devices with their start and end apart: 10 -> 10, of which waited for: 5 -> 4; matrix products, arithmetic and copies ran while one was open for 24% -> 27% of each run, Pallas kernels for 0% -> 0%
where the time goes in v5:
time: 143 us; the launch traced here: 142 us
  starting transfers between devices  37 us (26%)
  other arithmetic  36.2 us (25%)
  waiting for transfers between devices  32.8 us (23%)
  local copies, waits for them, and re-layouts  26.6 us (19%)
  matrix products  6.69 us (5%)
  between operations  2.35 us (2%)
    all_to_all x1, waiting for transfers between devices, local(): cycle = lax.all_to_all(work, 'phi', split_axis=0, concat_axis=1, tiled=True)  14.5 us
    all_to_all x1, waiting for transfers between devices, local(): mine = lax.all_to_all(out, 'phi', split_axis=0, concat_axis=0, tiled=True)  14.5 us
    slice x36, local copies, waits for them, and re-layouts, up_r(): return jnp.concatenate([a[..., 1:], a[..., -1:]], axis=-1)  10.9 us
    unnamed x93, local copies, waits for them, and re-layouts  10.6 us
    all_to_all x1, starting transfers between devices, local(): mine = lax.all_to_all(out, 'phi', split_axis=0, concat_axis=0, tiled=True)  6.31 us
    all_to_all x1, starting transfers between devices, local(): cycle = lax.all_to_all(work, 'phi', split_axis=0, concat_axis=1, tiled=True)  6.13 us
    ppermute x1, starting transfers between devices, local(): lax.ppermute(up_send, 'theta', [(i + 1, i) for i in range(theta_count - 1)])  6.03 us
    cos x1, other arithmetic, fourier_rows(): return jnp.concatenate([jnp.cos(angle), jnp.sin(angle)], axis=-1)  5.31 us
  transfers between devices with their start and end apart: 10, of which 4 were waited for; matrix products, arithmetic and copies ran while one was open for 27% of the time, Pallas kernels for 0%

profile of v5, /device:TPU:1, one launch (start us, length us, event | category | flops | bytes accessed | tf_op | source)
XLA Modules:
  0.0 141.6 jit_solution(7729365635775220562)
XLA Ops:
  1.7 2.4 %fusion.26 = f32[4,4,96,128]{3,2,0,1:T(8,128)} fusion(f32[1,8,96,128]{3,2,0,1:T(8,128)S(1)} %slice_bitcast_fusion.3, pred[]{:T(512)S(6)} %eq.87, f32[3,8,96,128]{3,2,1,0:T(8,128)} %param.7), kind=kLoop, calls=%fused_computation.36 | loop fusion | flops 589824 | bytes 2359297 | tf_op jit(solution)/shard_map/jit(_where)/select_n | solution.py:163
  9.2 6.0 %collective-permute-start.1 = (f32[9,96,128]{2,1,0:T(8,128)}, f32[9,96,128]{2,1,0:T(8,128)}, u32[]{:S(2)}, u32[]{:S(2)}) collective-permute-start(f32[9,96,128]{2,1,0:T(8,128)} %pad_maximum_fusion.6), channel_id=1, source_target_pairs={{16,0},{32,16},{48,32},{64,48},{80,64},{96,80},{112,96},{128,112},... | collective-permute-start | bytes 1327112 | tf_op jit(solution)/shard_map/ppermute | solution.py:138
  15.2 2.2 %collective-permute-start = (f32[8,96,128]{2,1,0:T(8,128)}, f32[8,96,128]{2,1,0:T(8,128)}, u32[]{:S(2)}, u32[]{:S(2)}) collective-permute-start(f32[8,96,128]{2,1,0:T(8,128)} %get-tuple-element.38), channel_id=1, source_target_pairs={{0,16},{16,32},{32,48},{48,64},{64,80},{80,96},{96,112},{112,128},... | collective-permute-start | bytes 1179656 | tf_op jit(solution)/shard_map/ppermute | solution.py:134
  17.4 4.4 %fusion.31 = (f32[1536,128]{1,0:T(8,128)}, f32[1536,128]{1,0:T(8,128)}) fusion(), kind=kLoop, calls=%fused_computation.48 | loop fusion | flops 1769472 | bytes 1572864 | tf_op jit(solution)/shard_map/sin | solution.py:110
  23.2 5.3 %fusion.20 = (f32[16,99,128]{2,1,0:T(8,128)}, f32[16,99,128]{2,1,0:T(8,128)}) fusion(s32[16,99]{1,0:T(8,128)S(1)} %add_select_fusion.2), kind=kLoop, calls=%fused_computation.30 | loop fusion | flops 1824768 | bytes 1628352 | tf_op jit(solution)/shard_map/cos | solution.py:110
  31.5 1.4 %pad_maximum_fusion.29 = f32[8,11,1,128]{3,2,1,0:T(1,128)} fusion(f32[8,1,96,128]{3,2,1,0:T(8,128)S(1)} %broadcast_in_dim_broadcast_in_dim.4, f32[8,1,96,128]{3,2,1,0:T(8,128)S(1)} %slice_bitcast_fusion, f32[8,8,96,128]{3,2,1,0:T(8,128)S(1)} %constant_dynamic-update-slice_fusion, f32[8,1,96,128]{3,2,1,0:T(8,128)} %bitcast.2), kind=kLoop, calls=%fused_computation.341 | loop fusion | flops 33792 | bytes 4370432 | tf_op jit(solution)/shard_map/slice | solution.py:149
  32.9 1.4 %pad_maximum_fusion.26 = f32[8,11,2,128]{3,2,1,0:T(2,128)} fusion(f32[8,1,96,128]{3,2,1,0:T(8,128)S(1)} %broadcast_in_dim_broadcast_in_dim.4, f32[8,1,96,128]{3,2,1,0:T(8,128)S(1)} %slice_bitcast_fusion, f32[8,8,96,128]{3,2,1,0:T(8,128)S(1)} %constant_dynamic-update-slice_fusion, f32[8,1,96,128]{3,2,1,0:T(8,128)} %bitcast.2), kind=kLoop, calls=%fused_computation.334 | loop fusion | flops 67584 | bytes 4415488 | tf_op jit(solution)/shard_map/concatenate | solution.py:139
  34.4 1.6 %collective-permute-start.2 = (f32[8,11,1,128]{3,2,1,0:T(1,128)}, f32[8,11,1,128]{3,2,1,0:T(1,128)}, u32[]{:S(2)}, u32[]{:S(2)}) collective-permute-start(f32[8,11,1,128]{3,2,1,0:T(1,128)} %pad_maximum_fusion.29), channel_id=1, source_target_pairs={{0,1},{1,2},{2,3},{3,4},{4,5},{5,6},{6,7},{7,8},{8,9},{9,10},{10,1... | collective-permute-start | bytes 135176 | tf_op jit(solution)/shard_map/ppermute | solution.py:148
  36.0 4.5 %collective-permute-start.3 = (f32[8,11,2,128]{3,2,1,0:T(2,128)}, f32[8,11,2,128]{3,2,1,0:T(2,128)}, u32[]{:S(2)}, u32[]{:S(2)}) collective-permute-start(f32[8,11,2,128]{3,2,1,0:T(2,128)} %pad_maximum_fusion.26), channel_id=1, source_target_pairs={{1,0},{2,1},{3,2},{4,3},{5,4},{6,5},{7,6},{8,7},{9,8},{10,9},{11,1... | collective-permute-start | bytes 270344 | tf_op jit(solution)/shard_map/ppermute | solution.py:151
  40.6 2.3 %collective-permute-done.2 = f32[8,11,1,128]{3,2,1,0:T(1,128)} collective-permute-done((f32[8,11,1,128]{3,2,1,0:T(1,128)}, f32[8,11,1,128]{3,2,1,0:T(1,128)}, u32[]{:S(2)}, u32[]{:S(2)}) %collective-permute-start.2) | collective-permute-done | bytes 45088 | tf_op jit(solution)/shard_map/ppermute | solution.py:148
  42.9 1.9 %pad_maximum_fusion = f32[8,11,99,128]{3,2,1,0:T(8,128)S(1)} fusion(f32[8,11,2,128]{3,2,1,0:T(2,128)} %collective-permute-done.3, f32[8,1,96,128]{3,2,1,0:T(8,128)} %copy-done.1, f32[8,1,96,128]{3,2,1,0:T(8,128)S(1)} %slice_bitcast_fusion, f32[8,8,96,128]{3,2,1,0:T(8,128)S(1)} %constant_dynamic-update-slice_fusion, f32[8,1,96,128]{3,2,1,0:T(8,128)} %bitcast.2, ...), kind=kLoop, calls=%fused_computation | loop fusion | flops 5575680 | bytes 8921088 | tf_op jit(solution)/shard_map/concatenate | solution.py:154
  44.8 2.2 %copy-done = f32[8,11,99,128]{3,2,1,0:T(8,128)} copy-done((f32[8,11,99,128]{3,2,1,0:T(8,128)}, f32[8,11,99,128]{3,2,1,0:T(8,128)S(1)}, u32[]{:S(2)}) %copy-start) | copy-done | bytes 4460568
  50.1 2.1 %bitcast_select_fusion = f32[16,96,128]{2,1,0:T(8,128)} fusion(f32[16,96,128]{2,1,0:T(8,128)} %collective-permute-done.4, f32[4,4,96,128]{3,2,0,1:T(8,128)S(1)} %copy-done.6, pred[]{:T(512)S(6)} %or.6), kind=kLoop, calls=%fused_computation.44 | loop fusion | flops 196608 | bytes 2359297 | tf_op jit(solution)/shard_map/jit(_where)/select_n | solution.py:169
  52.2 6.1 %all-to-all-start = ((f32[16,96,128]{2,1,0:T(8,128)}), f32[16,96,128]{2,1,0:T(8,128)}, u32[]{:S(2)}, u32[]{:S(2)}) async-start(f32[16,96,128]{2,1,0:T(8,128)} %bitcast_select_fusion), calls=%async_computation | async-start | bytes 1572864 | tf_op jit(solution)/shard_map/all_to_all | solution.py:171
  63.7 14.5 %all-to-all-done = f32[16,96,128]{2,1,0:T(8,128)} async-done(((f32[16,96,128]{2,1,0:T(8,128)}), f32[16,96,128]{2,1,0:T(8,128)}, u32[]{:S(2)}, u32[]{:S(2)}) %all-to-all-start) | async-done | bytes 786464 | tf_op jit(solution)/shard_map/all_to_all | solution.py:171
  78.1 4.3 %fusion.12 = f32[256,128,1]{1,0,2:T(8,128)S(1)} fusion(f32[1536,128]{1,0:T(8,128)} %bitcast.11, f32[1536,128]{1,0:T(8,128)} %get-tuple-element.172, f32[1536,128]{1,0:T(8,128)} %get-tuple-element.173, f32[256]{0:T(256)S(1)} %compare_select_fusion.1), kind=kOutput, calls=%fused_computation.23 | convolution fusion | flops 604405760 | bytes 2491392 | tf_op jit(solution)/shard_map/smr,mn->snr/dot_general | solution.py:196
  82.5 2.4 %fusion.1 = f32[16,99,128]{2,1,0:T(8,128)} fusion(f32[256,128,1]{1,0,2:T(8,128)S(1)} %fusion.12, f32[16,99,128]{2,1,0:T(8,128)S(1)} %copy-done.5, f32[16,99,128]{2,1,0:T(8,128)S(1)} %copy-done.4), kind=kOutput, calls=%fused_computation.4 | convolution fusion | flops 623259648 | bytes 2564096 | tf_op jit(solution)/shard_map/snr,kjn->ksjr/dot_general | solution.py:198
  84.9 6.3 %all-to-all-start.1 = ((f32[16,99,128]{2,1,0:T(8,128)}), f32[16,99,128]{2,1,0:T(8,128)S(1)}, u32[]{:S(2)}, u32[]{:S(2)}) async-start(f32[16,99,128]{2,1,0:T(8,128)} %fusion.1), calls=%async_computation.1 | async-start | bytes 1703936 | tf_op jit(solution)/shard_map/all_to_all | solution.py:200
  91.9 2.2 %maximum_select_fusion.12 = (f32[4,98,128]{2,1,0:T(8,128)S(1)}, f32[4,98,128]{2,1,0:T(8,128)}, f32[4,98,128]{2,1,0:T(8,128)S(1)}, f32[4,98,128]{2,1,0:T(8,128)}) fusion(f32[4,98,127]{2,1,0:T(8,128)} %get-tuple-element.146, f32[4,98,1]{2,1,0:T(8,128)} %get-tuple-element.148, pred[128]{0:T(512)(128)(4,1)S(1)} %iota_compare_fusion.1, ...), kind=kLoop, calls=%fused_computation.130 | loop fusion | flops 802816 | bytes 2809984 | tf_op jit(solution)/shard_map/jit(_where)/select_n | solution.py:78
  97.6 14.5 %all-to-all-done.1 = f32[16,99,128]{2,1,0:T(8,128)S(1)} async-done(((f32[16,99,128]{2,1,0:T(8,128)}), f32[16,99,128]{2,1,0:T(8,128)S(1)}, u32[]{:S(2)}, u32[]{:S(2)}) %all-to-all-start.1) | async-done | bytes 811040 | tf_op jit(solution)/shard_map/all_to_all | solution.py:200
  112.5 5.3 %collective-permute-start.6 = (f32[5,99,128]{2,0,1:T(8,128)S(1)}, f32[5,99,128]{2,0,1:T(8,128)S(1)}, u32[]{:S(2)}, u32[]{:S(2)}) collective-permute-start(f32[5,99,128]{2,0,1:T(8,128)S(1)} %pad_maximum_fusion.7), channel_id=1, source_target_pairs={{16,8},{17,9},{18,10},{19,11},{20,12},{21,13},{22,14},{23,15},{24,... | collective-permute-start | bytes 760328 | tf_op jit(solution)/shard_map/ppermute | solution.py:217
  118.9 2.5 %copy.89 = f32[8,11,99,128]{3,2,1,0:T(8,128)S(1)} copy(f32[8,11,99,128]{3,2,1,0:T(8,128)} %copy-done) | data formatting | bytes 8921088
  122.6 2.9 %collective-permute-start.7 = (f32[16,99,128]{2,0,1:T(8,128)S(1)}, f32[16,99,128]{2,0,1:T(8,128)S(1)}, u32[]{:S(2)}, u32[]{:S(2)}) collective-permute-start(f32[16,99,128]{2,0,1:T(8,128)S(1)} %copy.63), channel_id=1, source_target_pairs={{16,0},{224,240},{17,1},{225,241},{18,2},{226,242},{19,3},{227,243... | collective-permute-start | bytes 2433032 | tf_op jit(solution)/shard_map/ppermute | solution.py:202
  125.9 1.5 %collective-permute-done.7 = f32[16,99,128]{2,0,1:T(8,128)S(1)} collective-permute-done((f32[16,99,128]{2,0,1:T(8,128)S(1)}, f32[16,99,128]{2,0,1:T(8,128)S(1)}, u32[]{:S(2)}, u32[]{:S(2)}) %collective-permute-start.7) | collective-permute-done | bytes 811040 | tf_op jit(solution)/shard_map/ppermute | solution.py:202
  (217 shorter events, 39.0 us)
Async XLA Ops:
  4.0 46.1 %collective-permute-start.4 = (f32[16,96,128]{2,1,0:T(8,128)}, f32[16,96,128]{2,1,0:T(8,128)}, u32[]{:S(2)}, u32[]{:S(2)}) collective-permute-start(f32[16,96,128]{2,1,0:T(8,128)} %bitcast.8), channel_id=1, source_target_pairs={{0,16},{240,224},{1,17},{241,225},{2,18},{242,226},{3,19},{243,227... | collective-permute-start | bytes 2359304 | tf_op jit(solution)/shard_map/ppermute | solution.py:168
  7.5 14.3 %copy-start.41 = (s32[2,4]{1,0:T(2,128)S(1)}, s32[2,4]{1,0:T(2,128)}, u32[]{:S(2)}) copy-start(s32[2,4]{1,0:T(2,128)} %param.8) | copy-start | bytes 100
  9.2 20.4 %collective-permute-start.1 = (f32[9,96,128]{2,1,0:T(8,128)}, f32[9,96,128]{2,1,0:T(8,128)}, u32[]{:S(2)}, u32[]{:S(2)}) collective-permute-start(f32[9,96,128]{2,1,0:T(8,128)} %pad_maximum_fusion.6), channel_id=1, source_target_pairs={{16,0},{32,16},{48,32},{64,48},{80,64},{96,80},{112,96},{128,112},... | collective-permute-start | bytes 1327112 | tf_op jit(solution)/shard_map/ppermute | solution.py:138
  15.2 16.2 %collective-permute-start = (f32[8,96,128]{2,1,0:T(8,128)}, f32[8,96,128]{2,1,0:T(8,128)}, u32[]{:S(2)}, u32[]{:S(2)}) collective-permute-start(f32[8,96,128]{2,1,0:T(8,128)} %get-tuple-element.38), channel_id=1, source_target_pairs={{0,16},{16,32},{32,48},{48,64},{64,80},{80,96},{96,112},{112,128},... | collective-permute-start | bytes 1179656 | tf_op jit(solution)/shard_map/ppermute | solution.py:134
  23.1 5.4 %slice-start.2 = ((f32[3,8,96,128]{3,2,1,0:T(8,128)}), f32[2,8,96,128]{3,2,1,0:T(8,128)S(1)}, s32[]{:S(2)}) async-start(f32[3,8,96,128]{3,2,1,0:T(8,128)} %param.6), calls=%async_computation.4 | async-start | bytes 1572864 | tf_op jit(solution)/shard_map/slice | solution.py:159
  34.4 8.5 %collective-permute-start.2 = (f32[8,11,1,128]{3,2,1,0:T(1,128)}, f32[8,11,1,128]{3,2,1,0:T(1,128)}, u32[]{:S(2)}, u32[]{:S(2)}) collective-permute-start(f32[8,11,1,128]{3,2,1,0:T(1,128)} %pad_maximum_fusion.29), channel_id=1, source_target_pairs={{0,1},{1,2},{2,3},{3,4},{4,5},{5,6},{6,7},{7,8},{8,9},{9,10},{10,1... | collective-permute-start | bytes 135176 | tf_op jit(solution)/shard_map/ppermute | solution.py:148
  36.0 6.9 %collective-permute-start.3 = (f32[8,11,2,128]{3,2,1,0:T(2,128)}, f32[8,11,2,128]{3,2,1,0:T(2,128)}, u32[]{:S(2)}, u32[]{:S(2)}) collective-permute-start(f32[8,11,2,128]{3,2,1,0:T(2,128)} %pad_maximum_fusion.26), channel_id=1, source_target_pairs={{1,0},{2,1},{3,2},{4,3},{5,4},{6,5},{7,6},{8,7},{9,8},{10,9},{11,1... | collective-permute-start | bytes 270344 | tf_op jit(solution)/shard_map/ppermute | solution.py:151
  52.2 25.9 %all-to-all-start = ((f32[16,96,128]{2,1,0:T(8,128)}), f32[16,96,128]{2,1,0:T(8,128)}, u32[]{:S(2)}, u32[]{:S(2)}) async-start(f32[16,96,128]{2,1,0:T(8,128)} %bitcast_select_fusion), calls=%async_computation | async-start | bytes 1572864 | tf_op jit(solution)/shard_map/all_to_all | solution.py:171
  62.8 19.6 %copy-start.4 = (f32[16,99,128]{2,1,0:T(8,128)S(1)}, f32[16,99,128]{2,1,0:T(8,128)}, u32[]{:S(2)}) copy-start(f32[16,99,128]{2,1,0:T(8,128)} %get-tuple-element.162) | copy-start | bytes 2433028
  84.9 27.3 %all-to-all-start.1 = ((f32[16,99,128]{2,1,0:T(8,128)}), f32[16,99,128]{2,1,0:T(8,128)S(1)}, u32[]{:S(2)}, u32[]{:S(2)}) async-start(f32[16,99,128]{2,1,0:T(8,128)} %fusion.1), calls=%async_computation.1 | async-start | bytes 1703936 | tf_op jit(solution)/shard_map/all_to_all | solution.py:200
  97.6 20.3 %copy-start.10 = (f32[2,96,127]{2,1,0:T(8,128)S(1)}, f32[2,96,127]{2,1,0:T(8,128)}, u32[]{:S(2)}) copy-start(f32[2,96,127]{2,1,0:T(8,128)} %get-tuple-element.114) | copy-start | bytes 292612
  97.6 20.3 %copy-start.12 = (f32[2,96,127]{2,1,0:T(8,128)S(1)}, f32[2,96,127]{2,1,0:T(8,128)}, u32[]{:S(2)}) copy-start(f32[2,96,127]{2,1,0:T(8,128)} %get-tuple-element.115) | copy-start | bytes 292612
  97.6 20.3 %copy-start.14 = (f32[2,96,1]{2,1,0:T(8,128)S(1)}, f32[2,96,1]{2,1,0:T(8,128)}, u32[]{:S(2)}) copy-start(f32[2,96,1]{2,1,0:T(8,128)} %get-tuple-element.116) | copy-start | bytes 2308
  97.6 20.3 %copy-start.16 = (f32[2,96,1]{2,1,0:T(8,128)S(1)}, f32[2,96,1]{2,1,0:T(8,128)}, u32[]{:S(2)}) copy-start(f32[2,96,1]{2,1,0:T(8,128)} %get-tuple-element.117) | copy-start | bytes 2308
  97.6 20.3 %copy-start.17 = (f32[2,97,128]{2,1,0:T(8,128)S(1)}, f32[2,97,128]{2,1,0:T(8,128)}, u32[]{:S(2)}) copy-start(f32[2,97,128]{2,1,0:T(8,128)} %get-tuple-element.112) | copy-start | bytes 297988
  97.6 20.3 %copy-start.25 = (f32[3,96,128]{2,1,0:T(8,128)S(1)}, f32[3,96,128]{2,1,0:T(8,128)}, u32[]{:S(2)}) copy-start(f32[3,96,128]{2,1,0:T(8,128)} %get-tuple-element.110) | copy-start | bytes 442372
  97.6 20.3 %copy-start.36 = (f32[2,96,127]{2,1,0:T(8,128)S(1)}, f32[2,96,127]{2,1,0:T(8,128)}, u32[]{:S(2)}) copy-start(f32[2,96,127]{2,1,0:T(8,128)} %get-tuple-element.106) | copy-start | bytes 292612
  112.1 5.8 %copy-start.37 = (f32[2,96,127]{2,1,0:T(8,128)S(1)}, f32[2,96,127]{2,1,0:T(8,128)}, u32[]{:S(2)}) copy-start(f32[2,96,127]{2,1,0:T(8,128)} %get-tuple-element.107) | copy-start | bytes 292612
  112.1 5.8 %copy-start.38 = (f32[2,96,1]{2,1,0:T(8,128)S(1)}, f32[2,96,1]{2,1,0:T(8,128)}, u32[]{:S(2)}) copy-start(f32[2,96,1]{2,1,0:T(8,128)} %get-tuple-element.108) | copy-start | bytes 2308
  112.1 5.8 %copy-start.39 = (f32[2,96,1]{2,1,0:T(8,128)S(1)}, f32[2,96,1]{2,1,0:T(8,128)}, u32[]{:S(2)}) copy-start(f32[2,96,1]{2,1,0:T(8,128)} %get-tuple-element.109) | copy-start | bytes 2308
  112.5 13.0 %collective-permute-start.6 = (f32[5,99,128]{2,0,1:T(8,128)S(1)}, f32[5,99,128]{2,0,1:T(8,128)S(1)}, u32[]{:S(2)}, u32[]{:S(2)}) collective-permute-start(f32[5,99,128]{2,0,1:T(8,128)S(1)} %pad_maximum_fusion.7), channel_id=1, source_target_pairs={{16,8},{17,9},{18,10},{19,11},{20,12},{21,13},{22,14},{23,15},{24,... | collective-permute-start | bytes 760328 | tf_op jit(solution)/shard_map/ppermute | solution.py:217
  118.1 7.4 %collective-permute-start.5 = (f32[5,99,128]{2,0,1:T(8,128)S(1)}, f32[5,99,128]{2,0,1:T(8,128)S(1)}, u32[]{:S(2)}, u32[]{:S(2)}) collective-permute-start(f32[5,99,128]{2,0,1:T(8,128)S(1)} %pad_maximum_fusion.7), channel_id=1, source_target_pairs={{0,8},{1,9},{2,10},{3,11},{4,12},{5,13},{6,14},{7,15},{8,0},{9,1},... | collective-permute-start | bytes 760328 | tf_op jit(solution)/shard_map/ppermute | solution.py:212
  118.9 6.7 %copy-start.40 = (f32[8]{0:T(128)S(1)}, f32[8]{0:T(128)}, u32[]{:S(2)}) copy-start(f32[8]{0:T(128)} %constant.133.clone) | copy-start | bytes 100
  122.6 4.8 %collective-permute-start.7 = (f32[16,99,128]{2,0,1:T(8,128)S(1)}, f32[16,99,128]{2,0,1:T(8,128)S(1)}, u32[]{:S(2)}, u32[]{:S(2)}) collective-permute-start(f32[16,99,128]{2,0,1:T(8,128)S(1)} %copy.63), channel_id=1, source_target_pairs={{16,0},{224,240},{17,1},{225,241},{18,2},{226,242},{19,3},{227,243... | collective-permute-start | bytes 2433032 | tf_op jit(solution)/shard_map/ppermute | solution.py:202
  (31 other events, 67.9 us)

commit v6 on v4

--- a/solution.py
+++ b/solution.py
@@ -131,28 +131,6 @@
             for b in range(phi_count)
         ]
 
-    low_halo = lax.ppermute(
-        combined[:, ct - 1], "theta", [(i, i + 1) for i in range(theta_count - 1)]
-    )
-    up_send = jnp.concatenate([combined[:, 0], combined[6:7, 1]], axis=0)
-    up_halo = lax.ppermute(up_send, "theta", [(i + 1, i) for i in range(theta_count - 1)])
-    rows_ext = jnp.concatenate(
-        [
-            low_halo[:, None],
-            combined,
-            up_halo[:channels, None],
-            jnp.broadcast_to(up_halo[channels:], (channels, npc, nr))[:, None],
-        ],
-        axis=1,
-    )
-    left_cols = lax.ppermute(
-        rows_ext[:, :, npc - 1 :], "phi", [(i, (i + 1) % phi_count) for i in range(phi_count)]
-    )
-    right_cols = lax.ppermute(
-        rows_ext[:, :, :2], "phi", [((i + 1) % phi_count, i) for i in range(phi_count)]
-    )
-    early = jnp.concatenate([left_cols, rows_ext, right_cols], axis=2)
-
     north_side = t <= 1
     helper = (t == 1) | (t == theta_count - 2)
     half = channels * CAP // 2
@@ -197,6 +175,28 @@
     coeffs = coeffs * kept_weight[:, :, None]
     out = jnp.einsum("snr,kjn->ksjr", coeffs, synthesis, precision=lax.Precision.HIGHEST)
     out = out.reshape(phi_count * per_device, npc + 3, nr)
+    low_halo = lax.ppermute(
+        combined[:, ct - 1], "theta", [(i, i + 1) for i in range(theta_count - 1)]
+    )
+    up_send = jnp.concatenate([combined[:, 0], combined[6:7, 1]], axis=0)
+    up_halo = lax.ppermute(up_send, "theta", [(i + 1, i) for i in range(theta_count - 1)])
+    rows_ext = jnp.concatenate(
+        [
+            low_halo[:, None],
+            combined,
+            up_halo[:channels, None],
+            jnp.broadcast_to(up_halo[channels:], (channels, npc, nr))[:, None],
+        ],
+        axis=1,
+    )
+    left_cols = lax.ppermute(
+        rows_ext[:, :, npc - 1 :], "phi", [(i, (i + 1) % phi_count) for i in range(phi_count)]
+    )
+    right_cols = lax.ppermute(
+        rows_ext[:, :, :2], "phi", [((i + 1) % phi_count, i) for i in range(phi_count)]
+    )
+    early = jnp.concatenate([left_cols, rows_ext, right_cols], axis=2)
+
     mine = lax.all_to_all(out, "phi", split_axis=0, concat_axis=0, tiled=True)
 
     from_helper = lax.ppermute(mine, "theta", pairs_in)
@@ -223,6 +223,19 @@
             for b in range(phi_count)
         ],
     )
+    cap_start = jnp.where(at_north, 1, ct - CAP + 1)
+    kept_cap = lax.dynamic_slice_in_dim(early, cap_start, CAP, axis=1)
+    cap_block = jnp.where(at_north | at_south, cap_rows, kept_cap)
+    with_caps = lax.dynamic_update_slice_in_dim(early, cap_block, cap_start, axis=1)
+
+    near_rows = 2
+    rest_rows = ct - near_rows
+
+    def rows_from(x, first, count):
+        return advance(lax.dynamic_slice_in_dim(x, first, count + 3, axis=1))
+
+    rest = rows_from(with_caps, jnp.where(at_north, near_rows, 0), rest_rows)
+    (pole_ghost, helper_ghost), rest = lax.optimization_barrier(((pole_ghost, helper_ghost), rest))
     ghost_main = jnp.concatenate([pole_ghost[:per_half], helper_ghost[:per_half]], axis=0)
     ghost_main = ghost_main * parity[:, None, None]
     ghost_b = helper_ghost[per_half:] * parity[6]
@@ -239,11 +252,16 @@
     )
     offset = jnp.where(at_north, 0, ct - CAP + 1)
     kept_block = lax.dynamic_slice_in_dim(early, offset, CAP + 2, axis=1)
-    block = jnp.where(
-        at_north, north_block, jnp.where(at_south, south_block, kept_block)
-    )
+    block = jnp.where(at_north, north_block, jnp.where(at_south, south_block, kept_block))
     extended = lax.dynamic_update_slice_in_dim(early, block, offset, axis=1)
-    return advance(extended)
+
+    near = rows_from(extended, jnp.where(at_north, 0, rest_rows), near_rows)
+    outs = []
+    for a, c in zip(rest, near):
+        north_order = jnp.concatenate([c, a], axis=1)
+        other_order = jnp.concatenate([a, c], axis=1)
+        outs.append(jnp.where(at_north, north_order, other_order))
+    return tuple(outs)
 
 
 def solution(mesh):

time: 111 us -> 116 us (1.045)
  waiting for transfers between devices: 23.3 us -> 28.2 us
  starting transfers between devices: 31.2 us -> 34.2 us
  other arithmetic: 30.1 us -> 27.9 us
    ppermute x1, waiting for transfers between devices: 0.01 us -> 5.31 us  [local(): lax.ppermute(rows_ext[:, :, npc - 1:], 'phi', [(i, (i + 1) % phi_count) f...]
    dynamic_update_slice x1, other arithmetic: 3.56 us -> 0.55 us  [local(): extended = lax.dynamic_update_slice_in_dim(early, block, offset, axis=1)]
    ppermute x1, starting transfers between devices: 1.32 us -> 4.28 us  [local(): lax.ppermute(ghost_send, both, [(h * phi_count + b, a * phi_count + (b +...]
    ppermute x1, starting transfers between devices: 2.31 us -> 0.01 us  [local(): lax.ppermute(rows_ext[:, :, npc - 1:], 'phi', [(i, (i + 1) % phi_count) f...]
    ppermute x1, starting transfers between devices: 1.52 us -> 3.66 us  [local(): from_helper = lax.ppermute(mine, 'theta', pairs_in)]
    select_n x0 -> x2, other arithmetic: none -> 2.13 us  [local(): outs.append(jnp.where(at_north, north_order, other_order))]
    squeeze x1 -> x2, local copies, waits for them, and re-layouts: 2.6 us -> 0.52 us  [advance(): x[5][inner]]
    another operation x6 -> x10, other arithmetic: 4.05 us -> 2.2 us  [advance(): return (jnp.stack(densities), jnp.stack([new_radial, new_theta, new_phi]))]
  transfers between devices with their start and end apart: 10 -> 10, of which waited for: 5 -> 4; matrix products, arithmetic and copies ran while one was open for 24% -> 27% of each run, Pallas kernels for 0% -> 0%
where the time goes in v6:
time: 116 us; the launch traced here: 115 us
  starting transfers between devices  34.2 us (29%)
  waiting for transfers between devices  28.2 us (24%)
  other arithmetic  27.9 us (24%)
  local copies, waits for them, and re-layouts  16.2 us (14%)
  matrix products  6.74 us (6%)
  between operations  2 us (2%)
    ppermute x1, waiting for transfers between devices, local(): lax.ppermute(up_send, 'theta', [(i + 1, i) for i in range(theta_count - 1)])  12.8 us
    all_to_all x1, starting transfers between devices, local(): cycle = lax.all_to_all(work, 'phi', split_axis=0, concat_axis=1, tiled=True)  7.97 us
    all_to_all x1, waiting for transfers between devices, local(): cycle = lax.all_to_all(work, 'phi', split_axis=0, concat_axis=1, tiled=True)  6.66 us
    all_to_all x1, starting transfers between devices, local(): mine = lax.all_to_all(out, 'phi', split_axis=0, concat_axis=0, tiled=True)  6.4 us
    ppermute x1, waiting for transfers between devices, local(): lax.ppermute(rows_ext[:, :, npc - 1:], 'phi', [(i, (i + 1) % phi_count) f...  5.31 us
    cos x1, other arithmetic, fourier_rows(): return jnp.concatenate([jnp.cos(angle), jnp.sin(angle)], axis=-1)  5.28 us
    unnamed x19, local copies, waits for them, and re-layouts  5.17 us
    dot_general x1, matrix products, local(): jnp.einsum('smr,mn->snr', cycle, analysis, precision=lax.Precision.HIGHEST)  4.34 us
  transfers between devices with their start and end apart: 10, of which 4 were waited for; matrix products, arithmetic and copies ran while one was open for 27% of the time, Pallas kernels for 0%

profile of v6, /device:TPU:1, one launch (start us, length us, event | category | flops | bytes accessed | tf_op | source)
XLA Modules:
  0.0 115.2 jit_solution(2551088384986569136)
XLA Ops:
  1.8 1.3 %fusion.26 = f32[4,4,96,128]{3,2,0,1:T(8,128)S(1)} fusion(f32[1,8,96,128]{3,2,0,1:T(8,128)S(1)} %slice_bitcast_fusion.3, pred[]{:T(512)S(6)} %eq.75, f32[3,8,96,128]{3,2,1,0:T(8,128)} %param.7), kind=kLoop, calls=%fused_computation.36 | loop fusion | flops 589824 | bytes 2359297 | tf_op jit(solution)/shard_map/jit(_where)/select_n | solution.py:141
  3.2 1.3 %collective-permute-start.4 = (f32[16,96,128]{2,1,0:T(8,128)S(1)}, f32[16,96,128]{2,1,0:T(8,128)S(1)}, u32[]{:S(2)}, u32[]{:S(2)}) collective-permute-start(f32[16,96,128]{2,1,0:T(8,128)S(1)} %bitcast.102), channel_id=1, source_target_pairs={{0,16},{240,224},{1,17},{241,225},{2,18},{242,226},{3,19},{243,227... | collective-permute-start | bytes 2359304 | tf_op jit(solution)/shard_map/ppermute | solution.py:146
  6.0 3.4 %collective-permute-done.4 = f32[16,96,128]{2,1,0:T(8,128)S(1)} collective-permute-done((f32[16,96,128]{2,1,0:T(8,128)S(1)}, f32[16,96,128]{2,1,0:T(8,128)S(1)}, u32[]{:S(2)}, u32[]{:S(2)}) %collective-permute-start.4) | collective-permute-done | bytes 786464 | tf_op jit(solution)/shard_map/ppermute | solution.py:146
  10.4 8.0 %all-to-all-start = ((f32[16,96,128]{2,1,0:T(8,128)}), f32[16,96,128]{2,1,0:T(8,128)}, u32[]{:S(2)}, u32[]{:S(2)}) async-start(f32[16,96,128]{2,1,0:T(8,128)} %bitcast_select_fusion), calls=%async_computation | async-start | bytes 1572864 | tf_op jit(solution)/shard_map/all_to_all | solution.py:149
  19.6 1.4 %constant_dynamic-update-slice_fusion.1 = f32[8,8,96,128]{3,2,1,0:T(8,128)S(1)} fusion(f32[8,8,96,128]{3,2,1,0:T(8,128)S(1)} %constant_dynamic-update-slice_fusion.2, f32[3,8,96,128]{3,2,1,0:T(8,128)} %param.6), kind=kLoop, calls=%fused_computation.251 | loop fusion | bytes 2359296
  21.9 5.3 %fusion.20 = (f32[16,99,128]{2,1,0:T(8,128)}, f32[16,99,128]{2,1,0:T(8,128)}) fusion(s32[16,99]{1,0:T(8,128)S(1)} %add_select_fusion.2), kind=kLoop, calls=%fused_computation.30 | loop fusion | flops 1824768 | bytes 1628352 | tf_op jit(solution)/shard_map/cos | solution.py:110
  27.1 4.3 %fusion.29 = (f32[1536,128]{1,0:T(8,128)}, f32[1536,128]{1,0:T(8,128)}) fusion(), kind=kLoop, calls=%fused_computation.45 | loop fusion | flops 1769472 | bytes 1572864 | tf_op jit(solution)/shard_map/sin | solution.py:110
  31.5 6.7 %all-to-all-done = f32[16,96,128]{2,1,0:T(8,128)} async-done(((f32[16,96,128]{2,1,0:T(8,128)}), f32[16,96,128]{2,1,0:T(8,128)}, u32[]{:S(2)}, u32[]{:S(2)}) %all-to-all-start) | async-done | bytes 786464 | tf_op jit(solution)/shard_map/all_to_all | solution.py:149
  38.2 4.3 %fusion.12 = f32[256,128,1]{1,0,2:T(8,128)S(1)} fusion(f32[1536,128]{1,0:T(8,128)} %bitcast.11, f32[1536,128]{1,0:T(8,128)} %get-tuple-element.124, f32[1536,128]{1,0:T(8,128)} %get-tuple-element.125, f32[256]{0:T(256)S(1)} %compare_select_fusion.1), kind=kOutput, calls=%fused_computation.22 | convolution fusion | flops 604405760 | bytes 2491392 | tf_op jit(solution)/shard_map/smr,mn->snr/dot_general | solution.py:174
  42.5 2.4 %fusion.1 = f32[16,99,128]{2,1,0:T(8,128)} fusion(f32[256,128,1]{1,0,2:T(8,128)S(1)} %fusion.12, f32[16,99,128]{2,1,0:T(8,128)S(1)} %copy-done.3, f32[16,99,128]{2,1,0:T(8,128)S(1)} %copy-done.2), kind=kOutput, calls=%fused_computation.4 | convolution fusion | flops 623259648 | bytes 2564096 | tf_op jit(solution)/shard_map/snr,kjn->ksjr/dot_general | solution.py:176
  44.9 6.4 %all-to-all-start.1 = ((f32[16,99,128]{2,1,0:T(8,128)}), f32[16,99,128]{2,1,0:T(8,128)}, u32[]{:S(2)}, u32[]{:S(2)}) async-start(f32[16,99,128]{2,1,0:T(8,128)} %fusion.1), calls=%async_computation.1 | async-start | bytes 1703936 | tf_op jit(solution)/shard_map/all_to_all | solution.py:200
  51.3 1.4 %constant_dynamic-update-slice_fusion = f32[8,8,96,128]{3,2,1,0:T(8,128)S(1)} fusion(f32[8,8,96,128]{3,2,1,0:T(8,128)S(1)} %constant_dynamic-update-slice_fusion.1, f32[3,8,96,128]{3,2,1,0:T(8,128)} %param.7), kind=kLoop, calls=%fused_computation.250 | loop fusion | bytes 2359296 | tf_op jit(solution)/shard_map/concatenate | solution.py:114
  52.8 2.8 %collective-permute-start.1 = (f32[9,96,128]{2,1,0:T(8,128)S(1)}, f32[9,96,128]{2,1,0:T(8,128)S(1)}, u32[]{:S(2)}, u32[]{:S(2)}) collective-permute-start(f32[9,96,128]{2,1,0:T(8,128)S(1)} %pad_maximum_fusion.6), channel_id=1, source_target_pairs={{16,0},{32,16},{48,32},{64,48},{80,64},{96,80},{112,96},{128,112},... | collective-permute-start | bytes 1327112 | tf_op jit(solution)/shard_map/ppermute | solution.py:182
  55.5 4.3 %collective-permute-start = (f32[8,96,128]{2,1,0:T(8,128)S(1)}, f32[8,96,128]{2,1,0:T(8,128)S(1)}, u32[]{:S(2)}, u32[]{:S(2)}) collective-permute-start(f32[8,96,128]{2,1,0:T(8,128)S(1)} %get-tuple-element.34), channel_id=1, source_target_pairs={{0,16},{16,32},{32,48},{48,64},{64,80},{80,96},{96,112},{112,128},... | collective-permute-start | bytes 1179656 | tf_op jit(solution)/shard_map/ppermute | solution.py:178
  59.9 12.8 %collective-permute-done.1 = f32[9,96,128]{2,1,0:T(8,128)S(1)} collective-permute-done((f32[9,96,128]{2,1,0:T(8,128)S(1)}, f32[9,96,128]{2,1,0:T(8,128)S(1)}, u32[]{:S(2)}, u32[]{:S(2)}) %collective-permute-start.1) | collective-permute-done | bytes 442400 | tf_op jit(solution)/shard_map/ppermute | solution.py:182
  74.3 2.2 %copy.63 = f32[16,99,128]{2,0,1:T(8,128)} copy(f32[16,99,128]{2,1,0:T(8,128)} %all-to-all-done.1) | data formatting | bytes 1622016 | tf_op jit(solution)/shard_map/all_to_all | solution.py:200
  76.5 3.7 %collective-permute-start.7 = (f32[16,99,128]{2,0,1:T(8,128)}, f32[16,99,128]{2,0,1:T(8,128)}, u32[]{:S(2)}, u32[]{:S(2)}) collective-permute-start(f32[16,99,128]{2,0,1:T(8,128)} %copy.63), channel_id=1, source_target_pairs={{16,0},{224,240},{17,1},{225,241},{18,2},{226,242},{19,3},{227,243... | collective-permute-start | bytes 2433032 | tf_op jit(solution)/shard_map/ppermute | solution.py:202
  80.1 1.4 %pad_maximum_fusion.23 = f32[8,11,1,128]{3,2,1,0:T(1,128)} fusion(f32[8,1,96,128]{3,2,1,0:T(8,128)} %copy-done, f32[8,1,96,128]{3,2,1,0:T(8,128)S(1)} %slice_bitcast_fusion, f32[8,8,96,128]{3,2,1,0:T(8,128)S(1)} %constant_dynamic-update-slice_fusion, f32[8,1,96,128]{3,2,1,0:T(8,128)} %bitcast.100), kind=kLoop, calls=%fused_computation.248 | loop fusion | flops 33792 | bytes 4370432 | tf_op jit(solution)/shard_map/slice | solution.py:193
  81.6 2.8 %collective-permute-start.3 = (f32[8,11,2,128]{3,2,1,0:T(2,128)}, f32[8,11,2,128]{3,2,1,0:T(2,128)}, u32[]{:S(2)}, u32[]{:S(2)}) collective-permute-start(f32[8,11,2,128]{3,2,1,0:T(2,128)} %pad_maximum_fusion.20), channel_id=1, source_target_pairs={{1,0},{2,1},{3,2},{4,3},{5,4},{6,5},{7,6},{8,7},{9,8},{10,9},{11,1... | collective-permute-start | bytes 270344 | tf_op jit(solution)/shard_map/ppermute | solution.py:195
  84.4 5.3 %collective-permute-done.2 = f32[8,11,1,128]{3,2,1,0:T(1,128)} collective-permute-done((f32[8,11,1,128]{3,2,1,0:T(1,128)}, f32[8,11,1,128]{3,2,1,0:T(1,128)}, u32[]{:S(2)}, u32[]{:S(2)}) %collective-permute-start.2) | collective-permute-done | bytes 45088 | tf_op jit(solution)/shard_map/ppermute | solution.py:192
  89.7 1.9 %pad_maximum_fusion = f32[8,11,99,128]{3,2,1,0:T(8,128)S(1)} fusion(f32[8,11,2,128]{3,2,1,0:T(2,128)} %collective-permute-done.3, f32[8,1,96,128]{3,2,1,0:T(8,128)} %copy-done, f32[8,1,96,128]{3,2,1,0:T(8,128)S(1)} %slice_bitcast_fusion, f32[8,8,96,128]{3,2,1,0:T(8,128)S(1)} %constant_dynamic-update-slice_fusion, f32[8,1,96,128]{3,2,1,0:T(8,128)} %bitcast.101, ...), kind=kLoop, calls=%fused_computation | loop fusion | flops 5575680 | bytes 8921088 | tf_op jit(solution)/shard_map/concatenate | solution.py:198
  94.8 4.3 %collective-permute-start.6 = (f32[5,99,128]{2,0,1:T(8,128)S(1)}, f32[5,99,128]{2,0,1:T(8,128)S(1)}, u32[]{:S(2)}, u32[]{:S(2)}) collective-permute-start(f32[5,99,128]{2,0,1:T(8,128)S(1)} %pad_maximum_fusion.7), channel_id=1, source_target_pairs={{16,8},{17,9},{18,10},{19,11},{20,12},{21,13},{22,14},{23,15},{24,... | collective-permute-start | bytes 760328 | tf_op jit(solution)/shard_map/ppermute | solution.py:217
  99.1 1.4 %copy.67 = f32[16,99,128]{2,1,0:T(8,128)S(1)} copy(f32[16,99,128]{2,0,1:T(8,128)} %collective-permute-done.7) | data formatting | bytes 1622016 | tf_op jit(solution)/shard_map/ppermute | solution.py:202
  100.5 1.3 %pad_maximum_fusion.1 = f32[32,99,128]{2,1,0:T(8,128)S(1)} fusion(f32[16,99,128]{2,1,0:T(8,128)S(1)} %copy.67, f32[16,99,128]{2,1,0:T(8,128)} %all-to-all-done.1), kind=kLoop, calls=%fused_computation.8 | loop fusion | flops 405504 | bytes 3244032 | tf_op jit(solution)/shard_map/concatenate | solution.py:204
  (118 shorter events, 23.0 us)
Async XLA Ops:
  0.6 5.2 %slice-start = ((f32[3,8,96,128]{3,2,1,0:T(8,128)}), f32[2,8,96,128]{3,2,1,0:T(8,128)S(1)}, s32[]{:S(2)}) async-start(f32[3,8,96,128]{3,2,1,0:T(8,128)} %param.6), calls=%async_computation.2 | async-start | bytes 1572864 | tf_op jit(solution)/shard_map/slice | solution.py:137
  0.6 3.8 %copy-start.6 = (s32[2,4]{1,0:T(2,128)S(1)}, s32[2,4]{1,0:T(2,128)}, u32[]{:S(2)}) copy-start(s32[2,4]{1,0:T(2,128)} %param.8) | copy-start | bytes 100
  0.7 5.1 %copy-start.4 = (f32[2,8,96,128]{3,2,1,0:T(8,128)S(1)}, f32[2,8,96,128]{3,2,1,0:T(8,128)}, u32[]{:S(2)}) copy-start(f32[2,8,96,128]{3,2,1,0:T(8,128)} %param.5) | copy-start | bytes 2359300
  3.2 6.3 %collective-permute-start.4 = (f32[16,96,128]{2,1,0:T(8,128)S(1)}, f32[16,96,128]{2,1,0:T(8,128)S(1)}, u32[]{:S(2)}, u32[]{:S(2)}) collective-permute-start(f32[16,96,128]{2,1,0:T(8,128)S(1)} %bitcast.102), channel_id=1, source_target_pairs={{0,16},{240,224},{1,17},{241,225},{2,18},{242,226},{3,19},{243,227... | collective-permute-start | bytes 2359304 | tf_op jit(solution)/shard_map/ppermute | solution.py:146
  10.4 27.7 %all-to-all-start = ((f32[16,96,128]{2,1,0:T(8,128)}), f32[16,96,128]{2,1,0:T(8,128)}, u32[]{:S(2)}, u32[]{:S(2)}) async-start(f32[16,96,128]{2,1,0:T(8,128)} %bitcast_select_fusion), calls=%async_computation | async-start | bytes 1572864 | tf_op jit(solution)/shard_map/all_to_all | solution.py:149
  38.1 4.4 %copy-start.2 = (f32[16,99,128]{2,1,0:T(8,128)S(1)}, f32[16,99,128]{2,1,0:T(8,128)}, u32[]{:S(2)}) copy-start(f32[16,99,128]{2,1,0:T(8,128)} %get-tuple-element.118) | copy-start | bytes 2433028
  38.1 4.4 %copy-start.3 = (f32[16,99,128]{2,1,0:T(8,128)S(1)}, f32[16,99,128]{2,1,0:T(8,128)}, u32[]{:S(2)}) copy-start(f32[16,99,128]{2,1,0:T(8,128)} %get-tuple-element.119) | copy-start | bytes 2433028
  44.9 29.4 %all-to-all-start.1 = ((f32[16,99,128]{2,1,0:T(8,128)}), f32[16,99,128]{2,1,0:T(8,128)}, u32[]{:S(2)}, u32[]{:S(2)}) async-start(f32[16,99,128]{2,1,0:T(8,128)} %fusion.1), calls=%async_computation.1 | async-start | bytes 1703936 | tf_op jit(solution)/shard_map/all_to_all | solution.py:200
  52.8 19.9 %collective-permute-start.1 = (f32[9,96,128]{2,1,0:T(8,128)S(1)}, f32[9,96,128]{2,1,0:T(8,128)S(1)}, u32[]{:S(2)}, u32[]{:S(2)}) collective-permute-start(f32[9,96,128]{2,1,0:T(8,128)S(1)} %pad_maximum_fusion.6), channel_id=1, source_target_pairs={{16,0},{32,16},{48,32},{64,48},{80,64},{96,80},{112,96},{128,112},... | collective-permute-start | bytes 1327112 | tf_op jit(solution)/shard_map/ppermute | solution.py:182
  55.5 17.1 %collective-permute-start = (f32[8,96,128]{2,1,0:T(8,128)S(1)}, f32[8,96,128]{2,1,0:T(8,128)S(1)}, u32[]{:S(2)}, u32[]{:S(2)}) collective-permute-start(f32[8,96,128]{2,1,0:T(8,128)S(1)} %get-tuple-element.34), channel_id=1, source_target_pairs={{0,16},{16,32},{32,48},{48,64},{64,80},{80,96},{96,112},{112,128},... | collective-permute-start | bytes 1179656 | tf_op jit(solution)/shard_map/ppermute | solution.py:178
  72.7 0.8 copy-start.1
  72.7 0.8 copy-start
  76.5 22.6 %collective-permute-start.7 = (f32[16,99,128]{2,0,1:T(8,128)}, f32[16,99,128]{2,0,1:T(8,128)}, u32[]{:S(2)}, u32[]{:S(2)}) collective-permute-start(f32[16,99,128]{2,0,1:T(8,128)} %copy.63), channel_id=1, source_target_pairs={{16,0},{224,240},{17,1},{225,241},{18,2},{226,242},{19,3},{227,243... | collective-permute-start | bytes 2433032 | tf_op jit(solution)/shard_map/ppermute | solution.py:202
  81.6 8.2 %collective-permute-start.3 = (f32[8,11,2,128]{3,2,1,0:T(2,128)}, f32[8,11,2,128]{3,2,1,0:T(2,128)}, u32[]{:S(2)}, u32[]{:S(2)}) collective-permute-start(f32[8,11,2,128]{3,2,1,0:T(2,128)} %pad_maximum_fusion.20), channel_id=1, source_target_pairs={{1,0},{2,1},{3,2},{4,3},{5,4},{6,5},{7,6},{8,7},{9,8},{10,9},{11,1... | collective-permute-start | bytes 270344 | tf_op jit(solution)/shard_map/ppermute | solution.py:195
  84.4 5.3 %collective-permute-start.2 = (f32[8,11,1,128]{3,2,1,0:T(1,128)}, f32[8,11,1,128]{3,2,1,0:T(1,128)}, u32[]{:S(2)}, u32[]{:S(2)}) collective-permute-start(f32[8,11,1,128]{3,2,1,0:T(1,128)} %pad_maximum_fusion.23), channel_id=1, source_target_pairs={{0,1},{1,2},{2,3},{3,4},{4,5},{5,6},{6,7},{7,8},{8,9},{9,10},{10,1... | collective-permute-start | bytes 135176 | tf_op jit(solution)/shard_map/ppermute | solution.py:192
  94.1 14.4 %collective-permute-start.5 = (f32[5,99,128]{2,0,1:T(8,128)S(1)}, f32[5,99,128]{2,0,1:T(8,128)S(1)}, u32[]{:S(2)}, u32[]{:S(2)}) collective-permute-start(f32[5,99,128]{2,0,1:T(8,128)S(1)} %pad_maximum_fusion.7), channel_id=1, source_target_pairs={{0,8},{1,9},{2,10},{3,11},{4,12},{5,13},{6,14},{7,15},{8,0},{9,1},... | collective-permute-start | bytes 760328 | tf_op jit(solution)/shard_map/ppermute | solution.py:212
  94.8 13.7 %collective-permute-start.6 = (f32[5,99,128]{2,0,1:T(8,128)S(1)}, f32[5,99,128]{2,0,1:T(8,128)S(1)}, u32[]{:S(2)}, u32[]{:S(2)}) collective-permute-start(f32[5,99,128]{2,0,1:T(8,128)S(1)} %pad_maximum_fusion.7), channel_id=1, source_target_pairs={{16,8},{17,9},{18,10},{19,11},{20,12},{21,13},{22,14},{23,15},{24,... | collective-permute-start | bytes 760328 | tf_op jit(solution)/shard_map/ppermute | solution.py:217
  108.4 0.7 copy-start.5

commit v7 on v6

--- a/solution.py
+++ b/solution.py
@@ -198,6 +198,7 @@
     early = jnp.concatenate([left_cols, rows_ext, right_cols], axis=2)
 
     mine = lax.all_to_all(out, "phi", split_axis=0, concat_axis=0, tiled=True)
+    mine, early = lax.optimization_barrier((mine, early))
 
     from_helper = lax.ppermute(mine, "theta", pairs_in)
     per_half = channels // 2

time: 116 us -> 113 us (0.974)
  the two profiles are of different devices: /device:TPU:1 before, /device:TPU:28 now
where the time goes in v7:
time: 113 us; the launch traced here: 112 us
  waiting for transfers between devices  31 us (27%)
  other arithmetic  29.4 us (26%)
  starting transfers between devices  27.6 us (24%)
  local copies, waits for them, and re-layouts  15.5 us (14%)
  matrix products  6.74 us (6%)
  between operations  2.05 us (2%)
    all_to_all x1, waiting for transfers between devices, local(): cycle = lax.all_to_all(work, 'phi', split_axis=0, concat_axis=1, tiled=True)  9.78 us
    all_to_all x1, starting transfers between devices, local(): cycle = lax.all_to_all(work, 'phi', split_axis=0, concat_axis=1, tiled=True)  9.25 us
    ppermute x1, waiting for transfers between devices, local(): lax.ppermute(combined[:, ct - 1], 'theta', [(i, i + 1) for i in range(the...  7.68 us
    ppermute x1, waiting for transfers between devices, local(): lax.ppermute(up_send, 'theta', [(i + 1, i) for i in range(theta_count - 1)])  7.44 us
    ppermute x1, waiting for transfers between devices, local(): lax.ppermute(rows_ext[:, :, npc - 1:], 'phi', [(i, (i + 1) % phi_count) f...  6.14 us
    cos x1, other arithmetic, fourier_rows(): return jnp.concatenate([jnp.cos(angle), jnp.sin(angle)], axis=-1)  5.3 us
    ppermute x1, starting transfers between devices, local(): lax.ppermute(rows_ext[:, :, :2], 'phi', [((i + 1) % phi_count, i) for i i...  4.38 us
    dot_general x1, matrix products, local(): jnp.einsum('smr,mn->snr', cycle, analysis, precision=lax.Precision.HIGHEST)  4.34 us
  transfers between devices with their start and end apart: 10, of which 4 were waited for; matrix products, arithmetic and copies ran while one was open for 28% of the time, Pallas kernels for 0%

profile of v7, /device:TPU:28, one launch (start us, length us, event | category | flops | bytes accessed | tf_op | source)
XLA Modules:
  0.0 112.3 jit_solution(654539253029407260)
XLA Ops:
  1.8 2.2 %fusion.26 = f32[4,4,96,128]{3,2,0,1:T(8,128)} fusion(f32[1,8,96,128]{3,2,0,1:T(8,128)S(1)} %slice_bitcast_fusion.3, pred[]{:T(512)S(6)} %eq.75, f32[3,8,96,128]{3,2,1,0:T(8,128)} %param.7), kind=kLoop, calls=%fused_computation.36 | loop fusion | flops 589824 | bytes 2359297 | tf_op jit(solution)/shard_map/jit(_where)/select_n | solution.py:141
  4.0 1.3 %collective-permute-start = (f32[16,96,128]{2,1,0:T(8,128)}, f32[16,96,128]{2,1,0:T(8,128)}, u32[]{:S(2)}, u32[]{:S(2)}) collective-permute-start(f32[16,96,128]{2,1,0:T(8,128)} %bitcast.1), channel_id=1, source_target_pairs={{0,16},{240,224},{1,17},{241,225},{2,18},{242,226},{3,19},{243,227... | collective-permute-start | bytes 2359304 | tf_op jit(solution)/shard_map/ppermute | solution.py:146
  8.9 1.4 %constant_dynamic-update-slice_fusion.1 = f32[8,8,96,128]{3,2,1,0:T(8,128)S(1)} fusion(f32[8,8,96,128]{3,2,1,0:T(8,128)S(1)} %constant_dynamic-update-slice_fusion.2, f32[3,8,96,128]{3,2,1,0:T(8,128)} %param.6), kind=kLoop, calls=%fused_computation.251 | loop fusion | bytes 2359296
  11.6 2.1 %bitcast_select_fusion = f32[16,96,128]{2,1,0:T(8,128)} fusion(f32[16,96,128]{2,1,0:T(8,128)} %collective-permute-done, f32[4,4,96,128]{3,2,0,1:T(8,128)S(1)} %copy_select_fusion, pred[]{:T(512)S(6)} %or.6), kind=kLoop, calls=%fused_computation.41 | loop fusion | flops 196608 | bytes 2359297 | tf_op jit(solution)/shard_map/jit(_where)/select_n | solution.py:147
  13.7 9.2 %all-to-all-start = ((f32[16,96,128]{2,1,0:T(8,128)}), f32[16,96,128]{2,1,0:T(8,128)}, u32[]{:S(2)}, u32[]{:S(2)}) async-start(f32[16,96,128]{2,1,0:T(8,128)} %bitcast_select_fusion), calls=%async_computation | async-start | bytes 1572864 | tf_op jit(solution)/shard_map/all_to_all | solution.py:149
  23.0 1.4 %constant_dynamic-update-slice_fusion = f32[8,8,96,128]{3,2,1,0:T(8,128)S(1)} fusion(f32[8,8,96,128]{3,2,1,0:T(8,128)S(1)} %constant_dynamic-update-slice_fusion.1, f32[3,8,96,128]{3,2,1,0:T(8,128)} %param.7), kind=kLoop, calls=%fused_computation.250 | loop fusion | bytes 2359296 | tf_op jit(solution)/shard_map/concatenate | solution.py:114
  24.4 1.4 %slice_bitcast_fusion.7 = f32[1,96,128]{2,1,0:T(8,128)} fusion(f32[3,8,96,128]{3,2,1,0:T(8,128)} %param.7), kind=kLoop, calls=%fused_computation.247 | loop fusion | bytes 98304 | tf_op jit(solution)/shard_map/squeeze | solution.py:181
  26.6 5.3 %fusion.20 = (f32[16,99,128]{2,1,0:T(8,128)}, f32[16,99,128]{2,1,0:T(8,128)}) fusion(s32[16,99]{1,0:T(8,128)S(1)} %add_select_fusion.2), kind=kLoop, calls=%fused_computation.30 | loop fusion | flops 1824768 | bytes 1628352 | tf_op jit(solution)/shard_map/cos | solution.py:110
  31.9 4.3 %fusion.29 = (f32[1536,128]{1,0:T(8,128)}, f32[1536,128]{1,0:T(8,128)}) fusion(), kind=kLoop, calls=%fused_computation.45 | loop fusion | flops 1769472 | bytes 1572864 | tf_op jit(solution)/shard_map/sin | solution.py:110
  36.3 9.8 %all-to-all-done = f32[16,96,128]{2,1,0:T(8,128)} async-done(((f32[16,96,128]{2,1,0:T(8,128)}), f32[16,96,128]{2,1,0:T(8,128)}, u32[]{:S(2)}, u32[]{:S(2)}) %all-to-all-start) | async-done | bytes 786464 | tf_op jit(solution)/shard_map/all_to_all | solution.py:149
  46.0 4.3 %fusion.12 = f32[256,128,1]{1,0,2:T(8,128)S(1)} fusion(f32[1536,128]{1,0:T(8,128)} %bitcast.4, f32[1536,128]{1,0:T(8,128)} %get-tuple-element.128, f32[1536,128]{1,0:T(8,128)} %get-tuple-element.129, f32[256]{0:T(256)S(1)} %compare_select_fusion.1), kind=kOutput, calls=%fused_computation.22 | convolution fusion | flops 604405760 | bytes 2491392 | tf_op jit(solution)/shard_map/smr,mn->snr/dot_general | solution.py:174
  50.4 2.4 %fusion.1 = f32[16,99,128]{2,1,0:T(8,128)} fusion(f32[256,128,1]{1,0,2:T(8,128)S(1)} %fusion.12, f32[16,99,128]{2,1,0:T(8,128)S(1)} %copy-done.2, f32[16,99,128]{2,1,0:T(8,128)S(1)} %copy-done.1), kind=kOutput, calls=%fused_computation.4 | convolution fusion | flops 623259648 | bytes 2564096 | tf_op jit(solution)/shard_map/snr,kjn->ksjr/dot_general | solution.py:176
  52.8 4.3 %all-to-all-start.1 = ((f32[16,99,128]{2,1,0:T(8,128)}), f32[16,99,128]{2,1,0:T(8,128)}, u32[]{:S(2)}, u32[]{:S(2)}) async-start(f32[16,99,128]{2,1,0:T(8,128)} %fusion.1), calls=%async_computation.1 | async-start | bytes 1703936 | tf_op jit(solution)/shard_map/all_to_all | solution.py:200
  58.0 1.9 %collective-permute-start.2 = (f32[9,96,128]{2,1,0:T(8,128)S(1)}, f32[9,96,128]{2,1,0:T(8,128)S(1)}, u32[]{:S(2)}, u32[]{:S(2)}) collective-permute-start(f32[9,96,128]{2,1,0:T(8,128)S(1)} %pad_maximum_fusion.6), channel_id=1, source_target_pairs={{16,0},{32,16},{48,32},{64,48},{80,64},{96,80},{112,96},{128,112},... | collective-permute-start | bytes 1327112 | tf_op jit(solution)/shard_map/ppermute | solution.py:182
  59.9 2.4 %collective-permute-start.1 = (f32[8,96,128]{2,1,0:T(8,128)}, f32[8,96,128]{2,1,0:T(8,128)S(1)}, u32[]{:S(2)}, u32[]{:S(2)}) collective-permute-start(f32[8,96,128]{2,1,0:T(8,128)} %get-tuple-element.38), channel_id=1, source_target_pairs={{0,16},{16,32},{32,48},{48,64},{64,80},{80,96},{96,112},{112,128},... | collective-permute-start | bytes 1179656 | tf_op jit(solution)/shard_map/ppermute | solution.py:178
  62.3 7.4 %collective-permute-done.2 = f32[9,96,128]{2,1,0:T(8,128)S(1)} collective-permute-done((f32[9,96,128]{2,1,0:T(8,128)S(1)}, f32[9,96,128]{2,1,0:T(8,128)S(1)}, u32[]{:S(2)}, u32[]{:S(2)}) %collective-permute-start.2) | collective-permute-done | bytes 442400 | tf_op jit(solution)/shard_map/ppermute | solution.py:182
  69.8 7.7 %collective-permute-done.1 = f32[8,96,128]{2,1,0:T(8,128)S(1)} collective-permute-done((f32[8,96,128]{2,1,0:T(8,128)}, f32[8,96,128]{2,1,0:T(8,128)S(1)}, u32[]{:S(2)}, u32[]{:S(2)}) %collective-permute-start.1) | collective-permute-done | bytes 393248 | tf_op jit(solution)/shard_map/ppermute | solution.py:178
  77.6 4.4 %collective-permute-start.4 = (f32[8,11,2,128]{3,2,1,0:T(2,128)S(1)}, f32[8,11,2,128]{3,2,1,0:T(2,128)S(1)}, u32[]{:S(2)}, u32[]{:S(2)}) collective-permute-start(f32[8,11,2,128]{3,2,1,0:T(2,128)S(1)} %pad_maximum_fusion.20), channel_id=1, source_target_pairs={{1,0},{2,1},{3,2},{4,3},{5,4},{6,5},{7,6},{8,7},{9,8},{10,9},{11,1... | collective-permute-start | bytes 270344 | tf_op jit(solution)/shard_map/ppermute | solution.py:195
  82.1 6.1 %collective-permute-done.3 = f32[8,11,1,128]{3,2,1,0:T(1,128)S(1)} collective-permute-done((f32[8,11,1,128]{3,2,1,0:T(1,128)S(1)}, f32[8,11,1,128]{3,2,1,0:T(1,128)S(1)}, u32[]{:S(2)}, u32[]{:S(2)}) %collective-permute-start.3) | collective-permute-done | bytes 45088 | tf_op jit(solution)/shard_map/ppermute | solution.py:192
  88.2 2.6 %pad_maximum_fusion = f32[8,11,99,128]{3,2,1,0:T(8,128)} fusion(f32[8,11,2,128]{3,2,1,0:T(2,128)S(1)} %collective-permute-done.4, f32[8,1,96,128]{3,2,1,0:T(8,128)S(1)} %broadcast_in_dim_broadcast_in_dim.4, f32[8,1,96,128]{3,2,1,0:T(8,128)S(1)} %slice_bitcast_fusion, f32[8,8,96,128]{3,2,1,0:T(8,128)S(1)} %constant_dynamic-update-slice_fusion, ...), kind=kLoop, calls=%fused_computation | loop fusion | flops 5575680 | bytes 8921088 | tf_op jit(solution)/shard_map/concatenate | solution.py:198
  90.8 1.3 %copy.63 = f32[16,99,128]{2,0,1:T(8,128)S(1)} copy(f32[16,99,128]{2,1,0:T(8,128)} %all-to-all-done.1) | data formatting | bytes 1622016 | tf_op jit(solution)/shard_map/optimization_barrier | solution.py:201
  92.1 1.3 %collective-permute-start.7 = (f32[16,99,128]{2,0,1:T(8,128)S(1)}, f32[16,99,128]{2,0,1:T(8,128)S(1)}, u32[]{:S(2)}, u32[]{:S(2)}) collective-permute-start(f32[16,99,128]{2,0,1:T(8,128)S(1)} %copy.63), channel_id=1, source_target_pairs={{16,0},{224,240},{17,1},{225,241},{18,2},{226,242},{19,3},{227,243... | collective-permute-start | bytes 2433032 | tf_op jit(solution)/shard_map/ppermute | solution.py:203
  95.5 1.8 %collective-permute-start.6 = (f32[5,99,128]{2,0,1:T(8,128)S(1)}, f32[5,99,128]{2,0,1:T(8,128)S(1)}, u32[]{:S(2)}, u32[]{:S(2)}) collective-permute-start(f32[5,99,128]{2,0,1:T(8,128)S(1)} %pad_maximum_fusion.7), channel_id=1, source_target_pairs={{16,8},{17,9},{18,10},{19,11},{20,12},{21,13},{22,14},{23,15},{24,... | collective-permute-start | bytes 760328 | tf_op jit(solution)/shard_map/ppermute | solution.py:218
  97.6 1.3 %pad_maximum_fusion.1 = f32[32,99,128]{2,1,0:T(8,128)S(1)} fusion(f32[16,99,128]{2,1,0:T(8,128)S(1)} %copy.67, f32[16,99,128]{2,1,0:T(8,128)} %all-to-all-done.1), kind=kLoop, calls=%fused_computation.8 | loop fusion | flops 405504 | bytes 3244032 | tf_op jit(solution)/shard_map/concatenate | solution.py:205
  (124 shorter events, 22.6 us)
Async XLA Ops:
  0.6 4.7 %copy-start = (f32[3,8,96,128]{3,2,1,0:T(8,128)S(1)}, f32[3,8,96,128]{3,2,1,0:T(8,128)}, u32[]{:S(2)}) copy-start(f32[3,8,96,128]{3,2,1,0:T(8,128)} %param.6) | copy-start | bytes 3538948
  0.6 5.6 %copy-start.5 = (s32[2,4]{1,0:T(2,128)S(1)}, s32[2,4]{1,0:T(2,128)}, u32[]{:S(2)}) copy-start(s32[2,4]{1,0:T(2,128)} %param.8) | copy-start | bytes 100
  4.0 7.6 %collective-permute-start = (f32[16,96,128]{2,1,0:T(8,128)}, f32[16,96,128]{2,1,0:T(8,128)}, u32[]{:S(2)}, u32[]{:S(2)}) collective-permute-start(f32[16,96,128]{2,1,0:T(8,128)} %bitcast.1), channel_id=1, source_target_pairs={{0,16},{240,224},{1,17},{241,225},{2,18},{242,226},{3,19},{243,227... | collective-permute-start | bytes 2359304 | tf_op jit(solution)/shard_map/ppermute | solution.py:146
  7.6 2.7 %copy-start.3 = (f32[2,8,96,128]{3,2,1,0:T(8,128)S(1)}, f32[2,8,96,128]{3,2,1,0:T(8,128)}, u32[]{:S(2)}) copy-start(f32[2,8,96,128]{3,2,1,0:T(8,128)} %slice.680) | copy-start | bytes 2359300
  13.7 32.3 %all-to-all-start = ((f32[16,96,128]{2,1,0:T(8,128)}), f32[16,96,128]{2,1,0:T(8,128)}, u32[]{:S(2)}, u32[]{:S(2)}) async-start(f32[16,96,128]{2,1,0:T(8,128)} %bitcast_select_fusion), calls=%async_computation | async-start | bytes 1572864 | tf_op jit(solution)/shard_map/all_to_all | solution.py:149
  46.0 4.4 %copy-start.1 = (f32[16,99,128]{2,1,0:T(8,128)S(1)}, f32[16,99,128]{2,1,0:T(8,128)}, u32[]{:S(2)}) copy-start(f32[16,99,128]{2,1,0:T(8,128)} %get-tuple-element.122) | copy-start | bytes 2433028
  46.0 4.4 %copy-start.2 = (f32[16,99,128]{2,1,0:T(8,128)S(1)}, f32[16,99,128]{2,1,0:T(8,128)}, u32[]{:S(2)}) copy-start(f32[16,99,128]{2,1,0:T(8,128)} %get-tuple-element.123) | copy-start | bytes 2433028
  52.8 38.0 %all-to-all-start.1 = ((f32[16,99,128]{2,1,0:T(8,128)}), f32[16,99,128]{2,1,0:T(8,128)}, u32[]{:S(2)}, u32[]{:S(2)}) async-start(f32[16,99,128]{2,1,0:T(8,128)} %fusion.1), calls=%async_computation.1 | async-start | bytes 1703936 | tf_op jit(solution)/shard_map/all_to_all | solution.py:200
  58.0 11.8 %collective-permute-start.2 = (f32[9,96,128]{2,1,0:T(8,128)S(1)}, f32[9,96,128]{2,1,0:T(8,128)S(1)}, u32[]{:S(2)}, u32[]{:S(2)}) collective-permute-start(f32[9,96,128]{2,1,0:T(8,128)S(1)} %pad_maximum_fusion.6), channel_id=1, source_target_pairs={{16,0},{32,16},{48,32},{64,48},{80,64},{96,80},{112,96},{128,112},... | collective-permute-start | bytes 1327112 | tf_op jit(solution)/shard_map/ppermute | solution.py:182
  59.9 17.6 %collective-permute-start.1 = (f32[8,96,128]{2,1,0:T(8,128)}, f32[8,96,128]{2,1,0:T(8,128)S(1)}, u32[]{:S(2)}, u32[]{:S(2)}) collective-permute-start(f32[8,96,128]{2,1,0:T(8,128)} %get-tuple-element.38), channel_id=1, source_target_pairs={{0,16},{16,32},{32,48},{48,64},{64,80},{80,96},{96,112},{112,128},... | collective-permute-start | bytes 1179656 | tf_op jit(solution)/shard_map/ppermute | solution.py:178
  77.6 10.7 %collective-permute-start.4 = (f32[8,11,2,128]{3,2,1,0:T(2,128)S(1)}, f32[8,11,2,128]{3,2,1,0:T(2,128)S(1)}, u32[]{:S(2)}, u32[]{:S(2)}) collective-permute-start(f32[8,11,2,128]{3,2,1,0:T(2,128)S(1)} %pad_maximum_fusion.20), channel_id=1, source_target_pairs={{1,0},{2,1},{3,2},{4,3},{5,4},{6,5},{7,6},{8,7},{9,8},{10,9},{11,1... | collective-permute-start | bytes 270344 | tf_op jit(solution)/shard_map/ppermute | solution.py:195
  82.0 6.2 %collective-permute-start.3 = (f32[8,11,1,128]{3,2,1,0:T(1,128)S(1)}, f32[8,11,1,128]{3,2,1,0:T(1,128)S(1)}, u32[]{:S(2)}, u32[]{:S(2)}) collective-permute-start(f32[8,11,1,128]{3,2,1,0:T(1,128)S(1)} %pad_maximum_fusion.23), channel_id=1, source_target_pairs={{0,1},{1,2},{2,3},{3,4},{4,5},{5,6},{6,7},{7,8},{8,9},{9,10},{10,1... | collective-permute-start | bytes 135176 | tf_op jit(solution)/shard_map/ppermute | solution.py:192
  92.1 5.2 %collective-permute-start.7 = (f32[16,99,128]{2,0,1:T(8,128)S(1)}, f32[16,99,128]{2,0,1:T(8,128)S(1)}, u32[]{:S(2)}, u32[]{:S(2)}) collective-permute-start(f32[16,99,128]{2,0,1:T(8,128)S(1)} %copy.63), channel_id=1, source_target_pairs={{16,0},{224,240},{17,1},{225,241},{18,2},{226,242},{19,3},{227,243... | collective-permute-start | bytes 2433032 | tf_op jit(solution)/shard_map/ppermute | solution.py:203
  93.5 5.5 %slice-start.2 = ((s8[4685824]{0:T(1024)(128)(4,1)}), s8[491520]{0:T(1024)(128)(4,1)S(1)}, s32[]{:S(2)}) async-start(s8[4685824]{0:T(1024)(128)(4,1)} %bitcast.98), calls=%async_computation.4 | async-start | bytes 983040
  94.5 2.7 %slice-start = ((s8[4685824]{0:T(1024)(128)(4,1)}), s8[4194304]{0:T(1024)(128)(4,1)S(1)}, s32[]{:S(2)}) async-start(s8[4685824]{0:T(1024)(128)(4,1)} %bitcast.96), calls=%async_computation.2 | async-start | bytes 8388608
  94.6 2.6 %slice-start.1 = ((s8[4685824]{0:T(1024)(128)(4,1)}), s8[491520]{0:T(1024)(128)(4,1)S(1)}, s32[]{:S(2)}) async-start(s8[4685824]{0:T(1024)(128)(4,1)} %bitcast.96), calls=%async_computation.3 | async-start | bytes 983040
  94.6 4.4 %slice-start.3 = ((s8[4685824]{0:T(1024)(128)(4,1)}), s8[4194304]{0:T(1024)(128)(4,1)S(1)}, s32[]{:S(2)}) async-start(s8[4685824]{0:T(1024)(128)(4,1)} %bitcast.98), calls=%async_computation.5 | async-start | bytes 8388608
  94.6 11.0 %collective-permute-start.5 = (f32[5,99,128]{2,0,1:T(8,128)S(1)}, f32[5,99,128]{2,0,1:T(8,128)S(1)}, u32[]{:S(2)}, u32[]{:S(2)}) collective-permute-start(f32[5,99,128]{2,0,1:T(8,128)S(1)} %pad_maximum_fusion.7), channel_id=1, source_target_pairs={{0,8},{1,9},{2,10},{3,11},{4,12},{5,13},{6,14},{7,15},{8,0},{9,1},... | collective-permute-start | bytes 760328 | tf_op jit(solution)/shard_map/ppermute | solution.py:213
  95.5 10.1 %collective-permute-start.6 = (f32[5,99,128]{2,0,1:T(8,128)S(1)}, f32[5,99,128]{2,0,1:T(8,128)S(1)}, u32[]{:S(2)}, u32[]{:S(2)}) collective-permute-start(f32[5,99,128]{2,0,1:T(8,128)S(1)} %pad_maximum_fusion.7), channel_id=1, source_target_pairs={{16,8},{17,9},{18,10},{19,11},{20,12},{21,13},{22,14},{23,15},{24,... | collective-permute-start | bytes 760328 | tf_op jit(solution)/shard_map/ppermute | solution.py:218
  105.5 0.7 copy-start.4

commit v8 on v6

--- a/solution.py
+++ b/solution.py
@@ -147,34 +147,6 @@
     work = jnp.where(helper, handed, cap_of(first_half))
     per_device = half // phi_count
     cycle = lax.all_to_all(work, "phi", split_axis=0, concat_axis=1, tiled=True)
-    analysis = fourier_rows(jnp.arange(cycle_len, dtype=jnp.int32), cycle_len)
-    dst_cols = (
-        jnp.arange(phi_count, dtype=jnp.int32)[:, None] * npc
-        - 1
-        + jnp.arange(npc + 3, dtype=jnp.int32)[None, :]
-    ) % cycle_len
-    synthesis = fourier_rows(dst_cols, cycle_len)
-
-    pole_pick = jnp.where(north_side, 0, 1).astype(jnp.int32)
-    level_row = lax.dynamic_index_in_dim(levels, pole_pick, 0, keepdims=False)
-    slot_ids = p * per_device + jnp.arange(per_device, dtype=jnp.int32)
-    row_ids = slot_ids // (channels // 2)
-    slot_levels = jnp.sum(
-        jnp.where(
-            row_ids[:, None] == jnp.arange(CAP, dtype=jnp.int32)[None, :], level_row[None, :], 0
-        ),
-        axis=1,
-    )
-    limits = jnp.right_shift(jnp.int32(KMAX), slot_levels)
-    column_order = jnp.arange(2 * KMAX, dtype=jnp.int32) % KMAX
-    column_weight = jnp.where(column_order == 0, 1.0 / cycle_len, 2.0 / cycle_len).astype(
-        jnp.float32
-    )
-    kept_weight = jnp.where(column_order[None, :] < limits[:, None], column_weight[None, :], 0.0)
-    coeffs = jnp.einsum("smr,mn->snr", cycle, analysis, precision=lax.Precision.HIGHEST)
-    coeffs = coeffs * kept_weight[:, :, None]
-    out = jnp.einsum("snr,kjn->ksjr", coeffs, synthesis, precision=lax.Precision.HIGHEST)
-    out = out.reshape(phi_count * per_device, npc + 3, nr)
     low_halo = lax.ppermute(
         combined[:, ct - 1], "theta", [(i, i + 1) for i in range(theta_count - 1)]
     )
@@ -197,6 +169,35 @@
     )
     early = jnp.concatenate([left_cols, rows_ext, right_cols], axis=2)
 
+    cycle, early = lax.optimization_barrier((cycle, early))
+    analysis = fourier_rows(jnp.arange(cycle_len, dtype=jnp.int32), cycle_len)
+    dst_cols = (
+        jnp.arange(phi_count, dtype=jnp.int32)[:, None] * npc
+        - 1
+        + jnp.arange(npc + 3, dtype=jnp.int32)[None, :]
+    ) % cycle_len
+    synthesis = fourier_rows(dst_cols, cycle_len)
+
+    pole_pick = jnp.where(north_side, 0, 1).astype(jnp.int32)
+    level_row = lax.dynamic_index_in_dim(levels, pole_pick, 0, keepdims=False)
+    slot_ids = p * per_device + jnp.arange(per_device, dtype=jnp.int32)
+    row_ids = slot_ids // (channels // 2)
+    slot_levels = jnp.sum(
+        jnp.where(
+            row_ids[:, None] == jnp.arange(CAP, dtype=jnp.int32)[None, :], level_row[None, :], 0
+        ),
+        axis=1,
+    )
+    limits = jnp.right_shift(jnp.int32(KMAX), slot_levels)
+    column_order = jnp.arange(2 * KMAX, dtype=jnp.int32) % KMAX
+    column_weight = jnp.where(column_order == 0, 1.0 / cycle_len, 2.0 / cycle_len).astype(
+        jnp.float32
+    )
+    kept_weight = jnp.where(column_order[None, :] < limits[:, None], column_weight[None, :], 0.0)
+    coeffs = jnp.einsum("smr,mn->snr", cycle, analysis, precision=lax.Precision.HIGHEST)
+    coeffs = coeffs * kept_weight[:, :, None]
+    out = jnp.einsum("snr,kjn->ksjr", coeffs, synthesis, precision=lax.Precision.HIGHEST)
+    out = out.reshape(phi_count * per_device, npc + 3, nr)
     mine = lax.all_to_all(out, "phi", split_axis=0, concat_axis=0, tiled=True)
 
     from_helper = lax.ppermute(mine, "theta", pairs_in)

time: 116 us -> 113 us (0.974)
  blocking collectives: 0 us -> 26.2 us
  waiting for transfers between devices: 28.2 us -> 5.3 us
  local copies, waits for them, and re-layouts: 16.2 us -> 13 us
  starting transfers between devices: 34.2 us -> 31.3 us
    all_to_all x0 -> x1, blocking collectives: none -> 26.2 us  [local(): mine = lax.all_to_all(out, 'phi', split_axis=0, concat_axis=0, tiled=True)]
    ppermute x1, waiting for transfers between devices: 12.8 us -> 0.01 us  [local(): lax.ppermute(up_send, 'theta', [(i + 1, i) for i in range(theta_count - 1)])]
    all_to_all x1, waiting for transfers between devices: 6.66 us -> 0.01 us  [local(): cycle = lax.all_to_all(work, 'phi', split_axis=0, concat_axis=1, tiled=True)]
    all_to_all x1 -> x0, starting transfers between devices: 6.4 us -> none  [local(): mine = lax.all_to_all(out, 'phi', split_axis=0, concat_axis=0, tiled=True)]
    ppermute x1, waiting for transfers between devices: 3.42 us -> 0.01 us  [local(): handed = lax.ppermute(cap_of(second_half), 'theta', pairs_out)]
    ppermute x1, starting transfers between devices: 2.76 us -> 6.05 us  [local(): lax.ppermute(up_send, 'theta', [(i + 1, i) for i in range(theta_count - 1)])]
    ppermute x1, starting transfers between devices: 4.31 us -> 2.18 us  [local(): lax.ppermute(combined[:, ct - 1], 'theta', [(i, i + 1) for i in range(the...]
    all_to_all x1, local copies, waits for them, and re-layouts: 2.2 us -> 0.16 us  [local(): mine = lax.all_to_all(out, 'phi', split_axis=0, concat_axis=0, tiled=True)]
  transfers between devices with their start and end apart: 10 -> 9, of which waited for: 4 -> 1; matrix products, arithmetic and copies ran while one was open for 27% -> 26% of each run, Pallas kernels for 0% -> 0%
where the time goes in v8:
time: 113 us; the launch traced here: 112 us
  starting transfers between devices  31.3 us (28%)
  other arithmetic  28.7 us (25%)
  blocking collectives  26.2 us (23%)
  local copies, waits for them, and re-layouts  13 us (12%)
  matrix products  5.83 us (5%)
  waiting for transfers between devices  5.3 us (5%)
  between operations  2.08 us (2%)
    all_to_all x1, blocking collectives, local(): mine = lax.all_to_all(out, 'phi', split_axis=0, concat_axis=0, tiled=True)  26.2 us
    all_to_all x1, starting transfers between devices, local(): cycle = lax.all_to_all(work, 'phi', split_axis=0, concat_axis=1, tiled=True)  8.91 us
    ppermute x1, starting transfers between devices, local(): lax.ppermute(up_send, 'theta', [(i + 1, i) for i in range(theta_count - 1)])  6.05 us
    cos x1, other arithmetic, fourier_rows(): return jnp.concatenate([jnp.cos(angle), jnp.sin(angle)], axis=-1)  5.34 us
    ppermute x1, waiting for transfers between devices, local(): lax.ppermute(rows_ext[:, :, npc - 1:], 'phi', [(i, (i + 1) % phi_count) f...  5.28 us
    dot_general x1, matrix products, local(): jnp.einsum('smr,mn->snr', cycle, analysis, precision=lax.Precision.HIGHEST)  4.34 us
    sin x1, other arithmetic, fourier_rows(): return jnp.concatenate([jnp.cos(angle), jnp.sin(angle)], axis=-1)  4.33 us
    ppermute x1, starting transfers between devices, local(): lax.ppermute(ghost_send, both, [(h * phi_count + b, a * phi_count + (b +...  4.3 us
  transfers between devices with their start and end apart: 9, of which 1 were waited for; matrix products, arithmetic and copies ran while one was open for 26% of the time, Pallas kernels for 0%

profile of v8, /device:TPU:1, one launch (start us, length us, event | category | flops | bytes accessed | tf_op | source)
XLA Modules:
  0.0 112.5 jit_solution(9987727483488787418)
XLA Ops:
  0.6 1.0 slice_bitcast_fusion.3
  1.7 2.4 %fusion.26 = f32[4,4,96,128]{3,2,0,1:T(8,128)} fusion(f32[1,8,96,128]{3,2,0,1:T(8,128)S(1)} %slice_bitcast_fusion.3, pred[]{:T(512)S(6)} %eq.75, f32[3,8,96,128]{3,2,1,0:T(8,128)} %param.7), kind=kLoop, calls=%fused_computation.36 | loop fusion | flops 589824 | bytes 2359297 | tf_op jit(solution)/shard_map/jit(_where)/select_n | solution.py:141
  4.0 1.4 %collective-permute-start = (f32[16,96,128]{2,1,0:T(8,128)}, f32[16,96,128]{2,1,0:T(8,128)}, u32[]{:S(2)}, u32[]{:S(2)}) collective-permute-start(f32[16,96,128]{2,1,0:T(8,128)} %bitcast.1), channel_id=1, source_target_pairs={{0,16},{240,224},{1,17},{241,225},{2,18},{242,226},{3,19},{243,227... | collective-permute-start | bytes 2359304 | tf_op jit(solution)/shard_map/ppermute | solution.py:146
  7.4 0.8 pad_maximum_fusion.6
  8.2 6.1 %collective-permute-start.2 = (f32[9,96,128]{2,1,0:T(8,128)}, f32[9,96,128]{2,1,0:T(8,128)}, u32[]{:S(2)}, u32[]{:S(2)}) collective-permute-start(f32[9,96,128]{2,1,0:T(8,128)} %pad_maximum_fusion.6), channel_id=1, source_target_pairs={{16,0},{32,16},{48,32},{64,48},{80,64},{96,80},{112,96},{128,112},... | collective-permute-start | bytes 1327112 | tf_op jit(solution)/shard_map/ppermute | solution.py:154
  14.3 2.2 %collective-permute-start.1 = (f32[8,96,128]{2,1,0:T(8,128)}, f32[8,96,128]{2,1,0:T(8,128)S(1)}, u32[]{:S(2)}, u32[]{:S(2)}) collective-permute-start(f32[8,96,128]{2,1,0:T(8,128)} %get-tuple-element.38), channel_id=1, source_target_pairs={{0,16},{16,32},{32,48},{48,64},{64,80},{80,96},{96,112},{112,128},... | collective-permute-start | bytes 1179656 | tf_op jit(solution)/shard_map/ppermute | solution.py:150
  16.4 0.9 slice.680
  17.4 1.5 %fusion.24 = (f32[4,4,96,128]{3,2,1,0:T(8,128)S(1)}, f32[4,4,96,128]{3,2,1,0:T(8,128)S(1)}) fusion(f32[2,8,96,128]{3,2,1,0:T(8,128)} %param.5, f32[2,8,96,128]{3,2,1,0:T(8,128)} %slice.680), kind=kLoop, calls=%fused_computation.34 | loop fusion | flops 393216 | bytes 3145728 | tf_op jit(solution)/shard_map/concatenate | solution.py:137
  19.1 2.1 %bitcast_select_fusion = f32[16,96,128]{2,1,0:T(8,128)} fusion(f32[16,96,128]{2,1,0:T(8,128)} %collective-permute-done, f32[4,4,96,128]{3,2,0,1:T(8,128)S(1)} %copy_select_fusion, pred[]{:T(512)S(6)} %or.6), kind=kLoop, calls=%fused_computation.41 | loop fusion | flops 196608 | bytes 2359297 | tf_op jit(solution)/shard_map/jit(_where)/select_n | solution.py:147
  21.2 8.9 %all-to-all-start = ((f32[16,96,128]{2,1,0:T(8,128)}), f32[16,96,128]{2,1,0:T(8,128)}, u32[]{:S(2)}, u32[]{:S(2)}) async-start(f32[16,96,128]{2,1,0:T(8,128)} %bitcast_select_fusion), calls=%async_computation | async-start | bytes 1572864 | tf_op jit(solution)/shard_map/all_to_all | solution.py:149
  30.1 5.3 %fusion.20 = (f32[16,99,128]{2,1,0:T(8,128)}, f32[16,99,128]{2,1,0:T(8,128)}) fusion(s32[16,99]{1,0:T(8,128)S(1)} %add_select_fusion.2), kind=kLoop, calls=%fused_computation.30 | loop fusion | flops 1824768 | bytes 1628352 | tf_op jit(solution)/shard_map/cos | solution.py:110
  36.8 4.3 %fusion.30 = (f32[1536,128]{1,0:T(8,128)}, f32[1536,128]{1,0:T(8,128)}) fusion(), kind=kLoop, calls=%fused_computation.46 | loop fusion | flops 1769472 | bytes 1572864 | tf_op jit(solution)/shard_map/sin | solution.py:110
  42.0 1.0 slice_bitcast_fusion
  43.1 3.5 %collective-permute-start.4 = (f32[8,11,2,128]{3,2,1,0:T(2,128)S(1)}, f32[8,11,2,128]{3,2,1,0:T(2,128)S(1)}, u32[]{:S(2)}, u32[]{:S(2)}) collective-permute-start(f32[8,11,2,128]{3,2,1,0:T(2,128)S(1)} %pad_maximum_fusion.20), channel_id=1, source_target_pairs={{1,0},{2,1},{3,2},{4,3},{5,4},{6,5},{7,6},{8,7},{9,8},{10,9},{11,1... | collective-permute-start | bytes 270344 | tf_op jit(solution)/shard_map/ppermute | solution.py:167
  46.8 5.3 %collective-permute-done.3 = f32[8,11,1,128]{3,2,1,0:T(1,128)S(1)} collective-permute-done((f32[8,11,1,128]{3,2,1,0:T(1,128)S(1)}, f32[8,11,1,128]{3,2,1,0:T(1,128)S(1)}, u32[]{:S(2)}, u32[]{:S(2)}) %collective-permute-start.3) | collective-permute-done | bytes 45088 | tf_op jit(solution)/shard_map/ppermute | solution.py:164
  52.1 2.6 %pad_maximum_fusion = f32[8,11,99,128]{3,2,1,0:T(8,128)} fusion(f32[8,11,2,128]{3,2,1,0:T(2,128)S(1)} %collective-permute-done.4, f32[8,1,96,128]{3,2,1,0:T(8,128)S(1)} %broadcast_in_dim_broadcast_in_dim.4, f32[8,1,96,128]{3,2,1,0:T(8,128)S(1)} %slice_bitcast_fusion, f32[8,8,96,128]{3,2,1,0:T(8,128)S(1)} %constant_dynamic-update-slice_fusion, ...), kind=kLoop, calls=%fused_computation | loop fusion | flops 5575680 | bytes 8921088 | tf_op jit(solution)/shard_map/concatenate | solution.py:170
  54.7 4.3 %fusion.12 = f32[256,128,1]{1,0,2:T(8,128)S(1)} fusion(f32[1536,128]{1,0:T(8,128)} %get-tuple-element.128, f32[1536,128]{1,0:T(8,128)} %get-tuple-element.129, f32[1,1536,128]{2,1,0:T(8,128)} %bitcast.4, f32[256]{0:T(256)S(1)} %compare_select_fusion.1), kind=kOutput, calls=%fused_computation.22 | convolution fusion | flops 604405760 | bytes 2491392 | tf_op jit(solution)/shard_map/smr,mn->snr/dot_general | solution.py:197
  59.0 1.5 %fusion.1 = f32[16,99,128]{2,1,0:T(8,128)S(1)} fusion(f32[256,128,1]{1,0,2:T(8,128)S(1)} %fusion.12, f32[16,99,128]{2,1,0:T(8,128)S(1)} %copy-done.3, f32[16,99,128]{2,1,0:T(8,128)S(1)} %copy-done.2), kind=kOutput, calls=%fused_computation.4 | convolution fusion | flops 623259648 | bytes 2564096 | tf_op jit(solution)/shard_map/snr,kjn->ksjr/dot_general | solution.py:199
  60.5 26.2 %all_to_all.17 = f32[16,99,128]{2,1,0:T(8,128)S(1)} all-to-all(f32[16,99,128]{2,1,0:T(8,128)S(1)} %fusion.1), channel_id=1, replica_groups=mesh['theta'=16,'phi'=16] {'phi'}, dimensions={0} | all-to-all | bytes 1622016 | tf_op jit(solution)/shard_map/all_to_all | solution.py:201
  86.9 4.1 %collective-permute-start.7 = (f32[16,99,128]{2,0,1:T(8,128)S(1)}, f32[16,99,128]{2,0,1:T(8,128)S(1)}, u32[]{:S(2)}, u32[]{:S(2)}) collective-permute-start(f32[16,99,128]{2,0,1:T(8,128)S(1)} %copy.63), channel_id=1, source_target_pairs={{16,0},{224,240},{17,1},{225,241},{18,2},{226,242},{19,3},{227,243... | collective-permute-start | bytes 2433032 | tf_op jit(solution)/shard_map/ppermute | solution.py:203
  91.1 2.2 %slice-done.1 = s8[4194304]{0:T(1024)(128)(4,1)S(1)} async-done(((s8[4685824]{0:T(1024)(128)(4,1)}), s8[4194304]{0:T(1024)(128)(4,1)S(1)}, s32[]{:S(2)}) %slice-start.1) | async-done | bytes 4194328
  94.3 4.3 %collective-permute-start.6 = (f32[5,99,128]{2,0,1:T(8,128)S(1)}, f32[5,99,128]{2,0,1:T(8,128)S(1)}, u32[]{:S(2)}, u32[]{:S(2)}) collective-permute-start(f32[5,99,128]{2,0,1:T(8,128)S(1)} %pad_maximum_fusion.7), channel_id=1, source_target_pairs={{16,8},{17,9},{18,10},{19,11},{20,12},{21,13},{22,14},{23,15},{24,... | collective-permute-start | bytes 760328 | tf_op jit(solution)/shard_map/ppermute | solution.py:218
  110.2 1.0 maximum_select_fusion.3
  111.3 1.2 %maximum_select_fusion.2 = f32[3,8,96,128]{3,2,1,0:T(8,128)} fusion(f32[3,6,96,128]{3,2,1,0:T(8,128)S(1)} %pad_maximum_fusion.2, f32[1,2,96,128]{3,2,1,0:T(8,128)S(1)} %get-tuple-element.121, f32[1,2,96,128]{3,2,1,0:T(8,128)S(1)} %get-tuple-element.120, f32[1,2,96,128]{3,2,1,0:T(8,128)S(1)} %fusion.90, pred[]{:T(512)S(6)} %eq.75), kind=kLoop, calls=%fused_computation.20 | loop fusion | flops 2064384 | bytes 2359297 | tf_op jit(solution)/shard_map/jit(_where)/select_n | solution.py:264
  (125 shorter events, 16.3 us)
Async XLA Ops:
  1.7 4.6 %copy-start.4 = (f32[2,8,96,128]{3,2,1,0:T(8,128)S(1)}, f32[2,8,96,128]{3,2,1,0:T(8,128)}, u32[]{:S(2)}) copy-start(f32[2,8,96,128]{3,2,1,0:T(8,128)} %param.5) | copy-start | bytes 2359300
  1.7 4.7 %copy-start.1 = (f32[3,8,96,128]{3,2,1,0:T(8,128)S(1)}, f32[3,8,96,128]{3,2,1,0:T(8,128)}, u32[]{:S(2)}) copy-start(f32[3,8,96,128]{3,2,1,0:T(8,128)} %param.6) | copy-start | bytes 3538948
  4.0 2.4 %copy-start = (f32[3,8,96,128]{3,2,1,0:T(8,128)S(1)}, f32[3,8,96,128]{3,2,1,0:T(8,128)}, u32[]{:S(2)}) copy-start(f32[3,8,96,128]{3,2,1,0:T(8,128)} %param.7) | copy-start | bytes 3538948
  4.0 15.0 %collective-permute-start = (f32[16,96,128]{2,1,0:T(8,128)}, f32[16,96,128]{2,1,0:T(8,128)}, u32[]{:S(2)}, u32[]{:S(2)}) collective-permute-start(f32[16,96,128]{2,1,0:T(8,128)} %bitcast.1), channel_id=1, source_target_pairs={{0,16},{240,224},{1,17},{241,225},{2,18},{242,226},{3,19},{243,227... | collective-permute-start | bytes 2359304 | tf_op jit(solution)/shard_map/ppermute | solution.py:146
  8.2 33.0 %collective-permute-start.2 = (f32[9,96,128]{2,1,0:T(8,128)}, f32[9,96,128]{2,1,0:T(8,128)}, u32[]{:S(2)}, u32[]{:S(2)}) collective-permute-start(f32[9,96,128]{2,1,0:T(8,128)} %pad_maximum_fusion.6), channel_id=1, source_target_pairs={{16,0},{32,16},{48,32},{64,48},{80,64},{96,80},{112,96},{128,112},... | collective-permute-start | bytes 1327112 | tf_op jit(solution)/shard_map/ppermute | solution.py:154
  14.3 28.8 %collective-permute-start.1 = (f32[8,96,128]{2,1,0:T(8,128)}, f32[8,96,128]{2,1,0:T(8,128)S(1)}, u32[]{:S(2)}, u32[]{:S(2)}) collective-permute-start(f32[8,96,128]{2,1,0:T(8,128)} %get-tuple-element.38), channel_id=1, source_target_pairs={{0,16},{16,32},{32,48},{48,64},{64,80},{80,96},{96,112},{112,128},... | collective-permute-start | bytes 1179656 | tf_op jit(solution)/shard_map/ppermute | solution.py:150
  19.0 16.4 %copy-start.6 = (s32[2,4]{1,0:T(2,128)S(1)}, s32[2,4]{1,0:T(2,128)}, u32[]{:S(2)}) copy-start(s32[2,4]{1,0:T(2,128)} %param.8) | copy-start | bytes 100
  21.2 33.5 %all-to-all-start = ((f32[16,96,128]{2,1,0:T(8,128)}), f32[16,96,128]{2,1,0:T(8,128)}, u32[]{:S(2)}, u32[]{:S(2)}) async-start(f32[16,96,128]{2,1,0:T(8,128)} %bitcast_select_fusion), calls=%async_computation | async-start | bytes 1572864 | tf_op jit(solution)/shard_map/all_to_all | solution.py:149
  43.1 8.9 %collective-permute-start.4 = (f32[8,11,2,128]{3,2,1,0:T(2,128)S(1)}, f32[8,11,2,128]{3,2,1,0:T(2,128)S(1)}, u32[]{:S(2)}, u32[]{:S(2)}) collective-permute-start(f32[8,11,2,128]{3,2,1,0:T(2,128)S(1)} %pad_maximum_fusion.20), channel_id=1, source_target_pairs={{1,0},{2,1},{3,2},{4,3},{5,4},{6,5},{7,6},{8,7},{9,8},{10,9},{11,1... | collective-permute-start | bytes 270344 | tf_op jit(solution)/shard_map/ppermute | solution.py:167
  46.7 5.4 %collective-permute-start.3 = (f32[8,11,1,128]{3,2,1,0:T(1,128)S(1)}, f32[8,11,1,128]{3,2,1,0:T(1,128)S(1)}, u32[]{:S(2)}, u32[]{:S(2)}) collective-permute-start(f32[8,11,1,128]{3,2,1,0:T(1,128)S(1)} %pad_maximum_fusion.23), channel_id=1, source_target_pairs={{0,1},{1,2},{2,3},{3,4},{4,5},{5,6},{6,7},{7,8},{8,9},{9,10},{10,1... | collective-permute-start | bytes 135176 | tf_op jit(solution)/shard_map/ppermute | solution.py:164
  54.7 4.4 %copy-start.2 = (f32[16,99,128]{2,1,0:T(8,128)S(1)}, f32[16,99,128]{2,1,0:T(8,128)}, u32[]{:S(2)}) copy-start(f32[16,99,128]{2,1,0:T(8,128)} %get-tuple-element.122) | copy-start | bytes 2433028
  54.7 4.4 %copy-start.3 = (f32[16,99,128]{2,1,0:T(8,128)S(1)}, f32[16,99,128]{2,1,0:T(8,128)}, u32[]{:S(2)}) copy-start(f32[16,99,128]{2,1,0:T(8,128)} %get-tuple-element.123) | copy-start | bytes 2433028
  86.7 4.3 %slice-start = ((s8[4685824]{0:T(1024)(128)(4,1)}), s8[491520]{0:T(1024)(128)(4,1)S(1)}, s32[]{:S(2)}) async-start(s8[4685824]{0:T(1024)(128)(4,1)} %bitcast.98), calls=%async_computation.2 | async-start | bytes 983040
  86.9 11.7 %collective-permute-start.7 = (f32[16,99,128]{2,0,1:T(8,128)S(1)}, f32[16,99,128]{2,0,1:T(8,128)S(1)}, u32[]{:S(2)}, u32[]{:S(2)}) collective-permute-start(f32[16,99,128]{2,0,1:T(8,128)S(1)} %copy.63), channel_id=1, source_target_pairs={{16,0},{224,240},{17,1},{225,241},{18,2},{226,242},{19,3},{227,243... | collective-permute-start | bytes 2433032 | tf_op jit(solution)/shard_map/ppermute | solution.py:203
  91.0 2.2 %slice-start.1 = ((s8[4685824]{0:T(1024)(128)(4,1)}), s8[4194304]{0:T(1024)(128)(4,1)S(1)}, s32[]{:S(2)}) async-start(s8[4685824]{0:T(1024)(128)(4,1)} %bitcast.98), calls=%async_computation.3 | async-start | bytes 8388608
  91.0 8.1 %slice-start.2 = ((s8[4685824]{0:T(1024)(128)(4,1)}), s8[4194304]{0:T(1024)(128)(4,1)S(1)}, s32[]{:S(2)}) async-start(s8[4685824]{0:T(1024)(128)(4,1)} %bitcast.100), calls=%async_computation.4 | async-start | bytes 8388608
  93.2 6.0 %slice-start.3 = ((s8[4685824]{0:T(1024)(128)(4,1)}), s8[491520]{0:T(1024)(128)(4,1)S(1)}, s32[]{:S(2)}) async-start(s8[4685824]{0:T(1024)(128)(4,1)} %bitcast.100), calls=%async_computation.5 | async-start | bytes 983040
  93.5 12.3 %collective-permute-start.5 = (f32[5,99,128]{2,0,1:T(8,128)S(1)}, f32[5,99,128]{2,0,1:T(8,128)S(1)}, u32[]{:S(2)}, u32[]{:S(2)}) collective-permute-start(f32[5,99,128]{2,0,1:T(8,128)S(1)} %pad_maximum_fusion.7), channel_id=1, source_target_pairs={{0,8},{1,9},{2,10},{3,11},{4,12},{5,13},{6,14},{7,15},{8,0},{9,1},... | collective-permute-start | bytes 760328 | tf_op jit(solution)/shard_map/ppermute | solution.py:213
  94.3 11.5 %collective-permute-start.6 = (f32[5,99,128]{2,0,1:T(8,128)S(1)}, f32[5,99,128]{2,0,1:T(8,128)S(1)}, u32[]{:S(2)}, u32[]{:S(2)}) collective-permute-start(f32[5,99,128]{2,0,1:T(8,128)S(1)} %pad_maximum_fusion.7), channel_id=1, source_target_pairs={{16,8},{17,9},{18,10},{19,11},{20,12},{21,13},{22,14},{23,15},{24,... | collective-permute-start | bytes 760328 | tf_op jit(solution)/shard_map/ppermute | solution.py:218
  105.6 0.7 copy-start.5

commit v9 on v4

--- a/solution.py
+++ b/solution.py
@@ -193,9 +193,9 @@
         jnp.float32
     )
     kept_weight = jnp.where(column_order[None, :] < limits[:, None], column_weight[None, :], 0.0)
-    coeffs = jnp.einsum("smr,mn->snr", cycle, analysis, precision=lax.Precision.HIGHEST)
+    coeffs = jnp.einsum("smr,mn->snr", cycle, analysis, precision=lax.Precision.HIGH)
     coeffs = coeffs * kept_weight[:, :, None]
-    out = jnp.einsum("snr,kjn->ksjr", coeffs, synthesis, precision=lax.Precision.HIGHEST)
+    out = jnp.einsum("snr,kjn->ksjr", coeffs, synthesis, precision=lax.Precision.HIGH)
     out = out.reshape(phi_count * per_device, npc + 3, nr)
     mine = lax.all_to_all(out, "phi", split_axis=0, concat_axis=0, tiled=True)
 

time: 111 us -> 110 us (level)
  matrix products: 6.74 us -> 4.86 us
    dot_general x2, matrix products: 6.74 us -> 4.86 us  [the longest x1 3.13 us: local(): jnp.einsum('smr,mn->snr', cycle, analysis, precision=lax.Precision.HIGH)]
where the time goes in v9:
time: 110 us; the launch traced here: 108 us
  starting transfers between devices  31.2 us (28%)
  other arithmetic  30.1 us (27%)
  waiting for transfers between devices  23.3 us (21%)
  local copies, waits for them, and re-layouts  17.2 us (16%)
  matrix products  4.86 us (4%)
  between operations  1.85 us (2%)
    ppermute x1, waiting for transfers between devices, local(): lax.ppermute(up_send, 'theta', [(i + 1, i) for i in range(theta_count - 1)])  11.9 us
    all_to_all x1, starting transfers between devices, local(): cycle = lax.all_to_all(work, 'phi', split_axis=0, concat_axis=1, tiled=True)  7.97 us
    all_to_all x1, waiting for transfers between devices, local(): cycle = lax.all_to_all(work, 'phi', split_axis=0, concat_axis=1, tiled=True)  6.65 us
    all_to_all x1, starting transfers between devices, local(): mine = lax.all_to_all(out, 'phi', split_axis=0, concat_axis=0, tiled=True)  6.4 us
    cos x1, other arithmetic, fourier_rows(): return jnp.concatenate([jnp.cos(angle), jnp.sin(angle)], axis=-1)  5.26 us
    sin x1, other arithmetic, fourier_rows(): return jnp.concatenate([jnp.cos(angle), jnp.sin(angle)], axis=-1)  4.36 us
    ppermute x1, starting transfers between devices, local(): lax.ppermute(combined[:, ct - 1], 'theta', [(i, i + 1) for i in range(the...  4.3 us
    another operation x6, other arithmetic, advance(): return (jnp.stack(densities), jnp.stack([new_radial, new_theta, new_phi]))  4.05 us
  transfers between devices with their start and end apart: 10, of which 5 were waited for; matrix products, arithmetic and copies ran while one was open for 24% of the time, Pallas kernels for 0%

profile of v9, /device:TPU:1, one launch (start us, length us, event | category | flops | bytes accessed | tf_op | source)
XLA Modules:
  0.0 108.5 jit_solution(17639051637672326137)
XLA Ops:
  1.8 1.3 %fusion.26 = f32[4,4,96,128]{3,2,0,1:T(8,128)S(1)} fusion(f32[1,8,96,128]{3,2,0,1:T(8,128)S(1)} %slice_bitcast_fusion.11, pred[]{:T(512)S(6)} %eq.61, f32[3,8,96,128]{3,2,1,0:T(8,128)} %param.7), kind=kLoop, calls=%fused_computation.34 | loop fusion | flops 589824 | bytes 2359297 | tf_op jit(solution)/shard_map/jit(_where)/select_n | solution.py:163
  6.0 3.4 %collective-permute-done.4 = f32[16,96,128]{2,1,0:T(8,128)S(1)} collective-permute-done((f32[16,96,128]{2,1,0:T(8,128)S(1)}, f32[16,96,128]{2,1,0:T(8,128)S(1)}, u32[]{:S(2)}, u32[]{:S(2)}) %collective-permute-start.4) | collective-permute-done | bytes 786464 | tf_op jit(solution)/shard_map/ppermute | solution.py:168
  10.4 8.0 %all-to-all-start = ((f32[16,96,128]{2,1,0:T(8,128)}), f32[16,96,128]{2,1,0:T(8,128)}, u32[]{:S(2)}, u32[]{:S(2)}) async-start(f32[16,96,128]{2,1,0:T(8,128)} %bitcast_select_fusion), calls=%async_computation | async-start | bytes 1572864 | tf_op jit(solution)/shard_map/all_to_all | solution.py:171
  19.6 1.4 %constant_dynamic-update-slice_fusion.1 = f32[8,8,96,128]{3,2,1,0:T(8,128)S(1)} fusion(f32[8,8,96,128]{3,2,1,0:T(8,128)S(1)} %constant_dynamic-update-slice_fusion.2, f32[3,8,96,128]{3,2,1,0:T(8,128)} %param.6), kind=kLoop, calls=%fused_computation.157 | loop fusion | bytes 2359296
  21.9 5.3 %fusion.20 = (f32[16,99,128]{2,1,0:T(8,128)}, f32[16,99,128]{2,1,0:T(8,128)}) fusion(s32[16,99]{1,0:T(8,128)S(1)} %add_select_fusion.2), kind=kLoop, calls=%fused_computation.28 | loop fusion | flops 1824768 | bytes 1628352 | tf_op jit(solution)/shard_map/cos | solution.py:110
  27.1 4.4 %fusion.29 = (f32[1536,128]{1,0:T(8,128)}, f32[1536,128]{1,0:T(8,128)}) fusion(), kind=kLoop, calls=%fused_computation.43 | loop fusion | flops 1769472 | bytes 1572864 | tf_op jit(solution)/shard_map/sin | solution.py:110
  31.5 6.7 %all-to-all-done = f32[16,96,128]{2,1,0:T(8,128)} async-done(((f32[16,96,128]{2,1,0:T(8,128)}), f32[16,96,128]{2,1,0:T(8,128)}, u32[]{:S(2)}, u32[]{:S(2)}) %all-to-all-start) | async-done | bytes 786464 | tf_op jit(solution)/shard_map/all_to_all | solution.py:171
  38.1 3.1 %fusion.12 = f32[256,128,1]{1,0,2:T(8,128)S(1)} fusion(f32[1536,128]{1,0:T(8,128)} %bitcast.11, f32[1536,128]{1,0:T(8,128)} %get-tuple-element.62, f32[1536,128]{1,0:T(8,128)} %get-tuple-element.63, f32[256]{0:T(256)S(1)} %compare_select_fusion.1), kind=kOutput, calls=%fused_computation.21 | convolution fusion | flops 302415872 | bytes 2491392 | tf_op jit(solution)/shard_map/smr,mn->snr/dot_general | solution.py:196
  41.3 1.7 %fusion.1 = f32[16,99,128]{2,1,0:T(8,128)} fusion(f32[256,128,1]{1,0,2:T(8,128)S(1)} %fusion.12, f32[16,99,128]{2,1,0:T(8,128)S(1)} %copy-done.4, f32[16,99,128]{2,1,0:T(8,128)S(1)} %copy-done.3), kind=kOutput, calls=%fused_computation.4 | convolution fusion | flops 311832576 | bytes 2564096 | tf_op jit(solution)/shard_map/snr,kjn->ksjr/dot_general | solution.py:198
  43.0 6.4 %all-to-all-start.1 = ((f32[16,99,128]{2,1,0:T(8,128)}), f32[16,99,128]{2,1,0:T(8,128)}, u32[]{:S(2)}, u32[]{:S(2)}) async-start(f32[16,99,128]{2,1,0:T(8,128)} %fusion.1), calls=%async_computation.1 | async-start | bytes 1703936 | tf_op jit(solution)/shard_map/all_to_all | solution.py:200
  49.5 1.4 %constant_dynamic-update-slice_fusion = f32[8,8,96,128]{3,2,1,0:T(8,128)S(1)} fusion(f32[8,8,96,128]{3,2,1,0:T(8,128)S(1)} %constant_dynamic-update-slice_fusion.1, f32[3,8,96,128]{3,2,1,0:T(8,128)} %param.7), kind=kLoop, calls=%fused_computation.156 | loop fusion | bytes 2359296 | tf_op jit(solution)/shard_map/concatenate | solution.py:114
  52.4 2.8 %collective-permute-start.1 = (f32[9,96,128]{2,1,0:T(8,128)}, f32[9,96,128]{2,1,0:T(8,128)}, u32[]{:S(2)}, u32[]{:S(2)}) collective-permute-start(f32[9,96,128]{2,1,0:T(8,128)} %pad_maximum_fusion.6), channel_id=1, source_target_pairs={{16,0},{32,16},{48,32},{64,48},{80,64},{96,80},{112,96},{128,112},... | collective-permute-start | bytes 1327112 | tf_op jit(solution)/shard_map/ppermute | solution.py:138
  55.2 4.3 %collective-permute-start = (f32[8,96,128]{2,1,0:T(8,128)}, f32[8,96,128]{2,1,0:T(8,128)}, u32[]{:S(2)}, u32[]{:S(2)}) collective-permute-start(f32[8,96,128]{2,1,0:T(8,128)} %get-tuple-element.14), channel_id=1, source_target_pairs={{0,16},{16,32},{32,48},{48,64},{64,80},{80,96},{96,112},{112,128},... | collective-permute-start | bytes 1179656 | tf_op jit(solution)/shard_map/ppermute | solution.py:134
  59.5 11.9 %collective-permute-done.1 = f32[9,96,128]{2,1,0:T(8,128)} collective-permute-done((f32[9,96,128]{2,1,0:T(8,128)}, f32[9,96,128]{2,1,0:T(8,128)}, u32[]{:S(2)}, u32[]{:S(2)}) %collective-permute-start.1) | collective-permute-done | bytes 442400 | tf_op jit(solution)/shard_map/ppermute | solution.py:138
  73.3 1.4 %pad_maximum_fusion.17 = f32[8,11,1,128]{3,2,1,0:T(1,128)} fusion(f32[8,1,96,128]{3,2,1,0:T(8,128)S(1)} %broadcast_in_dim_broadcast_in_dim.4, f32[8,1,96,128]{3,2,1,0:T(8,128)S(1)} %slice_bitcast_fusion.8, f32[8,8,96,128]{3,2,1,0:T(8,128)S(1)} %constant_dynamic-update-slice_fusion, f32[8,1,96,128]{3,2,1,0:T(8,128)} %bitcast.2), kind=kLoop, calls=%fused_computation.154 | loop fusion | flops 33792 | bytes 4370432 | tf_op jit(solution)/shard_map/slice | solution.py:149
  74.8 2.3 %collective-permute-start.2 = (f32[8,11,1,128]{3,2,1,0:T(1,128)}, f32[8,11,1,128]{3,2,1,0:T(1,128)}, u32[]{:S(2)}, u32[]{:S(2)}) collective-permute-start(f32[8,11,1,128]{3,2,1,0:T(1,128)} %pad_maximum_fusion.17), channel_id=1, source_target_pairs={{0,1},{1,2},{2,3},{3,4},{4,5},{5,6},{6,7},{7,8},{8,9},{9,10},{10,1... | collective-permute-start | bytes 135176 | tf_op jit(solution)/shard_map/ppermute | solution.py:148
  77.1 1.4 %pad_maximum_fusion.14 = f32[8,11,2,128]{3,2,1,0:T(2,128)} fusion(f32[8,1,96,128]{3,2,1,0:T(8,128)S(1)} %broadcast_in_dim_broadcast_in_dim.4, f32[8,1,96,128]{3,2,1,0:T(8,128)S(1)} %slice_bitcast_fusion.8, f32[8,8,96,128]{3,2,1,0:T(8,128)S(1)} %constant_dynamic-update-slice_fusion, f32[8,1,96,128]{3,2,1,0:T(8,128)} %bitcast.2), kind=kLoop, calls=%fused_computation.147 | loop fusion | flops 67584 | bytes 4415488 | tf_op jit(solution)/shard_map/concatenate | solution.py:139
  78.5 2.6 %collective-permute-start.3 = (f32[8,11,2,128]{3,2,1,0:T(2,128)}, f32[8,11,2,128]{3,2,1,0:T(2,128)}, u32[]{:S(2)}, u32[]{:S(2)}) collective-permute-start(f32[8,11,2,128]{3,2,1,0:T(2,128)} %pad_maximum_fusion.14), channel_id=1, source_target_pairs={{1,0},{2,1},{3,2},{4,3},{5,4},{6,5},{7,6},{8,7},{9,8},{10,9},{11,1... | collective-permute-start | bytes 270344 | tf_op jit(solution)/shard_map/ppermute | solution.py:151
  81.2 1.4 %copy.63 = f32[16,99,128]{2,0,1:T(8,128)S(1)} copy(f32[16,99,128]{2,1,0:T(8,128)} %all-to-all-done.1) | data formatting | bytes 1622016 | tf_op jit(solution)/shard_map/all_to_all | solution.py:200
  83.6 1.3 %collective-permute-start.6 = (f32[5,99,128]{2,0,1:T(8,128)S(1)}, f32[5,99,128]{2,0,1:T(8,128)S(1)}, u32[]{:S(2)}, u32[]{:S(2)}) collective-permute-start(f32[5,99,128]{2,0,1:T(8,128)S(1)} %pad_maximum_fusion.7), channel_id=1, source_target_pairs={{16,8},{17,9},{18,10},{19,11},{20,12},{21,13},{22,14},{23,15},{24,... | collective-permute-start | bytes 760328 | tf_op jit(solution)/shard_map/ppermute | solution.py:217
  85.6 1.8 %pad_maximum_fusion = f32[8,11,99,128]{3,2,1,0:T(8,128)S(1)} fusion(f32[8,11,2,128]{3,2,1,0:T(2,128)} %collective-permute-done.3, f32[8,1,96,128]{3,2,1,0:T(8,128)S(1)} %copy-done.2, f32[8,1,96,128]{3,2,1,0:T(8,128)S(1)} %slice_bitcast_fusion.8, f32[8,8,96,128]{3,2,1,0:T(8,128)S(1)} %constant_dynamic-update-slice_fusion, f32[8,1,96,128]{3,2,1,0:T(8,128)} %bitcast.2, ...), kind=kLoop, calls=%fused_computation | loop fusion | flops 5575680 | bytes 8921088 | tf_op jit(solution)/shard_map/concatenate | solution.py:154
  87.4 1.5 %collective-permute-start.7 = (f32[16,99,128]{2,0,1:T(8,128)S(1)}, f32[16,99,128]{2,0,1:T(8,128)S(1)}, u32[]{:S(2)}, u32[]{:S(2)}) collective-permute-start(f32[16,99,128]{2,0,1:T(8,128)S(1)} %copy.63), channel_id=1, source_target_pairs={{16,0},{224,240},{17,1},{225,241},{18,2},{226,242},{19,3},{227,243... | collective-permute-start | bytes 2433032 | tf_op jit(solution)/shard_map/ppermute | solution.py:202
  93.2 3.6 %fusion = f32[8,11,99,128]{3,2,1,0:T(8,128)} fusion(f32[8,11,99,128]{3,2,1,0:T(8,128)} %copy-done, s32[]{:T(128)S(6)} %select_n.154, f32[8,1,99,128]{3,2,1,0:T(8,128)S(1)} %slice-done, f32[8,4,99,128]{3,2,1,0:T(8,128)S(1)} %bitcast.70, f32[8,1,99,128]{3,2,1,0:T(8,128)S(1)} %copy.69, f32[8,1,99,128]{3,2,1,0:T(8,128)S(1)} %broadcast_in_dim_broadcast_in_dim.5, ...), kind=kLoop, calls=%fused_computation.2 | loop fusion | flops 3649536 | bytes 7950342 | tf_op jit(solution)/shard_map/dynamic_update_slice | solution.py:245
  96.8 2.6 %slice_bitcast_fusion.2 = (f32[11,99,128]{2,1,0:T(8,128)S(1)}, f32[11,99,128]{2,1,0:T(8,128)S(1)}, f32[11,99,128]{2,1,0:T(8,128)S(1)}, f32[11,99,128]{2,1,0:T(8,...) fusion(f32[8,11,99,128]{3,2,1,0:T(8,128)} %fusion), kind=kLoop, calls=%fused_computation.48 | loop fusion | bytes 8921088 | tf_op jit(solution)/shard_map/squeeze | solution.py:94
  (89 shorter events, 24.7 us)
Async XLA Ops:
  0.6 5.2 %slice-start.1 = ((f32[3,8,96,128]{3,2,1,0:T(8,128)}), f32[2,8,96,128]{3,2,1,0:T(8,128)S(1)}, s32[]{:S(2)}) async-start(f32[3,8,96,128]{3,2,1,0:T(8,128)} %param.6), calls=%async_computation.3 | async-start | bytes 1572864 | tf_op jit(solution)/shard_map/slice | solution.py:159
  0.6 3.8 %copy-start.7 = (s32[2,4]{1,0:T(2,128)S(1)}, s32[2,4]{1,0:T(2,128)}, u32[]{:S(2)}) copy-start(s32[2,4]{1,0:T(2,128)} %param.8) | copy-start | bytes 100
  0.7 5.1 %copy-start.5 = (f32[2,8,96,128]{3,2,1,0:T(8,128)S(1)}, f32[2,8,96,128]{3,2,1,0:T(8,128)}, u32[]{:S(2)}) copy-start(f32[2,8,96,128]{3,2,1,0:T(8,128)} %param.5) | copy-start | bytes 2359300
  3.2 6.3 %collective-permute-start.4 = (f32[16,96,128]{2,1,0:T(8,128)S(1)}, f32[16,96,128]{2,1,0:T(8,128)S(1)}, u32[]{:S(2)}, u32[]{:S(2)}) collective-permute-start(f32[16,96,128]{2,1,0:T(8,128)S(1)} %bitcast.72), channel_id=1, source_target_pairs={{0,16},{240,224},{1,17},{241,225},{2,18},{242,226},{3,19},{243,227... | collective-permute-start | bytes 2359304 | tf_op jit(solution)/shard_map/ppermute | solution.py:168
  10.4 27.7 %all-to-all-start = ((f32[16,96,128]{2,1,0:T(8,128)}), f32[16,96,128]{2,1,0:T(8,128)}, u32[]{:S(2)}, u32[]{:S(2)}) async-start(f32[16,96,128]{2,1,0:T(8,128)} %bitcast_select_fusion), calls=%async_computation | async-start | bytes 1572864 | tf_op jit(solution)/shard_map/all_to_all | solution.py:171
  38.1 3.1 %copy-start.3 = (f32[16,99,128]{2,1,0:T(8,128)S(1)}, f32[16,99,128]{2,1,0:T(8,128)}, u32[]{:S(2)}) copy-start(f32[16,99,128]{2,1,0:T(8,128)} %get-tuple-element.58) | copy-start | bytes 2433028
  38.1 3.1 %copy-start.4 = (f32[16,99,128]{2,1,0:T(8,128)S(1)}, f32[16,99,128]{2,1,0:T(8,128)}, u32[]{:S(2)}) copy-start(f32[16,99,128]{2,1,0:T(8,128)} %get-tuple-element.59) | copy-start | bytes 2433028
  43.0 38.1 %all-to-all-start.1 = ((f32[16,99,128]{2,1,0:T(8,128)}), f32[16,99,128]{2,1,0:T(8,128)}, u32[]{:S(2)}, u32[]{:S(2)}) async-start(f32[16,99,128]{2,1,0:T(8,128)} %fusion.1), calls=%async_computation.1 | async-start | bytes 1703936 | tf_op jit(solution)/shard_map/all_to_all | solution.py:200
  52.4 19.0 %collective-permute-start.1 = (f32[9,96,128]{2,1,0:T(8,128)}, f32[9,96,128]{2,1,0:T(8,128)}, u32[]{:S(2)}, u32[]{:S(2)}) collective-permute-start(f32[9,96,128]{2,1,0:T(8,128)} %pad_maximum_fusion.6), channel_id=1, source_target_pairs={{16,0},{32,16},{48,32},{64,48},{80,64},{96,80},{112,96},{128,112},... | collective-permute-start | bytes 1327112 | tf_op jit(solution)/shard_map/ppermute | solution.py:138
  55.2 18.1 %collective-permute-start = (f32[8,96,128]{2,1,0:T(8,128)}, f32[8,96,128]{2,1,0:T(8,128)}, u32[]{:S(2)}, u32[]{:S(2)}) collective-permute-start(f32[8,96,128]{2,1,0:T(8,128)} %get-tuple-element.14), channel_id=1, source_target_pairs={{0,16},{16,32},{32,48},{48,64},{64,80},{80,96},{96,112},{112,128},... | collective-permute-start | bytes 1179656 | tf_op jit(solution)/shard_map/ppermute | solution.py:134
  73.3 5.2 %copy-start.1 = (f32[8,1,96,128]{3,2,1,0:T(8,128)}, f32[8,1,96,128]{3,2,1,0:T(8,128)S(1)}, u32[]{:S(2)}) copy-start(f32[8,1,96,128]{3,2,1,0:T(8,128)S(1)} %broadcast_in_dim_broadcast_in_dim.4) | copy-start | bytes 1179652
  74.8 10.8 %collective-permute-start.2 = (f32[8,11,1,128]{3,2,1,0:T(1,128)}, f32[8,11,1,128]{3,2,1,0:T(1,128)}, u32[]{:S(2)}, u32[]{:S(2)}) collective-permute-start(f32[8,11,1,128]{3,2,1,0:T(1,128)} %pad_maximum_fusion.17), channel_id=1, source_target_pairs={{0,1},{1,2},{2,3},{3,4},{4,5},{5,6},{6,7},{7,8},{8,9},{9,10},{10,1... | collective-permute-start | bytes 135176 | tf_op jit(solution)/shard_map/ppermute | solution.py:148
  78.5 7.1 %collective-permute-start.3 = (f32[8,11,2,128]{3,2,1,0:T(2,128)}, f32[8,11,2,128]{3,2,1,0:T(2,128)}, u32[]{:S(2)}, u32[]{:S(2)}) collective-permute-start(f32[8,11,2,128]{3,2,1,0:T(2,128)} %pad_maximum_fusion.14), channel_id=1, source_target_pairs={{1,0},{2,1},{3,2},{4,3},{5,4},{6,5},{7,6},{8,7},{9,8},{10,9},{11,1... | collective-permute-start | bytes 270344 | tf_op jit(solution)/shard_map/ppermute | solution.py:151
  81.2 4.5 %copy-start.2 = (f32[8,1,96,128]{3,2,1,0:T(8,128)S(1)}, f32[8,1,96,128]{3,2,1,0:T(8,128)}, u32[]{:S(2)}) copy-start(f32[8,1,96,128]{3,2,1,0:T(8,128)} %copy-done.1) | copy-start | bytes 1179652
  83.6 6.2 %copy-start.6 = (f32[8]{0:T(128)S(1)}, f32[8]{0:T(128)}, u32[]{:S(2)}) copy-start(f32[8]{0:T(128)} %constant.116.clone) | copy-start | bytes 100
  83.6 6.1 %collective-permute-start.6 = (f32[5,99,128]{2,0,1:T(8,128)S(1)}, f32[5,99,128]{2,0,1:T(8,128)S(1)}, u32[]{:S(2)}, u32[]{:S(2)}) collective-permute-start(f32[5,99,128]{2,0,1:T(8,128)S(1)} %pad_maximum_fusion.7), channel_id=1, source_target_pairs={{16,8},{17,9},{18,10},{19,11},{20,12},{21,13},{22,14},{23,15},{24,... | collective-permute-start | bytes 760328 | tf_op jit(solution)/shard_map/ppermute | solution.py:217
  84.9 4.9 %collective-permute-start.5 = (f32[5,99,128]{2,0,1:T(8,128)S(1)}, f32[5,99,128]{2,0,1:T(8,128)S(1)}, u32[]{:S(2)}, u32[]{:S(2)}) collective-permute-start(f32[5,99,128]{2,0,1:T(8,128)S(1)} %pad_maximum_fusion.7), channel_id=1, source_target_pairs={{0,8},{1,9},{2,10},{3,11},{4,12},{5,13},{6,14},{7,15},{8,0},{9,1},... | collective-permute-start | bytes 760328 | tf_op jit(solution)/shard_map/ppermute | solution.py:212
  87.4 3.5 %copy-start = (f32[8,11,99,128]{3,2,1,0:T(8,128)}, f32[8,11,99,128]{3,2,1,0:T(8,128)S(1)}, u32[]{:S(2)}) copy-start(f32[8,11,99,128]{3,2,1,0:T(8,128)S(1)} %pad_maximum_fusion) | copy-start | bytes 13381636
  87.4 3.2 %collective-permute-start.7 = (f32[16,99,128]{2,0,1:T(8,128)S(1)}, f32[16,99,128]{2,0,1:T(8,128)S(1)}, u32[]{:S(2)}, u32[]{:S(2)}) collective-permute-start(f32[16,99,128]{2,0,1:T(8,128)S(1)} %copy.63), channel_id=1, source_target_pairs={{16,0},{224,240},{17,1},{225,241},{18,2},{226,242},{19,3},{227,243... | collective-permute-start | bytes 2433032 | tf_op jit(solution)/shard_map/ppermute | solution.py:202
  92.2 1.0 slice-start

commit v10 on v6

--- a/solution.py
+++ b/solution.py
@@ -171,14 +171,16 @@
         jnp.float32
     )
     kept_weight = jnp.where(column_order[None, :] < limits[:, None], column_weight[None, :], 0.0)
-    coeffs = jnp.einsum("smr,mn->snr", cycle, analysis, precision=lax.Precision.HIGHEST)
+    coeffs = jnp.einsum("smr,mn->snr", cycle, analysis, precision=lax.Precision.HIGH)
     coeffs = coeffs * kept_weight[:, :, None]
-    out = jnp.einsum("snr,kjn->ksjr", coeffs, synthesis, precision=lax.Precision.HIGHEST)
+    out = jnp.einsum("snr,kjn->ksjr", coeffs, synthesis, precision=lax.Precision.HIGH)
     out = out.reshape(phi_count * per_device, npc + 3, nr)
+    mine = lax.all_to_all(out, "phi", split_axis=0, concat_axis=0, tiled=True)
+    mine, halo_src = lax.optimization_barrier((mine, combined))
     low_halo = lax.ppermute(
-        combined[:, ct - 1], "theta", [(i, i + 1) for i in range(theta_count - 1)]
-    )
-    up_send = jnp.concatenate([combined[:, 0], combined[6:7, 1]], axis=0)
+        halo_src[:, ct - 1], "theta", [(i, i + 1) for i in range(theta_count - 1)]
+    )
+    up_send = jnp.concatenate([halo_src[:, 0], halo_src[6:7, 1]], axis=0)
     up_halo = lax.ppermute(up_send, "theta", [(i + 1, i) for i in range(theta_count - 1)])
     rows_ext = jnp.concatenate(
         [
@@ -197,7 +199,6 @@
     )
     early = jnp.concatenate([left_cols, rows_ext, right_cols], axis=2)
 
-    mine = lax.all_to_all(out, "phi", split_axis=0, concat_axis=0, tiled=True)
 
     from_helper = lax.ppermute(mine, "theta", pairs_in)
     per_half = channels // 2
@@ -223,19 +224,6 @@
             for b in range(phi_count)
         ],
     )
-    cap_start = jnp.where(at_north, 1, ct - CAP + 1)
-    kept_cap = lax.dynamic_slice_in_dim(early, cap_start, CAP, axis=1)
-    cap_block = jnp.where(at_north | at_south, cap_rows, kept_cap)
-    with_caps = lax.dynamic_update_slice_in_dim(early, cap_block, cap_start, axis=1)
-
-    near_rows = 2
-    rest_rows = ct - near_rows
-
-    def rows_from(x, first, count):
-        return advance(lax.dynamic_slice_in_dim(x, first, count + 3, axis=1))
-
-    rest = rows_from(with_caps, jnp.where(at_north, near_rows, 0), rest_rows)
-    (pole_ghost, helper_ghost), rest = lax.optimization_barrier(((pole_ghost, helper_ghost), rest))
     ghost_main = jnp.concatenate([pole_ghost[:per_half], helper_ghost[:per_half]], axis=0)
     ghost_main = ghost_main * parity[:, None, None]
     ghost_b = helper_ghost[per_half:] * parity[6]
@@ -252,16 +240,11 @@
     )
     offset = jnp.where(at_north, 0, ct - CAP + 1)
     kept_block = lax.dynamic_slice_in_dim(early, offset, CAP + 2, axis=1)
-    block = jnp.where(at_north, north_block, jnp.where(at_south, south_block, kept_block))
+    block = jnp.where(
+        at_north, north_block, jnp.where(at_south, south_block, kept_block)
+    )
     extended = lax.dynamic_update_slice_in_dim(early, block, offset, axis=1)
-
-    near = rows_from(extended, jnp.where(at_north, 0, rest_rows), near_rows)
-    outs = []
-    for a, c in zip(rest, near):
-        north_order = jnp.concatenate([c, a], axis=1)
-        other_order = jnp.concatenate([a, c], axis=1)
-        outs.append(jnp.where(at_north, north_order, other_order))
-    return tuple(outs)
+    return advance(extended)
 
 
 def solution(mesh):

time: 116 us -> 121 us (1.043)
  the two profiles are of different devices: /device:TPU:1 before, /device:TPU:6 now
where the time goes in v10:
time: 121 us; the launch traced here: 120 us
  waiting for transfers between devices  39.5 us (33%)
  starting transfers between devices  36.3 us (30%)
  other arithmetic  24.3 us (20%)
  local copies, waits for them, and re-layouts  13.8 us (11%)
  matrix products  4.26 us (4%)
  between operations  1.72 us (1%)
    all_to_all x1, waiting for transfers between devices, local(): mine = lax.all_to_all(out, 'phi', split_axis=0, concat_axis=0, tiled=True)  18 us
    ppermute x1, starting transfers between devices, local(): lax.ppermute(up_send, 'theta', [(i + 1, i) for i in range(theta_count - 1)])  11 us
    all_to_all x1, waiting for transfers between devices, local(): cycle = lax.all_to_all(work, 'phi', split_axis=0, concat_axis=1, tiled=True)  10.7 us
    all_to_all x1, starting transfers between devices, local(): cycle = lax.all_to_all(work, 'phi', split_axis=0, concat_axis=1, tiled=True)  9.94 us
    all_to_all x1, starting transfers between devices, local(): mine = lax.all_to_all(out, 'phi', split_axis=0, concat_axis=0, tiled=True)  6.19 us
    ppermute x1, waiting for transfers between devices, local(): lax.ppermute(halo_src[:, ct - 1], 'theta', [(i, i + 1) for i in range(the...  5.24 us
    sin x1, other arithmetic, fourier_rows(): return jnp.concatenate([jnp.cos(angle), jnp.sin(angle)], axis=-1)  4.17 us
    another operation x6, other arithmetic, advance(): return (jnp.stack(densities), jnp.stack([new_radial, new_theta, new_phi]))  4.05 us
  transfers between devices with their start and end apart: 10, of which 6 were waited for; matrix products, arithmetic and copies ran while one was open for 12% of the time, Pallas kernels for 0%

profile of v10, /device:TPU:6, one launch (start us, length us, event | category | flops | bytes accessed | tf_op | source)
XLA Modules:
  0.0 119.8 jit_solution(9557438969216496796)
XLA Ops:
  0.7 1.1 slice_bitcast_fusion.11
  1.8 1.3 %fusion.26 = f32[4,4,96,128]{3,2,0,1:T(8,128)S(1)} fusion(f32[1,8,96,128]{3,2,0,1:T(8,128)S(1)} %slice_bitcast_fusion.11, pred[]{:T(512)S(6)} %eq.63, f32[3,8,96,128]{3,2,1,0:T(8,128)} %param.7), kind=kLoop, calls=%fused_computation.34 | loop fusion | flops 589824 | bytes 2359297 | tf_op jit(solution)/shard_map/jit(_where)/select_n | solution.py:141
  5.1 9.9 %all-to-all-start = ((f32[16,96,128]{2,1,0:T(8,128)}), f32[16,96,128]{2,1,0:T(8,128)S(1)}, u32[]{:S(2)}, u32[]{:S(2)}) async-start(f32[16,96,128]{2,1,0:T(8,128)} %bitcast_select_fusion), calls=%async_computation | async-start | bytes 1572864 | tf_op jit(solution)/shard_map/all_to_all | solution.py:149
  16.4 3.5 %fusion.20 = (f32[16,99,128]{2,1,0:T(8,128)S(1)}, f32[16,99,128]{2,1,0:T(8,128)S(1)}) fusion(s32[16,99]{1,0:T(8,128)S(1)} %add_select_fusion.2), kind=kLoop, calls=%fused_computation.28 | loop fusion | flops 1824768 | bytes 1628352 | tf_op jit(solution)/shard_map/cos | solution.py:110
  19.9 4.2 %fusion.29 = (f32[1536,128]{1,0:T(8,128)S(1)}, f32[1536,128]{1,0:T(8,128)}) fusion(), kind=kLoop, calls=%fused_computation.43 | loop fusion | flops 1769472 | bytes 1572864 | tf_op jit(solution)/shard_map/sin | solution.py:110
  24.1 10.7 %all-to-all-done = f32[16,96,128]{2,1,0:T(8,128)S(1)} async-done(((f32[16,96,128]{2,1,0:T(8,128)}), f32[16,96,128]{2,1,0:T(8,128)S(1)}, u32[]{:S(2)}, u32[]{:S(2)}) %all-to-all-start) | async-done | bytes 786464 | tf_op jit(solution)/shard_map/all_to_all | solution.py:149
  34.7 2.5 %fusion.12 = f32[256,128,1]{1,0,2:T(8,128)S(1)} fusion(f32[1536,128]{1,0:T(8,128)S(1)} %bitcast.71, f32[1536,128]{1,0:T(8,128)S(1)} %get-tuple-element.66, f32[1536,128]{1,0:T(8,128)} %get-tuple-element.67, f32[256]{0:T(256)S(1)} %compare_select_fusion.1), kind=kOutput, calls=%fused_computation.21 | convolution fusion | flops 302415872 | bytes 2491392 | tf_op jit(solution)/shard_map/smr,mn->snr/dot_general | solution.py:174
  37.3 1.7 %fusion.1 = f32[16,99,128]{2,1,0:T(8,128)} fusion(f32[256,128,1]{1,0,2:T(8,128)S(1)} %fusion.12, f32[16,99,128]{2,1,0:T(8,128)S(1)} %get-tuple-element.63, f32[16,99,128]{2,1,0:T(8,128)S(1)} %get-tuple-element.62), kind=kOutput, calls=%fused_computation.4 | convolution fusion | flops 311832576 | bytes 2564096 | tf_op jit(solution)/shard_map/snr,kjn->ksjr/dot_general | solution.py:176
  39.0 6.2 %all-to-all-start.1 = ((f32[16,99,128]{2,1,0:T(8,128)}), f32[16,99,128]{2,1,0:T(8,128)}, u32[]{:S(2)}, u32[]{:S(2)}) async-start(f32[16,99,128]{2,1,0:T(8,128)} %fusion.1), calls=%async_computation.1 | async-start | bytes 1703936 | tf_op jit(solution)/shard_map/all_to_all | solution.py:178
  45.2 1.2 constant_dynamic-update-slice_fusion.2
  46.4 1.4 %constant_dynamic-update-slice_fusion.1 = f32[8,8,96,128]{3,2,1,0:T(8,128)S(1)} fusion(f32[8,8,96,128]{3,2,1,0:T(8,128)S(1)} %constant_dynamic-update-slice_fusion.2, f32[3,8,96,128]{3,2,1,0:T(8,128)} %param.6), kind=kLoop, calls=%fused_computation.157 | loop fusion | bytes 2359296
  47.8 1.4 %constant_dynamic-update-slice_fusion = f32[8,8,96,128]{3,2,1,0:T(8,128)S(1)} fusion(f32[8,8,96,128]{3,2,1,0:T(8,128)S(1)} %constant_dynamic-update-slice_fusion.1, f32[3,8,96,128]{3,2,1,0:T(8,128)} %param.7), kind=kLoop, calls=%fused_computation.156 | loop fusion | bytes 2359296 | tf_op jit(solution)/shard_map/concatenate | solution.py:114
  49.1 18.0 %all-to-all-done.1 = f32[16,99,128]{2,1,0:T(8,128)} async-done(((f32[16,99,128]{2,1,0:T(8,128)}), f32[16,99,128]{2,1,0:T(8,128)}, u32[]{:S(2)}, u32[]{:S(2)}) %all-to-all-start.1) | async-done | bytes 811040 | tf_op jit(solution)/shard_map/all_to_all | solution.py:178
  67.1 1.3 %copy.43 = f32[16,99,128]{2,0,1:T(8,128)S(1)} copy(f32[16,99,128]{2,1,0:T(8,128)} %all-to-all-done.1) | data formatting | bytes 1622016 | tf_op jit(solution)/shard_map/optimization_barrier | solution.py:179
  71.7 11.0 %collective-permute-start.2 = (f32[9,96,128]{2,1,0:T(8,128)S(1)}, f32[9,96,128]{2,1,0:T(8,128)S(1)}, u32[]{:S(2)}, u32[]{:S(2)}) collective-permute-start(f32[9,96,128]{2,1,0:T(8,128)S(1)} %pad_maximum_fusion.6), channel_id=1, source_target_pairs={{16,0},{32,16},{48,32},{64,48},{80,64},{96,80},{112,96},{128,112},... | collective-permute-start | bytes 1327112 | tf_op jit(solution)/shard_map/ppermute | solution.py:184
  82.7 1.9 %collective-permute-start.1 = (f32[8,96,128]{2,1,0:T(8,128)S(1)}, f32[8,96,128]{2,1,0:T(8,128)S(1)}, u32[]{:S(2)}, u32[]{:S(2)}) collective-permute-start(f32[8,96,128]{2,1,0:T(8,128)S(1)} %get-tuple-element.18), channel_id=1, source_target_pairs={{0,16},{16,32},{32,48},{48,64},{64,80},{80,96},{96,112},{112,128},... | collective-permute-start | bytes 1179656 | tf_op jit(solution)/shard_map/ppermute | solution.py:180
  84.8 3.7 %collective-permute-done.2 = f32[9,96,128]{2,1,0:T(8,128)S(1)} collective-permute-done((f32[9,96,128]{2,1,0:T(8,128)S(1)}, f32[9,96,128]{2,1,0:T(8,128)S(1)}, u32[]{:S(2)}, u32[]{:S(2)}) %collective-permute-start.2) | collective-permute-done | bytes 442400 | tf_op jit(solution)/shard_map/ppermute | solution.py:184
  88.5 5.2 %collective-permute-done.1 = f32[8,96,128]{2,1,0:T(8,128)S(1)} collective-permute-done((f32[8,96,128]{2,1,0:T(8,128)S(1)}, f32[8,96,128]{2,1,0:T(8,128)S(1)}, u32[]{:S(2)}, u32[]{:S(2)}) %collective-permute-start.1) | collective-permute-done | bytes 393248 | tf_op jit(solution)/shard_map/ppermute | solution.py:180
  94.7 3.7 %collective-permute-start.4 = (f32[8,11,2,128]{3,2,1,0:T(2,128)S(1)}, f32[8,11,2,128]{3,2,1,0:T(2,128)S(1)}, u32[]{:S(2)}, u32[]{:S(2)}) collective-permute-start(f32[8,11,2,128]{3,2,1,0:T(2,128)S(1)} %pad_maximum_fusion.14), channel_id=1, source_target_pairs={{1,0},{2,1},{3,2},{4,3},{5,4},{6,5},{7,6},{8,7},{9,8},{10,9},{11,1... | collective-permute-start | bytes 270344 | tf_op jit(solution)/shard_map/ppermute | solution.py:197
  98.6 1.5 %collective-permute-done.3 = f32[8,11,1,128]{3,2,1,0:T(1,128)S(1)} collective-permute-done((f32[8,11,1,128]{3,2,1,0:T(1,128)S(1)}, f32[8,11,1,128]{3,2,1,0:T(1,128)S(1)}, u32[]{:S(2)}, u32[]{:S(2)}) %collective-permute-start.3) | collective-permute-done | bytes 45088 | tf_op jit(solution)/shard_map/ppermute | solution.py:194
  101.7 1.9 %pad_maximum_fusion.1 = f32[32,99,128]{2,1,0:T(8,128)S(1)} fusion(f32[16,99,128]{2,1,0:T(8,128)S(1)} %copy.47, f32[16,99,128]{2,1,0:T(8,128)} %all-to-all-done.1), kind=kLoop, calls=%fused_computation.8 | loop fusion | flops 405504 | bytes 3244032 | tf_op jit(solution)/shard_map/concatenate | solution.py:205
  104.6 3.6 %fusion = f32[8,11,99,128]{3,2,1,0:T(8,128)} fusion(f32[8,11,99,128]{3,2,1,0:T(8,128)} %copy-done, s32[]{:T(128)S(6)} %select_n.154, f32[8,1,99,128]{3,2,1,0:T(8,128)S(1)} %slice-done, f32[8,4,99,128]{3,2,1,0:T(8,128)S(1)} %bitcast.66, f32[8,1,99,128]{3,2,1,0:T(8,128)S(1)} %copy.49, f32[8,1,99,128]{3,2,1,0:T(8,128)S(1)} %broadcast_in_dim_broadcast_in_dim.5, ...), kind=kLoop, calls=%fused_computation.2 | loop fusion | flops 3649536 | bytes 7950342 | tf_op jit(solution)/shard_map/dynamic_update_slice | solution.py:246
  108.1 2.6 %slice_bitcast_fusion.2 = (f32[11,99,128]{2,1,0:T(8,128)S(1)}, f32[11,99,128]{2,1,0:T(8,128)S(1)}, f32[11,99,128]{2,1,0:T(8,128)S(1)}, f32[11,99,128]{2,1,0:T(8,...) fusion(f32[8,11,99,128]{3,2,1,0:T(8,128)} %fusion), kind=kLoop, calls=%fused_computation.48 | loop fusion | bytes 8921088 | tf_op jit(solution)/shard_map/squeeze | solution.py:94
  118.7 1.1 pad_maximum_fusion.2
  (81 shorter events, 17.5 us)
Async XLA Ops:
  0.6 3.2 %slice-start.1 = ((f32[3,8,96,128]{3,2,1,0:T(8,128)}), f32[2,8,96,128]{3,2,1,0:T(8,128)S(1)}, s32[]{:S(2)}) async-start(f32[3,8,96,128]{3,2,1,0:T(8,128)} %param.6), calls=%async_computation.3 | async-start | bytes 1572864 | tf_op jit(solution)/shard_map/slice | solution.py:137
  0.6 3.2 %copy-start.1 = (f32[2,8,96,128]{3,2,1,0:T(8,128)S(1)}, f32[2,8,96,128]{3,2,1,0:T(8,128)}, u32[]{:S(2)}) copy-start(f32[2,8,96,128]{3,2,1,0:T(8,128)} %param.5) | copy-start | bytes 2359300
  3.1 1.0 collective-permute-start
  4.1 10.9 %copy-start.3 = (s32[2,4]{1,0:T(2,128)S(1)}, s32[2,4]{1,0:T(2,128)}, u32[]{:S(2)}) copy-start(s32[2,4]{1,0:T(2,128)} %param.8) | copy-start | bytes 100
  5.1 29.6 %all-to-all-start = ((f32[16,96,128]{2,1,0:T(8,128)}), f32[16,96,128]{2,1,0:T(8,128)S(1)}, u32[]{:S(2)}, u32[]{:S(2)}) async-start(f32[16,96,128]{2,1,0:T(8,128)} %bitcast_select_fusion), calls=%async_computation | async-start | bytes 1572864 | tf_op jit(solution)/shard_map/all_to_all | solution.py:149
  39.0 28.1 %all-to-all-start.1 = ((f32[16,99,128]{2,1,0:T(8,128)}), f32[16,99,128]{2,1,0:T(8,128)}, u32[]{:S(2)}, u32[]{:S(2)}) async-start(f32[16,99,128]{2,1,0:T(8,128)} %fusion.1), calls=%async_computation.1 | async-start | bytes 1703936 | tf_op jit(solution)/shard_map/all_to_all | solution.py:178
  69.5 15.1 %collective-permute-start.6 = (f32[5,99,128]{2,0,1:T(8,128)S(1)}, f32[5,99,128]{2,0,1:T(8,128)S(1)}, u32[]{:S(2)}, u32[]{:S(2)}) collective-permute-start(f32[5,99,128]{2,0,1:T(8,128)S(1)} %pad_maximum_fusion.7), channel_id=1, source_target_pairs={{16,8},{17,9},{18,10},{19,11},{20,12},{21,13},{22,14},{23,15},{24,... | collective-permute-start | bytes 760328 | tf_op jit(solution)/shard_map/ppermute | solution.py:218
  70.2 14.5 %collective-permute-start.5 = (f32[5,99,128]{2,0,1:T(8,128)S(1)}, f32[5,99,128]{2,0,1:T(8,128)S(1)}, u32[]{:S(2)}, u32[]{:S(2)}) collective-permute-start(f32[5,99,128]{2,0,1:T(8,128)S(1)} %pad_maximum_fusion.7), channel_id=1, source_target_pairs={{0,8},{1,9},{2,10},{3,11},{4,12},{5,13},{6,14},{7,15},{8,0},{9,1},... | collective-permute-start | bytes 760328 | tf_op jit(solution)/shard_map/ppermute | solution.py:213
  70.9 30.5 %collective-permute-start.7 = (f32[16,99,128]{2,0,1:T(8,128)S(1)}, f32[16,99,128]{2,0,1:T(8,128)S(1)}, u32[]{:S(2)}, u32[]{:S(2)}) collective-permute-start(f32[16,99,128]{2,0,1:T(8,128)S(1)} %copy.43), channel_id=1, source_target_pairs={{16,0},{224,240},{17,1},{225,241},{18,2},{226,242},{19,3},{227,243... | collective-permute-start | bytes 2433032 | tf_op jit(solution)/shard_map/ppermute | solution.py:203
  71.7 16.8 %collective-permute-start.2 = (f32[9,96,128]{2,1,0:T(8,128)S(1)}, f32[9,96,128]{2,1,0:T(8,128)S(1)}, u32[]{:S(2)}, u32[]{:S(2)}) collective-permute-start(f32[9,96,128]{2,1,0:T(8,128)S(1)} %pad_maximum_fusion.6), channel_id=1, source_target_pairs={{16,0},{32,16},{48,32},{64,48},{80,64},{96,80},{112,96},{128,112},... | collective-permute-start | bytes 1327112 | tf_op jit(solution)/shard_map/ppermute | solution.py:184
  82.7 11.1 %collective-permute-start.1 = (f32[8,96,128]{2,1,0:T(8,128)S(1)}, f32[8,96,128]{2,1,0:T(8,128)S(1)}, u32[]{:S(2)}, u32[]{:S(2)}) collective-permute-start(f32[8,96,128]{2,1,0:T(8,128)S(1)} %get-tuple-element.18), channel_id=1, source_target_pairs={{0,16},{16,32},{32,48},{48,64},{64,80},{80,96},{96,112},{112,128},... | collective-permute-start | bytes 1179656 | tf_op jit(solution)/shard_map/ppermute | solution.py:180
  93.8 4.5 %copy-start.2 = (f32[8]{0:T(128)S(1)}, f32[8]{0:T(128)}, u32[]{:S(2)}) copy-start(f32[8]{0:T(128)} %constant.116.clone) | copy-start | bytes 100
  93.8 6.2 %collective-permute-start.3 = (f32[8,11,1,128]{3,2,1,0:T(1,128)S(1)}, f32[8,11,1,128]{3,2,1,0:T(1,128)S(1)}, u32[]{:S(2)}, u32[]{:S(2)}) collective-permute-start(f32[8,11,1,128]{3,2,1,0:T(1,128)S(1)} %pad_maximum_fusion.17), channel_id=1, source_target_pairs={{0,1},{1,2},{2,3},{3,4},{4,5},{5,6},{6,7},{7,8},{8,9},{9,10},{10,1... | collective-permute-start | bytes 135176 | tf_op jit(solution)/shard_map/ppermute | solution.py:194
  94.7 5.8 %collective-permute-start.4 = (f32[8,11,2,128]{3,2,1,0:T(2,128)S(1)}, f32[8,11,2,128]{3,2,1,0:T(2,128)S(1)}, u32[]{:S(2)}, u32[]{:S(2)}) collective-permute-start(f32[8,11,2,128]{3,2,1,0:T(2,128)S(1)} %pad_maximum_fusion.14), channel_id=1, source_target_pairs={{1,0},{2,1},{3,2},{4,3},{5,4},{6,5},{7,6},{8,7},{9,8},{10,9},{11,1... | collective-permute-start | bytes 270344 | tf_op jit(solution)/shard_map/ppermute | solution.py:197
  101.4 2.2 %copy-start = (f32[8,11,99,128]{3,2,1,0:T(8,128)}, f32[8,11,99,128]{3,2,1,0:T(8,128)S(1)}, u32[]{:S(2)}) copy-start(f32[8,11,99,128]{3,2,1,0:T(8,128)S(1)} %pad_maximum_fusion) | copy-start | bytes 13381636
  103.6 1.0 slice-start

commit v11 on v9

--- a/solution.py
+++ b/solution.py
@@ -156,17 +156,19 @@
     north_side = t <= 1
     helper = (t == 1) | (t == theta_count - 2)
     half = channels * CAP // 2
-    first_half = jnp.concatenate([density, velocity[:2]], axis=0)
-    second_half = jnp.concatenate([velocity[2:], bfield], axis=0)
-
-    def cap_of(fields):
-        rows = jnp.where(at_north, fields[:, :CAP], fields[:, ct - CAP :])
+    pair_rows = CAP // 2
+
+    def rows_at(first):
+        parts = [lax.dynamic_slice_in_dim(f, first, pair_rows, axis=1) for f in (density, velocity, bfield)]
+        rows = jnp.concatenate(parts, axis=0)
         return jnp.swapaxes(rows, 0, 1).reshape(half, npc, nr)
 
+    keep_first = jnp.where(at_north, 0, ct - pair_rows)
+    hand_first = jnp.where(at_north, pair_rows, ct - CAP)
     pairs_out = [(0, 1), (theta_count - 1, theta_count - 2)]
     pairs_in = [(1, 0), (theta_count - 2, theta_count - 1)]
-    handed = lax.ppermute(cap_of(second_half), "theta", pairs_out)
-    work = jnp.where(helper, handed, cap_of(first_half))
+    handed = lax.ppermute(rows_at(hand_first), "theta", pairs_out)
+    work = jnp.where(helper, handed, rows_at(keep_first))
     per_device = half // phi_count
     cycle = lax.all_to_all(work, "phi", split_axis=0, concat_axis=1, tiled=True)
     analysis = fourier_rows(jnp.arange(cycle_len, dtype=jnp.int32), cycle_len)
@@ -180,7 +182,8 @@
     pole_pick = jnp.where(north_side, 0, 1).astype(jnp.int32)
     level_row = lax.dynamic_index_in_dim(levels, pole_pick, 0, keepdims=False)
     slot_ids = p * per_device + jnp.arange(per_device, dtype=jnp.int32)
-    row_ids = slot_ids // (channels // 2)
+    row_base = jnp.where(north_side == helper, pair_rows, 0)
+    row_ids = row_base + slot_ids // channels
     slot_levels = jnp.sum(
         jnp.where(
             row_ids[:, None] == jnp.arange(CAP, dtype=jnp.int32)[None, :], level_row[None, :], 0
@@ -200,32 +203,28 @@
     mine = lax.all_to_all(out, "phi", split_axis=0, concat_axis=0, tiled=True)
 
     from_helper = lax.ppermute(mine, "theta", pairs_in)
-    per_half = channels // 2
-    cap_rows = jnp.concatenate([mine, from_helper], axis=0).reshape(2, CAP, per_half, npc + 3, nr)
-    cap_rows = jnp.transpose(cap_rows, (0, 2, 1, 3, 4)).reshape(channels, CAP, npc + 3, nr)
-    first_rows = mine[:per_half]
-    last_rows = mine[(CAP - 1) * per_half :]
-    spare_at = (CAP - 2) * per_half + 6 - per_half
-    spare = mine[spare_at : spare_at + 1]
-    ghost_send = jnp.concatenate([jnp.where(north_side, first_rows, last_rows), spare], axis=0)
+    spare = mine[6 : 7]
+    ghost_send = jnp.where(
+        north_side,
+        jnp.concatenate([mine[:channels], spare], axis=0),
+        jnp.concatenate([mine[channels:], spare], axis=0),
+    )
     turn = phi_count // 2
-    pole_ghost = lax.ppermute(
+    ghost = lax.ppermute(
         ghost_send,
         both,
         [(a * phi_count + b, a * phi_count + (b + turn) % phi_count) for a in poles for b in range(phi_count)],
     )
-    helper_ghost = lax.ppermute(
-        ghost_send,
-        both,
-        [
-            (h * phi_count + b, a * phi_count + (b + turn) % phi_count)
-            for h, a in ((1, 0), (theta_count - 2, theta_count - 1))
-            for b in range(phi_count)
-        ],
-    )
-    ghost_main = jnp.concatenate([pole_ghost[:per_half], helper_ghost[:per_half]], axis=0)
+    in_order = jnp.where(
+        at_north,
+        jnp.concatenate([mine, from_helper], axis=0),
+        jnp.concatenate([from_helper, mine], axis=0),
+    )
+    cap_rows = jnp.swapaxes(in_order.reshape(CAP, channels, npc + 3, nr), 0, 1)
+    ghost_main = ghost[:channels]
+    ghost_b = ghost[channels:]
     ghost_main = ghost_main * parity[:, None, None]
-    ghost_b = helper_ghost[per_half:] * parity[6]
+    ghost_b = ghost_b * parity[6]
     north_block = jnp.concatenate(
         [ghost_main[:, None], cap_rows, early[:, CAP + 1 : CAP + 2]], axis=1
     )

time: 110 us -> 113 us (1.027)
  local copies, waits for them, and re-layouts: 17.2 us -> 19.8 us
  starting transfers between devices: 31.2 us -> 33.3 us
    ppermute x1, starting transfers between devices: 1.52 us -> 4.73 us  [local(): from_helper = lax.ppermute(mine, 'theta', pairs_in)]
    dynamic_slice x0 -> x3, local copies, waits for them, and re-layouts: none -> 2.31 us  [rows_at(): lax.dynamic_slice_in_dim(f, first, pair_rows, axis=1)]
    broadcast_in_dim x0 -> x1, other arithmetic: none -> 1.42 us  [local(): ghost_main[:, None]]
    concatenate x3 -> x2, other arithmetic: 1.48 us -> 0.12 us  [rows_at(): rows = jnp.concatenate(parts, axis=0)]
    ppermute x2 -> x1, starting transfers between devices: 2.61 us -> 1.29 us  [local(): handed = lax.ppermute(rows_at(hand_first), 'theta', pairs_out)]
    slice x4 -> x2, local copies, waits for them, and re-layouts: 0.87 us -> 2.08 us  [the longest x1 1.27 us: local(): mine[channels:]]
    ppermute x1, local copies, waits for them, and re-layouts: 0.27 us -> 1.41 us  [local(): from_helper = lax.ppermute(mine, 'theta', pairs_in)]
    select_n x4 -> x3, other arithmetic: 2.45 us -> 3.49 us  [the longest x1 1.69 us: local(): jnp.where(at_north, jnp.concatenate([mine, from_helper], axis=0), jnp.con...]
  transfers between devices with their start and end apart: 10 -> 9, of which waited for: 5 -> 3; matrix products, arithmetic and copies ran while one was open for 24% -> 21% of each run, Pallas kernels for 0% -> 0%
where the time goes in v11:
time: 113 us; the launch traced here: 112 us
  starting transfers between devices  33.3 us (29%)
  other arithmetic  29.8 us (26%)
  waiting for transfers between devices  22.8 us (20%)
  local copies, waits for them, and re-layouts  19.8 us (18%)
  matrix products  4.87 us (4%)
  between operations  1.78 us (2%)
    ppermute x1, waiting for transfers between devices, local(): lax.ppermute(up_send, 'theta', [(i + 1, i) for i in range(theta_count - 1)])  12.7 us
    all_to_all x1, starting transfers between devices, local(): cycle = lax.all_to_all(work, 'phi', split_axis=0, concat_axis=1, tiled=True)  7.97 us
    all_to_all x1, waiting for transfers between devices, local(): cycle = lax.all_to_all(work, 'phi', split_axis=0, concat_axis=1, tiled=True)  6.64 us
    all_to_all x1, starting transfers between devices, local(): mine = lax.all_to_all(out, 'phi', split_axis=0, concat_axis=0, tiled=True)  6.4 us
    cos x1, other arithmetic, fourier_rows(): return jnp.concatenate([jnp.cos(angle), jnp.sin(angle)], axis=-1)  5.31 us
    ppermute x1, starting transfers between devices, local(): from_helper = lax.ppermute(mine, 'theta', pairs_in)  4.73 us
    sin x1, other arithmetic, fourier_rows(): return jnp.concatenate([jnp.cos(angle), jnp.sin(angle)], axis=-1)  4.32 us
    ppermute x1, starting transfers between devices, local(): lax.ppermute(combined[:, ct - 1], 'theta', [(i, i + 1) for i in range(the...  4.31 us
  transfers between devices with their start and end apart: 9, of which 3 were waited for; matrix products, arithmetic and copies ran while one was open for 21% of the time, Pallas kernels for 0%

profile of v11, /device:TPU:1, one launch (start us, length us, event | category | flops | bytes accessed | tf_op | source)
XLA Modules:
  0.0 112.4 jit_solution(55998841563473727)
XLA Ops:
  5.9 3.5 %collective-permute-done.4 = f32[16,96,128]{2,1,0:T(8,128)S(1)} collective-permute-done((f32[16,96,128]{2,1,0:T(8,128)S(1)}, f32[16,96,128]{2,1,0:T(8,128)S(1)}, u32[]{:S(2)}, u32[]{:S(2)}) %collective-permute-start.4) | collective-permute-done | bytes 786464 | tf_op jit(solution)/shard_map/ppermute | solution.py:170
  10.4 8.0 %all-to-all-start = ((f32[16,96,128]{2,1,0:T(8,128)}), f32[16,96,128]{2,1,0:T(8,128)}, u32[]{:S(2)}, u32[]{:S(2)}) async-start(f32[16,96,128]{2,1,0:T(8,128)} %bitcast_select_fusion), calls=%async_computation | async-start | bytes 1572864 | tf_op jit(solution)/shard_map/all_to_all | solution.py:173
  19.6 1.4 %constant_dynamic-update-slice_fusion.1 = f32[8,8,96,128]{3,2,1,0:T(8,128)S(1)} fusion(f32[8,8,96,128]{3,2,1,0:T(8,128)S(1)} %constant_dynamic-update-slice_fusion.2, f32[3,8,96,128]{3,2,1,0:T(8,128)} %param.6), kind=kLoop, calls=%fused_computation.149 | loop fusion | bytes 2359296
  21.8 5.3 %fusion.20 = (f32[16,99,128]{2,1,0:T(8,128)}, f32[16,99,128]{2,1,0:T(8,128)}) fusion(s32[16,99]{1,0:T(8,128)S(1)} %add_select_fusion.2), kind=kLoop, calls=%fused_computation.25 | loop fusion | flops 1824768 | bytes 1628352 | tf_op jit(solution)/shard_map/cos | solution.py:110
  27.1 4.3 %fusion.26 = (f32[1536,128]{1,0:T(8,128)}, f32[1536,128]{1,0:T(8,128)}) fusion(), kind=kLoop, calls=%fused_computation.36 | loop fusion | flops 1769472 | bytes 1572864 | tf_op jit(solution)/shard_map/sin | solution.py:110
  31.5 6.6 %all-to-all-done = f32[16,96,128]{2,1,0:T(8,128)} async-done(((f32[16,96,128]{2,1,0:T(8,128)}), f32[16,96,128]{2,1,0:T(8,128)}, u32[]{:S(2)}, u32[]{:S(2)}) %all-to-all-start) | async-done | bytes 786464 | tf_op jit(solution)/shard_map/all_to_all | solution.py:173
  38.1 3.1 %fusion.12 = f32[256,128,1]{1,0,2:T(8,128)S(1)} fusion(f32[1536,128]{1,0:T(8,128)} %bitcast.11, f32[1536,128]{1,0:T(8,128)} %get-tuple-element.68, f32[1536,128]{1,0:T(8,128)} %get-tuple-element.69, f32[256]{0:T(256)S(1)} %compare_select_fusion.1), kind=kOutput, calls=%fused_computation.18 | convolution fusion | flops 302415872 | bytes 2491392 | tf_op jit(solution)/shard_map/smr,mn->snr/dot_general | solution.py:199
  41.3 1.7 %fusion.1 = f32[16,99,128]{2,1,0:T(8,128)} fusion(f32[256,128,1]{1,0,2:T(8,128)S(1)} %fusion.12, f32[16,99,128]{2,1,0:T(8,128)S(1)} %copy-done.6, f32[16,99,128]{2,1,0:T(8,128)S(1)} %copy-done.5), kind=kOutput, calls=%fused_computation.4 | convolution fusion | flops 311832576 | bytes 2564096 | tf_op jit(solution)/shard_map/snr,kjn->ksjr/dot_general | solution.py:201
  43.0 6.4 %all-to-all-start.1 = ((f32[16,99,128]{2,1,0:T(8,128)}), f32[16,99,128]{2,1,0:T(8,128)}, u32[]{:S(2)}, u32[]{:S(2)}) async-start(f32[16,99,128]{2,1,0:T(8,128)} %fusion.1), calls=%async_computation.1 | async-start | bytes 1703936 | tf_op jit(solution)/shard_map/all_to_all | solution.py:203
  49.4 1.4 %constant_dynamic-update-slice_fusion = f32[8,8,96,128]{3,2,1,0:T(8,128)S(1)} fusion(f32[8,8,96,128]{3,2,1,0:T(8,128)S(1)} %constant_dynamic-update-slice_fusion.1, f32[3,8,96,128]{3,2,1,0:T(8,128)} %param.7), kind=kLoop, calls=%fused_computation.148 | loop fusion | bytes 2359296 | tf_op jit(solution)/shard_map/concatenate | solution.py:114
  50.9 2.8 %collective-permute-start.1 = (f32[9,96,128]{2,1,0:T(8,128)S(1)}, f32[9,96,128]{2,1,0:T(8,128)S(1)}, u32[]{:S(2)}, u32[]{:S(2)}) collective-permute-start(f32[9,96,128]{2,1,0:T(8,128)S(1)} %pad_maximum_fusion.7), channel_id=1, source_target_pairs={{16,0},{32,16},{48,32},{64,48},{80,64},{96,80},{112,96},{128,112},... | collective-permute-start | bytes 1327112 | tf_op jit(solution)/shard_map/ppermute | solution.py:138
  53.6 4.3 %collective-permute-start = (f32[8,96,128]{2,1,0:T(8,128)S(1)}, f32[8,96,128]{2,1,0:T(8,128)S(1)}, u32[]{:S(2)}, u32[]{:S(2)}) collective-permute-start(f32[8,96,128]{2,1,0:T(8,128)S(1)} %get-tuple-element.14), channel_id=1, source_target_pairs={{0,16},{16,32},{32,48},{48,64},{64,80},{80,96},{96,112},{112,128},... | collective-permute-start | bytes 1179656 | tf_op jit(solution)/shard_map/ppermute | solution.py:134
  58.0 12.7 %collective-permute-done.1 = f32[9,96,128]{2,1,0:T(8,128)S(1)} collective-permute-done((f32[9,96,128]{2,1,0:T(8,128)S(1)}, f32[9,96,128]{2,1,0:T(8,128)S(1)}, u32[]{:S(2)}, u32[]{:S(2)}) %collective-permute-start.1) | collective-permute-done | bytes 442400 | tf_op jit(solution)/shard_map/ppermute | solution.py:138
  75.2 1.4 %collective-permute-start.5 = (f32[9,99,128]{2,1,0:T(8,128)}, f32[9,99,128]{2,1,0:T(8,128)}, u32[]{:S(2)}, u32[]{:S(2)}) collective-permute-start(f32[9,99,128]{2,1,0:T(8,128)} %fusion.32), channel_id=1, source_target_pairs={{0,8},{1,9},{2,10},{3,11},{4,12},{5,13},{6,14},{7,15},{8,0},{9,1},... | collective-permute-start | bytes 1368584 | tf_op jit(solution)/shard_map/ppermute | solution.py:213
  77.3 2.9 %collective-permute-start.2 = (f32[8,11,1,128]{3,2,1,0:T(1,128)}, f32[8,11,1,128]{3,2,1,0:T(1,128)}, u32[]{:S(2)}, u32[]{:S(2)}) collective-permute-start(f32[8,11,1,128]{3,2,1,0:T(1,128)} %pad_maximum_fusion.17), channel_id=1, source_target_pairs={{0,1},{1,2},{2,3},{3,4},{4,5},{5,6},{6,7},{7,8},{8,9},{9,10},{10,1... | collective-permute-start | bytes 135176 | tf_op jit(solution)/shard_map/ppermute | solution.py:148
  80.2 1.5 %collective-permute-start.3 = (f32[8,11,2,128]{3,2,1,0:T(2,128)}, f32[8,11,2,128]{3,2,1,0:T(2,128)}, u32[]{:S(2)}, u32[]{:S(2)}) collective-permute-start(f32[8,11,2,128]{3,2,1,0:T(2,128)} %pad_maximum_fusion.14), channel_id=1, source_target_pairs={{1,0},{2,1},{3,2},{4,3},{5,4},{6,5},{7,6},{8,7},{9,8},{10,9},{11,1... | collective-permute-start | bytes 270344 | tf_op jit(solution)/shard_map/ppermute | solution.py:151
  81.7 2.2 %copy.40 = f32[16,99,128]{2,0,1:T(8,128)} copy(f32[16,99,128]{2,1,0:T(8,128)} %all-to-all-done.1) | data formatting | bytes 1622016 | tf_op jit(solution)/shard_map/all_to_all | solution.py:203
  83.9 4.7 %collective-permute-start.6 = (f32[16,99,128]{2,0,1:T(8,128)}, f32[16,99,128]{2,0,1:T(8,128)}, u32[]{:S(2)}, u32[]{:S(2)}) collective-permute-start(f32[16,99,128]{2,0,1:T(8,128)} %copy.40), channel_id=1, source_target_pairs={{16,0},{224,240},{17,1},{225,241},{18,2},{226,242},{19,3},{227,243... | collective-permute-start | bytes 2433032 | tf_op jit(solution)/shard_map/ppermute | solution.py:205
  88.7 1.9 %pad_maximum_fusion = f32[8,11,99,128]{3,2,1,0:T(8,128)S(1)} fusion(f32[8,11,2,128]{3,2,1,0:T(2,128)} %collective-permute-done.3, f32[8,1,96,128]{3,2,1,0:T(8,128)} %copy-done.1, f32[8,1,96,128]{3,2,1,0:T(8,128)S(1)} %slice_bitcast_fusion.8, f32[8,8,96,128]{3,2,1,0:T(8,128)S(1)} %constant_dynamic-update-slice_fusion, f32[8,1,96,128]{3,2,1,0:T(8,128)} %bitcast.72, ...), kind=kLoop, calls=%fused_computation | loop fusion | flops 5575680 | bytes 8921088 | tf_op jit(solution)/shard_map/concatenate | solution.py:154
  91.5 1.4 %fusion.38 = f32[8,1,99,128]{3,2,1,0:T(8,128)S(1)} fusion(f32[9,99,128]{2,1,0:T(8,128)} %collective-permute-done.5, f32[8]{0:T(128)S(1)} %copy-done.8), kind=kLoop, calls=%fused_computation.84 | loop fusion | flops 101376 | bytes 811040 | tf_op jit(solution)/shard_map/broadcast_in_dim | solution.py:229
  92.9 1.4 %copy.41 = f32[16,99,128]{2,1,0:T(8,128)S(1)} copy(f32[16,99,128]{2,0,1:T(8,128)} %collective-permute-done.6) | data formatting | bytes 1622016 | tf_op jit(solution)/shard_map/ppermute | solution.py:205
  94.3 1.7 %maximum_select_fusion.2 = f32[32,99,128]{2,1,0:T(8,128)S(1)} fusion(f32[16,99,128]{2,1,0:T(8,128)S(1)} %copy.41, f32[16,99,128]{2,1,0:T(8,128)} %all-to-all-done.1, pred[]{:T(512)S(6)} %eq.64), kind=kLoop, calls=%fused_computation.8 | loop fusion | flops 1216512 | bytes 3244033 | tf_op jit(solution)/shard_map/jit(_where)/select_n | solution.py:218
  97.0 3.6 %fusion = f32[8,11,99,128]{3,2,1,0:T(8,128)} fusion(f32[8,11,99,128]{3,2,1,0:T(8,128)} %copy-done, s32[]{:T(128)S(6)} %select_n.172, f32[8,1,99,128]{3,2,1,0:T(8,128)S(1)} %slice-done, f32[8,4,99,128]{3,2,1,0:T(8,128)S(1)} %bitcast.69, f32[8,1,99,128]{3,2,1,0:T(8,128)S(1)} %fusion.38, f32[8,1,99,128]{3,2,1,0:T(8,128)S(1)} %broadcast_in_dim_broadcast_in_dim.5, ...), kind=kLoop, calls=%fused_computation.2 | loop fusion | flops 3649536 | bytes 7950342 | tf_op jit(solution)/shard_map/dynamic_update_slice | solution.py:244
  100.7 2.6 %slice_bitcast_fusion.2 = (f32[11,99,128]{2,1,0:T(8,128)S(1)}, f32[11,99,128]{2,1,0:T(8,128)S(1)}, f32[11,99,128]{2,1,0:T(8,128)S(1)}, f32[11,99,128]{2,1,0:T(8,...) fusion(f32[8,11,99,128]{3,2,1,0:T(8,128)} %fusion), kind=kLoop, calls=%fused_computation.43 | loop fusion | bytes 8921088 | tf_op jit(solution)/shard_map/squeeze | solution.py:94
  (87 shorter events, 23.7 us)
Async XLA Ops:
  0.6 2.3 %copy-start.7 = (f32[2,8,96,128]{3,2,1,0:T(8,128)S(1)}, f32[2,8,96,128]{3,2,1,0:T(8,128)}, u32[]{:S(2)}) copy-start(f32[2,8,96,128]{3,2,1,0:T(8,128)} %param.5) | copy-start | bytes 2359300
  3.0 1.6 %copy-start.9 = (s32[2,4]{1,0:T(2,128)S(1)}, s32[2,4]{1,0:T(2,128)}, u32[]{:S(2)}) copy-start(s32[2,4]{1,0:T(2,128)} %param.8) | copy-start | bytes 100
  3.1 6.3 %collective-permute-start.4 = (f32[16,96,128]{2,1,0:T(8,128)S(1)}, f32[16,96,128]{2,1,0:T(8,128)S(1)}, u32[]{:S(2)}, u32[]{:S(2)}) collective-permute-start(f32[16,96,128]{2,1,0:T(8,128)S(1)} %bitcast.74), channel_id=1, source_target_pairs={{0,16},{240,224},{1,17},{241,225},{2,18},{242,226},{3,19},{243,227... | collective-permute-start | bytes 2359304 | tf_op jit(solution)/shard_map/ppermute | solution.py:170
  10.4 27.7 %all-to-all-start = ((f32[16,96,128]{2,1,0:T(8,128)}), f32[16,96,128]{2,1,0:T(8,128)}, u32[]{:S(2)}, u32[]{:S(2)}) async-start(f32[16,96,128]{2,1,0:T(8,128)} %bitcast_select_fusion), calls=%async_computation | async-start | bytes 1572864 | tf_op jit(solution)/shard_map/all_to_all | solution.py:173
  38.1 3.1 %copy-start.5 = (f32[16,99,128]{2,1,0:T(8,128)S(1)}, f32[16,99,128]{2,1,0:T(8,128)}, u32[]{:S(2)}) copy-start(f32[16,99,128]{2,1,0:T(8,128)} %get-tuple-element.64) | copy-start | bytes 2433028
  38.1 3.1 %copy-start.6 = (f32[16,99,128]{2,1,0:T(8,128)S(1)}, f32[16,99,128]{2,1,0:T(8,128)}, u32[]{:S(2)}) copy-start(f32[16,99,128]{2,1,0:T(8,128)} %get-tuple-element.65) | copy-start | bytes 2433028
  43.0 29.3 %all-to-all-start.1 = ((f32[16,99,128]{2,1,0:T(8,128)}), f32[16,99,128]{2,1,0:T(8,128)}, u32[]{:S(2)}, u32[]{:S(2)}) async-start(f32[16,99,128]{2,1,0:T(8,128)} %fusion.1), calls=%async_computation.1 | async-start | bytes 1703936 | tf_op jit(solution)/shard_map/all_to_all | solution.py:203
  50.9 19.8 %collective-permute-start.1 = (f32[9,96,128]{2,1,0:T(8,128)S(1)}, f32[9,96,128]{2,1,0:T(8,128)S(1)}, u32[]{:S(2)}, u32[]{:S(2)}) collective-permute-start(f32[9,96,128]{2,1,0:T(8,128)S(1)} %pad_maximum_fusion.7), channel_id=1, source_target_pairs={{16,0},{32,16},{48,32},{64,48},{80,64},{96,80},{112,96},{128,112},... | collective-permute-start | bytes 1327112 | tf_op jit(solution)/shard_map/ppermute | solution.py:138
  53.6 17.0 %collective-permute-start = (f32[8,96,128]{2,1,0:T(8,128)S(1)}, f32[8,96,128]{2,1,0:T(8,128)S(1)}, u32[]{:S(2)}, u32[]{:S(2)}) collective-permute-start(f32[8,96,128]{2,1,0:T(8,128)S(1)} %get-tuple-element.14), channel_id=1, source_target_pairs={{0,16},{16,32},{32,48},{48,64},{64,80},{80,96},{96,112},{112,128},... | collective-permute-start | bytes 1179656 | tf_op jit(solution)/shard_map/ppermute | solution.py:134
  70.7 0.8 copy-start.3
  70.7 0.8 copy-start.1
  72.3 4.3 %copy-start.2 = (f32[8,1,96,128]{3,2,1,0:T(8,128)S(1)}, f32[8,1,96,128]{3,2,1,0:T(8,128)}, u32[]{:S(2)}) copy-start(f32[8,1,96,128]{3,2,1,0:T(8,128)} %copy-done.1) | copy-start | bytes 1179652
  72.3 4.3 %copy-start.4 = (f32[8,96,128]{2,1,0:T(8,128)S(1)}, f32[8,96,128]{2,1,0:T(8,128)}, u32[]{:S(2)}) copy-start(f32[8,96,128]{2,1,0:T(8,128)} %copy-done.3) | copy-start | bytes 1179652
  75.2 15.4 %collective-permute-start.5 = (f32[9,99,128]{2,1,0:T(8,128)}, f32[9,99,128]{2,1,0:T(8,128)}, u32[]{:S(2)}, u32[]{:S(2)}) collective-permute-start(f32[9,99,128]{2,1,0:T(8,128)} %fusion.32), channel_id=1, source_target_pairs={{0,8},{1,9},{2,10},{3,11},{4,12},{5,13},{6,14},{7,15},{8,0},{9,1},... | collective-permute-start | bytes 1368584 | tf_op jit(solution)/shard_map/ppermute | solution.py:213
  77.3 11.4 %collective-permute-start.2 = (f32[8,11,1,128]{3,2,1,0:T(1,128)}, f32[8,11,1,128]{3,2,1,0:T(1,128)}, u32[]{:S(2)}, u32[]{:S(2)}) collective-permute-start(f32[8,11,1,128]{3,2,1,0:T(1,128)} %pad_maximum_fusion.17), channel_id=1, source_target_pairs={{0,1},{1,2},{2,3},{3,4},{4,5},{5,6},{6,7},{7,8},{8,9},{9,10},{10,1... | collective-permute-start | bytes 135176 | tf_op jit(solution)/shard_map/ppermute | solution.py:148
  80.2 8.5 %collective-permute-start.3 = (f32[8,11,2,128]{3,2,1,0:T(2,128)}, f32[8,11,2,128]{3,2,1,0:T(2,128)}, u32[]{:S(2)}, u32[]{:S(2)}) collective-permute-start(f32[8,11,2,128]{3,2,1,0:T(2,128)} %pad_maximum_fusion.14), channel_id=1, source_target_pairs={{1,0},{2,1},{3,2},{4,3},{5,4},{6,5},{7,6},{8,7},{9,8},{10,9},{11,1... | collective-permute-start | bytes 270344 | tf_op jit(solution)/shard_map/ppermute | solution.py:151
  83.9 9.0 %collective-permute-start.6 = (f32[16,99,128]{2,0,1:T(8,128)}, f32[16,99,128]{2,0,1:T(8,128)}, u32[]{:S(2)}, u32[]{:S(2)}) collective-permute-start(f32[16,99,128]{2,0,1:T(8,128)} %copy.40), channel_id=1, source_target_pairs={{16,0},{224,240},{17,1},{225,241},{18,2},{226,242},{19,3},{227,243... | collective-permute-start | bytes 2433032 | tf_op jit(solution)/shard_map/ppermute | solution.py:205
  88.6 2.8 %copy-start.8 = (f32[8]{0:T(128)S(1)}, f32[8]{0:T(128)}, u32[]{:S(2)}) copy-start(f32[8]{0:T(128)} %constant.124.clone) | copy-start | bytes 100
  90.6 5.4 %copy-start = (f32[8,11,99,128]{3,2,1,0:T(8,128)}, f32[8,11,99,128]{3,2,1,0:T(8,128)S(1)}, u32[]{:S(2)}) copy-start(f32[8,11,99,128]{3,2,1,0:T(8,128)S(1)} %pad_maximum_fusion) | copy-start | bytes 13381636
  96.0 1.0 slice-start

commit v12 on v11

--- a/solution.py
+++ b/solution.py
@@ -131,10 +131,29 @@
             for b in range(phi_count)
         ]
 
+    north_side = t <= 1
+    helper = (t == 1) | (t == theta_count - 2)
+    half = channels * CAP // 2
+    pair_rows = CAP // 2
+
+    def rows_at(first):
+        parts = [lax.dynamic_slice_in_dim(f, first, pair_rows, axis=1) for f in (density, velocity, bfield)]
+        rows = jnp.concatenate(parts, axis=0)
+        return jnp.swapaxes(rows, 0, 1).reshape(half, npc, nr)
+
+    keep_first = jnp.where(at_north, 0, ct - pair_rows)
+    hand_first = jnp.where(at_north, pair_rows, ct - CAP)
+    pairs_out = [(0, 1), (theta_count - 1, theta_count - 2)]
+    pairs_in = [(1, 0), (theta_count - 2, theta_count - 1)]
+    handed = lax.ppermute(rows_at(hand_first), "theta", pairs_out)
+    work = jnp.where(helper, handed, rows_at(keep_first))
+    per_device = half // phi_count
+    work, halo_src = lax.optimization_barrier((work, combined))
+    cycle = lax.all_to_all(work, "phi", split_axis=0, concat_axis=1, tiled=True)
     low_halo = lax.ppermute(
-        combined[:, ct - 1], "theta", [(i, i + 1) for i in range(theta_count - 1)]
-    )
-    up_send = jnp.concatenate([combined[:, 0], combined[6:7, 1]], axis=0)
+        halo_src[:, ct - 1], "theta", [(i, i + 1) for i in range(theta_count - 1)]
+    )
+    up_send = jnp.concatenate([halo_src[:, 0], halo_src[6:7, 1]], axis=0)
     up_halo = lax.ppermute(up_send, "theta", [(i + 1, i) for i in range(theta_count - 1)])
     rows_ext = jnp.concatenate(
         [
@@ -153,24 +172,7 @@
     )
     early = jnp.concatenate([left_cols, rows_ext, right_cols], axis=2)
 
-    north_side = t <= 1
-    helper = (t == 1) | (t == theta_count - 2)
-    half = channels * CAP // 2
-    pair_rows = CAP // 2
-
-    def rows_at(first):
-        parts = [lax.dynamic_slice_in_dim(f, first, pair_rows, axis=1) for f in (density, velocity, bfield)]
-        rows = jnp.concatenate(parts, axis=0)
-        return jnp.swapaxes(rows, 0, 1).reshape(half, npc, nr)
-
-    keep_first = jnp.where(at_north, 0, ct - pair_rows)
-    hand_first = jnp.where(at_north, pair_rows, ct - CAP)
-    pairs_out = [(0, 1), (theta_count - 1, theta_count - 2)]
-    pairs_in = [(1, 0), (theta_count - 2, theta_count - 1)]
-    handed = lax.ppermute(rows_at(hand_first), "theta", pairs_out)
-    work = jnp.where(helper, handed, rows_at(keep_first))
-    per_device = half // phi_count
-    cycle = lax.all_to_all(work, "phi", split_axis=0, concat_axis=1, tiled=True)
+    cycle, early = lax.optimization_barrier((cycle, early))
     analysis = fourier_rows(jnp.arange(cycle_len, dtype=jnp.int32), cycle_len)
     dst_cols = (
         jnp.arange(phi_count, dtype=jnp.int32)[:, None] * npc

time: 113 us -> 107 us (0.947)
  the two profiles are of different devices: /device:TPU:1 before, /device:TPU:96 now
where the time goes in v12:
time: 107 us
  blocking collectives  27.3 us (26%)
  other arithmetic  24.3 us (23%)
  starting transfers between devices  21.4 us (20%)
  local copies, waits for them, and re-layouts  15.2 us (14%)
  waiting for transfers between devices  12.8 us (12%)
  matrix products  3.96 us (4%)
  between operations  1.7 us (2%)
    all_to_all x1, blocking collectives, local(): mine = lax.all_to_all(out, 'phi', split_axis=0, concat_axis=0, tiled=True)  27.3 us
    all_to_all x1, starting transfers between devices, local(): cycle = lax.all_to_all(work, 'phi', split_axis=0, concat_axis=1, tiled=True)  8.62 us
    ppermute x1, waiting for transfers between devices, local(): lax.ppermute(ghost_send, both, [(a * phi_count + b, a * phi_count + (b +...  7.09 us
    cos x1, other arithmetic, fourier_rows(): return jnp.concatenate([jnp.cos(angle), jnp.sin(angle)], axis=-1)  5.34 us
    sin x1, other arithmetic, fourier_rows(): return jnp.concatenate([jnp.cos(angle), jnp.sin(angle)], axis=-1)  4.32 us
    ppermute x1, waiting for transfers between devices, local(): lax.ppermute(rows_ext[:, :, :2], 'phi', [((i + 1) % phi_count, i) for i i...  4.15 us
    unnamed x16, local copies, waits for them, and re-layouts  4.13 us
    another operation x6, other arithmetic, advance(): return (jnp.stack(densities), jnp.stack([new_radial, new_theta, new_phi]))  4.05 us
  transfers between devices with their start and end apart: 8, of which 3 were waited for; matrix products, arithmetic and copies ran while one was open for 21% of the time, Pallas kernels for 0%

profile of v12, /device:TPU:96, one launch (start us, length us, event | category | flops | bytes accessed | tf_op | source)
XLA Modules:
  0.0 106.7 jit_solution(16736170178209638718)
XLA Ops:
  0.6 1.1 constant_dynamic-slice_fusion.3
  1.7 1.3 %constant_dynamic-slice_fusion.1 = (f32[3,2,96,128]{3,2,1,0:T(8,128)S(1)}, f32[3,2,96,128]{3,2,1,0:T(8,128)S(1)}, f32[3,2,96,128]{3,2,1,0:T(8,128)S(1)}, f32[3,2,96,128]{3,2,1,0:T(8,128)S(1)}) fusion(f32[3,8,96,128]{3,2,1,0:T(8,128)} %param.7, s32[]{:T(128)S(6)} %select_n.153, s32[]{:T(128)S(6)} %select_n.152, f32[3,8,96,128]{3,2,1,0:T(8,128)} %param.6), kind=kLoop, calls=%fused_computation.157 | loop fusion | bytes 2359304 | tf_op jit(solution)/shard_map/dynamic_slice | solution.py:140
  4.0 2.6 %collective-permute-start = (f32[16,96,128]{2,1,0:T(8,128)}, f32[16,96,128]{2,1,0:T(8,128)}, u32[]{:S(2)}, u32[]{:S(2)}) collective-permute-start(f32[16,96,128]{2,1,0:T(8,128)} %bitcast.1), channel_id=1, source_target_pairs={{0,16},{240,224},{1,17},{241,225},{2,18},{242,226},{3,19},{243,227... | collective-permute-start | bytes 2359304 | tf_op jit(solution)/shard_map/ppermute | solution.py:148
  7.7 1.2 %constant_dynamic-update-slice_fusion.2 = f32[8,8,96,128]{3,2,1,0:T(8,128)S(1)} fusion(f32[2,8,96,128]{3,2,1,0:T(8,128)} %param.5), kind=kLoop, calls=%fused_computation.151 | loop fusion | bytes 1572864
  8.9 1.4 %constant_dynamic-update-slice_fusion.1 = f32[8,8,96,128]{3,2,1,0:T(8,128)S(1)} fusion(f32[8,8,96,128]{3,2,1,0:T(8,128)S(1)} %constant_dynamic-update-slice_fusion.2, f32[3,8,96,128]{3,2,1,0:T(8,128)} %param.6), kind=kLoop, calls=%fused_computation.150 | loop fusion | bytes 2359296
  10.3 1.4 %constant_dynamic-update-slice_fusion = f32[8,8,96,128]{3,2,1,0:T(8,128)S(1)} fusion(f32[8,8,96,128]{3,2,1,0:T(8,128)S(1)} %constant_dynamic-update-slice_fusion.1, f32[3,8,96,128]{3,2,1,0:T(8,128)} %param.7), kind=kLoop, calls=%fused_computation.149 | loop fusion | bytes 2359296 | tf_op jit(solution)/shard_map/concatenate | solution.py:114
  13.6 1.3 %collective-permute-start.2 = (f32[9,96,128]{2,1,0:T(8,128)}, f32[9,96,128]{2,1,0:T(8,128)}, u32[]{:S(2)}, u32[]{:S(2)}) collective-permute-start(f32[9,96,128]{2,1,0:T(8,128)} %pad_maximum_fusion.7), channel_id=1, source_target_pairs={{16,0},{32,16},{48,32},{64,48},{80,64},{96,80},{112,96},{128,112},... | collective-permute-start | bytes 1327112 | tf_op jit(solution)/shard_map/ppermute | solution.py:157
  14.9 8.6 %all-to-all-start = ((f32[16,96,128]{2,1,0:T(8,128)}), f32[16,96,128]{2,1,0:T(8,128)}, u32[]{:S(2)}, u32[]{:S(2)}) async-start(f32[16,96,128]{2,1,0:T(8,128)} %bitcast_select_fusion), calls=%async_computation | async-start | bytes 1572864 | tf_op jit(solution)/shard_map/all_to_all | solution.py:152
  23.5 5.3 %fusion.20 = (f32[16,99,128]{2,1,0:T(8,128)}, f32[16,99,128]{2,1,0:T(8,128)}) fusion(s32[16,99]{1,0:T(8,128)S(1)} %add_select_fusion.2), kind=kLoop, calls=%fused_computation.25 | loop fusion | flops 1824768 | bytes 1628352 | tf_op jit(solution)/shard_map/cos | solution.py:110
  30.2 4.3 %fusion.27 = (f32[1536,128]{1,0:T(8,128)}, f32[1536,128]{1,0:T(8,128)}) fusion(), kind=kLoop, calls=%fused_computation.37 | loop fusion | flops 1769472 | bytes 1572864 | tf_op jit(solution)/shard_map/sin | solution.py:110
  34.5 2.5 %collective-permute-start.1 = (f32[8,96,128]{2,1,0:T(8,128)S(1)}, f32[8,96,128]{2,1,0:T(8,128)S(1)}, u32[]{:S(2)}, u32[]{:S(2)}) collective-permute-start(f32[8,96,128]{2,1,0:T(8,128)S(1)} %get-tuple-element.22), channel_id=1, source_target_pairs={{0,16},{16,32},{32,48},{48,64},{64,80},{80,96},{96,112},{112,128},... | collective-permute-start | bytes 1179656 | tf_op jit(solution)/shard_map/ppermute | solution.py:153
  37.8 1.0 slice_bitcast_fusion.8
  39.0 2.8 %collective-permute-start.3 = (f32[8,11,1,128]{3,2,1,0:T(1,128)S(1)}, f32[8,11,1,128]{3,2,1,0:T(1,128)S(1)}, u32[]{:S(2)}, u32[]{:S(2)}) collective-permute-start(f32[8,11,1,128]{3,2,1,0:T(1,128)S(1)} %pad_maximum_fusion.17), channel_id=1, source_target_pairs={{0,1},{1,2},{2,3},{3,4},{4,5},{5,6},{6,7},{7,8},{8,9},{9,10},{10,1... | collective-permute-start | bytes 135176 | tf_op jit(solution)/shard_map/ppermute | solution.py:167
  41.9 1.6 %collective-permute-done.3 = f32[8,11,1,128]{3,2,1,0:T(1,128)S(1)} collective-permute-done((f32[8,11,1,128]{3,2,1,0:T(1,128)S(1)}, f32[8,11,1,128]{3,2,1,0:T(1,128)S(1)}, u32[]{:S(2)}, u32[]{:S(2)}) %collective-permute-start.3) | collective-permute-done | bytes 45088 | tf_op jit(solution)/shard_map/ppermute | solution.py:167
  43.4 4.2 %collective-permute-done.4 = f32[8,11,2,128]{3,2,1,0:T(2,128)S(1)} collective-permute-done((f32[8,11,2,128]{3,2,1,0:T(2,128)S(1)}, f32[8,11,2,128]{3,2,1,0:T(2,128)S(1)}, u32[]{:S(2)}, u32[]{:S(2)}) %collective-permute-start.4) | collective-permute-done | bytes 90144 | tf_op jit(solution)/shard_map/ppermute | solution.py:170
  47.6 2.5 %pad_maximum_fusion = f32[8,11,99,128]{3,2,1,0:T(8,128)} fusion(f32[8,11,2,128]{3,2,1,0:T(2,128)S(1)} %collective-permute-done.4, f32[8,1,96,128]{3,2,1,0:T(8,128)S(1)} %broadcast_in_dim_broadcast_in_dim.4, f32[8,1,96,128]{3,2,1,0:T(8,128)S(1)} %slice_bitcast_fusion.8, f32[8,8,96,128]{3,2,1,0:T(8,128)S(1)} %constant_dynamic-update-slice_fusion, ...), kind=kLoop, calls=%fused_computation | loop fusion | flops 5575680 | bytes 8921088 | tf_op jit(solution)/shard_map/concatenate | solution.py:173
  50.1 3.1 %fusion.12 = f32[256,128,1]{1,0,2:T(8,128)S(1)} fusion(f32[1536,128]{1,0:T(8,128)} %get-tuple-element.78, f32[1536,128]{1,0:T(8,128)} %get-tuple-element.79, f32[1,1536,128]{2,1,0:T(8,128)} %bitcast.4, f32[256]{0:T(256)S(1)} %compare_select_fusion.1), kind=kOutput, calls=%fused_computation.18 | convolution fusion | flops 302415872 | bytes 2491392 | tf_op jit(solution)/shard_map/smr,mn->snr/dot_general | solution.py:201
  54.1 27.3 %all_to_all.17 = f32[16,99,128]{2,1,0:T(8,128)S(1)} all-to-all(f32[16,99,128]{2,1,0:T(8,128)S(1)} %fusion.1), channel_id=1, replica_groups=mesh['theta'=16,'phi'=16] {'phi'}, dimensions={0} | all-to-all | bytes 1622016 | tf_op jit(solution)/shard_map/all_to_all | solution.py:205
  81.6 2.1 %collective-permute-start.5 = (f32[9,99,128]{2,1,0:T(8,128)S(1)}, f32[9,99,128]{2,1,0:T(8,128)}, u32[]{:S(2)}, u32[]{:S(2)}) collective-permute-start(f32[9,99,128]{2,1,0:T(8,128)S(1)} %fusion.33), channel_id=1, source_target_pairs={{0,8},{1,9},{2,10},{3,11},{4,12},{5,13},{6,14},{7,15},{8,0},{9,1},... | collective-permute-start | bytes 1368584 | tf_op jit(solution)/shard_map/ppermute | solution.py:215
  83.8 1.5 %collective-permute-start.6 = (f32[16,99,128]{2,0,1:T(8,128)S(1)}, f32[16,99,128]{2,0,1:T(8,128)S(1)}, u32[]{:S(2)}, u32[]{:S(2)}) collective-permute-start(f32[16,99,128]{2,0,1:T(8,128)S(1)} %copy.28), channel_id=1, source_target_pairs={{16,0},{224,240},{17,1},{225,241},{18,2},{226,242},{19,3},{227,243... | collective-permute-start | bytes 2433032 | tf_op jit(solution)/shard_map/ppermute | solution.py:207
  85.3 7.1 %collective-permute-done.5 = f32[9,99,128]{2,1,0:T(8,128)} collective-permute-done((f32[9,99,128]{2,1,0:T(8,128)S(1)}, f32[9,99,128]{2,1,0:T(8,128)}, u32[]{:S(2)}, u32[]{:S(2)}) %collective-permute-start.5) | collective-permute-done | bytes 456224 | tf_op jit(solution)/shard_map/ppermute | solution.py:215
  93.2 1.1 %fusion.39 = f32[8,1,99,128]{3,2,1,0:T(8,128)S(1)} fusion(f32[9,99,128]{2,1,0:T(8,128)} %collective-permute-done.5, f32[8]{0:T(128)S(1)} %copy-done.3), kind=kLoop, calls=%fused_computation.85 | loop fusion | flops 101376 | bytes 811040 | tf_op jit(solution)/shard_map/broadcast_in_dim | solution.py:231
  95.1 1.5 %slice-done.1 = s8[4194304]{0:T(1024)(128)(4,1)S(1)} async-done(((s8[4685824]{0:T(1024)(128)(4,1)}), s8[4194304]{0:T(1024)(128)(4,1)S(1)}, s32[]{:S(2)}) %slice-start.1) | async-done | bytes 4194328
  105.6 1.1 %pad_maximum_fusion.1 = f32[3,8,96,128]{3,2,1,0:T(8,128)} fusion(f32[1,8,96,128]{3,2,1,0:T(8,128)S(1)} %get-tuple-element.71, f32[1,8,96,128]{3,2,1,0:T(8,128)S(1)} %get-tuple-element.70, f32[1,8,96,128]{3,2,1,0:T(8,128)S(1)} %fusion.55), kind=kLoop, calls=%fused_computation.16 | loop fusion | flops 589824 | bytes 2359296 | tf_op jit(solution)/shard_map/stack | solution.py:103
  (80 shorter events, 17.2 us)
Async XLA Ops:
  4.0 7.7 %collective-permute-start = (f32[16,96,128]{2,1,0:T(8,128)}, f32[16,96,128]{2,1,0:T(8,128)}, u32[]{:S(2)}, u32[]{:S(2)}) collective-permute-start(f32[16,96,128]{2,1,0:T(8,128)} %bitcast.1), channel_id=1, source_target_pairs={{0,16},{240,224},{1,17},{241,225},{2,18},{242,226},{3,19},{243,227... | collective-permute-start | bytes 2359304 | tf_op jit(solution)/shard_map/ppermute | solution.py:148
  8.9 2.9 %copy-start.2 = (f32[8,2,96,128]{3,2,0,1:T(8,128)S(1)}, f32[8,2,96,128]{3,2,0,1:T(8,128)}, u32[]{:S(2)}) copy-start(f32[8,2,96,128]{3,2,0,1:T(8,128)} %copy.41) | copy-start | bytes 2359300
  12.8 16.1 %copy-start.4 = (s32[2,4]{1,0:T(2,128)S(1)}, s32[2,4]{1,0:T(2,128)}, u32[]{:S(2)}) copy-start(s32[2,4]{1,0:T(2,128)} %param.8) | copy-start | bytes 100
  13.6 23.4 %collective-permute-start.2 = (f32[9,96,128]{2,1,0:T(8,128)}, f32[9,96,128]{2,1,0:T(8,128)}, u32[]{:S(2)}, u32[]{:S(2)}) collective-permute-start(f32[9,96,128]{2,1,0:T(8,128)} %pad_maximum_fusion.7), channel_id=1, source_target_pairs={{16,0},{32,16},{48,32},{64,48},{80,64},{96,80},{112,96},{128,112},... | collective-permute-start | bytes 1327112 | tf_op jit(solution)/shard_map/ppermute | solution.py:157
  14.9 35.2 %all-to-all-start = ((f32[16,96,128]{2,1,0:T(8,128)}), f32[16,96,128]{2,1,0:T(8,128)}, u32[]{:S(2)}, u32[]{:S(2)}) async-start(f32[16,96,128]{2,1,0:T(8,128)} %bitcast_select_fusion), calls=%async_computation | async-start | bytes 1572864 | tf_op jit(solution)/shard_map/all_to_all | solution.py:152
  34.5 4.3 %collective-permute-start.1 = (f32[8,96,128]{2,1,0:T(8,128)S(1)}, f32[8,96,128]{2,1,0:T(8,128)S(1)}, u32[]{:S(2)}, u32[]{:S(2)}) collective-permute-start(f32[8,96,128]{2,1,0:T(8,128)S(1)} %get-tuple-element.22), channel_id=1, source_target_pairs={{0,16},{16,32},{32,48},{48,64},{64,80},{80,96},{96,112},{112,128},... | collective-permute-start | bytes 1179656 | tf_op jit(solution)/shard_map/ppermute | solution.py:153
  39.0 4.5 %collective-permute-start.3 = (f32[8,11,1,128]{3,2,1,0:T(1,128)S(1)}, f32[8,11,1,128]{3,2,1,0:T(1,128)S(1)}, u32[]{:S(2)}, u32[]{:S(2)}) collective-permute-start(f32[8,11,1,128]{3,2,1,0:T(1,128)S(1)} %pad_maximum_fusion.17), channel_id=1, source_target_pairs={{0,1},{1,2},{2,3},{3,4},{4,5},{5,6},{6,7},{7,8},{8,9},{9,10},{10,1... | collective-permute-start | bytes 135176 | tf_op jit(solution)/shard_map/ppermute | solution.py:167
  41.8 5.8 %collective-permute-start.4 = (f32[8,11,2,128]{3,2,1,0:T(2,128)S(1)}, f32[8,11,2,128]{3,2,1,0:T(2,128)S(1)}, u32[]{:S(2)}, u32[]{:S(2)}) collective-permute-start(f32[8,11,2,128]{3,2,1,0:T(2,128)S(1)} %pad_maximum_fusion.14), channel_id=1, source_target_pairs={{1,0},{2,1},{3,2},{4,3},{5,4},{6,5},{7,6},{8,7},{9,8},{10,9},{11,1... | collective-permute-start | bytes 270344 | tf_op jit(solution)/shard_map/ppermute | solution.py:170
  50.1 3.1 %copy-start = (f32[16,99,128]{2,1,0:T(8,128)S(1)}, f32[16,99,128]{2,1,0:T(8,128)}, u32[]{:S(2)}) copy-start(f32[16,99,128]{2,1,0:T(8,128)} %get-tuple-element.72) | copy-start | bytes 2433028
  50.1 3.2 %copy-start.1 = (f32[16,99,128]{2,1,0:T(8,128)S(1)}, f32[16,99,128]{2,1,0:T(8,128)}, u32[]{:S(2)}) copy-start(f32[16,99,128]{2,1,0:T(8,128)} %get-tuple-element.73) | copy-start | bytes 2433028
  81.5 11.8 %copy-start.3 = (f32[8]{0:T(128)S(1)}, f32[8]{0:T(128)}, u32[]{:S(2)}) copy-start(f32[8]{0:T(128)} %constant.124.clone) | copy-start | bytes 100
  81.5 13.6 %slice-start = ((s8[4685824]{0:T(1024)(128)(4,1)}), s8[491520]{0:T(1024)(128)(4,1)S(1)}, s32[]{:S(2)}) async-start(s8[4685824]{0:T(1024)(128)(4,1)} %bitcast.67), calls=%async_computation.2 | async-start | bytes 983040
  81.6 10.8 %collective-permute-start.5 = (f32[9,99,128]{2,1,0:T(8,128)S(1)}, f32[9,99,128]{2,1,0:T(8,128)}, u32[]{:S(2)}, u32[]{:S(2)}) collective-permute-start(f32[9,99,128]{2,1,0:T(8,128)S(1)} %fusion.33), channel_id=1, source_target_pairs={{0,8},{1,9},{2,10},{3,11},{4,12},{5,13},{6,14},{7,15},{8,0},{9,1},... | collective-permute-start | bytes 1368584 | tf_op jit(solution)/shard_map/ppermute | solution.py:215
  83.8 10.5 %collective-permute-start.6 = (f32[16,99,128]{2,0,1:T(8,128)S(1)}, f32[16,99,128]{2,0,1:T(8,128)S(1)}, u32[]{:S(2)}, u32[]{:S(2)}) collective-permute-start(f32[16,99,128]{2,0,1:T(8,128)S(1)} %copy.28), channel_id=1, source_target_pairs={{16,0},{224,240},{17,1},{225,241},{18,2},{226,242},{19,3},{227,243... | collective-permute-start | bytes 2433032 | tf_op jit(solution)/shard_map/ppermute | solution.py:207
  94.4 2.2 %slice-start.1 = ((s8[4685824]{0:T(1024)(128)(4,1)}), s8[4194304]{0:T(1024)(128)(4,1)S(1)}, s32[]{:S(2)}) async-start(s8[4685824]{0:T(1024)(128)(4,1)} %bitcast.67), calls=%async_computation.3 | async-start | bytes 8388608
  94.9 1.9 %slice-start.2 = ((f32[8,11,99,128]{3,2,1,0:T(8,128)}), f32[8,1,99,128]{3,2,1,0:T(8,128)S(1)}, s32[]{:S(2)}) async-start(f32[8,11,99,128]{3,2,1,0:T(8,128)} %pad_maximum_fusion), calls=%async_computation.4 | async-start | bytes 851968 | tf_op jit(solution)/shard_map/slice | solution.py:231

commit v13 on v12

--- a/solution.py
+++ b/solution.py
@@ -223,6 +223,19 @@
         jnp.concatenate([from_helper, mine], axis=0),
     )
     cap_rows = jnp.swapaxes(in_order.reshape(CAP, channels, npc + 3, nr), 0, 1)
+    cap_start = jnp.where(at_north, 1, ct - CAP + 1)
+    kept_cap = lax.dynamic_slice_in_dim(early, cap_start, CAP, axis=1)
+    cap_block = jnp.where(at_north | at_south, cap_rows, kept_cap)
+    with_caps = lax.dynamic_update_slice_in_dim(early, cap_block, cap_start, axis=1)
+
+    near_rows = 2
+    rest_rows = ct - near_rows
+
+    def rows_from(x, first, count):
+        return advance(lax.dynamic_slice_in_dim(x, first, count + 3, axis=1))
+
+    rest = rows_from(with_caps, jnp.where(at_north, near_rows, 0), rest_rows)
+    ghost, rest = lax.optimization_barrier((ghost, rest))
     ghost_main = ghost[:channels]
     ghost_b = ghost[channels:]
     ghost_main = ghost_main * parity[:, None, None]
@@ -244,7 +257,13 @@
         at_north, north_block, jnp.where(at_south, south_block, kept_block)
     )
     extended = lax.dynamic_update_slice_in_dim(early, block, offset, axis=1)
-    return advance(extended)
+    near = rows_from(extended, jnp.where(at_north, 0, rest_rows), near_rows)
+    outs = []
+    for a, c in zip(rest, near):
+        north_order = jnp.concatenate([c, a], axis=1)
+        other_order = jnp.concatenate([a, c], axis=1)
+        outs.append(jnp.where(at_north, north_order, other_order))
+    return tuple(outs)
 
 
 def solution(mesh):

time: 107 us -> 109 us (1.019)
  the two profiles are of different devices: /device:TPU:96 before, /device:TPU:1 now
where the time goes in v13:
time: 109 us; the launch traced here: 108 us
  other arithmetic  25.5 us (23%)
  starting transfers between devices  25.1 us (23%)
  blocking collectives  23.1 us (21%)
  local copies, waits for them, and re-layouts  19.9 us (18%)
  waiting for transfers between devices  8.11 us (7%)
  matrix products  3.96 us (4%)
  between operations  1.87 us (2%)
    all_to_all x1, blocking collectives, local(): mine = lax.all_to_all(out, 'phi', split_axis=0, concat_axis=0, tiled=True)  23.1 us
    all_to_all x1, starting transfers between devices, local(): cycle = lax.all_to_all(work, 'phi', split_axis=0, concat_axis=1, tiled=True)  9.85 us
    unnamed x19, local copies, waits for them, and re-layouts  6.44 us
    cos x1, other arithmetic, fourier_rows(): return jnp.concatenate([jnp.cos(angle), jnp.sin(angle)], axis=-1)  5.32 us
    ppermute x1, waiting for transfers between devices, local(): lax.ppermute(rows_ext[:, :, npc - 1:], 'phi', [(i, (i + 1) % phi_count) f...  4.98 us
    ppermute x1, starting transfers between devices, local(): lax.ppermute(rows_ext[:, :, :2], 'phi', [((i + 1) % phi_count, i) for i i...  4.48 us
    sin x1, other arithmetic, fourier_rows(): return jnp.concatenate([jnp.cos(angle), jnp.sin(angle)], axis=-1)  4.32 us
    ppermute x1, starting transfers between devices, local(): lax.ppermute(halo_src[:, ct - 1], 'theta', [(i, i + 1) for i in range(the...  3.91 us
  transfers between devices with their start and end apart: 8, of which 3 were waited for; matrix products, arithmetic and copies ran while one was open for 29% of the time, Pallas kernels for 0%

profile of v13, /device:TPU:1, one launch (start us, length us, event | category | flops | bytes accessed | tf_op | source)
XLA Modules:
  0.0 107.5 jit_solution(4346008916122766232)
XLA Ops:
  0.6 1.1 constant_dynamic-slice_fusion.3
  1.7 1.3 %constant_dynamic-slice_fusion.1 = (f32[3,2,96,128]{3,2,1,0:T(8,128)S(1)}, f32[3,2,96,128]{3,2,1,0:T(8,128)S(1)}, f32[3,2,96,128]{3,2,1,0:T(8,128)S(1)}, f32[3,2,96,128]{3,2,1,0:T(8,128)S(1)}) fusion(f32[3,8,96,128]{3,2,1,0:T(8,128)} %param.7, s32[]{:T(128)S(6)} %select_n.202, s32[]{:T(128)S(6)} %select_n.201, f32[3,8,96,128]{3,2,1,0:T(8,128)} %param.6), kind=kLoop, calls=%fused_computation.249 | loop fusion | bytes 2359304 | tf_op jit(solution)/shard_map/dynamic_slice | solution.py:140
  4.0 1.3 %collective-permute-start = (f32[16,96,128]{2,1,0:T(8,128)}, f32[16,96,128]{2,1,0:T(8,128)}, u32[]{:S(2)}, u32[]{:S(2)}) collective-permute-start(f32[16,96,128]{2,1,0:T(8,128)} %bitcast.1), channel_id=1, source_target_pairs={{0,16},{240,224},{1,17},{241,225},{2,18},{242,226},{3,19},{243,227... | collective-permute-start | bytes 2359304 | tf_op jit(solution)/shard_map/ppermute | solution.py:148
  6.3 1.2 %constant_dynamic-update-slice_fusion.2 = f32[8,8,96,128]{3,2,1,0:T(8,128)S(1)} fusion(f32[2,8,96,128]{3,2,1,0:T(8,128)} %param.5), kind=kLoop, calls=%fused_computation.243 | loop fusion | bytes 1572864
  7.5 1.4 %constant_dynamic-update-slice_fusion.1 = f32[8,8,96,128]{3,2,1,0:T(8,128)S(1)} fusion(f32[8,8,96,128]{3,2,1,0:T(8,128)S(1)} %constant_dynamic-update-slice_fusion.2, f32[3,8,96,128]{3,2,1,0:T(8,128)} %param.6), kind=kLoop, calls=%fused_computation.242 | loop fusion | bytes 2359296
  8.9 1.4 %constant_dynamic-update-slice_fusion = f32[8,8,96,128]{3,2,1,0:T(8,128)S(1)} fusion(f32[8,8,96,128]{3,2,1,0:T(8,128)S(1)} %constant_dynamic-update-slice_fusion.1, f32[3,8,96,128]{3,2,1,0:T(8,128)} %param.7), kind=kLoop, calls=%fused_computation.241 | loop fusion | bytes 2359296 | tf_op jit(solution)/shard_map/concatenate | solution.py:114
  10.7 2.1 %bitcast_select_fusion = f32[16,96,128]{2,1,0:T(8,128)} fusion(f32[16,96,128]{2,1,0:T(8,128)} %collective-permute-done, f32[8,2,96,128]{3,2,0,1:T(8,128)S(1)} %copy-done.2, pred[]{:T(512)S(6)} %or.6), kind=kLoop, calls=%fused_computation.34 | loop fusion | flops 196608 | bytes 2359297 | tf_op jit(solution)/shard_map/jit(_where)/select_n | solution.py:149
  14.2 9.9 %all-to-all-start = ((f32[16,96,128]{2,1,0:T(8,128)}), f32[16,96,128]{2,1,0:T(8,128)}, u32[]{:S(2)}, u32[]{:S(2)}) async-start(f32[16,96,128]{2,1,0:T(8,128)} %bitcast_select_fusion), calls=%async_computation | async-start | bytes 1572864 | tf_op jit(solution)/shard_map/all_to_all | solution.py:152
  24.1 1.6 %pad_maximum_fusion.7 = f32[9,96,128]{2,1,0:T(8,128)} fusion(f32[1,96,128]{2,1,0:T(8,128)} %slice_bitcast_fusion.4, f32[8,96,128]{2,1,0:T(8,128)S(1)} %get-tuple-element.41), kind=kLoop, calls=%fused_computation.54 | loop fusion | flops 110592 | bytes 884736 | tf_op jit(solution)/shard_map/concatenate | solution.py:156
  25.7 3.3 %collective-permute-start.2 = (f32[9,96,128]{2,1,0:T(8,128)}, f32[9,96,128]{2,1,0:T(8,128)}, u32[]{:S(2)}, u32[]{:S(2)}) collective-permute-start(f32[9,96,128]{2,1,0:T(8,128)} %pad_maximum_fusion.7), channel_id=1, source_target_pairs={{16,0},{32,16},{48,32},{64,48},{80,64},{96,80},{112,96},{128,112},... | collective-permute-start | bytes 1327112 | tf_op jit(solution)/shard_map/ppermute | solution.py:157
  29.0 5.3 %fusion.20 = (f32[16,99,128]{2,1,0:T(8,128)}, f32[16,99,128]{2,1,0:T(8,128)}) fusion(s32[16,99]{1,0:T(8,128)S(1)} %add_select_fusion.2), kind=kLoop, calls=%fused_computation.27 | loop fusion | flops 1824768 | bytes 1628352 | tf_op jit(solution)/shard_map/cos | solution.py:110
  35.6 4.3 %fusion.27 = (f32[1536,128]{1,0:T(8,128)}, f32[1536,128]{1,0:T(8,128)}) fusion(), kind=kLoop, calls=%fused_computation.39 | loop fusion | flops 1769472 | bytes 1572864 | tf_op jit(solution)/shard_map/sin | solution.py:110
  39.9 3.9 %collective-permute-start.1 = (f32[8,96,128]{2,1,0:T(8,128)S(1)}, f32[8,96,128]{2,1,0:T(8,128)S(1)}, u32[]{:S(2)}, u32[]{:S(2)}) collective-permute-start(f32[8,96,128]{2,1,0:T(8,128)S(1)} %copy-done.3), channel_id=1, source_target_pairs={{0,16},{16,32},{32,48},{48,64},{64,80},{80,96},{96,112},{112,128},... | collective-permute-start | bytes 1179656 | tf_op jit(solution)/shard_map/ppermute | solution.py:153
  44.6 1.0 slice_bitcast_fusion
  45.6 2.9 %collective-permute-done.1 = f32[8,96,128]{2,1,0:T(8,128)S(1)} collective-permute-done((f32[8,96,128]{2,1,0:T(8,128)S(1)}, f32[8,96,128]{2,1,0:T(8,128)S(1)}, u32[]{:S(2)}, u32[]{:S(2)}) %collective-permute-start.1) | collective-permute-done | bytes 393248 | tf_op jit(solution)/shard_map/ppermute | solution.py:153
  48.6 4.5 %collective-permute-start.4 = (f32[8,11,2,128]{3,2,1,0:T(2,128)S(1)}, f32[8,11,2,128]{3,2,1,0:T(2,128)S(1)}, u32[]{:S(2)}, u32[]{:S(2)}) collective-permute-start(f32[8,11,2,128]{3,2,1,0:T(2,128)S(1)} %pad_maximum_fusion.20), channel_id=1, source_target_pairs={{1,0},{2,1},{3,2},{4,3},{5,4},{6,5},{7,6},{8,7},{9,8},{10,9},{11,1... | collective-permute-start | bytes 270344 | tf_op jit(solution)/shard_map/ppermute | solution.py:170
  53.2 5.0 %collective-permute-done.3 = f32[8,11,1,128]{3,2,1,0:T(1,128)S(1)} collective-permute-done((f32[8,11,1,128]{3,2,1,0:T(1,128)S(1)}, f32[8,11,1,128]{3,2,1,0:T(1,128)S(1)}, u32[]{:S(2)}, u32[]{:S(2)}) %collective-permute-start.3) | collective-permute-done | bytes 45088 | tf_op jit(solution)/shard_map/ppermute | solution.py:167
  58.2 2.6 %pad_maximum_fusion = f32[8,11,99,128]{3,2,1,0:T(8,128)} fusion(f32[8,11,2,128]{3,2,1,0:T(2,128)S(1)} %collective-permute-done.4, f32[8,1,96,128]{3,2,1,0:T(8,128)S(1)} %broadcast_in_dim_broadcast_in_dim.4, f32[8,1,96,128]{3,2,1,0:T(8,128)S(1)} %slice_bitcast_fusion, f32[8,8,96,128]{3,2,1,0:T(8,128)S(1)} %constant_dynamic-update-slice_fusion, ...), kind=kLoop, calls=%fused_computation | loop fusion | flops 5575680 | bytes 8921088 | tf_op jit(solution)/shard_map/concatenate | solution.py:173
  60.8 3.1 %fusion.12 = f32[256,128,1]{1,0,2:T(8,128)S(1)} fusion(f32[1536,128]{1,0:T(8,128)} %get-tuple-element.138, f32[1536,128]{1,0:T(8,128)} %get-tuple-element.139, f32[1,1536,128]{2,1,0:T(8,128)} %bitcast.4, f32[256]{0:T(256)S(1)} %compare_select_fusion.1), kind=kOutput, calls=%fused_computation.19 | convolution fusion | flops 302415872 | bytes 2491392 | tf_op jit(solution)/shard_map/smr,mn->snr/dot_general | solution.py:201
  64.8 23.1 %all_to_all.17 = f32[16,99,128]{2,1,0:T(8,128)S(1)} all-to-all(f32[16,99,128]{2,1,0:T(8,128)S(1)} %fusion.1), channel_id=1, replica_groups=mesh['theta'=16,'phi'=16] {'phi'}, dimensions={0} | all-to-all | bytes 1622016 | tf_op jit(solution)/shard_map/all_to_all | solution.py:205
  88.0 1.3 %collective-permute-start.6 = (f32[16,99,128]{2,0,1:T(8,128)S(1)}, f32[16,99,128]{2,0,1:T(8,128)S(1)}, u32[]{:S(2)}, u32[]{:S(2)}) collective-permute-start(f32[16,99,128]{2,0,1:T(8,128)S(1)} %copy.28), channel_id=1, source_target_pairs={{16,0},{224,240},{17,1},{225,241},{18,2},{226,242},{19,3},{227,243... | collective-permute-start | bytes 2433032 | tf_op jit(solution)/shard_map/ppermute | solution.py:207
  89.4 2.5 %copy.49 = f32[8,11,99,128]{3,2,1,0:T(8,128)S(1)} copy(f32[8,11,99,128]{3,2,1,0:T(8,128)} %pad_maximum_fusion) | data formatting | bytes 8921088
  91.9 1.1 %slice-done.1 = s8[4194304]{0:T(1024)(128)(4,1)S(1)} async-done(((s8[4685824]{0:T(1024)(128)(4,1)}), s8[4194304]{0:T(1024)(128)(4,1)S(1)}, s32[]{:S(2)}) %slice-start.1) | async-done | bytes 4194328
  106.4 1.2 %maximum_select_fusion.3 = f32[3,8,96,128]{3,2,1,0:T(8,128)} fusion(f32[3,6,96,128]{3,2,1,0:T(8,128)S(1)} %pad_maximum_fusion.1, f32[1,2,96,128]{3,2,1,0:T(8,128)S(1)} %get-tuple-element.129, f32[1,2,96,128]{3,2,1,0:T(8,128)S(1)} %get-tuple-element.128, f32[1,2,96,128]{3,2,1,0:T(8,128)S(1)} %fusion.88, pred[]{:T(512)S(6)} %eq.78), kind=kLoop, calls=%fused_computation.17 | loop fusion | flops 2064384 | bytes 2359297 | tf_op jit(solution)/shard_map/jit(_where)/select_n | solution.py:265
  (113 shorter events, 19.4 us)
Async XLA Ops:
  4.0 6.6 %collective-permute-start = (f32[16,96,128]{2,1,0:T(8,128)}, f32[16,96,128]{2,1,0:T(8,128)}, u32[]{:S(2)}, u32[]{:S(2)}) collective-permute-start(f32[16,96,128]{2,1,0:T(8,128)} %bitcast.1), channel_id=1, source_target_pairs={{0,16},{240,224},{1,17},{241,225},{2,18},{242,226},{3,19},{243,227... | collective-permute-start | bytes 2359304 | tf_op jit(solution)/shard_map/ppermute | solution.py:148
  7.5 3.2 %copy-start.2 = (f32[8,2,96,128]{3,2,0,1:T(8,128)S(1)}, f32[8,2,96,128]{3,2,0,1:T(8,128)}, u32[]{:S(2)}) copy-start(f32[8,2,96,128]{3,2,0,1:T(8,128)} %copy.41) | copy-start | bytes 2359300
  13.4 20.9 %copy-start.5 = (s32[2,4]{1,0:T(2,128)S(1)}, s32[2,4]{1,0:T(2,128)}, u32[]{:S(2)}) copy-start(s32[2,4]{1,0:T(2,128)} %param.8) | copy-start | bytes 100
  14.2 46.6 %all-to-all-start = ((f32[16,96,128]{2,1,0:T(8,128)}), f32[16,96,128]{2,1,0:T(8,128)}, u32[]{:S(2)}, u32[]{:S(2)}) async-start(f32[16,96,128]{2,1,0:T(8,128)} %bitcast_select_fusion), calls=%async_computation | async-start | bytes 1572864 | tf_op jit(solution)/shard_map/all_to_all | solution.py:152
  25.7 14.2 %copy-start.3 = (f32[8,96,128]{2,1,0:T(8,128)S(1)}, f32[8,96,128]{2,1,0:T(8,128)}, u32[]{:S(2)}) copy-start(f32[8,96,128]{2,1,0:T(8,128)} %get-tuple-element.40) | copy-start | bytes 1179652
  25.7 18.1 %collective-permute-start.2 = (f32[9,96,128]{2,1,0:T(8,128)}, f32[9,96,128]{2,1,0:T(8,128)}, u32[]{:S(2)}, u32[]{:S(2)}) collective-permute-start(f32[9,96,128]{2,1,0:T(8,128)} %pad_maximum_fusion.7), channel_id=1, source_target_pairs={{16,0},{32,16},{48,32},{64,48},{80,64},{96,80},{112,96},{128,112},... | collective-permute-start | bytes 1327112 | tf_op jit(solution)/shard_map/ppermute | solution.py:157
  39.9 8.6 %collective-permute-start.1 = (f32[8,96,128]{2,1,0:T(8,128)S(1)}, f32[8,96,128]{2,1,0:T(8,128)S(1)}, u32[]{:S(2)}, u32[]{:S(2)}) collective-permute-start(f32[8,96,128]{2,1,0:T(8,128)S(1)} %copy-done.3), channel_id=1, source_target_pairs={{0,16},{16,32},{32,48},{48,64},{64,80},{80,96},{96,112},{112,128},... | collective-permute-start | bytes 1179656 | tf_op jit(solution)/shard_map/ppermute | solution.py:153
  48.6 9.6 %collective-permute-start.4 = (f32[8,11,2,128]{3,2,1,0:T(2,128)S(1)}, f32[8,11,2,128]{3,2,1,0:T(2,128)S(1)}, u32[]{:S(2)}, u32[]{:S(2)}) collective-permute-start(f32[8,11,2,128]{3,2,1,0:T(2,128)S(1)} %pad_maximum_fusion.20), channel_id=1, source_target_pairs={{1,0},{2,1},{3,2},{4,3},{5,4},{6,5},{7,6},{8,7},{9,8},{10,9},{11,1... | collective-permute-start | bytes 270344 | tf_op jit(solution)/shard_map/ppermute | solution.py:170
  53.1 5.1 %collective-permute-start.3 = (f32[8,11,1,128]{3,2,1,0:T(1,128)S(1)}, f32[8,11,1,128]{3,2,1,0:T(1,128)S(1)}, u32[]{:S(2)}, u32[]{:S(2)}) collective-permute-start(f32[8,11,1,128]{3,2,1,0:T(1,128)S(1)} %pad_maximum_fusion.23), channel_id=1, source_target_pairs={{0,1},{1,2},{2,3},{3,4},{4,5},{5,6},{6,7},{7,8},{8,9},{9,10},{10,1... | collective-permute-start | bytes 135176 | tf_op jit(solution)/shard_map/ppermute | solution.py:167
  60.8 3.1 %copy-start = (f32[16,99,128]{2,1,0:T(8,128)S(1)}, f32[16,99,128]{2,1,0:T(8,128)}, u32[]{:S(2)}) copy-start(f32[16,99,128]{2,1,0:T(8,128)} %get-tuple-element.130) | copy-start | bytes 2433028
  60.8 3.2 %copy-start.1 = (f32[16,99,128]{2,1,0:T(8,128)S(1)}, f32[16,99,128]{2,1,0:T(8,128)}, u32[]{:S(2)}) copy-start(f32[16,99,128]{2,1,0:T(8,128)} %get-tuple-element.131) | copy-start | bytes 2433028
  87.9 4.0 %slice-start = ((s8[4685824]{0:T(1024)(128)(4,1)}), s8[491520]{0:T(1024)(128)(4,1)S(1)}, s32[]{:S(2)}) async-start(s8[4685824]{0:T(1024)(128)(4,1)} %bitcast.95), calls=%async_computation.2 | async-start | bytes 983040
  88.0 6.0 %collective-permute-start.6 = (f32[16,99,128]{2,0,1:T(8,128)S(1)}, f32[16,99,128]{2,0,1:T(8,128)S(1)}, u32[]{:S(2)}, u32[]{:S(2)}) collective-permute-start(f32[16,99,128]{2,0,1:T(8,128)S(1)} %copy.28), channel_id=1, source_target_pairs={{16,0},{224,240},{17,1},{225,241},{18,2},{226,242},{19,3},{227,243... | collective-permute-start | bytes 2433032 | tf_op jit(solution)/shard_map/ppermute | solution.py:207
  89.4 3.6 %slice-start.1 = ((s8[4685824]{0:T(1024)(128)(4,1)}), s8[4194304]{0:T(1024)(128)(4,1)S(1)}, s32[]{:S(2)}) async-start(s8[4685824]{0:T(1024)(128)(4,1)} %bitcast.95), calls=%async_computation.3 | async-start | bytes 8388608
  93.2 8.1 %collective-permute-start.5 = (f32[9,99,128]{2,1,0:T(8,128)S(1)}, f32[9,99,128]{2,1,0:T(8,128)S(1)}, u32[]{:S(2)}, u32[]{:S(2)}) collective-permute-start(f32[9,99,128]{2,1,0:T(8,128)S(1)} %fusion.30), channel_id=1, source_target_pairs={{0,8},{1,9},{2,10},{3,11},{4,12},{5,13},{6,14},{7,15},{8,0},{9,1},... | collective-permute-start | bytes 1368584 | tf_op jit(solution)/shard_map/ppermute | solution.py:215
  100.8 0.7 copy-start.4

commit v14 on v12

--- a/solution.py
+++ b/solution.py
@@ -148,12 +148,11 @@
     handed = lax.ppermute(rows_at(hand_first), "theta", pairs_out)
     work = jnp.where(helper, handed, rows_at(keep_first))
     per_device = half // phi_count
-    work, halo_src = lax.optimization_barrier((work, combined))
+    low_send = jnp.concatenate([f[:, ct - 1] for f in (density, velocity, bfield)], axis=0)
+    up_send = jnp.concatenate([f[:, 0] for f in (density, velocity, bfield)] + [bfield[1:2, 1]], axis=0)
+    work, low_send, up_send = lax.optimization_barrier((work, low_send, up_send))
     cycle = lax.all_to_all(work, "phi", split_axis=0, concat_axis=1, tiled=True)
-    low_halo = lax.ppermute(
-        halo_src[:, ct - 1], "theta", [(i, i + 1) for i in range(theta_count - 1)]
-    )
-    up_send = jnp.concatenate([halo_src[:, 0], halo_src[6:7, 1]], axis=0)
+    low_halo = lax.ppermute(low_send, "theta", [(i, i + 1) for i in range(theta_count - 1)])
     up_halo = lax.ppermute(up_send, "theta", [(i + 1, i) for i in range(theta_count - 1)])
     rows_ext = jnp.concatenate(
         [

time: 107 us -> 114 us (1.065)
  the two profiles are of different devices: /device:TPU:96 before, /device:TPU:34 now
where the time goes in v14:
time: 114 us
  blocking collectives  29.1 us (26%)
  other arithmetic  28.1 us (25%)
  starting transfers between devices  22 us (19%)
  waiting for transfers between devices  15 us (13%)
  local copies, waits for them, and re-layouts  13.7 us (12%)
  matrix products  3.96 us (3%)
  between operations  1.73 us (2%)
    all_to_all x1, blocking collectives, local(): mine = lax.all_to_all(out, 'phi', split_axis=0, concat_axis=0, tiled=True)  29.1 us
    all_to_all x1, starting transfers between devices, local(): cycle = lax.all_to_all(work, 'phi', split_axis=0, concat_axis=1, tiled=True)  9.5 us
    ppermute x1, waiting for transfers between devices, local(): lax.ppermute(ghost_send, both, [(a * phi_count + b, a * phi_count + (b +...  6.95 us
    ppermute x1, waiting for transfers between devices, local(): lax.ppermute(rows_ext[:, :, npc - 1:], 'phi', [(i, (i + 1) % phi_count) f...  6.42 us
    cos x1, other arithmetic, fourier_rows(): return jnp.concatenate([jnp.cos(angle), jnp.sin(angle)], axis=-1)  5.35 us
    sin x1, other arithmetic, fourier_rows(): return jnp.concatenate([jnp.cos(angle), jnp.sin(angle)], axis=-1)  4.28 us
    another operation x6, other arithmetic, advance(): return (jnp.stack(densities), jnp.stack([new_radial, new_theta, new_phi]))  4.05 us
    concatenate x1, other arithmetic, local(): early = jnp.concatenate([left_cols, rows_ext, right_cols], axis=2)  3.49 us
  transfers between devices with their start and end apart: 8, of which 3 were waited for; matrix products, arithmetic and copies ran while one was open for 22% of the time, Pallas kernels for 0%

profile of v14, /device:TPU:34, one launch (start us, length us, event | category | flops | bytes accessed | tf_op | source)
XLA Modules:
  0.0 113.6 jit_solution(10653442437473977172)
XLA Ops:
  0.6 1.1 constant_dynamic-slice_fusion.3
  1.7 1.3 %constant_dynamic-slice_fusion.1 = (f32[3,2,96,128]{3,2,1,0:T(8,128)S(1)}, f32[3,2,96,128]{3,2,1,0:T(8,128)S(1)}, f32[3,2,96,128]{3,2,1,0:T(8,128)S(1)}, f32[3,2,96,128]{3,2,1,0:T(8,128)S(1)}) fusion(f32[3,8,96,128]{3,2,1,0:T(8,128)} %param.7, s32[]{:T(128)S(6)} %select_n.153, s32[]{:T(128)S(6)} %select_n.152, f32[3,8,96,128]{3,2,1,0:T(8,128)} %param.6), kind=kLoop, calls=%fused_computation.161 | loop fusion | bytes 2359304 | tf_op jit(solution)/shard_map/dynamic_slice | solution.py:140
  4.1 2.8 %collective-permute-start = (f32[16,96,128]{2,1,0:T(8,128)}, f32[16,96,128]{2,1,0:T(8,128)}, u32[]{:S(2)}, u32[]{:S(2)}) collective-permute-start(f32[16,96,128]{2,1,0:T(8,128)} %bitcast.1), channel_id=1, source_target_pairs={{0,16},{240,224},{1,17},{241,225},{2,18},{242,226},{3,19},{243,227... | collective-permute-start | bytes 2359304 | tf_op jit(solution)/shard_map/ppermute | solution.py:148
  9.2 2.1 %copy.62 = f32[8,2,96,128]{3,2,0,1:T(8,128)} copy(f32[8,2,96,128]{3,2,1,0:T(8,128)} %pad_maximum_fusion.3) | data formatting | bytes 1572864 | tf_op jit(solution)/shard_map/concatenate | solution.py:141
  12.7 1.9 %pad_maximum_fusion.8 = f32[8,96,128]{2,1,0:T(8,128)} fusion(f32[3,96,128]{2,1,0:T(8,128)} %get-tuple-element.29, f32[3,96,128]{2,1,0:T(8,128)} %get-tuple-element.84, f32[2,96,128]{2,1,0:T(8,128)} %get-tuple-element.39), kind=kLoop, calls=%fused_computation.130 | loop fusion | flops 196608 | bytes 786432 | tf_op jit(solution)/shard_map/concatenate | solution.py:151
  15.4 4.3 %fusion.27 = (f32[1536,128]{1,0:T(8,128)}, f32[1536,128]{1,0:T(8,128)}) fusion(), kind=kLoop, calls=%fused_computation.37 | loop fusion | flops 1769472 | bytes 1572864 | tf_op jit(solution)/shard_map/sin | solution.py:110
  19.7 1.0 bitcast_select_fusion
  20.7 1.4 %collective-permute-start.2 = (f32[9,96,128]{2,1,0:T(8,128)}, f32[9,96,128]{2,1,0:T(8,128)}, u32[]{:S(2)}, u32[]{:S(2)}) collective-permute-start(f32[9,96,128]{2,1,0:T(8,128)} %pad_maximum_fusion.7), channel_id=1, source_target_pairs={{16,0},{32,16},{48,32},{64,48},{80,64},{96,80},{112,96},{128,112},... | collective-permute-start | bytes 1327112 | tf_op jit(solution)/shard_map/ppermute | solution.py:156
  22.2 9.5 %all-to-all-start = ((f32[16,96,128]{2,1,0:T(8,128)}), f32[16,96,128]{2,1,0:T(8,128)}, u32[]{:S(2)}, u32[]{:S(2)}) async-start(f32[16,96,128]{2,1,0:T(8,128)} %bitcast_select_fusion), calls=%async_computation | async-start | bytes 1572864 | tf_op jit(solution)/shard_map/all_to_all | solution.py:154
  31.7 5.4 %fusion.20 = (f32[16,99,128]{2,1,0:T(8,128)}, f32[16,99,128]{2,1,0:T(8,128)}) fusion(s32[16,99]{1,0:T(8,128)S(1)} %add_select_fusion.2), kind=kLoop, calls=%fused_computation.25 | loop fusion | flops 1824768 | bytes 1628352 | tf_op jit(solution)/shard_map/cos | solution.py:110
  37.1 2.5 %collective-permute-start.1 = (f32[8,96,128]{2,1,0:T(8,128)S(1)}, f32[8,96,128]{2,1,0:T(8,128)S(1)}, u32[]{:S(2)}, u32[]{:S(2)}) collective-permute-start(f32[8,96,128]{2,1,0:T(8,128)S(1)} %copy-done.6), channel_id=1, source_target_pairs={{0,16},{16,32},{32,48},{48,64},{64,80},{80,96},{96,112},{112,128},... | collective-permute-start | bytes 1179656 | tf_op jit(solution)/shard_map/ppermute | solution.py:155
  40.4 1.0 slice_bitcast_fusion.8
  41.5 1.5 %collective-permute-start.3 = (f32[8,11,1,128]{3,2,1,0:T(1,128)S(1)}, f32[8,11,1,128]{3,2,1,0:T(1,128)S(1)}, u32[]{:S(2)}, u32[]{:S(2)}) collective-permute-start(f32[8,11,1,128]{3,2,1,0:T(1,128)S(1)} %pad_maximum_fusion.20), channel_id=1, source_target_pairs={{0,1},{1,2},{2,3},{3,4},{4,5},{5,6},{6,7},{7,8},{8,9},{9,10},{10,1... | collective-permute-start | bytes 135176 | tf_op jit(solution)/shard_map/ppermute | solution.py:166
  43.7 6.4 %collective-permute-done.3 = f32[8,11,1,128]{3,2,1,0:T(1,128)S(1)} collective-permute-done((f32[8,11,1,128]{3,2,1,0:T(1,128)S(1)}, f32[8,11,1,128]{3,2,1,0:T(1,128)S(1)}, u32[]{:S(2)}, u32[]{:S(2)}) %collective-permute-start.3) | collective-permute-done | bytes 45088 | tf_op jit(solution)/shard_map/ppermute | solution.py:166
  50.1 1.6 %collective-permute-done.4 = f32[8,11,2,128]{3,2,1,0:T(2,128)S(1)} collective-permute-done((f32[8,11,2,128]{3,2,1,0:T(2,128)S(1)}, f32[8,11,2,128]{3,2,1,0:T(2,128)S(1)}, u32[]{:S(2)}, u32[]{:S(2)}) %collective-permute-start.4) | collective-permute-done | bytes 90144 | tf_op jit(solution)/shard_map/ppermute | solution.py:169
  51.8 3.5 %pad_maximum_fusion = f32[8,11,99,128]{3,2,1,0:T(8,128)} fusion(f32[8,11,2,128]{3,2,1,0:T(2,128)S(1)} %collective-permute-done.4, f32[8,1,96,128]{3,2,1,0:T(8,128)S(1)} %broadcast_in_dim_broadcast_in_dim.4, f32[8,1,96,128]{3,2,1,0:T(8,128)S(1)} %slice_bitcast_fusion.8, f32[3,8,96,128]{3,2,1,0:T(8,128)S(1)} %copy-done, f32[3,8,96,128]{3,2,1,0:T(8,128)S(1)} %copy-done.1, ...), kind=kLoop, calls=%fused_computation | loop fusion | flops 7805952 | bytes 8921088 | tf_op jit(solution)/shard_map/concatenate | solution.py:172
  55.3 3.1 %fusion.12 = f32[256,128,1]{1,0,2:T(8,128)S(1)} fusion(f32[1536,128]{1,0:T(8,128)} %get-tuple-element.86, f32[1536,128]{1,0:T(8,128)} %get-tuple-element.87, f32[1,1536,128]{2,1,0:T(8,128)} %bitcast.11, f32[256]{0:T(256)S(1)} %compare_select_fusion.1), kind=kOutput, calls=%fused_computation.18 | convolution fusion | flops 302415872 | bytes 2491392 | tf_op jit(solution)/shard_map/smr,mn->snr/dot_general | solution.py:200
  59.3 29.1 %all_to_all.17 = f32[16,99,128]{2,1,0:T(8,128)S(1)} all-to-all(f32[16,99,128]{2,1,0:T(8,128)S(1)} %fusion.1), channel_id=1, replica_groups=mesh['theta'=16,'phi'=16] {'phi'}, dimensions={0} | all-to-all | bytes 1622016 | tf_op jit(solution)/shard_map/all_to_all | solution.py:204
  88.6 2.2 %collective-permute-start.5 = (f32[9,99,128]{2,1,0:T(8,128)S(1)}, f32[9,99,128]{2,1,0:T(8,128)}, u32[]{:S(2)}, u32[]{:S(2)}) collective-permute-start(f32[9,99,128]{2,1,0:T(8,128)S(1)} %fusion.33), channel_id=1, source_target_pairs={{0,8},{1,9},{2,10},{3,11},{4,12},{5,13},{6,14},{7,15},{8,0},{9,1},... | collective-permute-start | bytes 1368584 | tf_op jit(solution)/shard_map/ppermute | solution.py:214
  90.9 1.5 %collective-permute-start.6 = (f32[16,99,128]{2,0,1:T(8,128)S(1)}, f32[16,99,128]{2,0,1:T(8,128)S(1)}, u32[]{:S(2)}, u32[]{:S(2)}) collective-permute-start(f32[16,99,128]{2,0,1:T(8,128)S(1)} %copy.43), channel_id=1, source_target_pairs={{16,0},{224,240},{17,1},{225,241},{18,2},{226,242},{19,3},{227,243... | collective-permute-start | bytes 2433032 | tf_op jit(solution)/shard_map/ppermute | solution.py:206
  92.4 7.0 %collective-permute-done.5 = f32[9,99,128]{2,1,0:T(8,128)} collective-permute-done((f32[9,99,128]{2,1,0:T(8,128)S(1)}, f32[9,99,128]{2,1,0:T(8,128)}, u32[]{:S(2)}, u32[]{:S(2)}) %collective-permute-start.5) | collective-permute-done | bytes 456224 | tf_op jit(solution)/shard_map/ppermute | solution.py:214
  100.2 1.1 fusion.39
  102.0 1.5 %slice-done.1 = s8[4194304]{0:T(1024)(128)(4,1)S(1)} async-done(((s8[4685824]{0:T(1024)(128)(4,1)}), s8[4194304]{0:T(1024)(128)(4,1)S(1)}, s32[]{:S(2)}) %slice-start.1) | async-done | bytes 4194328
  112.5 1.1 pad_maximum_fusion.1
  (87 shorter events, 18.1 us)
Async XLA Ops:
  3.0 3.8 %copy-start = (f32[3,8,96,128]{3,2,1,0:T(8,128)S(1)}, f32[3,8,96,128]{3,2,1,0:T(8,128)}, u32[]{:S(2)}) copy-start(f32[3,8,96,128]{3,2,1,0:T(8,128)} %param.7) | copy-start | bytes 3538948
  3.0 3.8 %copy-start.1 = (f32[3,8,96,128]{3,2,1,0:T(8,128)S(1)}, f32[3,8,96,128]{3,2,1,0:T(8,128)}, u32[]{:S(2)}) copy-start(f32[3,8,96,128]{3,2,1,0:T(8,128)} %param.6) | copy-start | bytes 3538948
  3.1 4.5 %copy-start.2 = (f32[2,8,96,128]{3,2,1,0:T(8,128)S(1)}, f32[2,8,96,128]{3,2,1,0:T(8,128)}, u32[]{:S(2)}) copy-start(f32[2,8,96,128]{3,2,1,0:T(8,128)} %param.5) | copy-start | bytes 2359300
  4.1 15.6 %collective-permute-start = (f32[16,96,128]{2,1,0:T(8,128)}, f32[16,96,128]{2,1,0:T(8,128)}, u32[]{:S(2)}, u32[]{:S(2)}) collective-permute-start(f32[16,96,128]{2,1,0:T(8,128)} %bitcast.1), channel_id=1, source_target_pairs={{0,16},{240,224},{1,17},{241,225},{2,18},{242,226},{3,19},{243,227... | collective-permute-start | bytes 2359304 | tf_op jit(solution)/shard_map/ppermute | solution.py:148
  7.6 3.7 %copy-start.8 = (s32[2,4]{1,0:T(2,128)S(1)}, s32[2,4]{1,0:T(2,128)}, u32[]{:S(2)}) copy-start(s32[2,4]{1,0:T(2,128)} %param.8) | copy-start | bytes 100
  12.7 7.0 %copy-start.5 = (f32[8,2,96,128]{3,2,0,1:T(8,128)S(1)}, f32[8,2,96,128]{3,2,0,1:T(8,128)}, u32[]{:S(2)}) copy-start(f32[8,2,96,128]{3,2,0,1:T(8,128)} %copy.62) | copy-start | bytes 2359300
  20.7 16.4 %copy-start.6 = (f32[8,96,128]{2,1,0:T(8,128)S(1)}, f32[8,96,128]{2,1,0:T(8,128)}, u32[]{:S(2)}) copy-start(f32[8,96,128]{2,1,0:T(8,128)} %pad_maximum_fusion.8) | copy-start | bytes 1179652
  20.7 18.9 %collective-permute-start.2 = (f32[9,96,128]{2,1,0:T(8,128)}, f32[9,96,128]{2,1,0:T(8,128)}, u32[]{:S(2)}, u32[]{:S(2)}) collective-permute-start(f32[9,96,128]{2,1,0:T(8,128)} %pad_maximum_fusion.7), channel_id=1, source_target_pairs={{16,0},{32,16},{48,32},{64,48},{80,64},{96,80},{112,96},{128,112},... | collective-permute-start | bytes 1327112 | tf_op jit(solution)/shard_map/ppermute | solution.py:156
  22.2 33.1 %all-to-all-start = ((f32[16,96,128]{2,1,0:T(8,128)}), f32[16,96,128]{2,1,0:T(8,128)}, u32[]{:S(2)}, u32[]{:S(2)}) async-start(f32[16,96,128]{2,1,0:T(8,128)} %bitcast_select_fusion), calls=%async_computation | async-start | bytes 1572864 | tf_op jit(solution)/shard_map/all_to_all | solution.py:154
  37.1 4.3 %collective-permute-start.1 = (f32[8,96,128]{2,1,0:T(8,128)S(1)}, f32[8,96,128]{2,1,0:T(8,128)S(1)}, u32[]{:S(2)}, u32[]{:S(2)}) collective-permute-start(f32[8,96,128]{2,1,0:T(8,128)S(1)} %copy-done.6), channel_id=1, source_target_pairs={{0,16},{16,32},{32,48},{48,64},{64,80},{80,96},{96,112},{112,128},... | collective-permute-start | bytes 1179656 | tf_op jit(solution)/shard_map/ppermute | solution.py:155
  41.5 8.7 %collective-permute-start.3 = (f32[8,11,1,128]{3,2,1,0:T(1,128)S(1)}, f32[8,11,1,128]{3,2,1,0:T(1,128)S(1)}, u32[]{:S(2)}, u32[]{:S(2)}) collective-permute-start(f32[8,11,1,128]{3,2,1,0:T(1,128)S(1)} %pad_maximum_fusion.20), channel_id=1, source_target_pairs={{0,1},{1,2},{2,3},{3,4},{4,5},{5,6},{6,7},{7,8},{8,9},{9,10},{10,1... | collective-permute-start | bytes 135176 | tf_op jit(solution)/shard_map/ppermute | solution.py:166
  43.1 8.7 %collective-permute-start.4 = (f32[8,11,2,128]{3,2,1,0:T(2,128)S(1)}, f32[8,11,2,128]{3,2,1,0:T(2,128)S(1)}, u32[]{:S(2)}, u32[]{:S(2)}) collective-permute-start(f32[8,11,2,128]{3,2,1,0:T(2,128)S(1)} %pad_maximum_fusion.15), channel_id=1, source_target_pairs={{1,0},{2,1},{3,2},{4,3},{5,4},{6,5},{7,6},{8,7},{9,8},{10,9},{11,1... | collective-permute-start | bytes 270344 | tf_op jit(solution)/shard_map/ppermute | solution.py:169
  55.3 3.1 %copy-start.3 = (f32[16,99,128]{2,1,0:T(8,128)S(1)}, f32[16,99,128]{2,1,0:T(8,128)}, u32[]{:S(2)}) copy-start(f32[16,99,128]{2,1,0:T(8,128)} %get-tuple-element.78) | copy-start | bytes 2433028
  55.3 3.2 %copy-start.4 = (f32[16,99,128]{2,1,0:T(8,128)S(1)}, f32[16,99,128]{2,1,0:T(8,128)}, u32[]{:S(2)}) copy-start(f32[16,99,128]{2,1,0:T(8,128)} %get-tuple-element.79) | copy-start | bytes 2433028
  88.4 13.6 %slice-start = ((s8[4685824]{0:T(1024)(128)(4,1)}), s8[491520]{0:T(1024)(128)(4,1)S(1)}, s32[]{:S(2)}) async-start(s8[4685824]{0:T(1024)(128)(4,1)} %bitcast.85), calls=%async_computation.2 | async-start | bytes 983040
  88.5 11.7 %copy-start.7 = (f32[8]{0:T(128)S(1)}, f32[8]{0:T(128)}, u32[]{:S(2)}) copy-start(f32[8]{0:T(128)} %constant.124.clone) | copy-start | bytes 100
  88.6 10.8 %collective-permute-start.5 = (f32[9,99,128]{2,1,0:T(8,128)S(1)}, f32[9,99,128]{2,1,0:T(8,128)}, u32[]{:S(2)}, u32[]{:S(2)}) collective-permute-start(f32[9,99,128]{2,1,0:T(8,128)S(1)} %fusion.33), channel_id=1, source_target_pairs={{0,8},{1,9},{2,10},{3,11},{4,12},{5,13},{6,14},{7,15},{8,0},{9,1},... | collective-permute-start | bytes 1368584 | tf_op jit(solution)/shard_map/ppermute | solution.py:214
  90.9 10.4 %collective-permute-start.6 = (f32[16,99,128]{2,0,1:T(8,128)S(1)}, f32[16,99,128]{2,0,1:T(8,128)S(1)}, u32[]{:S(2)}, u32[]{:S(2)}) collective-permute-start(f32[16,99,128]{2,0,1:T(8,128)S(1)} %copy.43), channel_id=1, source_target_pairs={{16,0},{224,240},{17,1},{225,241},{18,2},{226,242},{19,3},{227,243... | collective-permute-start | bytes 2433032 | tf_op jit(solution)/shard_map/ppermute | solution.py:206
  101.3 2.2 %slice-start.1 = ((s8[4685824]{0:T(1024)(128)(4,1)}), s8[4194304]{0:T(1024)(128)(4,1)S(1)}, s32[]{:S(2)}) async-start(s8[4685824]{0:T(1024)(128)(4,1)} %bitcast.85), calls=%async_computation.3 | async-start | bytes 8388608
  101.8 1.9 %slice-start.2 = ((f32[8,11,99,128]{3,2,1,0:T(8,128)}), f32[8,1,99,128]{3,2,1,0:T(8,128)S(1)}, s32[]{:S(2)}) async-start(f32[8,11,99,128]{3,2,1,0:T(8,128)} %pad_maximum_fusion), calls=%async_computation.4 | async-start | bytes 851968 | tf_op jit(solution)/shard_map/slice | solution.py:230

commit v15 on v12

--- a/solution.py
+++ b/solution.py
@@ -179,7 +179,7 @@
         - 1
         + jnp.arange(npc + 3, dtype=jnp.int32)[None, :]
     ) % cycle_len
-    synthesis = fourier_rows(dst_cols, cycle_len)
+    synthesis = jnp.take(analysis, dst_cols.reshape(-1), axis=0).reshape(phi_count, npc + 3, 2 * KMAX)
 
     pole_pick = jnp.where(north_side, 0, 1).astype(jnp.int32)
     level_row = lax.dynamic_index_in_dim(levels, pole_pick, 0, keepdims=False)

time: 107 us -> 114 us (1.065)
  the two profiles are of different devices: /device:TPU:96 before, /device:TPU:38 now
where the time goes in v15:
time: 114 us
  blocking collectives  30.6 us (27%)
  other arithmetic  22.7 us (20%)
  local copies, waits for them, and re-layouts  22.1 us (19%)
  starting transfers between devices  21.2 us (19%)
  waiting for transfers between devices  10.9 us (10%)
  matrix products  4.26 us (4%)
  between operations  1.79 us (2%)
    all_to_all x1, blocking collectives, local(): mine = lax.all_to_all(out, 'phi', split_axis=0, concat_axis=0, tiled=True)  30.6 us
    ppermute x1, waiting for transfers between devices, local(): lax.ppermute(halo_src[:, ct - 1], 'theta', [(i, i + 1) for i in range(the...  10.9 us
    all_to_all x1, starting transfers between devices, local(): cycle = lax.all_to_all(work, 'phi', split_axis=0, concat_axis=1, tiled=True)  9.5 us
    gather x2, local copies, waits for them, and re-layouts, local(): jnp.take(analysis, dst_cols.reshape(-1), axis=0)  8.25 us
    sin x1, other arithmetic, fourier_rows(): return jnp.concatenate([jnp.cos(angle), jnp.sin(angle)], axis=-1)  4.69 us
    another operation x6, other arithmetic, advance(): return (jnp.stack(densities), jnp.stack([new_radial, new_theta, new_phi]))  4.05 us
    unnamed x32, local copies, waits for them, and re-layouts  3.97 us
    ppermute x1, starting transfers between devices, local(): lax.ppermute(up_send, 'theta', [(i + 1, i) for i in range(theta_count - 1)])  3.73 us
  transfers between devices with their start and end apart: 8, of which 1 were waited for; matrix products, arithmetic and copies ran while one was open for 23% of the time, Pallas kernels for 0%

profile of v15, /device:TPU:38, one launch (start us, length us, event | category | flops | bytes accessed | tf_op | source)
XLA Modules:
  0.0 113.6 jit_solution(17840794217025808505)
XLA Ops:
  0.6 1.1 constant_dynamic-slice_fusion.3
  1.7 1.4 %constant_dynamic-slice_fusion.1 = (f32[3,2,96,128]{3,2,1,0:T(8,128)S(1)}, f32[3,2,96,128]{3,2,1,0:T(8,128)S(1)}, f32[3,2,96,128]{3,2,1,0:T(8,128)S(1)}, f32[3,2,96,128]{3,2,1,0:T(8,128)S(1)}) fusion(f32[3,8,96,128]{3,2,1,0:T(8,128)} %param.7, s32[]{:T(128)S(6)} %select_n.178, s32[]{:T(128)S(6)} %select_n.177, f32[3,8,96,128]{3,2,1,0:T(8,128)} %param.6), kind=kLoop, calls=%fused_computation.152 | loop fusion | bytes 2359304 | tf_op jit(solution)/shard_map/dynamic_slice | solution.py:140
  4.1 1.5 %collective-permute-start = (f32[16,96,128]{2,1,0:T(8,128)}, f32[16,96,128]{2,1,0:T(8,128)}, u32[]{:S(2)}, u32[]{:S(2)}) collective-permute-start(f32[16,96,128]{2,1,0:T(8,128)} %bitcast.1), channel_id=1, source_target_pairs={{0,16},{240,224},{1,17},{241,225},{2,18},{242,226},{3,19},{243,227... | collective-permute-start | bytes 2359304 | tf_op jit(solution)/shard_map/ppermute | solution.py:148
  6.9 1.4 %constant_dynamic-update-slice_fusion.1 = f32[8,8,96,128]{3,2,1,0:T(8,128)S(1)} fusion(f32[8,8,96,128]{3,2,1,0:T(8,128)S(1)} %constant_dynamic-update-slice_fusion.2, f32[3,8,96,128]{3,2,1,0:T(8,128)} %param.6), kind=kLoop, calls=%fused_computation.149 | loop fusion | bytes 2359296
  8.7 4.7 %fusion.11 = (f32[1536,128]{1,0:T(8,128)}, f32[1536,128]{1,0:T(8,128)}) fusion(), kind=kLoop, calls=%fused_computation.26 | loop fusion | flops 1769472 | bytes 1572864 | tf_op jit(solution)/shard_map/sin | solution.py:110
  13.4 1.0 bitcast_select_fusion
  15.3 3.7 %collective-permute-start.2 = (f32[9,96,128]{2,1,0:T(8,128)S(1)}, f32[9,96,128]{2,1,0:T(8,128)S(1)}, u32[]{:S(2)}, u32[]{:S(2)}) collective-permute-start(f32[9,96,128]{2,1,0:T(8,128)S(1)} %pad_maximum_fusion.8), channel_id=1, source_target_pairs={{16,0},{32,16},{48,32},{64,48},{80,64},{96,80},{112,96},{128,112},... | collective-permute-start | bytes 1327112 | tf_op jit(solution)/shard_map/ppermute | solution.py:157
  20.4 9.5 %all-to-all-start = ((f32[16,96,128]{2,1,0:T(8,128)}), f32[16,96,128]{2,1,0:T(8,128)}, u32[]{:S(2)}, u32[]{:S(2)}) async-start(f32[16,96,128]{2,1,0:T(8,128)} %bitcast_select_fusion), calls=%async_computation | async-start | bytes 1572864 | tf_op jit(solution)/shard_map/all_to_all | solution.py:152
  29.9 1.6 %pad_maximum_fusion.1 = f32[1536,256]{1,0:T(8,128)S(1)} fusion(f32[1536,128]{1,0:T(8,128)} %get-tuple-element.76, f32[1536,128]{1,0:T(8,128)} %get-tuple-element.77), kind=kLoop, calls=%fused_computation.9 | loop fusion | flops 393216 | bytes 3145728 | tf_op jit(solution)/shard_map/concatenate | solution.py:110
  31.6 1.9 %collective-permute-start.1 = (f32[8,96,128]{2,1,0:T(8,128)S(1)}, f32[8,96,128]{2,1,0:T(8,128)S(1)}, u32[]{:S(2)}, u32[]{:S(2)}) collective-permute-start(f32[8,96,128]{2,1,0:T(8,128)S(1)} %copy-done.10), channel_id=1, source_target_pairs={{0,16},{16,32},{32,48},{48,64},{64,80},{80,96},{96,112},{112,128},... | collective-permute-start | bytes 1179656 | tf_op jit(solution)/shard_map/ppermute | solution.py:153
  34.3 1.0 slice_bitcast_fusion.8
  35.3 10.9 %collective-permute-done.1 = f32[8,96,128]{2,1,0:T(8,128)S(1)} collective-permute-done((f32[8,96,128]{2,1,0:T(8,128)S(1)}, f32[8,96,128]{2,1,0:T(8,128)S(1)}, u32[]{:S(2)}, u32[]{:S(2)}) %collective-permute-start.1) | collective-permute-done | bytes 393248 | tf_op jit(solution)/shard_map/ppermute | solution.py:153
  47.0 1.6 %collective-permute-start.3 = (f32[8,11,1,128]{3,2,1,0:T(1,128)}, f32[8,11,1,128]{3,2,1,0:T(1,128)}, u32[]{:S(2)}, u32[]{:S(2)}) collective-permute-start(f32[8,11,1,128]{3,2,1,0:T(1,128)} %pad_maximum_fusion.18), channel_id=1, source_target_pairs={{0,1},{1,2},{2,3},{3,4},{4,5},{5,6},{6,7},{7,8},{8,9},{9,10},{10,1... | collective-permute-start | bytes 135176 | tf_op jit(solution)/shard_map/ppermute | solution.py:167
  49.8 5.3 %gather_fusion = f32[1584,256]{1,0:T(8,128)} fusion(f32[1536,256]{1,0:T(8,128)S(1)} %pad_maximum_fusion.1, s32[2048]{0:T(1024)S(1)} %pad_clamp_fusion), kind=kCustom, calls=%fused_computation | custom fusion | bytes 3250368 | tf_op jit(solution)/shard_map/jit(_take)/gather | solution.py:182
  55.0 3.0 %gather.7 = f32[16,99,256]{2,1,0:T(8,128)} reshape(f32[1584,256]{1,0:T(8,128)} %gather_fusion) | data formatting | bytes 3244032 | tf_op jit(solution)/shard_map/jit(_take)/gather | solution.py:182
  58.0 3.6 %pad_maximum_fusion = f32[8,11,99,128]{3,2,1,0:T(8,128)} fusion(f32[8,11,2,128]{3,2,1,0:T(2,128)} %collective-permute-done.4, f32[8,1,96,128]{3,2,1,0:T(8,128)} %copy-done.4, f32[8,1,96,128]{3,2,1,0:T(8,128)S(1)} %slice_bitcast_fusion.8, f32[8,8,96,128]{3,2,1,0:T(8,128)S(1)} %copy-done.2, f32[8,1,96,128]{3,2,1,0:T(8,128)} %bitcast.73, ...), kind=kLoop, calls=%fused_computation.1 | loop fusion | flops 5575680 | bytes 8921088 | tf_op jit(solution)/shard_map/concatenate | solution.py:173
  61.6 3.1 %fusion.3 = f32[256,128,1]{1,0,2:T(8,128)S(1)} fusion(f32[1,1536,128]{2,1,0:T(8,128)} %bitcast.4, f32[256]{0:T(256)S(1)} %compare_select_fusion.3, f32[1536,128]{1,0:T(8,128)} %get-tuple-element.76, f32[1536,128]{1,0:T(8,128)} %get-tuple-element.77), kind=kOutput, calls=%fused_computation.13 | convolution fusion | flops 302415872 | bytes 2491392 | tf_op jit(solution)/shard_map/smr,mn->snr/dot_general | solution.py:201
  64.8 1.1 fusion.1
  65.9 30.6 %all_to_all.17 = f32[16,99,128]{2,1,0:T(8,128)S(1)} all-to-all(f32[16,99,128]{2,1,0:T(8,128)S(1)} %fusion.1), channel_id=1, replica_groups=mesh['theta'=16,'phi'=16] {'phi'}, dimensions={0} | all-to-all | bytes 1622016 | tf_op jit(solution)/shard_map/all_to_all | solution.py:205
  96.6 1.6 %collective-permute-start.5 = (f32[9,99,128]{2,1,0:T(8,128)S(1)}, f32[9,99,128]{2,1,0:T(8,128)}, u32[]{:S(2)}, u32[]{:S(2)}) collective-permute-start(f32[9,99,128]{2,1,0:T(8,128)S(1)} %fusion.17), channel_id=1, source_target_pairs={{0,8},{1,9},{2,10},{3,11},{4,12},{5,13},{6,14},{7,15},{8,0},{9,1},... | collective-permute-start | bytes 1368584 | tf_op jit(solution)/shard_map/ppermute | solution.py:215
  100.2 1.1 fusion.23
  102.0 1.5 %slice-done.1 = s8[4194304]{0:T(1024)(128)(4,1)S(1)} async-done(((s8[4685824]{0:T(1024)(128)(4,1)}), s8[4194304]{0:T(1024)(128)(4,1)S(1)}, s32[]{:S(2)}) %slice-start.1) | async-done | bytes 4194328
  111.1 0.9 pad_maximum_fusion.5
  112.5 1.1 pad_maximum_fusion.2
  (102 shorter events, 17.4 us)
Async XLA Ops:
  1.7 3.9 %copy-start.8 = (f32[2,8,96,128]{3,2,1,0:T(8,128)S(1)}, f32[2,8,96,128]{3,2,1,0:T(8,128)}, u32[]{:S(2)}) copy-start(f32[2,8,96,128]{3,2,1,0:T(8,128)} %param.5) | copy-start | bytes 2359300
  4.1 9.3 %collective-permute-start = (f32[16,96,128]{2,1,0:T(8,128)}, f32[16,96,128]{2,1,0:T(8,128)}, u32[]{:S(2)}, u32[]{:S(2)}) collective-permute-start(f32[16,96,128]{2,1,0:T(8,128)} %bitcast.1), channel_id=1, source_target_pairs={{0,16},{240,224},{1,17},{241,225},{2,18},{242,226},{3,19},{243,227... | collective-permute-start | bytes 2359304 | tf_op jit(solution)/shard_map/ppermute | solution.py:148
  6.9 1.6 %copy-start.7 = (f32[3,8,96,128]{3,2,1,0:T(8,128)S(1)}, f32[3,8,96,128]{3,2,1,0:T(8,128)}, u32[]{:S(2)}) copy-start(f32[3,8,96,128]{3,2,1,0:T(8,128)} %param.7) | copy-start | bytes 3538948
  8.5 4.9 %copy-start.6 = (f32[8,2,96,128]{3,2,0,1:T(8,128)S(1)}, f32[8,2,96,128]{3,2,0,1:T(8,128)}, u32[]{:S(2)}) copy-start(f32[8,2,96,128]{3,2,0,1:T(8,128)} %copy.41) | copy-start | bytes 2359300
  8.6 6.6 %copy-start = (f32[8,8,96,128]{3,2,1,0:T(8,128)}, f32[8,8,96,128]{3,2,1,0:T(8,128)S(1)}, u32[]{:S(2)}) copy-start(f32[8,8,96,128]{3,2,1,0:T(8,128)S(1)} %constant_dynamic-update-slice_fusion) | copy-start | bytes 9437188
  13.4 5.7 %copy-start.12 = (s32[2,4]{1,0:T(2,128)S(1)}, s32[2,4]{1,0:T(2,128)}, u32[]{:S(2)}) copy-start(s32[2,4]{1,0:T(2,128)} %param.8) | copy-start | bytes 100
  15.3 16.3 %copy-start.10 = (f32[8,96,128]{2,1,0:T(8,128)S(1)}, f32[8,96,128]{2,1,0:T(8,128)}, u32[]{:S(2)}) copy-start(f32[8,96,128]{2,1,0:T(8,128)} %get-tuple-element.22) | copy-start | bytes 1179652
  15.3 18.2 %collective-permute-start.2 = (f32[9,96,128]{2,1,0:T(8,128)S(1)}, f32[9,96,128]{2,1,0:T(8,128)S(1)}, u32[]{:S(2)}, u32[]{:S(2)}) collective-permute-start(f32[9,96,128]{2,1,0:T(8,128)S(1)} %pad_maximum_fusion.8), channel_id=1, source_target_pairs={{16,0},{32,16},{48,32},{64,48},{80,64},{96,80},{112,96},{128,112},... | collective-permute-start | bytes 1327112 | tf_op jit(solution)/shard_map/ppermute | solution.py:157
  20.4 41.2 %all-to-all-start = ((f32[16,96,128]{2,1,0:T(8,128)}), f32[16,96,128]{2,1,0:T(8,128)}, u32[]{:S(2)}, u32[]{:S(2)}) async-start(f32[16,96,128]{2,1,0:T(8,128)} %bitcast_select_fusion), calls=%async_computation | async-start | bytes 1572864 | tf_op jit(solution)/shard_map/all_to_all | solution.py:152
  29.9 16.3 %copy-start.1 = (f32[8,8,96,128]{3,2,1,0:T(8,128)S(1)}, f32[8,8,96,128]{3,2,1,0:T(8,128)}, u32[]{:S(2)}) copy-start(f32[8,8,96,128]{3,2,1,0:T(8,128)} %copy-done) | copy-start | bytes 9437188
  31.6 14.6 %collective-permute-start.1 = (f32[8,96,128]{2,1,0:T(8,128)S(1)}, f32[8,96,128]{2,1,0:T(8,128)S(1)}, u32[]{:S(2)}, u32[]{:S(2)}) collective-permute-start(f32[8,96,128]{2,1,0:T(8,128)S(1)} %copy-done.10), channel_id=1, source_target_pairs={{0,16},{16,32},{32,48},{48,64},{64,80},{80,96},{96,112},{112,128},... | collective-permute-start | bytes 1179656 | tf_op jit(solution)/shard_map/ppermute | solution.py:153
  33.5 0.8 copy-start.9
  46.2 3.2 %copy-start.5 = (f32[8,96,128]{2,1,0:T(8,128)}, f32[8,96,128]{2,1,0:T(8,128)S(1)}, u32[]{:S(2)}) copy-start(f32[8,96,128]{2,1,0:T(8,128)S(1)} %collective-permute-done.1) | copy-start | bytes 1179652
  46.2 3.1 %copy-start.4 = (f32[8,1,96,128]{3,2,1,0:T(8,128)}, f32[8,1,96,128]{3,2,1,0:T(8,128)S(1)}, u32[]{:S(2)}) copy-start(f32[8,1,96,128]{3,2,1,0:T(8,128)S(1)} %broadcast_in_dim_broadcast_in_dim.4) | copy-start | bytes 1179652
  47.0 11.0 %collective-permute-start.3 = (f32[8,11,1,128]{3,2,1,0:T(1,128)}, f32[8,11,1,128]{3,2,1,0:T(1,128)}, u32[]{:S(2)}, u32[]{:S(2)}) collective-permute-start(f32[8,11,1,128]{3,2,1,0:T(1,128)} %pad_maximum_fusion.18), channel_id=1, source_target_pairs={{0,1},{1,2},{2,3},{3,4},{4,5},{5,6},{6,7},{7,8},{8,9},{9,10},{10,1... | collective-permute-start | bytes 135176 | tf_op jit(solution)/shard_map/ppermute | solution.py:167
  49.4 8.6 %collective-permute-start.4 = (f32[8,11,2,128]{3,2,1,0:T(2,128)}, f32[8,11,2,128]{3,2,1,0:T(2,128)}, u32[]{:S(2)}, u32[]{:S(2)}) collective-permute-start(f32[8,11,2,128]{3,2,1,0:T(2,128)} %pad_maximum_fusion.15), channel_id=1, source_target_pairs={{1,0},{2,1},{3,2},{4,3},{5,4},{6,5},{7,6},{8,7},{9,8},{10,9},{11,1... | collective-permute-start | bytes 270344 | tf_op jit(solution)/shard_map/ppermute | solution.py:170
  55.0 3.0 %copy-start.2 = (f32[8,8,96,128]{3,2,1,0:T(8,128)S(1)}, f32[8,8,96,128]{3,2,1,0:T(8,128)}, u32[]{:S(2)}) copy-start(f32[8,8,96,128]{3,2,1,0:T(8,128)} %copy-done) | copy-start | bytes 9437188
  61.6 3.1 %copy-start.3 = (f32[16,99,256]{2,1,0:T(8,128)S(1)}, f32[16,99,256]{2,1,0:T(8,128)}, u32[]{:S(2)}) copy-start(f32[16,99,256]{2,1,0:T(8,128)} %gather.7) | copy-start | bytes 4866052
  96.5 3.7 %copy-start.11 = (f32[8]{0:T(128)S(1)}, f32[8]{0:T(128)}, u32[]{:S(2)}) copy-start(f32[8]{0:T(128)} %constant.131.clone) | copy-start | bytes 100
  96.5 5.5 %slice-start = ((s8[4685824]{0:T(1024)(128)(4,1)}), s8[491520]{0:T(1024)(128)(4,1)S(1)}, s32[]{:S(2)}) async-start(s8[4685824]{0:T(1024)(128)(4,1)} %bitcast.67), calls=%async_computation.2 | async-start | bytes 983040
  96.6 2.7 %collective-permute-start.5 = (f32[9,99,128]{2,1,0:T(8,128)S(1)}, f32[9,99,128]{2,1,0:T(8,128)}, u32[]{:S(2)}, u32[]{:S(2)}) collective-permute-start(f32[9,99,128]{2,1,0:T(8,128)S(1)} %fusion.17), channel_id=1, source_target_pairs={{0,8},{1,9},{2,10},{3,11},{4,12},{5,13},{6,14},{7,15},{8,0},{9,1},... | collective-permute-start | bytes 1368584 | tf_op jit(solution)/shard_map/ppermute | solution.py:215
  98.4 2.9 %collective-permute-start.6 = (f32[16,99,128]{2,0,1:T(8,128)S(1)}, f32[16,99,128]{2,0,1:T(8,128)S(1)}, u32[]{:S(2)}, u32[]{:S(2)}) collective-permute-start(f32[16,99,128]{2,0,1:T(8,128)S(1)} %copy.28), channel_id=1, source_target_pairs={{16,0},{224,240},{17,1},{225,241},{18,2},{226,242},{19,3},{227,243... | collective-permute-start | bytes 2433032 | tf_op jit(solution)/shard_map/ppermute | solution.py:207
  101.3 2.2 %slice-start.1 = ((s8[4685824]{0:T(1024)(128)(4,1)}), s8[4194304]{0:T(1024)(128)(4,1)S(1)}, s32[]{:S(2)}) async-start(s8[4685824]{0:T(1024)(128)(4,1)} %bitcast.67), calls=%async_computation.3 | async-start | bytes 8388608
  101.8 1.9 %slice-start.2 = ((f32[8,11,99,128]{3,2,1,0:T(8,128)}), f32[8,1,99,128]{3,2,1,0:T(8,128)S(1)}, s32[]{:S(2)}) async-start(f32[8,11,99,128]{3,2,1,0:T(8,128)} %pad_maximum_fusion), calls=%async_computation.4 | async-start | bytes 851968 | tf_op jit(solution)/shard_map/slice | solution.py:231

commit v16 on v15

--- a/solution.py
+++ b/solution.py
@@ -173,13 +173,20 @@
     early = jnp.concatenate([left_cols, rows_ext, right_cols], axis=2)
 
     cycle, early = lax.optimization_barrier((cycle, early))
-    analysis = fourier_rows(jnp.arange(cycle_len, dtype=jnp.int32), cycle_len)
-    dst_cols = (
-        jnp.arange(phi_count, dtype=jnp.int32)[:, None] * npc
-        - 1
-        + jnp.arange(npc + 3, dtype=jnp.int32)[None, :]
-    ) % cycle_len
-    synthesis = jnp.take(analysis, dst_cols.reshape(-1), axis=0).reshape(phi_count, npc + 3, 2 * KMAX)
+    orders = jnp.arange(KMAX, dtype=jnp.int32)
+    scale = 2.0 * math.pi / cycle_len
+    block_phase = ((jnp.arange(phi_count, dtype=jnp.int32) * npc)[:, None] * orders) % cycle_len
+    ca = jnp.cos(block_phase.astype(jnp.float32) * scale)[:, None]
+    sa = jnp.sin(block_phase.astype(jnp.float32) * scale)[:, None]
+
+    def fourier_blocks(first, count):
+        inner = ((jnp.arange(count, dtype=jnp.int32) + first)[:, None] * orders) % cycle_len
+        cb = jnp.cos(inner.astype(jnp.float32) * scale)[None]
+        sb = jnp.sin(inner.astype(jnp.float32) * scale)[None]
+        return jnp.concatenate([ca * cb - sa * sb, sa * cb + ca * sb], axis=-1)
+
+    analysis = fourier_blocks(0, npc).reshape(cycle_len, 2 * KMAX)
+    synthesis = fourier_blocks(-1, npc + 3)
 
     pole_pick = jnp.where(north_side, 0, 1).astype(jnp.int32)
     level_row = lax.dynamic_index_in_dim(levels, pole_pick, 0, keepdims=False)

time: 114 us -> 106 us (0.930)
  the two profiles are of different devices: /device:TPU:38 before, /device:TPU:34 now
where the time goes in v16:
time: 106 us; the launch traced here: 105 us
  blocking collectives  29.1 us (27%)
  starting transfers between devices  21.7 us (20%)
  other arithmetic  21.2 us (20%)
  waiting for transfers between devices  14.7 us (14%)
  local copies, waits for them, and re-layouts  13.1 us (12%)
  matrix products  3.96 us (4%)
  between operations  1.63 us (2%)
    all_to_all x1, blocking collectives, local(): mine = lax.all_to_all(out, 'phi', split_axis=0, concat_axis=0, tiled=True)  29.1 us
    all_to_all x1, starting transfers between devices, local(): cycle = lax.all_to_all(work, 'phi', split_axis=0, concat_axis=1, tiled=True)  9.5 us
    ppermute x1, waiting for transfers between devices, local(): lax.ppermute(ghost_send, both, [(a * phi_count + b, a * phi_count + (b +...  6.98 us
    ppermute x1, waiting for transfers between devices, local(): lax.ppermute(rows_ext[:, :, npc - 1:], 'phi', [(i, (i + 1) % phi_count) f...  6.04 us
    another operation x6, other arithmetic, advance(): return (jnp.stack(densities), jnp.stack([new_radial, new_theta, new_phi]))  4.05 us
    sub x2, other arithmetic, fourier_blocks(): return jnp.concatenate([ca * cb - sa * sb, sa * cb + ca * sb], axis=-1)  3.59 us
    unnamed x18, local copies, waits for them, and re-layouts  3.19 us
    dot_general x1, matrix products, local(): jnp.einsum('smr,mn->snr', cycle, analysis, precision=lax.Precision.HIGH)  3.13 us
  transfers between devices with their start and end apart: 8, of which 3 were waited for; matrix products, arithmetic and copies ran while one was open for 16% of the time, Pallas kernels for 0%

profile of v16, /device:TPU:34, one launch (start us, length us, event | category | flops | bytes accessed | tf_op | source)
XLA Modules:
  0.0 105.4 jit_solution(2782599977882526260)
XLA Ops:
  0.6 1.1 %constant_dynamic-slice_fusion.3 = (f32[2,2,96,128]{3,2,1,0:T(8,128)S(1)}, f32[2,2,96,128]{3,2,1,0:T(8,128)S(1)}) fusion(f32[2,8,96,128]{3,2,1,0:T(8,128)} %param.5, s32[]{:T(128)S(6)} %select_n.174, s32[]{:T(128)S(6)} %select_n.173), kind=kLoop, calls=%fused_computation.167 | loop fusion | bytes 786440 | tf_op jit(solution)/shard_map/dynamic_slice | solution.py:140
  1.7 1.4 %constant_dynamic-slice_fusion.1 = (f32[3,2,96,128]{3,2,1,0:T(8,128)S(1)}, f32[3,2,96,128]{3,2,1,0:T(8,128)S(1)}, f32[3,2,96,128]{3,2,1,0:T(8,128)S(1)}, f32[3,2,96,128]{3,2,1,0:T(8,128)S(1)}) fusion(f32[3,8,96,128]{3,2,1,0:T(8,128)} %param.7, s32[]{:T(128)S(6)} %select_n.174, s32[]{:T(128)S(6)} %select_n.173, f32[3,8,96,128]{3,2,1,0:T(8,128)} %param.6), kind=kLoop, calls=%fused_computation.165 | loop fusion | bytes 2359304 | tf_op jit(solution)/shard_map/dynamic_slice | solution.py:140
  4.1 2.6 %collective-permute-start = (f32[16,96,128]{2,1,0:T(8,128)}, f32[16,96,128]{2,1,0:T(8,128)}, u32[]{:S(2)}, u32[]{:S(2)}) collective-permute-start(f32[16,96,128]{2,1,0:T(8,128)} %bitcast.1), channel_id=1, source_target_pairs={{0,16},{240,224},{1,17},{241,225},{2,18},{242,226},{3,19},{243,227... | collective-permute-start | bytes 2359304 | tf_op jit(solution)/shard_map/ppermute | solution.py:148
  8.6 1.4 %constant_dynamic-update-slice_fusion.1 = f32[8,8,96,128]{3,2,1,0:T(8,128)S(1)} fusion(f32[8,8,96,128]{3,2,1,0:T(8,128)S(1)} %constant_dynamic-update-slice_fusion.2, f32[3,8,96,128]{3,2,1,0:T(8,128)} %param.6), kind=kLoop, calls=%fused_computation.156 | loop fusion | bytes 2359296
  10.4 1.4 %multiply_subtract_fusion.1 = (f32[16,96,128]{2,1,0:T(8,128)}, f32[16,96,128]{2,1,0:T(8,128)}) fusion(f32[96,128]{1,0:T(8,128)S(1)} %get-tuple-element.84, f32[16,128]{1,0:T(8,128)S(1)} %get-tuple-element.81, f32[96,128]{1,0:T(8,128)S(1)} %get-tuple-element.85, f32[16,128]{1,0:T(8,128)S(1)} %get-tuple-element.80), kind=kLoop, calls=%fused_computation.25 | loop fusion | flops 1179648 | bytes 1687552 | tf_op jit(solution)/shard_map/sub | solution.py:186
  13.7 1.3 %collective-permute-start.2 = (f32[9,96,128]{2,1,0:T(8,128)}, f32[9,96,128]{2,1,0:T(8,128)}, u32[]{:S(2)}, u32[]{:S(2)}) collective-permute-start(f32[9,96,128]{2,1,0:T(8,128)} %pad_maximum_fusion.7), channel_id=1, source_target_pairs={{16,0},{32,16},{48,32},{64,48},{80,64},{96,80},{112,96},{128,112},... | collective-permute-start | bytes 1327112 | tf_op jit(solution)/shard_map/ppermute | solution.py:157
  14.9 9.5 %all-to-all-start = ((f32[16,96,128]{2,1,0:T(8,128)}), f32[16,96,128]{2,1,0:T(8,128)}, u32[]{:S(2)}, u32[]{:S(2)}) async-start(f32[16,96,128]{2,1,0:T(8,128)} %bitcast_select_fusion), calls=%async_computation | async-start | bytes 1572864 | tf_op jit(solution)/shard_map/all_to_all | solution.py:152
  24.5 1.6 %fusion.58 = (f32[99,128]{1,0:T(8,128)}, f32[99,128]{1,0:T(8,128)}) fusion(s32[99]{0:T(128)} %iota_add_fusion), kind=kLoop, calls=%fused_computation.139 | loop fusion | flops 114048 | bytes 101772 | tf_op jit(solution)/shard_map/cos | solution.py:184
  26.0 1.3 %fusion.74 = s32[]{:T(128)} fusion(s32[2,4]{1,0:T(2,128)} %param.8, s32[]{:T(128)S(6)} %select_n.184, s32[]{:T(128)} %bitcast.17), kind=kLoop, calls=%fused_computation.175 | loop fusion | flops 11 | bytes 28 | tf_op jit(solution)/shard_map/reduce_sum | solution.py:196
  27.9 2.2 %multiply_subtract_fusion = (f32[16,99,128]{2,1,0:T(8,128)}, f32[16,99,128]{2,1,0:T(8,128)}) fusion(f32[99,128]{1,0:T(8,128)} %get-tuple-element.79, f32[16,128]{1,0:T(8,128)S(1)} %get-tuple-element.81, f32[99,128]{1,0:T(8,128)} %get-tuple-element.78, f32[16,128]{1,0:T(8,128)S(1)} %get-tuple-element.80), kind=kLoop, calls=%fused_computation.18 | loop fusion | flops 1216512 | bytes 1739776 | tf_op jit(solution)/shard_map/sub | solution.py:186
  30.2 2.5 %collective-permute-start.1 = (f32[8,96,128]{2,1,0:T(8,128)S(1)}, f32[8,96,128]{2,1,0:T(8,128)S(1)}, u32[]{:S(2)}, u32[]{:S(2)}) collective-permute-start(f32[8,96,128]{2,1,0:T(8,128)S(1)} %get-tuple-element.22), channel_id=1, source_target_pairs={{0,16},{16,32},{32,48},{48,64},{64,80},{80,96},{96,112},{112,128},... | collective-permute-start | bytes 1179656 | tf_op jit(solution)/shard_map/ppermute | solution.py:153
  33.5 1.0 slice_bitcast_fusion.8
  34.6 1.5 %collective-permute-start.3 = (f32[8,11,1,128]{3,2,1,0:T(1,128)S(1)}, f32[8,11,1,128]{3,2,1,0:T(1,128)S(1)}, u32[]{:S(2)}, u32[]{:S(2)}) collective-permute-start(f32[8,11,1,128]{3,2,1,0:T(1,128)S(1)} %pad_maximum_fusion.17), channel_id=1, source_target_pairs={{0,1},{1,2},{2,3},{3,4},{4,5},{5,6},{6,7},{7,8},{8,9},{9,10},{10,1... | collective-permute-start | bytes 135176 | tf_op jit(solution)/shard_map/ppermute | solution.py:167
  36.8 6.0 %collective-permute-done.3 = f32[8,11,1,128]{3,2,1,0:T(1,128)S(1)} collective-permute-done((f32[8,11,1,128]{3,2,1,0:T(1,128)S(1)}, f32[8,11,1,128]{3,2,1,0:T(1,128)S(1)}, u32[]{:S(2)}, u32[]{:S(2)}) %collective-permute-start.3) | collective-permute-done | bytes 45088 | tf_op jit(solution)/shard_map/ppermute | solution.py:167
  42.9 1.7 %collective-permute-done.4 = f32[8,11,2,128]{3,2,1,0:T(2,128)S(1)} collective-permute-done((f32[8,11,2,128]{3,2,1,0:T(2,128)S(1)}, f32[8,11,2,128]{3,2,1,0:T(2,128)S(1)}, u32[]{:S(2)}, u32[]{:S(2)}) %collective-permute-start.4) | collective-permute-done | bytes 90144 | tf_op jit(solution)/shard_map/ppermute | solution.py:170
  44.5 2.6 %pad_maximum_fusion = f32[8,11,99,128]{3,2,1,0:T(8,128)} fusion(f32[8,11,2,128]{3,2,1,0:T(2,128)S(1)} %collective-permute-done.4, f32[8,1,96,128]{3,2,1,0:T(8,128)S(1)} %broadcast_in_dim_broadcast_in_dim.4, f32[8,1,96,128]{3,2,1,0:T(8,128)S(1)} %slice_bitcast_fusion.8, f32[8,8,96,128]{3,2,1,0:T(8,128)S(1)} %constant_dynamic-update-slice_fusion, ...), kind=kLoop, calls=%fused_computation | loop fusion | flops 5575680 | bytes 8921088 | tf_op jit(solution)/shard_map/concatenate | solution.py:173
  47.1 3.1 %fusion.12 = f32[256,128,1]{1,0,2:T(8,128)S(1)} fusion(f32[1536,128]{1,0:T(8,128)} %bitcast.77, f32[1536,128]{1,0:T(8,128)} %bitcast.76, f32[1,1536,128]{2,1,0:T(8,128)} %bitcast.4, f32[256]{0:T(256)S(1)} %compare_select_fusion.1), kind=kOutput, calls=%fused_computation.16 | convolution fusion | flops 302415872 | bytes 2491392 | tf_op jit(solution)/shard_map/smr,mn->snr/dot_general | solution.py:208
  51.1 29.1 %all_to_all.17 = f32[16,99,128]{2,1,0:T(8,128)S(1)} all-to-all(f32[16,99,128]{2,1,0:T(8,128)S(1)} %fusion.1), channel_id=1, replica_groups=mesh['theta'=16,'phi'=16] {'phi'}, dimensions={0} | all-to-all | bytes 1622016 | tf_op jit(solution)/shard_map/all_to_all | solution.py:212
  80.3 2.2 %collective-permute-start.5 = (f32[9,99,128]{2,1,0:T(8,128)S(1)}, f32[9,99,128]{2,1,0:T(8,128)}, u32[]{:S(2)}, u32[]{:S(2)}) collective-permute-start(f32[9,99,128]{2,1,0:T(8,128)S(1)} %fusion.19), channel_id=1, source_target_pairs={{0,8},{1,9},{2,10},{3,11},{4,12},{5,13},{6,14},{7,15},{8,0},{9,1},... | collective-permute-start | bytes 1368584 | tf_op jit(solution)/shard_map/ppermute | solution.py:222
  82.6 1.5 %collective-permute-start.6 = (f32[16,99,128]{2,0,1:T(8,128)S(1)}, f32[16,99,128]{2,0,1:T(8,128)S(1)}, u32[]{:S(2)}, u32[]{:S(2)}) collective-permute-start(f32[16,99,128]{2,0,1:T(8,128)S(1)} %copy.28), channel_id=1, source_target_pairs={{16,0},{224,240},{17,1},{225,241},{18,2},{226,242},{19,3},{227,243... | collective-permute-start | bytes 2433032 | tf_op jit(solution)/shard_map/ppermute | solution.py:214
  84.1 7.0 %collective-permute-done.5 = f32[9,99,128]{2,1,0:T(8,128)} collective-permute-done((f32[9,99,128]{2,1,0:T(8,128)S(1)}, f32[9,99,128]{2,1,0:T(8,128)}, u32[]{:S(2)}, u32[]{:S(2)}) %collective-permute-start.5) | collective-permute-done | bytes 456224 | tf_op jit(solution)/shard_map/ppermute | solution.py:222
  91.9 1.1 %fusion.25 = f32[8,1,99,128]{3,2,1,0:T(8,128)S(1)} fusion(f32[9,99,128]{2,1,0:T(8,128)} %collective-permute-done.5, f32[8]{0:T(128)S(1)} %copy-done.5), kind=kLoop, calls=%fused_computation.71 | loop fusion | flops 101376 | bytes 811040 | tf_op jit(solution)/shard_map/broadcast_in_dim | solution.py:238
  93.8 1.5 %slice-done.1 = s8[4194304]{0:T(1024)(128)(4,1)S(1)} async-done(((s8[4685824]{0:T(1024)(128)(4,1)}), s8[4194304]{0:T(1024)(128)(4,1)S(1)}, s32[]{:S(2)}) %slice-start.1) | async-done | bytes 4194328
  104.3 1.1 %pad_maximum_fusion.1 = f32[3,8,96,128]{3,2,1,0:T(8,128)} fusion(f32[1,8,96,128]{3,2,1,0:T(8,128)S(1)} %get-tuple-element.71, f32[1,8,96,128]{3,2,1,0:T(8,128)S(1)} %get-tuple-element.70, f32[1,8,96,128]{3,2,1,0:T(8,128)S(1)} %fusion.41), kind=kLoop, calls=%fused_computation.14 | loop fusion | flops 589824 | bytes 2359296 | tf_op jit(solution)/shard_map/stack | solution.py:103
  (85 shorter events, 18.1 us)
Async XLA Ops:
  1.7 5.0 %copy-start.4 = (f32[2,8,96,128]{3,2,1,0:T(8,128)S(1)}, f32[2,8,96,128]{3,2,1,0:T(8,128)}, u32[]{:S(2)}) copy-start(f32[2,8,96,128]{3,2,1,0:T(8,128)} %param.5) | copy-start | bytes 2359300
  4.1 7.7 %collective-permute-start = (f32[16,96,128]{2,1,0:T(8,128)}, f32[16,96,128]{2,1,0:T(8,128)}, u32[]{:S(2)}, u32[]{:S(2)}) collective-permute-start(f32[16,96,128]{2,1,0:T(8,128)} %bitcast.1), channel_id=1, source_target_pairs={{0,16},{240,224},{1,17},{241,225},{2,18},{242,226},{3,19},{243,227... | collective-permute-start | bytes 2359304 | tf_op jit(solution)/shard_map/ppermute | solution.py:148
  8.6 1.6 %copy-start.3 = (f32[3,8,96,128]{3,2,1,0:T(8,128)S(1)}, f32[3,8,96,128]{3,2,1,0:T(8,128)}, u32[]{:S(2)}) copy-start(f32[3,8,96,128]{3,2,1,0:T(8,128)} %param.7) | copy-start | bytes 3538948
  10.2 1.6 %copy-start.2 = (f32[8,2,96,128]{3,2,0,1:T(8,128)S(1)}, f32[8,2,96,128]{3,2,0,1:T(8,128)}, u32[]{:S(2)}) copy-start(f32[8,2,96,128]{3,2,0,1:T(8,128)} %copy.41) | copy-start | bytes 2359300
  13.7 19.0 %collective-permute-start.2 = (f32[9,96,128]{2,1,0:T(8,128)}, f32[9,96,128]{2,1,0:T(8,128)}, u32[]{:S(2)}, u32[]{:S(2)}) collective-permute-start(f32[9,96,128]{2,1,0:T(8,128)} %pad_maximum_fusion.7), channel_id=1, source_target_pairs={{16,0},{32,16},{48,32},{64,48},{80,64},{96,80},{112,96},{128,112},... | collective-permute-start | bytes 1327112 | tf_op jit(solution)/shard_map/ppermute | solution.py:157
  14.9 32.1 %all-to-all-start = ((f32[16,96,128]{2,1,0:T(8,128)}), f32[16,96,128]{2,1,0:T(8,128)}, u32[]{:S(2)}, u32[]{:S(2)}) async-start(f32[16,96,128]{2,1,0:T(8,128)} %bitcast_select_fusion), calls=%async_computation | async-start | bytes 1572864 | tf_op jit(solution)/shard_map/all_to_all | solution.py:152
  30.2 4.3 %collective-permute-start.1 = (f32[8,96,128]{2,1,0:T(8,128)S(1)}, f32[8,96,128]{2,1,0:T(8,128)S(1)}, u32[]{:S(2)}, u32[]{:S(2)}) collective-permute-start(f32[8,96,128]{2,1,0:T(8,128)S(1)} %get-tuple-element.22), channel_id=1, source_target_pairs={{0,16},{16,32},{32,48},{48,64},{64,80},{80,96},{96,112},{112,128},... | collective-permute-start | bytes 1179656 | tf_op jit(solution)/shard_map/ppermute | solution.py:153
  34.6 8.3 %collective-permute-start.3 = (f32[8,11,1,128]{3,2,1,0:T(1,128)S(1)}, f32[8,11,1,128]{3,2,1,0:T(1,128)S(1)}, u32[]{:S(2)}, u32[]{:S(2)}) collective-permute-start(f32[8,11,1,128]{3,2,1,0:T(1,128)S(1)} %pad_maximum_fusion.17), channel_id=1, source_target_pairs={{0,1},{1,2},{2,3},{3,4},{4,5},{5,6},{6,7},{7,8},{8,9},{9,10},{10,1... | collective-permute-start | bytes 135176 | tf_op jit(solution)/shard_map/ppermute | solution.py:167
  36.2 8.3 %collective-permute-start.4 = (f32[8,11,2,128]{3,2,1,0:T(2,128)S(1)}, f32[8,11,2,128]{3,2,1,0:T(2,128)S(1)}, u32[]{:S(2)}, u32[]{:S(2)}) collective-permute-start(f32[8,11,2,128]{3,2,1,0:T(2,128)S(1)} %pad_maximum_fusion.14), channel_id=1, source_target_pairs={{1,0},{2,1},{3,2},{4,3},{5,4},{6,5},{7,6},{8,7},{9,8},{10,9},{11,1... | collective-permute-start | bytes 270344 | tf_op jit(solution)/shard_map/ppermute | solution.py:170
  47.1 3.1 %copy-start = (f32[16,99,128]{2,1,0:T(8,128)S(1)}, f32[16,99,128]{2,1,0:T(8,128)}, u32[]{:S(2)}) copy-start(f32[16,99,128]{2,1,0:T(8,128)} %get-tuple-element.72) | copy-start | bytes 2433028
  47.1 3.2 %copy-start.1 = (f32[16,99,128]{2,1,0:T(8,128)S(1)}, f32[16,99,128]{2,1,0:T(8,128)}, u32[]{:S(2)}) copy-start(f32[16,99,128]{2,1,0:T(8,128)} %get-tuple-element.73) | copy-start | bytes 2433028
  80.2 11.8 %copy-start.5 = (f32[8]{0:T(128)S(1)}, f32[8]{0:T(128)}, u32[]{:S(2)}) copy-start(f32[8]{0:T(128)} %constant.124.clone) | copy-start | bytes 100
  80.2 13.6 %slice-start = ((s8[4685824]{0:T(1024)(128)(4,1)}), s8[491520]{0:T(1024)(128)(4,1)S(1)}, s32[]{:S(2)}) async-start(s8[4685824]{0:T(1024)(128)(4,1)} %bitcast.69), calls=%async_computation.2 | async-start | bytes 983040
  80.3 10.8 %collective-permute-start.5 = (f32[9,99,128]{2,1,0:T(8,128)S(1)}, f32[9,99,128]{2,1,0:T(8,128)}, u32[]{:S(2)}, u32[]{:S(2)}) collective-permute-start(f32[9,99,128]{2,1,0:T(8,128)S(1)} %fusion.19), channel_id=1, source_target_pairs={{0,8},{1,9},{2,10},{3,11},{4,12},{5,13},{6,14},{7,15},{8,0},{9,1},... | collective-permute-start | bytes 1368584 | tf_op jit(solution)/shard_map/ppermute | solution.py:222
  82.6 10.4 %collective-permute-start.6 = (f32[16,99,128]{2,0,1:T(8,128)S(1)}, f32[16,99,128]{2,0,1:T(8,128)S(1)}, u32[]{:S(2)}, u32[]{:S(2)}) collective-permute-start(f32[16,99,128]{2,0,1:T(8,128)S(1)} %copy.28), channel_id=1, source_target_pairs={{16,0},{224,240},{17,1},{225,241},{18,2},{226,242},{19,3},{227,243... | collective-permute-start | bytes 2433032 | tf_op jit(solution)/shard_map/ppermute | solution.py:214
  93.1 2.2 %slice-start.1 = ((s8[4685824]{0:T(1024)(128)(4,1)}), s8[4194304]{0:T(1024)(128)(4,1)S(1)}, s32[]{:S(2)}) async-start(s8[4685824]{0:T(1024)(128)(4,1)} %bitcast.69), calls=%async_computation.3 | async-start | bytes 8388608
  93.6 1.9 %slice-start.2 = ((f32[8,11,99,128]{3,2,1,0:T(8,128)}), f32[8,1,99,128]{3,2,1,0:T(8,128)S(1)}, s32[]{:S(2)}) async-start(f32[8,11,99,128]{3,2,1,0:T(8,128)} %pad_maximum_fusion), calls=%async_computation.4 | async-start | bytes 851968 | tf_op jit(solution)/shard_map/slice | solution.py:238
